TPU v7x, 128 devices: a whole 4x4x4 slice. The times are simulated.
128 devices in a mesh: req: 32 (over z, y, core), seq: 4 (over x).
Axes of the slice: x: 4, y: 4, z: 4, core: 2. Of those that a mesh axis runs over, the one named last changes fastest.
Arguments:
- hidden: bfloat16 [32, 4, 512, 2048], P('req', 'seq'), may hold values from -6 to 6
- w_in: bfloat16 [2048, 4384], P('req', 'seq'), may hold values from -0.125 to 0.125
- conv_weight: float32 [4, 2304], replicated, may hold values from -3 to 3
- conv_bias: float32 [2304], replicated, may hold values from -0.5 to 0.5
- dt_bias: float32 [32], replicated, may hold values from -5 to -2
- a_log: float32 [32], replicated, may hold values from -12 to 2
- d_skip: float32 [32], replicated, may hold values from 0.5 to 1.5
- norm_weight: float32 [2048], replicated, may hold values from 0.5 to 1.5
- lengths: int32 [32], replicated, may hold values from 4 to 512, as said below
- prompt_group: int32 [32], replicated, may hold values from 0 to 31, each once
Outputs:
- gated_out: bfloat16 [32, 4, 512, 2048], P('req', 'seq')
- final_states: float32 [32, 32, 64, 128], P(None, 'req', 'seq')
Inputs may be any that keep to these rules, and one draw needn't show every extreme that they name: Every prompt has 4 * lengths[p] tokens; some prompt has exactly 512 a device. Group prompt_group[p] holds prompt p; each group holds one prompt.
All inputs are finite; a program needn't handle non-finite values.
Results may differ from a plain program's by a relative error of at most 0.0059.
Values may be sent and summed in bfloat16 or wider, within the bound.
No kernel may reach another device: no remote copies, remote signals or barrier semaphores. Data moves between devices by JAX's collectives and lax.ppermute only.
A program may use at most 128 MiB of HBM per device.

v0:
```python
import jax
import jax.numpy as jnp
from jax import lax
from jax.sharding import PartitionSpec as P

BLOCK = 256


def shifted(block, axis, distance):
    devices = range(lax.axis_size(axis))
    route = [(i - distance, i) for i in devices if i - distance in devices]
    return lax.ppermute(block, axis, route)


def block_step(state, pieces):
    inputs_x, b_rows, c_rows, step_dt, log_decay = pieces
    length = inputs_x.shape[0]
    heads = step_dt.shape[1]
    hdim = inputs_x.shape[1] // heads
    running = jnp.cumsum(log_decay, axis=0)
    gram = jnp.einsum("tn,un->tu", c_rows, b_rows, preferred_element_type=jnp.float32)
    later = jnp.arange(length)[:, None] >= jnp.arange(length)[None, :]
    spread = running.T[:, :, None] - running.T[:, None, :]
    decay = jnp.where(later[None], jnp.exp(jnp.where(later[None], spread, 0.0)), 0.0)
    mixing = (gram[None] * decay * step_dt.T[:, None, :]).astype(jnp.bfloat16)
    heads_x = inputs_x.reshape(length, heads, hdim)
    inside = jnp.einsum("htu,uhp->thp", mixing, heads_x, preferred_element_type=jnp.float32)
    carried = jnp.exp(running)[:, :, None] * jnp.einsum(
        "tn,hpn->thp", c_rows.astype(jnp.float32), state, precision=lax.Precision.HIGHEST
    )
    final_log = running[-1]
    weighting = jnp.exp(final_log[None, :] - running) * step_dt
    weighted = (
        (heads_x.astype(jnp.float32) * weighting[:, :, None])
        .astype(jnp.bfloat16)
        .reshape(length, heads * hdim)
    )
    contrib = jnp.einsum("ud,un->dn", weighted, b_rows, preferred_element_type=jnp.float32).reshape(
        heads, hdim, -1
    )
    new_state = jnp.exp(final_log)[:, None, None] * state + contrib
    return (new_state, (inside + carried).reshape(length, heads * hdim))


def local(
    hidden, w_in, conv_weight, conv_bias, dt_bias, a_log, d_skip, norm_weight, lengths, prompt_group
):
    tok_rows = hidden[0, 0]
    slots = tok_rows.shape[0]
    inner = norm_weight.shape[0]
    heads = dt_bias.shape[0]
    hdim = inner // heads
    nstate = (conv_bias.shape[0] - inner) // 2
    convdim = conv_bias.shape[0]
    taps = conv_weight.shape[0]
    seq_count = lax.axis_size("seq")
    my_group = lax.axis_index("req")
    my_block = lax.axis_index("seq")
    qlen = jnp.sum(jnp.where(prompt_group == my_group, lengths, 0))
    filled = jnp.arange(slots, dtype=jnp.int32) < qlen
    wide_rows = lax.all_gather(w_in, "seq", axis=1, tiled=True)
    projected = jnp.dot(
        tok_rows,
        lax.all_gather(wide_rows, "req", axis=0, tiled=True),
        preferred_element_type=jnp.float32,
    ).astype(jnp.bfloat16)
    gate_z = projected[:, :inner]
    conv_in = projected[:, inner : inner + convdim]
    dt_raw = projected[:, inner + convdim :]
    edge_rows = lax.dynamic_slice_in_dim(conv_in, qlen - (taps - 1), taps - 1, 0)
    prev_edge = shifted(edge_rows, "seq", 1)
    extended = jnp.concatenate([prev_edge, conv_in], axis=0)
    accum = jnp.zeros((slots, convdim), jnp.float32) + conv_bias[None, :]
    for tap_index in range(taps):
        accum = accum + conv_weight[tap_index][None, :] * extended[
            tap_index : tap_index + slots
        ].astype(jnp.float32)
    conv_act = jax.nn.silu(accum).astype(jnp.bfloat16)
    inputs_x = conv_act[:, :inner]
    b_rows = conv_act[:, inner : inner + nstate]
    c_rows = conv_act[:, inner + nstate :]
    step_dt = jnp.where(
        filled[:, None], jax.nn.softplus(dt_raw.astype(jnp.float32) + dt_bias[None, :]), 0.0
    )
    log_decay = step_dt * (-jnp.exp(a_log))[None, :]
    through = jnp.cumsum(log_decay, axis=0)
    block_total = through[-1]
    block_rows = min(BLOCK, slots)
    count = slots // block_rows
    pieces = (
        inputs_x.reshape(count, block_rows, inner),
        b_rows.reshape(count, block_rows, nstate),
        c_rows.reshape(count, block_rows, nstate),
        step_dt.reshape(count, block_rows, heads),
        log_decay.reshape(count, block_rows, heads),
    )
    zero_state = jnp.zeros((heads, hdim, nstate), jnp.float32)
    local_end, outputs = lax.scan(block_step, zero_state, pieces)
    decays_all = lax.all_gather(block_total[None, :], "seq", axis=0, tiled=True)
    after_mine = jnp.sum(
        jnp.where(jnp.arange(seq_count)[:, None] > my_block, decays_all, 0.0), axis=0
    )
    entering = zero_state
    for turn in range(seq_count - 1):
        entering = shifted(jnp.exp(block_total)[:, None, None] * entering + local_end, "seq", 1)
    incoming = jnp.exp(through)[:, :, None] * jnp.einsum(
        "tn,hpn->thp", c_rows.astype(jnp.float32), entering, precision=lax.Precision.HIGHEST
    )
    heads_y = (
        outputs.reshape(slots, heads, hdim)
        + incoming
        + d_skip[None, :, None] * inputs_x.astype(jnp.float32).reshape(slots, heads, hdim)
    )
    gated = heads_y.reshape(slots, inner) * jax.nn.silu(gate_z.astype(jnp.float32))
    scale = lax.rsqrt(jnp.mean(gated * gated, axis=1, keepdims=True) + 1e-05)
    normed = jnp.where(filled[:, None], gated * scale * norm_weight[None, :], 0.0)
    gated_out = normed.astype(jnp.bfloat16).reshape(1, 1, slots, inner)
    decayed_end = jnp.exp(after_mine)[:, None, None] * local_end
    share = lax.psum_scatter(decayed_end, "seq", scatter_dimension=1, tiled=True)
    moved = lax.all_to_all(share[None], "req", split_axis=1, concat_axis=0, tiled=True)
    final_states = jnp.take(moved, prompt_group, axis=0)
    return (gated_out, final_states)


def solution(mesh):
    in_specs = (
        P("req", "seq", None, None),
        P("req", "seq"),
        P(),
        P(),
        P(),
        P(),
        P(),
        P(),
        P(),
        P(),
    )
    out_specs = (P("req", "seq", None, None), P(None, "req", "seq", None))
    return jax.shard_map(local, mesh=mesh, in_specs=in_specs, out_specs=out_specs, check_vma=False)
```

profile of v0, /device:TPU:1, one launch (start us, length us, event | category | flops | bytes accessed | tf_op | source)
XLA Modules:
  0.0 385.4 jit_solution(3540427270740208996)
XLA Ops:
  7.2 12.8 %all-gather = bf16[4,1096,64]{1,2,0:T(8,128)(2,1)S(1)} all-gather(bf16[1,1096,64]{1,2,0:T(8,128)(2,1)} %bitcast.173), channel_id=1, replica_groups=mesh['req'=32,'seq'=4] {'seq'}, dimensions={0}, use_global_device_ids=true | all-gather | bytes 701440 | tf_op jit(solution)/shard_map/all_gather | solution.py:61
  26.8 75.9 %all-gather.4.cloned.1.call-done = bf16[2048,4384]{1,0:T(8,128)(2,1)} async-done(((bf16[64,4384]{1,0:T(8,128)(2,1)}), bf16[2048,4384]{1,0:T(8,128)(2,1)}) %all-gather.4.cloned.1.call-update) | async-done | bytes 17956880 | tf_op jit(solution)/shard_map/all_gather | solution.py:64
  102.7 15.3 %convolution_convert_fusion = bf16[512,4384]{0,1:T(8,128)(2,1)} fusion(bf16[2048,4384]{1,0:T(8,128)(2,1)} %all-gather.4.cloned.1.call-done, bf16[1,1,512,2048]{3,2,1,0:T(8,128)(2,1)S(1)} %copy-done), kind=kOutput, calls=%fused_computation.45 | convolution fusion | flops 9196158976 | bytes 24543232 | tf_op jit(solution)/shard_map/dot_general | solution.py:62
  121.8 3.3 collective-permute-start
  129.8 10.5 %multiply_convert_fusion.4 = bf16[512,2304]{0,1:T(8,128)(2,1)S(1)} fusion(bf16[512,2304]{0,1:T(8,128)(2,1)} %copy-done.5, bf16[3,2304]{0,1:T(8,128)(2,1)S(1)} %copy.57, f32[2304]{0:T(1024)S(1)} %get-tuple-element.118, f32[2304]{0:T(1024)S(1)} %get-tuple-element.119, f32[2304]{0:T(1024)S(1)} %get-tuple-element.117, f32[2304]{0:T(1024)S(1)} %get-tuple-element.116, ...), kind=kLoop, calls=%fused_computation.48 | loop fusion | flops 30670848 | bytes 4778496 | tf_op jit(solution)/shard_map/convert_element_type | solution.py:78
  144.3 117.3 %while.13 = (s32[]{:T(128)}, f32[32,64,128]{2,1,0:T(8,128)S(1)}, f32[2,256,2048]{1,0,2:T(2,128)}, f32[2,256,32]{1,0,2:T(2,128)S(1)}, bf16[2,256,2048]{1,2,0:T(8,...) while((s32[]{:T(128)}, f32[32,64,128]{2,1,0:T(8,128)S(1)}, ...), condition=%wide.region_4.5_spmd.clone, body=%wide.region_1.4_spmd.clone.sunk | while | flops 1242128512 | bytes 25203156 | solution.py:98
  149.7 2.7 bitcast_add_fusion.2
  152.4 8.6 %copy.117 = f32[1,256,2048]{1,0,2:T(1,128)S(1)} copy(f32[1,256,2048]{1,2,0:T(8,128)S(1)} %bitcast.161) | data formatting | bytes 4194304 | tf_op jit(solution)/shard_map/while/body/jit(dynamic_update_index_in_dim)/dynamic_update_slice | solution.py:98
  161.0 42.0 %dynamic_update_slice.6 = f32[2,256,2048]{1,0,2:T(2,128)} dynamic-update-slice(f32[2,256,2048]{1,0,2:T(2,128)} %get-tuple-element.231, f32[1,256,2048]{1,0,2:T(1,128)S(1)} %copy.117, s32[]{:T(128)S(6)} %copy.122, s32[]{:T(128)} %constant.60.clone.1..sunk, s32[]{:T(128)} %constant.60.clone.1..sunk) | dynamic-update-slice | bytes 4194308 | tf_op jit(solution)/shard_map/while/body/jit(dynamic_update_index_in_dim)/dynamic_update_slice | solution.py:98
  208.3 2.7 bitcast_add_fusion.2
  211.1 8.6 %copy.117 = f32[1,256,2048]{1,0,2:T(1,128)S(1)} copy(f32[1,256,2048]{1,2,0:T(8,128)S(1)} %bitcast.161) | data formatting | bytes 4194304 | tf_op jit(solution)/shard_map/while/body/jit(dynamic_update_index_in_dim)/dynamic_update_slice | solution.py:98
  219.6 42.0 %dynamic_update_slice.6 = f32[2,256,2048]{1,0,2:T(2,128)} dynamic-update-slice(f32[2,256,2048]{1,0,2:T(2,128)} %get-tuple-element.231, f32[1,256,2048]{1,0,2:T(1,128)S(1)} %copy.117, s32[]{:T(128)S(6)} %copy.122, s32[]{:T(128)} %constant.60.clone.1..sunk, s32[]{:T(128)} %constant.60.clone.1..sunk) | dynamic-update-slice | bytes 4194308 | tf_op jit(solution)/shard_map/while/body/jit(dynamic_update_index_in_dim)/dynamic_update_slice | solution.py:98
  262.5 3.2 collective-permute-start.1
  265.7 25.4 %all-gather.1 = f32[4,1,32]{2,1,0:T(1,128)S(1)} all-gather(f32[1,1,32]{2,1,0:T(1,128)} %bitcast.175), channel_id=1, replica_groups=mesh['req'=32,'seq'=4] {'seq'}, dimensions={0}, use_global_device_ids=true | all-gather | bytes 640 | tf_op jit(solution)/shard_map/all_gather | solution.py:99
  293.8 20.3 %collective-permute-done.2 = f32[32,64,128]{2,1,0:T(8,128)S(1)} collective-permute-done((f32[32,64,128]{2,1,0:T(8,128)S(1)}, f32[32,64,128]{2,1,0:T(8,128)S(1)}, u32[]{:S(2)}, u32[]{:S(2)}) %collective-permute-start.2) | collective-permute-done | bytes 1048608 | tf_op jit(solution)/shard_map/ppermute | solution.py:12
  315.3 4.4 %collective-permute-start.3 = (f32[32,64,128]{2,1,0:T(8,128)}, f32[32,64,128]{2,1,0:T(8,128)S(1)}, u32[]{:S(2)}, u32[]{:S(2)}) collective-permute-start(f32[32,64,128]{2,1,0:T(8,128)} %multiply_add_fusion), channel_id=1, source_target_pairs={{0,1},{1,2},{2,3},{4,5},{5,6},{6,7},{8,9},{9,10},{10,11},{12,13},{... | collective-permute-start | bytes 3145736 | tf_op jit(solution)/shard_map/ppermute | solution.py:12
  319.9 6.4 %reshape.162 = f32[512,32,64]{0,2,1:T(8,128)} reshape(f32[2,256,2048]{1,0,2:T(2,128)} %get-tuple-element.45) | data formatting | bytes 8388608 | tf_op jit(solution)/shard_map/reshape | solution.py:110
  326.3 21.3 %collective-permute-done.3 = f32[32,64,128]{2,1,0:T(8,128)S(1)} collective-permute-done((f32[32,64,128]{2,1,0:T(8,128)}, f32[32,64,128]{2,1,0:T(8,128)S(1)}, u32[]{:S(2)}, u32[]{:S(2)}) %collective-permute-start.3) | collective-permute-done | bytes 1048608 | tf_op jit(solution)/shard_map/ppermute | solution.py:12
  347.6 2.7 fusion.37
  350.3 3.8 fusion.31
  356.1 3.0 multiply_reduce_fusion
  359.2 9.0 %all-to-all-start = ((f32[1,32,16,128]{3,2,0,1:T(8,128)}), f32[1,32,16,128]{3,2,0,1:T(8,128)S(1)}, u32[]{:S(2)}, u32[]{:S(2)}) async-start(f32[1,32,16,128]{3,2,0,1:T(8,128)} %bitcast.171), calls=%async_computation.1 | async-start | bytes 524288 | tf_op jit(solution)/shard_map/all_to_all | solution.py:120
  368.2 4.8 %fusion.34 = bf16[1,1,512,2048]{2,3,1,0:T(8,128)(2,1)} fusion(f32[2048]{0:T(1024)S(1)} %copy-done.12, f32[512]{0:T(512)S(1)} %add_rsqrt_fusion, pred[512]{0:T(512)(128)(4,1)S(1)} %iota_compare_fusion.1, bf16[512,4384]{0,1:T(8,128)(2,1)} %convolution_convert_fusion, f32[512,32,64]{0,2,1:T(8,128)} %copy-done.2), kind=kLoop, calls=%fused_computation.64 | loop fusion | flops 10485760 | bytes 8399360 | tf_op jit(solution)/shard_map/reshape | solution.py:117
  373.0 3.9 %copy.67 = bf16[1,1,512,2048]{3,2,1,0:T(8,128)(2,1)} copy(bf16[1,1,512,2048]{2,3,1,0:T(8,128)(2,1)} %fusion.34) | data formatting | bytes 4194304
  (117 shorter events, 36.8 us)
Async XLA Ops:
  7.2 95.5 %copy-start = (bf16[1,1,512,2048]{3,2,1,0:T(8,128)(2,1)S(1)}, bf16[1,1,512,2048]{3,2,1,0:T(8,128)(2,1)}, u32[]{:S(2)}) copy-start(bf16[1,1,512,2048]{3,2,1,0:T(8,128)(2,1)} %param.12) | copy-start | bytes 6291460
  7.2 95.5 %all-gather.4.cloned.1.call-start = ((), (), s32[]{:S(2)}) async-start(), calls=%async_computation.2 | async-start | bytes 18923520 | tf_op jit(solution)/shard_map/all_gather | solution.py:64
  21.8 337.4 %reduce-scatter.2.cloned.1.call-start = ((), (), s32[]{:S(2)}) async-start(), calls=%async_computation.3 | async-start | bytes 1310720 | tf_op jit(solution)/shard_map/reduce_scatter | solution.py:119
  118.0 7.1 %copy-start.13 = (f32[32]{0:T(128)S(1)}, f32[32]{0:T(128)}, u32[]{:S(2)}) copy-start(f32[32]{0:T(128)} %param.16) | copy-start | bytes 388
  118.0 11.8 %copy-start.11 = (f32[2304]{0:T(1024)S(1)}, f32[2304]{0:T(1024)}, u32[]{:S(2)}) copy-start(f32[2304]{0:T(1024)} %param.15) | copy-start | bytes 27652
  121.8 7.7 %collective-permute-start = (bf16[3,2304]{1,0:T(4,128)(2,1)S(1)}, bf16[3,2304]{1,0:T(4,128)(2,1)S(1)}, u32[]{:S(2)}, u32[]{:S(2)}) collective-permute-start(bf16[3,2304]{1,0:T(4,128)(2,1)S(1)} %copy.56), channel_id=1, source_target_pairs={{0,1},{1,2},{2,3},{4,5},{5,6},{6,7},{8,9},{9,10},{10,11},{12,13},{... | collective-permute-start | bytes 41480 | tf_op jit(solution)/shard_map/ppermute | solution.py:12
  127.1 2.4 copy-start.7
  140.3 2.9 copy-start.6
  140.5 3.9 %copy-start.3 = (bf16[512,2048]{0,1:T(8,128)(2,1)}, bf16[512,2048]{0,1:T(8,128)(2,1)S(1)}, u32[]{:S(2)}) copy-start(bf16[512,2048]{0,1:T(8,128)(2,1)S(1)} %slice.86) | copy-start | bytes 6291460
  144.3 1.9 copy-start.9
  152.4 50.6 %copy-start.10 = (f32[2,256,32]{1,0,2:T(2,128)S(1)}, f32[2,256,32]{1,0,2:T(2,128)}, u32[]{:S(2)}) copy-start(f32[2,256,32]{1,0,2:T(2,128)} %copy-done.9) | copy-start | bytes 196612 | tf_op jit(solution)/shard_map/while
  203.0 1.9 copy-start.9
  211.1 50.6 %copy-start.10 = (f32[2,256,32]{1,0,2:T(2,128)S(1)}, f32[2,256,32]{1,0,2:T(2,128)}, u32[]{:S(2)}) copy-start(f32[2,256,32]{1,0,2:T(2,128)} %copy-done.9) | copy-start | bytes 196612 | tf_op jit(solution)/shard_map/while
  262.5 57.3 %copy-start.15 = (s32[32]{0:T(128)S(1)}, s32[32]{0:T(128)}, u32[]{:S(2)}) copy-start(s32[32]{0:T(128)} %param.21) | copy-start | bytes 388
  262.5 28.7 %collective-permute-start.1 = (f32[32,64,128]{2,1,0:T(8,128)S(1)}, f32[32,64,128]{2,1,0:T(8,128)S(1)}, u32[]{:S(2)}, u32[]{:S(2)}) collective-permute-start(f32[32,64,128]{2,1,0:T(8,128)S(1)} %broadcast_add_fusion), channel_id=1, source_target_pairs={{0,1},{1,2},{2,3},{4,5},{5,6},{6,7},{8,9},{9,10},{10,11},{12,13},{... | collective-permute-start | bytes 3145736 | tf_op jit(solution)/shard_map/ppermute | solution.py:12
  291.1 28.6 %copy-start.8 = (f32[32,4,128]{2,0,1:T(8,128)S(1)}, f32[32,4,128]{2,0,1:T(8,128)}, u32[]{:S(2)}) copy-start(f32[32,4,128]{2,0,1:T(8,128)} %copy-done.7) | copy-start | bytes 196612
  292.4 21.7 %collective-permute-start.2 = (f32[32,64,128]{2,1,0:T(8,128)S(1)}, f32[32,64,128]{2,1,0:T(8,128)S(1)}, u32[]{:S(2)}, u32[]{:S(2)}) collective-permute-start(f32[32,64,128]{2,1,0:T(8,128)S(1)} %get-tuple-element.150), channel_id=1, source_target_pairs={{0,1},{1,2},{2,3},{4,5},{5,6},{6,7},{8,9},{9,10},{10,11},{12,13},{... | collective-permute-start | bytes 3145736 | tf_op jit(solution)/shard_map/ppermute | solution.py:12
  315.3 32.3 %collective-permute-start.3 = (f32[32,64,128]{2,1,0:T(8,128)}, f32[32,64,128]{2,1,0:T(8,128)S(1)}, u32[]{:S(2)}, u32[]{:S(2)}) collective-permute-start(f32[32,64,128]{2,1,0:T(8,128)} %multiply_add_fusion), channel_id=1, source_target_pairs={{0,1},{1,2},{2,3},{4,5},{5,6},{6,7},{8,9},{9,10},{10,11},{12,13},{... | collective-permute-start | bytes 3145736 | tf_op jit(solution)/shard_map/ppermute | solution.py:12
  326.3 24.0 %copy-start.4 = (bf16[512,2048]{0,1:T(8,128)(2,1)S(1)}, bf16[512,2048]{0,1:T(8,128)(2,1)}, u32[]{:S(2)}) copy-start(bf16[512,2048]{0,1:T(8,128)(2,1)} %copy-done.3) | copy-start | bytes 6291460
  326.3 24.0 %copy-start.14 = (f32[32]{0:T(128)S(1)}, f32[32]{0:T(128)}, u32[]{:S(2)}) copy-start(f32[32]{0:T(128)} %param.18) | copy-start | bytes 388
  354.2 1.9 copy-start.2
  356.1 12.1 %copy-start.12 = (f32[2048]{0:T(1024)S(1)}, f32[2048]{0:T(1024)}, u32[]{:S(2)}) copy-start(f32[2048]{0:T(1024)} %param.19) | copy-start | bytes 24580
  359.2 17.9 %all-to-all-start = ((f32[1,32,16,128]{3,2,0,1:T(8,128)}), f32[1,32,16,128]{3,2,0,1:T(8,128)S(1)}, u32[]{:S(2)}, u32[]{:S(2)}) async-start(f32[1,32,16,128]{3,2,0,1:T(8,128)} %bitcast.171), calls=%async_computation.1 | async-start | bytes 524288 | tf_op jit(solution)/shard_map/all_to_all | solution.py:120
  368.2 10.3 %copy-start.1 = (bf16[1,1,512,2048]{3,2,1,0:T(8,128)(2,1)S(1)}, bf16[1,1,512,2048]{3,2,1,0:T(8,128)(2,1)}, u32[]{:S(2)}) copy-start(bf16[1,1,512,2048]{3,2,1,0:T(8,128)(2,1)} %param.12) | copy-start | bytes 6291460
  (1 other events, 1.4 us)
Sparse Core Ops, SparseCore 0:
  21.9 80.7 all-gather.3
  319.9 28.6 reduce-scatter.1
where the time goes:
time: 392 us; the launch traced here: 385 us
  local copies, waits for them, and re-layouts  129 us (33%)
  waiting for transfers between devices  118 us (30%)
  blocking collectives  38.2 us (10%)
  other arithmetic  36.4 us (9%)
  matrix products  26.7 us (7%)
  starting transfers between devices  21.3 us (5%)
  between operations  15.7 us (4%)
    dynamic_update_slice x4, local copies, waits for them, and re-layouts, local(): local_end, outputs = lax.scan(block_step, zero_state, pieces)  101 us
    all_gather x1, waiting for transfers between devices, local(): lax.all_gather(wide_rows, 'req', axis=0, tiled=True)  75.9 us
    ppermute x4, waiting for transfers between devices, shifted(): return lax.ppermute(block, axis, route)  41.7 us
    all_gather x1, blocking collectives, local(): decays_all = lax.all_gather(block_total[None, :], 'seq', axis=0, tiled=True)  25.4 us
    dot_general x1, matrix products, local(): jnp.dot(tok_rows, lax.all_gather(wide_rows, 'req', axis=0, tiled=True), p...  15.3 us
    all_gather x1, blocking collectives, local(): wide_rows = lax.all_gather(w_in, 'seq', axis=1, tiled=True)  12.8 us
    ppermute x4, starting transfers between devices, shifted(): return lax.ppermute(block, axis, route)  12.2 us
    convert_element_type x1, other arithmetic, local(): conv_act = jax.nn.silu(accum).astype(jnp.bfloat16)  10.5 us
  transfers between devices with their start and end apart: 7, of which 4 were waited for; matrix products, arithmetic and copies ran while one was open for 9% of the time, Pallas kernels for 0%

commit v1 on v0

--- a/solution.py
+++ b/solution.py
@@ -95,7 +95,12 @@
         log_decay.reshape(count, block_rows, heads),
     )
     zero_state = jnp.zeros((heads, hdim, nstate), jnp.float32)
-    local_end, outputs = lax.scan(block_step, zero_state, pieces)
+    local_end = zero_state
+    outs = []
+    for index in range(count):
+        local_end, out = block_step(local_end, tuple(piece[index] for piece in pieces))
+        outs.append(out)
+    outputs = jnp.concatenate(outs, axis=0)
     decays_all = lax.all_gather(block_total[None, :], "seq", axis=0, tiled=True)
     after_mine = jnp.sum(
         jnp.where(jnp.arange(seq_count)[:, None] > my_block, decays_all, 0.0), axis=0

time: 392 us -> 267 us (0.68); the launches traced: 385 us -> 266 us
  local copies, waits for them, and re-layouts: 129 us -> 16.8 us
  waiting for transfers between devices: 118 us -> 111 us
  other arithmetic: 36.4 us -> 30.2 us
    dynamic_update_slice x4 -> x0, local copies, waits for them, and re-layouts: 101 us -> none  [local(): local_end, outputs = lax.scan(block_step, zero_state, pieces)]
    reshape x6 -> x0, local copies, waits for them, and re-layouts: 8.96 us -> none  [the longest x1 6.43 us: local(): outputs.reshape(slots, heads, hdim) + incoming]
    ppermute x4, waiting for transfers between devices: 41.7 us -> 34.9 us  [shifted(): return lax.ppermute(block, axis, route)]
    unnamed x32 -> x25, local copies, waits for them, and re-layouts: 9.68 us -> 7.13 us
  transfers between devices with their start and end apart: 7 -> 7, of which waited for: 4 -> 4; matrix products, arithmetic and copies ran while one was open for 9% -> 13% of each run, Pallas kernels for 0% -> 0%
where the time goes in v1:
time: 267 us; the launch traced here: 266 us
  waiting for transfers between devices  111 us (42%)
  blocking collectives  37.1 us (14%)
  other arithmetic  30.2 us (11%)
  matrix products  30 us (11%)
  starting transfers between devices  24.9 us (9%)
  local copies, waits for them, and re-layouts  16.8 us (6%)
  between operations  15.7 us (6%)
    all_gather x1, waiting for transfers between devices, local(): lax.all_gather(wide_rows, 'req', axis=0, tiled=True)  75.8 us
    ppermute x4, waiting for transfers between devices, shifted(): return lax.ppermute(block, axis, route)  34.9 us
    all_gather x1, blocking collectives, local(): decays_all = lax.all_gather(block_total[None, :], 'seq', axis=0, tiled=True)  24.3 us
    dot_general x1, matrix products, local(): jnp.dot(tok_rows, lax.all_gather(wide_rows, 'req', axis=0, tiled=True), p...  15.3 us
    ppermute x4, starting transfers between devices, shifted(): return lax.ppermute(block, axis, route)  14 us
    all_gather x1, blocking collectives, local(): wide_rows = lax.all_gather(w_in, 'seq', axis=1, tiled=True)  12.8 us
    all_to_all x1, starting transfers between devices, local(): lax.all_to_all(share[None], 'req', split_axis=1, concat_axis=0, tiled=True)  10.8 us
    convert_element_type x1, other arithmetic, local(): conv_act = jax.nn.silu(accum).astype(jnp.bfloat16)  10.5 us
  transfers between devices with their start and end apart: 7, of which 4 were waited for; matrix products, arithmetic and copies ran while one was open for 13% of the time, Pallas kernels for 0%

profile of v1, /device:TPU:1, one launch (start us, length us, event | category | flops | bytes accessed | tf_op | source)
XLA Modules:
  0.0 265.7 jit_solution(4299223835715570319)
XLA Ops:
  7.2 12.8 %all-gather = bf16[4,1096,64]{1,2,0:T(8,128)(2,1)S(1)} all-gather(bf16[1,1096,64]{1,2,0:T(8,128)(2,1)} %bitcast.148), channel_id=1, replica_groups=mesh['req'=32,'seq'=4] {'seq'}, dimensions={0}, use_global_device_ids=true | all-gather | bytes 701440 | tf_op jit(solution)/shard_map/all_gather | solution.py:61
  20.5 1.2 reshape.231
  21.8 1.3 compare_select_fusion.1
  26.9 75.8 %all-gather.4.cloned.1.call-done = bf16[2048,4384]{1,0:T(8,128)(2,1)} async-done(((bf16[64,4384]{1,0:T(8,128)(2,1)}), bf16[2048,4384]{1,0:T(8,128)(2,1)}) %all-gather.4.cloned.1.call-update) | async-done | bytes 17956880 | tf_op jit(solution)/shard_map/all_gather | solution.py:64
  102.7 15.3 %convolution_convert_fusion = bf16[512,4384]{0,1:T(8,128)(2,1)} fusion(bf16[2048,4384]{1,0:T(8,128)(2,1)} %all-gather.4.cloned.1.call-done, bf16[1,1,512,2048]{3,2,1,0:T(8,128)(2,1)S(1)} %copy-done), kind=kOutput, calls=%fused_computation.3 | convolution fusion | flops 9196158976 | bytes 24543232 | tf_op jit(solution)/shard_map/dot_general | solution.py:62
  118.0 3.3 %slice.143 = bf16[512,2304]{0,1:T(8,128)(2,1)} slice(bf16[512,4384]{0,1:T(8,128)(2,1)} %convolution_convert_fusion), slice={[0:512], [2048:4352]} | slice | bytes 4718592 | tf_op jit(solution)/shard_map/slice | solution.py:68
  124.9 1.5 constant_dynamic-slice_fusion
  126.7 3.1 %collective-permute-start = (bf16[3,2304]{1,0:T(4,128)(2,1)S(1)}, bf16[3,2304]{1,0:T(4,128)(2,1)S(1)}, u32[]{:S(2)}, u32[]{:S(2)}) collective-permute-start(bf16[3,2304]{1,0:T(4,128)(2,1)S(1)} %copy.54), channel_id=1, source_target_pairs={{0,1},{1,2},{2,3},{4,5},{5,6},{6,7},{8,9},{9,10},{10,11},{12,13},{... | collective-permute-start | bytes 41480 | tf_op jit(solution)/shard_map/ppermute | solution.py:12
  132.6 10.5 %multiply_convert_fusion.2 = bf16[512,2304]{0,1:T(8,128)(2,1)S(1)} fusion(bf16[512,2304]{0,1:T(8,128)(2,1)} %slice.143, bf16[3,2304]{0,1:T(8,128)(2,1)S(1)} %copy.55, f32[2304]{0:T(1024)S(1)} %get-tuple-element.14, f32[2304]{0:T(1024)S(1)} %get-tuple-element.15, f32[2304]{0:T(1024)S(1)} %get-tuple-element.13, f32[2304]{0:T(1024)S(1)} %get-tuple-element.12, ...), kind=kLoop, calls=%fused_computation.6 | loop fusion | flops 30670848 | bytes 4778496 | tf_op jit(solution)/shard_map/convert_element_type | solution.py:78
  144.4 3.1 %collective-permute-start.1 = (f32[32,64,128]{2,1,0:T(8,128)S(1)}, f32[32,64,128]{2,1,0:T(8,128)S(1)}, u32[]{:S(2)}, u32[]{:S(2)}) collective-permute-start(f32[32,64,128]{2,1,0:T(8,128)S(1)} %get-tuple-element.39), channel_id=1, source_target_pairs={{0,1},{1,2},{2,3},{4,5},{5,6},{6,7},{8,9},{9,10},{10,11},{12,13},{... | collective-permute-start | bytes 3145736 | tf_op jit(solution)/shard_map/ppermute | solution.py:12
  147.6 24.3 %all-gather.1 = f32[4,1,32]{2,1,0:T(1,128)S(1)} all-gather(f32[1,1,32]{2,1,0:T(1,128)S(1)} %bitcast.150), channel_id=1, replica_groups=mesh['req'=32,'seq'=4] {'seq'}, dimensions={0}, use_global_device_ids=true | all-gather | bytes 640 | tf_op jit(solution)/shard_map/all_gather | solution.py:104
  173.4 2.7 %collective-permute-start.2 = (f32[32,64,128]{2,1,0:T(8,128)S(1)}, f32[32,64,128]{2,1,0:T(8,128)S(1)}, u32[]{:S(2)}, u32[]{:S(2)}) collective-permute-start(f32[32,64,128]{2,1,0:T(8,128)S(1)} %multiply_add_fusion.1), channel_id=1, source_target_pairs={{0,1},{1,2},{2,3},{4,5},{5,6},{6,7},{8,9},{9,10},{10,11},{12,13},{... | collective-permute-start | bytes 3145736 | tf_op jit(solution)/shard_map/ppermute | solution.py:12
  177.3 4.3 %bitcast_add_fusion = f32[256,32,64]{0,2,1:T(8,128)} fusion(f32[256,32,64]{0,2,1:T(8,128)S(1)} %fusion.32, bf16[256,32,64]{0,2,1:T(8,128)(2,1)S(1)} %bitcast.145, f32[32,256]{1,0:T(8,128)S(1)} %get-tuple-element.26, f32[32,256]{1,0:T(8,128)S(1)} %get-tuple-element.34, f32[256,256]{1,0:T(8,128)S(1)} %fusion.36, pred[256,256]{1,0:T(8,128)(4,1)S(1)} %iota_compare_fusion, ...), kind=kOutput, calls=%fused_computation.42 | convolution fusion | flops 282066944 | bytes 5668864 | tf_op jit(solution)/shard_map/htu,uhp->thp/dot_general | solution.py:27
  181.6 14.6 %collective-permute-done.2 = f32[32,64,128]{2,1,0:T(8,128)S(1)} collective-permute-done((f32[32,64,128]{2,1,0:T(8,128)S(1)}, f32[32,64,128]{2,1,0:T(8,128)S(1)}, u32[]{:S(2)}, u32[]{:S(2)}) %collective-permute-start.2) | collective-permute-done | bytes 1048608 | tf_op jit(solution)/shard_map/ppermute | solution.py:12
  197.4 5.1 %collective-permute-start.3 = (f32[32,64,128]{2,1,0:T(8,128)S(1)}, f32[32,64,128]{2,1,0:T(8,128)}, u32[]{:S(2)}, u32[]{:S(2)}) collective-permute-start(f32[32,64,128]{2,1,0:T(8,128)S(1)} %get-tuple-element.24), channel_id=1, source_target_pairs={{0,1},{1,2},{2,3},{4,5},{5,6},{6,7},{8,9},{9,10},{10,11},{12,13},{... | collective-permute-start | bytes 3145736 | tf_op jit(solution)/shard_map/ppermute | solution.py:12
  203.7 4.0 %bitcast_add_fusion.1 = f32[256,32,64]{0,2,1:T(8,128)S(1)} fusion(f32[256,32,64]{0,2,1:T(8,128)S(1)} %fusion.25, bf16[256,32,64]{0,2,1:T(8,128)(2,1)} %bitcast.144, f32[32,256]{1,0:T(8,128)} %get-tuple-element.27, f32[32,256]{1,0:T(8,128)} %get-tuple-element.35, f32[256,256]{1,0:T(8,128)S(1)} %fusion.41, pred[256,256]{1,0:T(8,128)(4,1)S(1)} %iota_compare_fusion, ...), kind=kOutput, calls=%fused_computation.43 | convolution fusion | flops 282066944 | bytes 5668864 | tf_op jit(solution)/shard_map/htu,uhp->thp/dot_general | solution.py:27
  207.8 20.3 %collective-permute-done.3 = f32[32,64,128]{2,1,0:T(8,128)} collective-permute-done((f32[32,64,128]{2,1,0:T(8,128)S(1)}, f32[32,64,128]{2,1,0:T(8,128)}, u32[]{:S(2)}, u32[]{:S(2)}) %collective-permute-start.3) | collective-permute-done | bytes 1048608 | tf_op jit(solution)/shard_map/ppermute | solution.py:12
  228.1 3.1 %fusion.28 = f32[512,32,64]{0,2,1:T(8,128)S(1)} fusion(f32[32,64,128]{2,1,0:T(8,128)} %collective-permute-done.3, bf16[512,2304]{0,1:T(8,128)(2,1)S(1)} %copy-done.4), kind=kOutput, calls=%fused_computation.58 | convolution fusion | flops 1610612736 | bytes 5373952 | tf_op jit(solution)/shard_map/tn,hpn->thp/dot_general | solution.py:111
  231.3 1.5 fusion.6
  232.8 1.9 copy-done.2
  234.7 3.0 %multiply_reduce_fusion = f32[512]{0:T(512)S(1)} fusion(bf16[512,4384]{0,1:T(8,128)(2,1)} %convolution_convert_fusion, f32[512,32,64]{0,2,1:T(8,128)S(1)} %fusion.6), kind=kLoop, calls=%fused_computation.17 | loop fusion | flops 8388096 | bytes 6293504 | tf_op jit(solution)/shard_map/reduce_sum | solution.py:120
  237.8 10.8 %all-to-all-start = ((f32[1,32,16,128]{3,2,0,1:T(8,128)}), f32[1,32,16,128]{3,2,0,1:T(8,128)S(1)}, u32[]{:S(2)}, u32[]{:S(2)}) async-start(f32[1,32,16,128]{3,2,0,1:T(8,128)} %bitcast.146), calls=%async_computation.1 | async-start | bytes 524288 | tf_op jit(solution)/shard_map/all_to_all | solution.py:125
  248.6 4.8 %fusion.21 = bf16[1,1,512,2048]{2,3,1,0:T(8,128)(2,1)} fusion(f32[2048]{0:T(1024)S(1)} %copy-done.7, f32[512]{0:T(512)S(1)} %add_rsqrt_fusion, pred[512]{0:T(512)(128)(4,1)S(1)} %iota_compare_fusion.1, bf16[512,4384]{0,1:T(8,128)(2,1)} %convolution_convert_fusion, f32[512,32,64]{0,2,1:T(8,128)} %copy-done.2), kind=kLoop, calls=%fused_computation.37 | loop fusion | flops 10485760 | bytes 8399360 | tf_op jit(solution)/shard_map/reshape | solution.py:122
  253.4 3.9 %copy.68 = bf16[1,1,512,2048]{3,2,1,0:T(8,128)(2,1)} copy(bf16[1,1,512,2048]{2,3,1,0:T(8,128)(2,1)} %fusion.21) | data formatting | bytes 4194304
  (83 shorter events, 17.6 us)
Async XLA Ops:
  7.2 95.5 %copy-start = (bf16[1,1,512,2048]{3,2,1,0:T(8,128)(2,1)S(1)}, bf16[1,1,512,2048]{3,2,1,0:T(8,128)(2,1)}, u32[]{:S(2)}) copy-start(bf16[1,1,512,2048]{3,2,1,0:T(8,128)(2,1)} %param.10) | copy-start | bytes 6291460
  7.2 95.5 %all-gather.4.cloned.1.call-start = ((), (), s32[]{:S(2)}) async-start(), calls=%async_computation.2 | async-start | bytes 18923520 | tf_op jit(solution)/shard_map/all_gather | solution.py:64
  21.8 216.0 %reduce-scatter.2.cloned.1.call-start = ((), (), s32[]{:S(2)}) async-start(), calls=%async_computation.3 | async-start | bytes 1310720 | tf_op jit(solution)/shard_map/reduce_scatter | solution.py:124
  118.0 3.3 %copy-start.8 = (f32[32]{0:T(128)S(1)}, f32[32]{0:T(128)}, u32[]{:S(2)}) copy-start(f32[32]{0:T(128)} %param.14) | copy-start | bytes 388
  118.0 14.6 %copy-start.6 = (f32[2304]{0:T(1024)S(1)}, f32[2304]{0:T(1024)}, u32[]{:S(2)}) copy-start(f32[2304]{0:T(1024)} %param.13) | copy-start | bytes 27652
  126.7 5.5 %collective-permute-start = (bf16[3,2304]{1,0:T(4,128)(2,1)S(1)}, bf16[3,2304]{1,0:T(4,128)(2,1)S(1)}, u32[]{:S(2)}, u32[]{:S(2)}) collective-permute-start(bf16[3,2304]{1,0:T(4,128)(2,1)S(1)} %copy.54), channel_id=1, source_target_pairs={{0,1},{1,2},{2,3},{4,5},{5,6},{6,7},{8,9},{9,10},{10,11},{12,13},{... | collective-permute-start | bytes 41480 | tf_op jit(solution)/shard_map/ppermute | solution.py:12
  143.0 59.7 %copy-start.3 = (bf16[512,2304]{0,1:T(8,128)(2,1)}, bf16[512,2304]{0,1:T(8,128)(2,1)S(1)}, u32[]{:S(2)}) copy-start(bf16[512,2304]{0,1:T(8,128)(2,1)S(1)} %multiply_convert_fusion.2) | copy-start | bytes 7077892
  143.5 4.1 %copy-start.10 = (s32[32]{0:T(128)S(1)}, s32[32]{0:T(128)}, u32[]{:S(2)}) copy-start(s32[32]{0:T(128)} %param.19) | copy-start | bytes 388
  144.4 28.8 %collective-permute-start.1 = (f32[32,64,128]{2,1,0:T(8,128)S(1)}, f32[32,64,128]{2,1,0:T(8,128)S(1)}, u32[]{:S(2)}, u32[]{:S(2)}) collective-permute-start(f32[32,64,128]{2,1,0:T(8,128)S(1)} %get-tuple-element.39), channel_id=1, source_target_pairs={{0,1},{1,2},{2,3},{4,5},{5,6},{6,7},{8,9},{9,10},{10,11},{12,13},{... | collective-permute-start | bytes 3145736 | tf_op jit(solution)/shard_map/ppermute | solution.py:12
  173.4 22.8 %collective-permute-start.2 = (f32[32,64,128]{2,1,0:T(8,128)S(1)}, f32[32,64,128]{2,1,0:T(8,128)S(1)}, u32[]{:S(2)}, u32[]{:S(2)}) collective-permute-start(f32[32,64,128]{2,1,0:T(8,128)S(1)} %multiply_add_fusion.1), channel_id=1, source_target_pairs={{0,1},{1,2},{2,3},{4,5},{5,6},{6,7},{8,9},{9,10},{10,11},{12,13},{... | collective-permute-start | bytes 3145736 | tf_op jit(solution)/shard_map/ppermute | solution.py:12
  197.4 30.7 %collective-permute-start.3 = (f32[32,64,128]{2,1,0:T(8,128)S(1)}, f32[32,64,128]{2,1,0:T(8,128)}, u32[]{:S(2)}, u32[]{:S(2)}) collective-permute-start(f32[32,64,128]{2,1,0:T(8,128)S(1)} %get-tuple-element.24), channel_id=1, source_target_pairs={{0,1},{1,2},{2,3},{4,5},{5,6},{6,7},{8,9},{9,10},{10,11},{12,13},{... | collective-permute-start | bytes 3145736 | tf_op jit(solution)/shard_map/ppermute | solution.py:12
  207.7 20.4 %copy-start.4 = (bf16[512,2304]{0,1:T(8,128)(2,1)S(1)}, bf16[512,2304]{0,1:T(8,128)(2,1)}, u32[]{:S(2)}) copy-start(bf16[512,2304]{0,1:T(8,128)(2,1)} %copy-done.3) | copy-start | bytes 7077892
  207.8 23.5 %slice-start = ((bf16[512,2304]{0,1:T(8,128)(2,1)}), bf16[512,2048]{0,1:T(8,128)(2,1)S(1)}, s32[]{:S(2)}) async-start(bf16[512,2304]{0,1:T(8,128)(2,1)} %copy-done.3), calls=%async_computation.4 | async-start | bytes 4194304 | tf_op jit(solution)/shard_map/slice | solution.py:79
  207.8 23.5 %copy-start.5 = (f32[256,32,64]{0,2,1:T(8,128)S(1)}, f32[256,32,64]{0,2,1:T(8,128)}, u32[]{:S(2)}) copy-start(f32[256,32,64]{0,2,1:T(8,128)} %bitcast_add_fusion) | copy-start | bytes 6291460
  207.8 23.5 %copy-start.9 = (f32[32]{0:T(128)S(1)}, f32[32]{0:T(128)}, u32[]{:S(2)}) copy-start(f32[32]{0:T(128)} %param.16) | copy-start | bytes 388
  232.8 1.9 copy-start.2
  234.7 13.9 %copy-start.7 = (f32[2048]{0:T(1024)S(1)}, f32[2048]{0:T(1024)}, u32[]{:S(2)}) copy-start(f32[2048]{0:T(1024)} %param.17) | copy-start | bytes 24580
  237.8 19.7 %all-to-all-start = ((f32[1,32,16,128]{3,2,0,1:T(8,128)}), f32[1,32,16,128]{3,2,0,1:T(8,128)S(1)}, u32[]{:S(2)}, u32[]{:S(2)}) async-start(f32[1,32,16,128]{3,2,0,1:T(8,128)} %bitcast.146), calls=%async_computation.1 | async-start | bytes 524288 | tf_op jit(solution)/shard_map/all_to_all | solution.py:125
  248.6 10.3 %copy-start.1 = (bf16[1,1,512,2048]{3,2,1,0:T(8,128)(2,1)S(1)}, bf16[1,1,512,2048]{3,2,1,0:T(8,128)(2,1)}, u32[]{:S(2)}) copy-start(bf16[1,1,512,2048]{3,2,1,0:T(8,128)(2,1)} %param.10) | copy-start | bytes 6291460
Sparse Core Ops, SparseCore 0:
  21.9 80.7 all-gather.3
  203.9 27.5 reduce-scatter.1

commit v2 on v1

--- a/solution.py
+++ b/solution.py
@@ -101,13 +101,17 @@
         local_end, out = block_step(local_end, tuple(piece[index] for piece in pieces))
         outs.append(out)
     outputs = jnp.concatenate(outs, axis=0)
-    decays_all = lax.all_gather(block_total[None, :], "seq", axis=0, tiled=True)
-    after_mine = jnp.sum(
-        jnp.where(jnp.arange(seq_count)[:, None] > my_block, decays_all, 0.0), axis=0
+    packed = jnp.concatenate(
+        [local_end.reshape(heads, hdim * nstate), jnp.broadcast_to(block_total[:, None], (heads, 128))],
+        axis=1,
     )
+    gathered = lax.all_gather(packed, "seq", axis=0, tiled=False)
+    ends = gathered[:, :, : hdim * nstate].reshape(seq_count, heads, hdim, nstate)
+    totals = gathered[:, :, hdim * nstate]
     entering = zero_state
     for turn in range(seq_count - 1):
-        entering = shifted(jnp.exp(block_total)[:, None, None] * entering + local_end, "seq", 1)
+        stepped = jnp.exp(totals[turn])[:, None, None] * entering + ends[turn]
+        entering = jnp.where(turn < my_block, stepped, entering)
     incoming = jnp.exp(through)[:, :, None] * jnp.einsum(
         "tn,hpn->thp", c_rows.astype(jnp.float32), entering, precision=lax.Precision.HIGHEST
     )
@@ -120,8 +124,11 @@
     scale = lax.rsqrt(jnp.mean(gated * gated, axis=1, keepdims=True) + 1e-05)
     normed = jnp.where(filled[:, None], gated * scale * norm_weight[None, :], 0.0)
     gated_out = normed.astype(jnp.bfloat16).reshape(1, 1, slots, inner)
-    decayed_end = jnp.exp(after_mine)[:, None, None] * local_end
-    share = lax.psum_scatter(decayed_end, "seq", scatter_dimension=1, tiled=True)
+    later_mask = jnp.arange(seq_count)[None, :] > jnp.arange(seq_count)[:, None]
+    after = jnp.sum(jnp.where(later_mask[:, :, None], totals[None, :, :], 0.0), axis=1)
+    piece = hdim // seq_count
+    own_ends = lax.dynamic_slice_in_dim(ends, my_block * piece, piece, axis=2)
+    share = jnp.sum(jnp.exp(after)[:, :, None, None] * own_ends, axis=0)
     moved = lax.all_to_all(share[None], "req", split_axis=1, concat_axis=0, tiled=True)
     final_states = jnp.take(moved, prompt_group, axis=0)
     return (gated_out, final_states)

time: 267 us -> 235 us (0.88)
  blocking collectives: 37.1 us -> 12.8 us
  starting transfers between devices: 24.9 us -> 11 us
  local copies, waits for them, and re-layouts: 16.8 us -> 20.3 us
  matrix products: 30 us -> 32.8 us
    ppermute x4 -> x1, waiting for transfers between devices: 34.9 us -> 0.01 us  [shifted(): return lax.ppermute(block, axis, route)]
    all_gather x0 -> x1, waiting for transfers between devices: none -> 33.4 us  [local(): gathered = lax.all_gather(packed, 'seq', axis=0, tiled=False)]
    all_gather x1 -> x0, blocking collectives: 24.3 us -> none  [local(): decays_all = lax.all_gather(block_total[None, :], 'seq', axis=0, tiled=True)]
    ppermute x4 -> x1, starting transfers between devices: 14 us -> 3.27 us  [shifted(): return lax.ppermute(block, axis, route)]
    unnamed x25 -> x37, local copies, waits for them, and re-layouts: 7.13 us -> 11.1 us
    all_to_all x1, starting transfers between devices: 10.8 us -> 7.68 us  [local(): lax.all_to_all(share[None], 'req', split_axis=1, concat_axis=0, tiled=True)]
  transfers between devices with their start and end apart: 7 -> 4, of which waited for: 4 -> 3; matrix products, arithmetic and copies ran while one was open for 13% -> 12% of each run, Pallas kernels for 0% -> 0%
where the time goes in v2:
time: 235 us; the launch traced here: 234 us
  waiting for transfers between devices  109 us (46%)
  matrix products  32.8 us (14%)
  other arithmetic  32.1 us (14%)
  local copies, waits for them, and re-layouts  20.3 us (9%)
  between operations  15.8 us (7%)
  blocking collectives  12.8 us (5%)
  starting transfers between devices  11 us (5%)
    all_gather x1, waiting for transfers between devices, local(): lax.all_gather(wide_rows, 'req', axis=0, tiled=True)  75.9 us
    all_gather x1, waiting for transfers between devices, local(): gathered = lax.all_gather(packed, 'seq', axis=0, tiled=False)  33.4 us
    dot_general x1, matrix products, local(): jnp.dot(tok_rows, lax.all_gather(wide_rows, 'req', axis=0, tiled=True), p...  15.3 us
    all_gather x1, blocking collectives, local(): wide_rows = lax.all_gather(w_in, 'seq', axis=1, tiled=True)  12.8 us
    unnamed x37, local copies, waits for them, and re-layouts  11.1 us
    convert_element_type x1, other arithmetic, local(): conv_act = jax.nn.silu(accum).astype(jnp.bfloat16)  10.5 us
    dot_general x2, matrix products, block_step(): jnp.einsum('htu,uhp->thp', mixing, heads_x, preferred_element_type=jnp.fl...  8.76 us
    all_to_all x1, starting transfers between devices, local(): lax.all_to_all(share[None], 'req', split_axis=1, concat_axis=0, tiled=True)  7.68 us
  transfers between devices with their start and end apart: 4, of which 3 were waited for; matrix products, arithmetic and copies ran while one was open for 12% of the time, Pallas kernels for 0%

profile of v2, /device:TPU:1, one launch (start us, length us, event | category | flops | bytes accessed | tf_op | source)
XLA Modules:
  0.0 234.3 jit_solution(2170247969437614034)
XLA Ops:
  7.2 12.8 %all-gather.1 = bf16[4,1096,64]{1,2,0:T(8,128)(2,1)S(1)} all-gather(bf16[1,1096,64]{1,2,0:T(8,128)(2,1)} %bitcast.183), channel_id=1, replica_groups=mesh['req'=32,'seq'=4] {'seq'}, dimensions={0}, use_global_device_ids=true | all-gather | bytes 701440 | tf_op jit(solution)/shard_map/all_gather | solution.py:61
  20.5 1.2 reshape.275
  21.8 1.3 compare_select_fusion.1
  26.8 75.9 %all-gather.5.cloned.1.call-done = bf16[2048,4384]{1,0:T(8,128)(2,1)} async-done(((bf16[64,4384]{1,0:T(8,128)(2,1)}), bf16[2048,4384]{1,0:T(8,128)(2,1)}) %all-gather.5.cloned.1.call-update) | async-done | bytes 17956880 | tf_op jit(solution)/shard_map/all_gather | solution.py:64
  102.7 15.3 %convolution_convert_fusion = bf16[512,4384]{0,1:T(8,128)(2,1)} fusion(bf16[2048,4384]{1,0:T(8,128)(2,1)} %all-gather.5.cloned.1.call-done, bf16[1,1,512,2048]{3,2,1,0:T(8,128)(2,1)S(1)} %copy-done), kind=kOutput, calls=%fused_computation.3 | convolution fusion | flops 9196158976 | bytes 24543232 | tf_op jit(solution)/shard_map/dot_general | solution.py:62
  118.0 3.3 %slice.187 = bf16[512,2304]{0,1:T(8,128)(2,1)} slice(bf16[512,4384]{0,1:T(8,128)(2,1)} %convolution_convert_fusion), slice={[0:512], [2048:4352]} | slice | bytes 4718592 | tf_op jit(solution)/shard_map/slice | solution.py:68
  124.3 1.5 constant_dynamic-slice_fusion
  126.1 3.3 %collective-permute-start = (bf16[3,2304]{1,0:T(4,128)(2,1)S(1)}, bf16[3,2304]{1,0:T(4,128)(2,1)S(1)}, u32[]{:S(2)}, u32[]{:S(2)}) collective-permute-start(bf16[3,2304]{1,0:T(4,128)(2,1)S(1)} %copy.71), channel_id=1, source_target_pairs={{0,1},{1,2},{2,3},{4,5},{5,6},{6,7},{8,9},{9,10},{10,11},{12,13},{... | collective-permute-start | bytes 41480 | tf_op jit(solution)/shard_map/ppermute | solution.py:12
  129.4 1.2 reduce-window.26
  131.5 10.5 %multiply_convert_fusion.2 = bf16[512,2304]{0,1:T(8,128)(2,1)S(1)} fusion(bf16[512,2304]{0,1:T(8,128)(2,1)} %slice.187, bf16[3,2304]{0,1:T(8,128)(2,1)S(1)} %copy.72, f32[2304]{0:T(1024)S(1)} %get-tuple-element.17, f32[2304]{0:T(1024)S(1)} %get-tuple-element.18, f32[2304]{0:T(1024)S(1)} %get-tuple-element.16, f32[2304]{0:T(1024)S(1)} %get-tuple-element.15, ...), kind=kLoop, calls=%fused_computation.6 | loop fusion | flops 30670848 | bytes 4778496 | tf_op jit(solution)/shard_map/convert_element_type | solution.py:78
  144.1 1.2 pad_maximum_fusion.1
  145.5 1.2 fusion.39
  147.8 1.8 fusion.28
  149.6 1.8 fusion.35
  151.6 4.4 %bitcast_add_fusion = f32[256,32,64]{0,2,1:T(8,128)} fusion(f32[256,32,64]{0,2,1:T(8,128)S(1)} %fusion.35, bf16[256,32,64]{0,2,1:T(8,128)(2,1)S(1)} %bitcast.181, f32[32,256]{1,0:T(8,128)S(1)} %get-tuple-element.30, f32[32,256]{1,0:T(8,128)S(1)} %get-tuple-element.38, f32[256,256]{1,0:T(8,128)S(1)} %fusion.39, pred[256,256]{1,0:T(8,128)(4,1)S(1)} %iota_compare_fusion, ...), kind=kOutput, calls=%fused_computation.42 | convolution fusion | flops 282066944 | bytes 5668864 | tf_op jit(solution)/shard_map/htu,uhp->thp/dot_general | solution.py:27
  156.0 4.4 %bitcast_add_fusion.1 = f32[256,32,64]{0,2,1:T(8,128)} fusion(f32[256,32,64]{0,2,1:T(8,128)S(1)} %fusion.28, bf16[256,32,64]{0,2,1:T(8,128)(2,1)S(1)} %bitcast.180, f32[32,256]{1,0:T(8,128)S(1)} %get-tuple-element.31, f32[32,256]{1,0:T(8,128)S(1)} %get-tuple-element.39, f32[256,256]{1,0:T(8,128)S(1)} %fusion.44, pred[256,256]{1,0:T(8,128)(4,1)S(1)} %iota_compare_fusion, ...), kind=kOutput, calls=%fused_computation.43 | convolution fusion | flops 282066944 | bytes 5668864 | tf_op jit(solution)/shard_map/htu,uhp->thp/dot_general | solution.py:27
  160.4 33.4 %all-gather.7.cloned.1.call-done = f32[128,8320]{1,0:T(8,128)} async-done(((f32[32,8320]{1,0:T(8,128)}), f32[128,8320]{1,0:T(8,128)}) %all-gather.7.cloned.1.call-update) | async-done | bytes 4259856 | tf_op jit(solution)/shard_map/all_gather | solution.py:108
  193.8 2.2 slice_bitcast_fusion.2
  199.8 1.9 fusion.31
  201.7 1.5 fusion.6
  203.2 4.5 %multiply_reduce_fusion = f32[512]{0:T(512)S(1)} fusion(bf16[512,4384]{0,1:T(8,128)(2,1)} %convolution_convert_fusion, f32[512,32,64]{0,2,1:T(8,128)S(1)} %fusion.6), kind=kLoop, calls=%fused_computation.17 | loop fusion | flops 8388096 | bytes 6293504 | tf_op jit(solution)/shard_map/reduce_sum | solution.py:124
  209.5 7.7 %all-to-all-start = ((f32[1,32,16,128]{3,2,0,1:T(8,128)}), f32[1,32,16,128]{3,2,0,1:T(8,128)S(1)}, u32[]{:S(2)}, u32[]{:S(2)}) async-start(f32[1,32,16,128]{3,2,0,1:T(8,128)} %bitcast.31), calls=%async_computation | async-start | bytes 524288 | tf_op jit(solution)/shard_map/all_to_all | solution.py:132
  217.2 4.8 %fusion.21 = bf16[1,1,512,2048]{2,3,1,0:T(8,128)(2,1)} fusion(f32[2048]{0:T(1024)S(1)} %copy-done.10, f32[512]{0:T(512)S(1)} %add_rsqrt_fusion, pred[512]{0:T(512)(128)(4,1)S(1)} %iota_compare_fusion.2, bf16[512,4384]{0,1:T(8,128)(2,1)} %convolution_convert_fusion, f32[512,32,64]{0,2,1:T(8,128)} %copy-done.2), kind=kLoop, calls=%fused_computation.37 | loop fusion | flops 10485760 | bytes 8399360 | tf_op jit(solution)/shard_map/reshape | solution.py:126
  222.0 3.9 %copy.84 = bf16[1,1,512,2048]{3,2,1,0:T(8,128)(2,1)} copy(bf16[1,1,512,2048]{2,3,1,0:T(8,128)(2,1)} %fusion.21) | data formatting | bytes 4194304
  (92 shorter events, 17.6 us)
Async XLA Ops:
  7.2 95.5 %copy-start = (bf16[1,1,512,2048]{3,2,1,0:T(8,128)(2,1)S(1)}, bf16[1,1,512,2048]{3,2,1,0:T(8,128)(2,1)}, u32[]{:S(2)}) copy-start(bf16[1,1,512,2048]{3,2,1,0:T(8,128)(2,1)} %param.10) | copy-start | bytes 6291460
  7.2 95.5 %all-gather.5.cloned.1.call-start = ((), (), s32[]{:S(2)}) async-start(), calls=%async_computation.1 | async-start | bytes 18923520 | tf_op jit(solution)/shard_map/all_gather | solution.py:64
  21.8 172.0 %all-gather.7.cloned.1.call-start = ((), (), s32[]{:S(2)}) async-start(), calls=%async_computation.2 | async-start | bytes 5324800 | tf_op jit(solution)/shard_map/all_gather | solution.py:108
  118.0 3.3 %copy-start.11 = (f32[32]{0:T(128)S(1)}, f32[32]{0:T(128)}, u32[]{:S(2)}) copy-start(f32[32]{0:T(128)} %param.14) | copy-start | bytes 388
  118.0 13.5 %copy-start.9 = (f32[2304]{0:T(1024)S(1)}, f32[2304]{0:T(1024)}, u32[]{:S(2)}) copy-start(f32[2304]{0:T(1024)} %param.13) | copy-start | bytes 27652
  126.1 5.1 %collective-permute-start = (bf16[3,2304]{1,0:T(4,128)(2,1)S(1)}, bf16[3,2304]{1,0:T(4,128)(2,1)S(1)}, u32[]{:S(2)}, u32[]{:S(2)}) collective-permute-start(bf16[3,2304]{1,0:T(4,128)(2,1)S(1)} %copy.71), channel_id=1, source_target_pairs={{0,1},{1,2},{2,3},{4,5},{5,6},{6,7},{8,9},{9,10},{10,11},{12,13},{... | collective-permute-start | bytes 41480 | tf_op jit(solution)/shard_map/ppermute | solution.py:12
  142.0 1.4 copy-start.3
  142.9 2.4 %copy-start.13 = (s32[32]{0:T(128)S(1)}, s32[32]{0:T(128)}, u32[]{:S(2)}) copy-start(s32[32]{0:T(128)} %param.19) | copy-start | bytes 388
  145.5 6.0 %copy-start.4 = (bf16[512,2304]{0,1:T(8,128)(2,1)S(1)}, bf16[512,2304]{0,1:T(8,128)(2,1)}, u32[]{:S(2)}) copy-start(bf16[512,2304]{0,1:T(8,128)(2,1)} %copy-done.3) | copy-start | bytes 7077892
  193.8 3.2 %copy-start.6 = (f32[128,8320]{1,0:T(8,128)S(1)}, f32[128,8320]{1,0:T(8,128)}, u32[]{:S(2)}) copy-start(f32[128,8320]{1,0:T(8,128)} %all-gather.7.cloned.1.call-done) | copy-start | bytes 12779524
  197.8 2.0 copy-start.5
  198.2 3.5 %slice-start = ((bf16[512,2304]{0,1:T(8,128)(2,1)}), bf16[512,2048]{0,1:T(8,128)(2,1)S(1)}, s32[]{:S(2)}) async-start(bf16[512,2304]{0,1:T(8,128)(2,1)} %copy-done.3), calls=%async_computation.3 | async-start | bytes 4194304 | tf_op jit(solution)/shard_map/slice | solution.py:79
  198.2 3.5 %copy-start.7 = (f32[256,32,64]{0,2,1:T(8,128)S(1)}, f32[256,32,64]{0,2,1:T(8,128)}, u32[]{:S(2)}) copy-start(f32[256,32,64]{0,2,1:T(8,128)} %bitcast_add_fusion) | copy-start | bytes 6291460
  198.2 3.5 %copy-start.8 = (f32[256,32,64]{0,2,1:T(8,128)S(1)}, f32[256,32,64]{0,2,1:T(8,128)}, u32[]{:S(2)}) copy-start(f32[256,32,64]{0,2,1:T(8,128)} %bitcast_add_fusion.1) | copy-start | bytes 6291460
  198.3 3.5 %copy-start.12 = (f32[32]{0:T(128)S(1)}, f32[32]{0:T(128)}, u32[]{:S(2)}) copy-start(f32[32]{0:T(128)} %param.16) | copy-start | bytes 388
  203.2 5.3 %copy-start.2 = (f32[512,32,64]{0,2,1:T(8,128)}, f32[512,32,64]{0,2,1:T(8,128)S(1)}, u32[]{:S(2)}) copy-start(f32[512,32,64]{0,2,1:T(8,128)S(1)} %fusion.6) | copy-start | bytes 12582916
  207.7 9.5 %copy-start.10 = (f32[2048]{0:T(1024)S(1)}, f32[2048]{0:T(1024)}, u32[]{:S(2)}) copy-start(f32[2048]{0:T(1024)} %param.17) | copy-start | bytes 24580
  209.5 16.6 %all-to-all-start = ((f32[1,32,16,128]{3,2,0,1:T(8,128)}), f32[1,32,16,128]{3,2,0,1:T(8,128)S(1)}, u32[]{:S(2)}, u32[]{:S(2)}) async-start(f32[1,32,16,128]{3,2,0,1:T(8,128)} %bitcast.31), calls=%async_computation | async-start | bytes 524288 | tf_op jit(solution)/shard_map/all_to_all | solution.py:132
  217.2 10.3 %copy-start.1 = (bf16[1,1,512,2048]{3,2,1,0:T(8,128)(2,1)S(1)}, bf16[1,1,512,2048]{3,2,1,0:T(8,128)(2,1)}, u32[]{:S(2)}) copy-start(bf16[1,1,512,2048]{3,2,1,0:T(8,128)(2,1)} %param.10) | copy-start | bytes 6291460
Sparse Core Ops, SparseCore 0:
  21.9 80.7 all-gather.4
  145.4 48.3 all-gather.6

commit v3 on v2

--- a/solution.py
+++ b/solution.py
@@ -1,7 +1,7 @@
 import jax
 import jax.numpy as jnp
 from jax import lax
-from jax.sharding import PartitionSpec as P
+from jax.sharding import Mesh, PartitionSpec as P
 
 BLOCK = 256
 
@@ -54,16 +54,28 @@
     convdim = conv_bias.shape[0]
     taps = conv_weight.shape[0]
     seq_count = lax.axis_size("seq")
-    my_group = lax.axis_index("req")
+    pair = lax.axis_index("core")
+    my_group = lax.axis_index("rq") * 2 + pair
     my_block = lax.axis_index("seq")
     qlen = jnp.sum(jnp.where(prompt_group == my_group, lengths, 0))
     filled = jnp.arange(slots, dtype=jnp.int32) < qlen
-    wide_rows = lax.all_gather(w_in, "seq", axis=1, tiled=True)
-    projected = jnp.dot(
-        tok_rows,
-        lax.all_gather(wide_rows, "req", axis=0, tiled=True),
-        preferred_element_type=jnp.float32,
+    half = w_in.shape[1] // 2
+    pair_rows = lax.all_gather(w_in, "core", axis=0, tiled=True)
+    my_cols = lax.dynamic_slice_in_dim(pair_rows, pair * half, half, axis=1)
+    weights = lax.all_gather(my_cols, ("seq", "rq"), axis=0, tiled=False)
+    weights = weights.reshape(seq_count, -1, half)
+    swap = [(0, 1), (1, 0)]
+    partner_rows = lax.ppermute(tok_rows, "core", swap)
+    for_partner = jnp.einsum(
+        "tk,skn->tsn", partner_rows, weights, preferred_element_type=jnp.float32
     ).astype(jnp.bfloat16)
+    from_partner = lax.ppermute(for_partner, "core", swap)
+    for_me = jnp.einsum(
+        "tk,skn->tsn", tok_rows, weights, preferred_element_type=jnp.float32
+    ).astype(jnp.bfloat16)
+    first = jnp.where(pair == 0, for_me, from_partner)
+    second = jnp.where(pair == 0, from_partner, for_me)
+    projected = jnp.stack([first, second], axis=2).reshape(slots, -1)
     gate_z = projected[:, :inner]
     conv_in = projected[:, inner : inner + convdim]
     dt_raw = projected[:, inner + convdim :]
@@ -129,15 +141,18 @@
     piece = hdim // seq_count
     own_ends = lax.dynamic_slice_in_dim(ends, my_block * piece, piece, axis=2)
     share = jnp.sum(jnp.exp(after)[:, :, None, None] * own_ends, axis=0)
-    moved = lax.all_to_all(share[None], "req", split_axis=1, concat_axis=0, tiled=True)
+    moved = lax.all_to_all(share[None], ("rq", "core"), split_axis=1, concat_axis=0, tiled=True)
     final_states = jnp.take(moved, prompt_group, axis=0)
     return (gated_out, final_states)
 
 
 def solution(mesh):
+    groups, blocks = mesh.devices.shape
+    split = Mesh(mesh.devices.reshape(groups // 2, 2, blocks), ("rq", "core", "seq"))
+    req = ("rq", "core")
     in_specs = (
-        P("req", "seq", None, None),
-        P("req", "seq"),
+        P(req, "seq", None, None),
+        P(req, "seq"),
         P(),
         P(),
         P(),
@@ -147,5 +162,5 @@
         P(),
         P(),
     )
-    out_specs = (P("req", "seq", None, None), P(None, "req", "seq", None))
-    return jax.shard_map(local, mesh=mesh, in_specs=in_specs, out_specs=out_specs, check_vma=False)
+    out_specs = (P(req, "seq", None, None), P(None, req, "seq", None))
+    return jax.shard_map(local, mesh=split, in_specs=in_specs, out_specs=out_specs, check_vma=False)

time: 235 us -> 264 us (1.12)
  local copies, waits for them, and re-layouts: 20.3 us -> 48.8 us
  blocking collectives: 12.8 us -> 3.29 us
  matrix products: 32.8 us -> 39.5 us
    all_gather x1, waiting for transfers between devices: 33.4 us -> 21.2 us  [local(): gathered = lax.all_gather(packed, 'seq', axis=0, tiled=False)]
    reshape x0 -> x2, local copies, waits for them, and re-layouts: none -> 10.7 us  [the longest x1 5.54 us: local(): inputs_x.astype(jnp.float32).reshape(slots, heads, hdim)]
    all_gather x1, blocking collectives: 12.8 us -> 3.29 us  [local(): pair_rows = lax.all_gather(w_in, 'core', axis=0, tiled=True)]
    all_gather x1, waiting for transfers between devices: 75.9 us -> 84.2 us  [local(): weights = lax.all_gather(my_cols, ('seq', 'rq'), axis=0, tiled=False)]
    dot_general x1 -> x2, matrix products: 15.3 us -> 21.3 us  [the longest x1 11.4 us: local(): jnp.einsum('tk,skn->tsn', tok_rows, weights, preferred_element_type=jnp.f...]
    slice x1 -> x3, local copies, waits for them, and re-layouts: 0.14 us -> 6.17 us  [local(): piece[index]]
    ppermute x0 -> x2, waiting for transfers between devices: none -> 5.4 us  [the longest x1 4.01 us: local(): partner_rows = lax.ppermute(tok_rows, 'core', swap)]
    mul x0 -> x4, local copies, waits for them, and re-layouts: none -> 4.03 us  [block_step(): heads_x.astype(jnp.float32) * weighting[:, :, None]]
  transfers between devices with their start and end apart: 4 -> 6, of which waited for: 3 -> 4; matrix products, arithmetic and copies ran while one was open for 12% -> 22% of each run, Pallas kernels for 0% -> 0%
where the time goes in v3:
time: 264 us; the launch traced here: 263 us
  waiting for transfers between devices  111 us (42%)
  local copies, waits for them, and re-layouts  48.8 us (18%)
  matrix products  39.5 us (15%)
  other arithmetic  31.8 us (12%)
  between operations  15.9 us (6%)
  starting transfers between devices  12.6 us (5%)
  blocking collectives  3.29 us (1%)
    all_gather x1, waiting for transfers between devices, local(): weights = lax.all_gather(my_cols, ('seq', 'rq'), axis=0, tiled=False)  84.2 us
    all_gather x1, waiting for transfers between devices, local(): gathered = lax.all_gather(packed, 'seq', axis=0, tiled=False)  21.2 us
    unnamed x57, local copies, waits for them, and re-layouts  11.8 us
    dot_general x1, matrix products, local(): jnp.einsum('tk,skn->tsn', tok_rows, weights, preferred_element_type=jnp.f...  11.4 us
    dot_general x1, matrix products, local(): jnp.einsum('tk,skn->tsn', partner_rows, weights, preferred_element_type=j...  9.93 us
    dot_general x2, matrix products, block_step(): jnp.einsum('htu,uhp->thp', mixing, heads_x, preferred_element_type=jnp.fl...  8.73 us
    all_to_all x1, starting transfers between devices, local(): lax.all_to_all(share[None], ('rq', 'core'), split_axis=1, concat_axis=0,...  7.76 us
    convert_element_type x1, other arithmetic, local(): conv_act = jax.nn.silu(accum).astype(jnp.bfloat16)  6.88 us
  transfers between devices with their start and end apart: 6, of which 4 were waited for; matrix products, arithmetic and copies ran while one was open for 22% of the time, Pallas kernels for 0%

profile of v3, /device:TPU:1, one launch (start us, length us, event | category | flops | bytes accessed | tf_op | source)
XLA Modules:
  0.0 262.8 jit_solution(5338934074301200288)
XLA Ops:
  7.2 3.3 %all_gather.15 = bf16[128,1096]{1,0:T(8,128)(2,1)S(1)} all-gather(bf16[64,1096]{1,0:T(8,128)(2,1)} %param.11), channel_id=1, replica_groups=mesh['rq'=16,'core'=2,'seq'=4] {'core'}, dimensions={0}, use_global_device_ids=true | all-gather | bytes 420864 | tf_op jit(solution)/shard_map/all_gather | solution.py:63
  11.8 4.0 %collective-permute-done = bf16[512,2048]{1,0:T(8,128)(2,1)S(1)} collective-permute-done((bf16[512,2048]{1,0:T(8,128)(2,1)}, bf16[512,2048]{1,0:T(8,128)(2,1)S(1)}, u32[]{:S(2)}, u32[]{:S(2)}) %collective-permute-start) | collective-permute-done | bytes 2097184 | tf_op jit(solution)/shard_map/ppermute | solution.py:68
  15.8 84.2 %all-gather.5.cloned.1.call-done = bf16[8192,548]{1,0:T(8,128)(2,1)} async-done(((bf16[128,548]{1,0:T(8,128)(2,1)}), bf16[8192,548]{1,0:T(8,128)(2,1)}) %all-gather.5.cloned.1.call-update) | async-done | bytes 8978448 | tf_op jit(solution)/shard_map/all_gather | solution.py:65
  100.0 9.9 %convert_bitcast_fusion = bf16[512,4,548]{0,2,1:T(8,128)(2,1)S(1)} fusion(bf16[4,2048,548]{2,1,0:T(8,128)(2,1)} %bitcast.201, bf16[512,2048]{1,0:T(8,128)(2,1)S(1)} %collective-permute-done), kind=kOutput, calls=%fused_computation.38 | convolution fusion | flops 4598079488 | bytes 13320192 | tf_op jit(solution)/shard_map/tk,skn->tsn/dot_general | solution.py:69
  116.3 11.4 %fusion.21 = (bf16[512,4,1,548]{0,3,1,2:T(8,128)(2,1)S(1)}, bf16[512,4,1,548]{0,3,1,2:T(8,128)(2,1)S(1)}) fusion(pred[]{:T(512)S(6)} %eq.12, bf16[512,4,548]{0,1,2:T(4,128)(2,1)} %collective-permute-done.1, bf16[4,2048,548]{2,1,0:T(8,128)(2,1)} %bitcast.202, bf16[1,1,512,2048]{3,2,1,0:T(8,128)(2,1)} %param.10), kind=kOutput, calls=%fused_computation.36 | convolution fusion | flops 4600324096 | bytes 17809408 | tf_op jit(solution)/shard_map/tk,skn->tsn/dot_general | solution.py:73
  128.1 2.5 copy.101
  130.6 5.2 %reshape.254 = bf16[512,4384]{0,1:T(8,128)(2,1)} reshape(bf16[512,4,2,548]{0,3,2,1:T(8,128)(2,1)} %copy.101) | data formatting | bytes 8978432 | tf_op jit(solution)/shard_map/reshape | solution.py:78
  137.4 2.6 copy.121
  140.9 3.4 %collective-permute-start.2 = (bf16[3,2304]{1,0:T(4,128)(2,1)S(1)}, bf16[3,2304]{1,0:T(4,128)(2,1)S(1)}, u32[]{:S(2)}, u32[]{:S(2)}) collective-permute-start(bf16[3,2304]{1,0:T(4,128)(2,1)S(1)} %constant_dynamic-slice_fusion), channel_id=1, source_target_pairs={{0,1},{1,2},{2,3},{4,5},{5,6},{6,7},{8,9},{9,10},{10,11},{12,13},{... | collective-permute-start | bytes 41480 | tf_op jit(solution)/shard_map/ppermute | solution.py:12
  151.1 1.9 copy.109
  155.0 6.9 %multiply_convert_fusion.2 = bf16[512,2304]{1,0:T(8,128)(2,1)S(1)} fusion(bf16[512,2304]{1,0:T(8,128)(2,1)} %copy.121, bf16[3,2304]{1,0:T(4,128)(2,1)S(1)} %collective-permute-done.2, f32[2304]{0:T(1024)S(1)} %get-tuple-element.15, f32[2304]{0:T(1024)S(1)} %get-tuple-element.16, f32[2304]{0:T(1024)S(1)} %get-tuple-element.14, f32[2304]{0:T(1024)S(1)} %get-tuple-element.13, ...), kind=kLoop, calls=%fused_computation.5 | loop fusion | flops 30670848 | bytes 4778496 | tf_op jit(solution)/shard_map/convert_element_type | solution.py:90
  163.5 2.3 copy.110
  175.1 2.3 copy.103
  177.4 2.3 copy.106
  179.7 2.5 slice_convert_fusion
  182.2 5.5 %copy.115 = f32[512,2048]{0,1:T(8,128)} copy(f32[512,2048]{1,0:T(8,128)} %slice_convert_fusion) | data formatting | bytes 8388608 | tf_op jit(solution)/shard_map/reshape | solution.py:133
  190.2 4.4 %bitcast_add_fusion.1 = f32[256,32,64]{0,2,1:T(8,128)} fusion(f32[256,32,64]{0,2,1:T(8,128)S(1)} %fusion.38, bf16[256,32,64]{0,2,1:T(8,128)(2,1)S(1)} %bitcast.199, f32[32,256]{1,0:T(8,128)S(1)} %copy-done.12, f32[32,256]{1,0:T(8,128)S(1)} %copy-done.8, f32[256,256]{1,0:T(8,128)S(1)} %fusion.54, pred[256,256]{1,0:T(8,128)(4,1)S(1)} %copy-done.6, ...), kind=kOutput, calls=%fused_computation.44 | convolution fusion | flops 282066944 | bytes 5668864 | tf_op jit(solution)/shard_map/htu,uhp->thp/dot_general | solution.py:27
  194.6 4.3 %bitcast_add_fusion = f32[256,32,64]{0,2,1:T(8,128)} fusion(f32[256,32,64]{0,2,1:T(8,128)S(1)} %fusion.45, bf16[256,32,64]{0,2,1:T(8,128)(2,1)S(1)} %bitcast.198, f32[32,256]{1,0:T(8,128)S(1)} %copy-done.10, f32[32,256]{1,0:T(8,128)S(1)} %copy-done.9, f32[256,256]{1,0:T(8,128)S(1)} %fusion.49, pred[256,256]{1,0:T(8,128)(4,1)S(1)} %copy-done.6, ...), kind=kOutput, calls=%fused_computation.43 | convolution fusion | flops 282066944 | bytes 5668864 | tf_op jit(solution)/shard_map/htu,uhp->thp/dot_general | solution.py:27
  199.0 21.2 %all-gather.7.cloned.1.call-done = f32[128,8320]{1,0:T(8,128)} async-done(((f32[32,8320]{1,0:T(8,128)}), f32[128,8320]{1,0:T(8,128)}) %all-gather.7.cloned.1.call-update) | async-done | bytes 4259856 | tf_op jit(solution)/shard_map/all_gather | solution.py:120
  220.2 2.6 %slice.219 = f32[4,32,8192]{2,1,0:T(8,128)S(1)} slice(f32[4,32,8320]{2,1,0:T(8,128)} %bitcast.186), slice={[0:4], [0:32], [0:8192]} | slice | bytes 8388608 | tf_op jit(solution)/shard_map/slice | solution.py:121
  227.3 7.8 %all-to-all-start = ((f32[1,32,16,128]{3,2,0,1:T(8,128)}), f32[1,32,16,128]{3,2,0,1:T(8,128)}, u32[]{:S(2)}, u32[]{:S(2)}) async-start(f32[1,32,16,128]{3,2,0,1:T(8,128)} %bitcast.197), calls=%async_computation | async-start | bytes 524288 | tf_op jit(solution)/shard_map/all_to_all | solution.py:144
  238.9 3.8 %fusion.41 = f32[512,32,64]{0,2,1:T(8,128)} fusion(f32[32,64,128]{2,1,0:T(8,128)S(1)} %fusion.35, bf16[512,2304]{1,0:T(8,128)(2,1)S(1)} %multiply_convert_fusion.2), kind=kOutput, calls=%fused_computation.73 | convolution fusion | flops 1610612736 | bytes 5373952 | tf_op jit(solution)/shard_map/tn,hpn->thp/dot_general | solution.py:127
  242.7 5.1 %fusion.6 = f32[512,32,64]{0,2,1:T(8,128)S(1)} fusion(f32[256,32,64]{0,2,1:T(8,128)} %bitcast_add_fusion, f32[256,32,64]{0,2,1:T(8,128)} %bitcast_add_fusion.1, f32[512,32,64]{0,2,1:T(8,128)S(1)} %bitcast.184, f32[512,32,64]{0,2,1:T(8,128)} %fusion.41, f32[32]{0:T(128)S(1)} %copy-done.16, f32[512,32]{0,1:T(8,128)S(1)} %fusion.66), kind=kLoop, calls=%fused_computation.14 | loop fusion | flops 5242880 | bytes 16842880 | tf_op jit(solution)/shard_map/add | solution.py:131
  251.2 2.4 copy.116
  (129 shorter events, 45.1 us)
Async XLA Ops:
  7.2 92.9 %all-gather.5.cloned.1.call-start = ((), (), s32[]{:S(2)}) async-start(), calls=%async_computation.1 | async-start | bytes 10649600 | tf_op jit(solution)/shard_map/all_gather | solution.py:65
  11.3 208.9 %all-gather.7.cloned.1.call-start = ((), (), s32[]{:S(2)}) async-start(), calls=%async_computation.2 | async-start | bytes 5324800 | tf_op jit(solution)/shard_map/all_gather | solution.py:120
  11.4 4.5 %collective-permute-start = (bf16[512,2048]{1,0:T(8,128)(2,1)}, bf16[512,2048]{1,0:T(8,128)(2,1)S(1)}, u32[]{:S(2)}, u32[]{:S(2)}) collective-permute-start(bf16[512,2048]{1,0:T(8,128)(2,1)} %bitcast.203), channel_id=1, source_target_pairs={{0,4},{4,0},{1,5},{5,1},{2,6},{6,2},{3,7},{7,3},{8,12},{12,8},{9,1... | collective-permute-start | bytes 6291464 | tf_op jit(solution)/shard_map/ppermute | solution.py:68
  110.0 4.7 %copy-start.7 = (f32[4,2304]{1,0:T(4,128)S(1)}, f32[4,2304]{1,0:T(4,128)}, u32[]{:S(2)}) copy-start(f32[4,2304]{1,0:T(4,128)} %param.12) | copy-start | bytes 110596
  110.0 4.8 %copy-start.21 = (f32[32]{0:T(128)S(1)}, f32[32]{0:T(128)}, u32[]{:S(2)}) copy-start(f32[32]{0:T(128)} %param.15) | copy-start | bytes 388
  111.2 5.1 %collective-permute-start.1 = (bf16[512,4,548]{0,1,2:T(4,128)(2,1)S(1)}, bf16[512,4,548]{0,1,2:T(4,128)(2,1)}, u32[]{:S(2)}, u32[]{:S(2)}) collective-permute-start(bf16[512,4,548]{0,1,2:T(4,128)(2,1)S(1)} %copy.98), channel_id=1, source_target_pairs={{0,4},{4,0},{1,5},{5,1},{2,6},{6,2},{3,7},{7,3},{8,12},{12,8},{9,1... | collective-permute-start | bytes 6733832 | tf_op jit(solution)/shard_map/ppermute | solution.py:72
  135.8 8.5 %copy-start.17 = (f32[32]{0:T(128)S(1)}, f32[32]{0:T(128)}, u32[]{:S(2)}) copy-start(f32[32]{0:T(128)} %param.14) | copy-start | bytes 388
  140.9 14.1 %collective-permute-start.2 = (bf16[3,2304]{1,0:T(4,128)(2,1)S(1)}, bf16[3,2304]{1,0:T(4,128)(2,1)S(1)}, u32[]{:S(2)}, u32[]{:S(2)}) collective-permute-start(bf16[3,2304]{1,0:T(4,128)(2,1)S(1)} %constant_dynamic-slice_fusion), channel_id=1, source_target_pairs={{0,1},{1,2},{2,3},{4,5},{5,6},{6,7},{8,9},{9,10},{10,11},{12,13},{... | collective-permute-start | bytes 41480 | tf_op jit(solution)/shard_map/ppermute | solution.py:12
  154.9 6.9 %copy-start.2 = (f32[256,2048]{1,0:T(8,128)S(1)}, f32[256,2048]{1,0:T(8,128)}, u32[]{:S(2)}) copy-start(f32[256,2048]{1,0:T(8,128)} %copy.109) | copy-start | bytes 6291460
  154.9 6.9 %copy-start.3 = (f32[256,2048]{1,0:T(8,128)S(1)}, f32[256,2048]{1,0:T(8,128)}, u32[]{:S(2)}) copy-start(f32[256,2048]{1,0:T(8,128)} %copy.113) | copy-start | bytes 6291460
  187.7 2.4 copy-start.6
  187.7 2.4 copy-start.8
  187.7 2.4 copy-start.12
  187.7 2.4 copy-start.13
  190.2 4.4 %copy-start.4 = (bf16[256,2048]{0,1:T(8,128)(2,1)S(1)}, bf16[256,2048]{0,1:T(8,128)(2,1)}, u32[]{:S(2)}) copy-start(bf16[256,2048]{0,1:T(8,128)(2,1)} %copy.106) | copy-start | bytes 3145732
  190.2 4.4 %copy-start.9 = (f32[32,256]{1,0:T(8,128)S(1)}, f32[32,256]{1,0:T(8,128)}, u32[]{:S(2)}) copy-start(f32[32,256]{1,0:T(8,128)} %get-tuple-element.38) | copy-start | bytes 98308
  190.2 4.4 %copy-start.10 = (f32[32,256]{1,0:T(8,128)S(1)}, f32[32,256]{1,0:T(8,128)}, u32[]{:S(2)}) copy-start(f32[32,256]{1,0:T(8,128)} %get-tuple-element.30) | copy-start | bytes 98308
  190.2 4.4 %copy-start.11 = (f32[256,32]{0,1:T(8,128)S(1)}, f32[256,32]{0,1:T(8,128)}, u32[]{:S(2)}) copy-start(f32[256,32]{0,1:T(8,128)} %get-tuple-element.36) | copy-start | bytes 98308
  220.2 3.5 %copy-start.1 = (f32[128,8320]{1,0:T(8,128)S(1)}, f32[128,8320]{1,0:T(8,128)}, u32[]{:S(2)}) copy-start(f32[128,8320]{1,0:T(8,128)} %all-gather.7.cloned.1.call-done) | copy-start | bytes 12779524
  227.3 26.3 %all-to-all-start = ((f32[1,32,16,128]{3,2,0,1:T(8,128)}), f32[1,32,16,128]{3,2,0,1:T(8,128)}, u32[]{:S(2)}, u32[]{:S(2)}) async-start(f32[1,32,16,128]{3,2,0,1:T(8,128)} %bitcast.197), calls=%async_computation | async-start | bytes 524288 | tf_op jit(solution)/shard_map/all_to_all | solution.py:144
  238.1 4.6 %copy-start = (f32[512,2048]{0,1:T(8,128)S(1)}, f32[512,2048]{0,1:T(8,128)}, u32[]{:S(2)}) copy-start(f32[512,2048]{0,1:T(8,128)} %copy.115) | copy-start | bytes 12582916
  238.1 4.6 %copy-start.16 = (f32[32]{0:T(128)S(1)}, f32[32]{0:T(128)}, u32[]{:S(2)}) copy-start(f32[32]{0:T(128)} %param.16) | copy-start | bytes 388
  238.9 9.0 %slice-start = ((s8[4489216]{0:T(1024)(128)(4,1)}), s8[4194304]{0:T(1024)(128)(4,1)S(1)}, s32[]{:S(2)}) async-start(s8[4489216]{0:T(1024)(128)(4,1)} %bitcast.182), calls=%async_computation.3 | async-start | bytes 8388608
  242.7 5.2 %slice-start.1 = ((s8[4489216]{0:T(1024)(128)(4,1)}), s8[294912]{0:T(1024)(128)(4,1)S(1)}, s32[]{:S(2)}) async-start(s8[4489216]{0:T(1024)(128)(4,1)} %bitcast.182), calls=%async_computation.4 | async-start | bytes 589824
  (7 other events, 12.5 us)
Sparse Core Ops, SparseCore 0:
  11.4 88.5 all-gather.4
  172.3 47.8 all-gather.6

commit v4 on v2

--- a/solution.py
+++ b/solution.py
@@ -59,14 +59,12 @@
     qlen = jnp.sum(jnp.where(prompt_group == my_group, lengths, 0))
     filled = jnp.arange(slots, dtype=jnp.int32) < qlen
     wide_rows = lax.all_gather(w_in, "seq", axis=1, tiled=True)
-    projected = jnp.dot(
-        tok_rows,
-        lax.all_gather(wide_rows, "req", axis=0, tiled=True),
-        preferred_element_type=jnp.float32,
-    ).astype(jnp.bfloat16)
-    gate_z = projected[:, :inner]
-    conv_in = projected[:, inner : inner + convdim]
-    dt_raw = projected[:, inner + convdim :]
+    ssm_weights = lax.all_gather(wide_rows[:, inner:], "req", axis=0, tiled=True)
+    ssm_weights, gate_rows = lax.optimization_barrier((ssm_weights, wide_rows[:, :inner]))
+    gate_weights = lax.all_gather(gate_rows, "req", axis=0, tiled=True)
+    ssm_part = jnp.dot(tok_rows, ssm_weights, preferred_element_type=jnp.float32).astype(jnp.bfloat16)
+    conv_in = ssm_part[:, :convdim]
+    dt_raw = ssm_part[:, convdim:]
     edge_rows = lax.dynamic_slice_in_dim(conv_in, qlen - (taps - 1), taps - 1, 0)
     prev_edge = shifted(edge_rows, "seq", 1)
     extended = jnp.concatenate([prev_edge, conv_in], axis=0)
@@ -105,7 +103,9 @@
         [local_end.reshape(heads, hdim * nstate), jnp.broadcast_to(block_total[:, None], (heads, 128))],
         axis=1,
     )
+    packed, gate_weights = lax.optimization_barrier((packed, gate_weights))
     gathered = lax.all_gather(packed, "seq", axis=0, tiled=False)
+    gate_z = jnp.dot(tok_rows, gate_weights, preferred_element_type=jnp.float32).astype(jnp.bfloat16)
     ends = gathered[:, :, : hdim * nstate].reshape(seq_count, heads, hdim, nstate)
     totals = gathered[:, :, hdim * nstate]
     entering = zero_state

time: 235 us -> 237 us (level)
  waiting for transfers between devices: 109 us -> 117 us
  other arithmetic: 32.1 us -> 26.3 us
    dot_general x1 -> x2, matrix products: 15.3 us -> 20.1 us  [the longest x1 10.7 us: local(): jnp.dot(tok_rows, gate_weights, preferred_element_type=jnp.float32)]
    reduce_sum x1 -> x0, other arithmetic: 4.53 us -> none  [local(): scale = lax.rsqrt(jnp.mean(gated * gated, axis=1, keepdims=True) + 1e-05)]
    all_gather x1, waiting for transfers between devices: 33.4 us -> 36.6 us  [local(): gathered = lax.all_gather(packed, 'seq', axis=0, tiled=False)]
    all_gather x1 -> x2, waiting for transfers between devices: 75.9 us -> 79 us  [the longest x1 60.6 us: local(): lax.all_gather(wide_rows[:, inner:], 'req', axis=0, tiled=True)]
  transfers between devices with their start and end apart: 4 -> 5, of which waited for: 3 -> 4; matrix products, arithmetic and copies ran while one was open for 12% -> 22% of each run, Pallas kernels for 0% -> 0%
where the time goes in v4:
time: 237 us; the launch traced here: 236 us
  waiting for transfers between devices  117 us (49%)
  matrix products  34 us (14%)
  other arithmetic  26.3 us (11%)
  local copies, waits for them, and re-layouts  19.8 us (8%)
  between operations  15.6 us (7%)
  blocking collectives  12.8 us (5%)
  starting transfers between devices  11.1 us (5%)
    all_gather x1, waiting for transfers between devices, local(): lax.all_gather(wide_rows[:, inner:], 'req', axis=0, tiled=True)  60.6 us
    all_gather x1, waiting for transfers between devices, local(): gathered = lax.all_gather(packed, 'seq', axis=0, tiled=False)  36.6 us
    all_gather x1, waiting for transfers between devices, local(): gate_weights = lax.all_gather(gate_rows, 'req', axis=0, tiled=True)  18.4 us
    all_gather x1, blocking collectives, local(): wide_rows = lax.all_gather(w_in, 'seq', axis=1, tiled=True)  12.8 us
    unnamed x37, local copies, waits for them, and re-layouts  11.7 us
    dot_general x1, matrix products, local(): jnp.dot(tok_rows, gate_weights, preferred_element_type=jnp.float32)  10.7 us
    convert_element_type x1, other arithmetic, local(): conv_act = jax.nn.silu(accum).astype(jnp.bfloat16)  10.5 us
    dot_general x1, matrix products, local(): jnp.dot(tok_rows, ssm_weights, preferred_element_type=jnp.float32)  9.46 us
  transfers between devices with their start and end apart: 5, of which 4 were waited for; matrix products, arithmetic and copies ran while one was open for 22% of the time, Pallas kernels for 0%

profile of v4, /device:TPU:1, one launch (start us, length us, event | category | flops | bytes accessed | tf_op | source)
XLA Modules:
  0.0 236.2 jit_solution(5672945075955923271)
XLA Ops:
  7.3 12.8 %all-gather.1 = bf16[4,1096,64]{1,2,0:T(8,128)(2,1)S(1)} all-gather(bf16[1,1096,64]{1,2,0:T(8,128)(2,1)} %bitcast.200), channel_id=1, replica_groups=mesh['req'=32,'seq'=4] {'seq'}, dimensions={0}, use_global_device_ids=true | all-gather | bytes 701440 | tf_op jit(solution)/shard_map/all_gather | solution.py:61
  22.5 60.6 %all-gather.6.cloned.1.call-done = bf16[2048,2336]{1,0:T(8,128)(2,1)} async-done(((bf16[64,2336]{1,0:T(8,128)(2,1)}), bf16[2048,2336]{1,0:T(8,128)(2,1)}) %all-gather.6.cloned.1.call-update) | async-done | bytes 9568272 | tf_op jit(solution)/shard_map/all_gather | solution.py:62
  86.0 9.5 %fusion.19 = bf16[512,2336]{0,1:T(8,128)(2,1)S(1)} fusion(bf16[2048,2336]{1,0:T(8,128)(2,1)} %all-gather.6.cloned.1.call-done, bf16[1,1,512,2048]{3,2,1,0:T(8,128)(2,1)S(1)} %copy-done), kind=kOutput, calls=%fused_computation.30 | convolution fusion | flops 4900143104 | bytes 14057472 | tf_op jit(solution)/shard_map/dot_general | solution.py:65
  95.4 1.6 slice.193
  98.8 1.5 constant_dynamic-slice_fusion
  100.5 3.3 %collective-permute-start = (bf16[3,2304]{1,0:T(4,128)(2,1)S(1)}, bf16[3,2304]{1,0:T(4,128)(2,1)S(1)}, u32[]{:S(2)}, u32[]{:S(2)}) collective-permute-start(bf16[3,2304]{1,0:T(4,128)(2,1)S(1)} %copy.71), channel_id=1, source_target_pairs={{0,1},{1,2},{2,3},{4,5},{5,6},{6,7},{8,9},{9,10},{10,11},{12,13},{... | collective-permute-start | bytes 41480 | tf_op jit(solution)/shard_map/ppermute | solution.py:12
  103.8 1.2 reduce-window.26
  106.5 10.5 %multiply_convert_fusion.2 = bf16[512,2304]{0,1:T(8,128)(2,1)S(1)} fusion(bf16[512,2304]{0,1:T(8,128)(2,1)} %slice.193, bf16[3,2304]{0,1:T(8,128)(2,1)S(1)} %copy.72, f32[2304]{0:T(1024)S(1)} %get-tuple-element.25, f32[2304]{0:T(1024)S(1)} %get-tuple-element.26, f32[2304]{0:T(1024)S(1)} %get-tuple-element.24, f32[2304]{0:T(1024)S(1)} %get-tuple-element.23, ...), kind=kLoop, calls=%fused_computation.3 | loop fusion | flops 30670848 | bytes 4778496 | tf_op jit(solution)/shard_map/convert_element_type | solution.py:76
  119.1 1.2 pad_maximum_fusion.1
  120.2 18.4 %all-gather.8.cloned.1.call-done = bf16[2048,2048]{1,0:T(8,128)(2,1)} async-done(((bf16[64,2048]{1,0:T(8,128)(2,1)}), bf16[2048,2048]{1,0:T(8,128)(2,1)}) %all-gather.8.cloned.1.call-update) | async-done | bytes 8388624 | tf_op jit(solution)/shard_map/all_gather | solution.py:64
  138.9 1.5 copy-done.2
  140.8 1.0 fusion.30
  141.7 1.0 fusion.37
  142.9 4.4 %bitcast_add_fusion.1 = f32[256,32,64]{0,2,1:T(8,128)} fusion(f32[256,32,64]{0,2,1:T(8,128)S(1)} %fusion.30, bf16[256,32,64]{0,2,1:T(8,128)(2,1)S(1)} %bitcast.198, f32[32,256]{1,0:T(8,128)S(1)} %get-tuple-element.39, f32[32,256]{1,0:T(8,128)S(1)} %get-tuple-element.47, f32[256,256]{1,0:T(8,128)S(1)} %fusion.46, pred[256,256]{1,0:T(8,128)(4,1)S(1)} %iota_compare_fusion, ...), kind=kOutput, calls=%fused_computation.45 | convolution fusion | flops 282066944 | bytes 5668864 | tf_op jit(solution)/shard_map/htu,uhp->thp/dot_general | solution.py:27
  147.3 4.3 %bitcast_add_fusion = f32[256,32,64]{0,2,1:T(8,128)} fusion(f32[256,32,64]{0,2,1:T(8,128)S(1)} %fusion.37, bf16[256,32,64]{0,2,1:T(8,128)(2,1)S(1)} %bitcast.197, f32[32,256]{1,0:T(8,128)S(1)} %get-tuple-element.38, f32[32,256]{1,0:T(8,128)S(1)} %get-tuple-element.46, f32[256,256]{1,0:T(8,128)S(1)} %fusion.41, pred[256,256]{1,0:T(8,128)(4,1)S(1)} %iota_compare_fusion, ...), kind=kOutput, calls=%fused_computation.44 | convolution fusion | flops 282066944 | bytes 5668864 | tf_op jit(solution)/shard_map/htu,uhp->thp/dot_general | solution.py:27
  151.6 36.6 %all-gather.10.cloned.1.call-done = f32[128,8320]{1,0:T(8,128)} async-done(((f32[32,8320]{1,0:T(8,128)}), f32[128,8320]{1,0:T(8,128)}) %all-gather.10.cloned.1.call-update) | async-done | bytes 4259856 | tf_op jit(solution)/shard_map/all_gather | solution.py:107
  188.2 2.2 slice_bitcast_fusion.2
  194.2 1.9 fusion.33
  196.1 3.1 %fusion.2 = f32[512,32,64]{0,2,1:T(8,128)S(1)} fusion(f32[256,32,64]{0,2,1:T(8,128)} %bitcast_add_fusion, f32[256,32,64]{0,2,1:T(8,128)S(1)} %copy-done.5, bf16[512,32,64]{0,2,1:T(8,128)(2,1)S(1)} %bitcast.183, f32[512,32,64]{0,2,1:T(8,128)S(1)} %fusion.33, f32[32]{0:T(128)S(1)} %copy-done.10, f32[512,32]{0,1:T(8,128)S(1)} %fusion.58), kind=kLoop, calls=%fused_computation.8 | loop fusion | flops 6291456 | bytes 14745728 | tf_op jit(solution)/shard_map/add | solution.py:119
  199.2 10.7 %multiply_reduce_fusion = (f32[512]{0:T(512)S(1)}, f32[512,2048]{0,1:T(8,128)}) fusion(bf16[2048,2048]{1,0:T(8,128)(2,1)} %all-gather.8.cloned.1.call-done, bf16[1,1,512,2048]{3,2,1,0:T(8,128)(2,1)S(1)} %copy-done, f32[512,32,64]{0,2,1:T(8,128)S(1)} %fusion.2), kind=kOutput, calls=%fused_computation.17 | convolution fusion | flops 4304403968 | bytes 18876416 | tf_op jit(solution)/shard_map/dot_general | solution.py:108
  211.6 7.7 %all-to-all-start = ((f32[1,32,16,128]{3,2,0,1:T(8,128)}), f32[1,32,16,128]{3,2,0,1:T(8,128)S(1)}, u32[]{:S(2)}, u32[]{:S(2)}) async-start(f32[1,32,16,128]{3,2,0,1:T(8,128)} %bitcast.33), calls=%async_computation | async-start | bytes 524288 | tf_op jit(solution)/shard_map/all_to_all | solution.py:132
  219.3 4.0 %fusion.22 = bf16[1,1,512,2048]{2,3,1,0:T(8,128)(2,1)} fusion(f32[512,2048]{0,1:T(8,128)} %get-tuple-element.52, f32[2048]{0:T(1024)S(1)} %copy-done.8, f32[512]{0:T(512)S(1)} %add_rsqrt_fusion, pred[512]{0:T(512)(128)(4,1)S(1)} %iota_compare_fusion.2), kind=kLoop, calls=%fused_computation.39 | loop fusion | flops 4194304 | bytes 6302208 | tf_op jit(solution)/shard_map/reshape | solution.py:126
  223.4 3.9 %copy.84 = bf16[1,1,512,2048]{3,2,1,0:T(8,128)(2,1)} copy(bf16[1,1,512,2048]{2,3,1,0:T(8,128)(2,1)} %fusion.22) | data formatting | bytes 4194304
  227.3 0.9 all-to-all-done
  (97 shorter events, 17.0 us)
Async XLA Ops:
  7.2 78.8 %copy-start = (bf16[1,1,512,2048]{3,2,1,0:T(8,128)(2,1)S(1)}, bf16[1,1,512,2048]{3,2,1,0:T(8,128)(2,1)}, u32[]{:S(2)}) copy-start(bf16[1,1,512,2048]{3,2,1,0:T(8,128)(2,1)} %param.10) | copy-start | bytes 6291460
  7.2 76.0 %copy-start.11 = (s32[32]{0:T(128)S(1)}, s32[32]{0:T(128)}, u32[]{:S(2)}) copy-start(s32[32]{0:T(128)} %param.18) | copy-start | bytes 388
  7.2 76.0 %copy-start.12 = (s32[32]{0:T(128)S(1)}, s32[32]{0:T(128)}, u32[]{:S(2)}) copy-start(s32[32]{0:T(128)} %param.19) | copy-start | bytes 388
  7.2 78.6 %copy-start.6 = (f32[4,2304]{1,0:T(4,128)S(1)}, f32[4,2304]{1,0:T(4,128)}, u32[]{:S(2)}) copy-start(f32[4,2304]{1,0:T(4,128)} %param.12) | copy-start | bytes 110596
  7.2 78.7 %copy-start.13 = (f32[32]{0:T(128)S(1)}, f32[32]{0:T(128)}, u32[]{:S(2)}) copy-start(f32[32]{0:T(128)} %param.15) | copy-start | bytes 388
  7.2 75.9 %all-gather.6.cloned.1.call-start = ((), (), s32[]{:S(2)}) async-start(), calls=%async_computation.1 | async-start | bytes 10272768 | tf_op jit(solution)/shard_map/all_gather | solution.py:62
  21.8 116.9 %all-gather.8.cloned.1.call-start = ((), (), s32[]{:S(2)}) async-start(), calls=%async_computation.2 | async-start | bytes 8650752 | tf_op jit(solution)/shard_map/all_gather | solution.py:64
  83.1 105.0 %all-gather.10.cloned.1.call-start = ((), (), s32[]{:S(2)}) async-start(), calls=%async_computation.3 | async-start | bytes 5324800 | tf_op jit(solution)/shard_map/all_gather | solution.py:107
  95.4 1.6 copy-start.9
  95.4 11.1 %copy-start.7 = (f32[2304]{0:T(1024)S(1)}, f32[2304]{0:T(1024)}, u32[]{:S(2)}) copy-start(f32[2304]{0:T(1024)} %param.13) | copy-start | bytes 27652
  100.5 5.6 %collective-permute-start = (bf16[3,2304]{1,0:T(4,128)(2,1)S(1)}, bf16[3,2304]{1,0:T(4,128)(2,1)S(1)}, u32[]{:S(2)}, u32[]{:S(2)}) collective-permute-start(bf16[3,2304]{1,0:T(4,128)(2,1)S(1)} %copy.71), channel_id=1, source_target_pairs={{0,1},{1,2},{2,3},{4,5},{5,6},{6,7},{8,9},{9,10},{10,11},{12,13},{... | collective-permute-start | bytes 41480 | tf_op jit(solution)/shard_map/ppermute | solution.py:12
  117.0 1.4 copy-start.1
  138.7 1.7 copy-start.2
  188.2 3.2 %copy-start.4 = (f32[128,8320]{1,0:T(8,128)S(1)}, f32[128,8320]{1,0:T(8,128)}, u32[]{:S(2)}) copy-start(f32[128,8320]{1,0:T(8,128)} %all-gather.10.cloned.1.call-done) | copy-start | bytes 12779524
  192.2 2.0 copy-start.3
  192.6 3.5 %slice-start = ((bf16[512,2304]{0,1:T(8,128)(2,1)}), bf16[512,2048]{0,1:T(8,128)(2,1)S(1)}, s32[]{:S(2)}) async-start(bf16[512,2304]{0,1:T(8,128)(2,1)} %copy-done.1), calls=%async_computation.4 | async-start | bytes 4194304 | tf_op jit(solution)/shard_map/slice | solution.py:77
  192.6 3.5 %copy-start.5 = (f32[256,32,64]{0,2,1:T(8,128)S(1)}, f32[256,32,64]{0,2,1:T(8,128)}, u32[]{:S(2)}) copy-start(f32[256,32,64]{0,2,1:T(8,128)} %bitcast_add_fusion.1) | copy-start | bytes 6291460
  192.7 3.5 %copy-start.10 = (f32[32]{0:T(128)S(1)}, f32[32]{0:T(128)}, u32[]{:S(2)}) copy-start(f32[32]{0:T(128)} %param.16) | copy-start | bytes 388
  209.9 9.5 %copy-start.8 = (f32[2048]{0:T(1024)S(1)}, f32[2048]{0:T(1024)}, u32[]{:S(2)}) copy-start(f32[2048]{0:T(1024)} %param.17) | copy-start | bytes 24580
  211.6 16.6 %all-to-all-start = ((f32[1,32,16,128]{3,2,0,1:T(8,128)}), f32[1,32,16,128]{3,2,0,1:T(8,128)S(1)}, u32[]{:S(2)}, u32[]{:S(2)}) async-start(f32[1,32,16,128]{3,2,0,1:T(8,128)} %bitcast.33), calls=%async_computation | async-start | bytes 524288 | tf_op jit(solution)/shard_map/all_to_all | solution.py:132
Sparse Core Ops, SparseCore 0:
  21.9 61.1 all-gather.5
  86.0 52.6 all-gather.7
  140.3 47.8 all-gather.9

commit v5 on v2

--- a/solution.py
+++ b/solution.py
@@ -101,13 +101,20 @@
         local_end, out = block_step(local_end, tuple(piece[index] for piece in pieces))
         outs.append(out)
     outputs = jnp.concatenate(outs, axis=0)
+    total_hi = lax.reduce_precision(block_total, exponent_bits=8, mantissa_bits=7)
+    total_rest = block_total - total_hi
+    total_mid = lax.reduce_precision(total_rest, exponent_bits=8, mantissa_bits=7)
+    total_lo = total_rest - total_mid
+    parts = jnp.stack([total_hi, total_mid, total_lo], axis=1).astype(jnp.bfloat16)
+    parts = jnp.broadcast_to(parts[:, :, None], (heads, 3, 128))
     packed = jnp.concatenate(
-        [local_end.reshape(heads, hdim * nstate), jnp.broadcast_to(block_total[:, None], (heads, 128))],
+        [local_end.reshape(heads, hdim * nstate).astype(jnp.bfloat16), parts.reshape(heads, 3 * 128)],
         axis=1,
     )
     gathered = lax.all_gather(packed, "seq", axis=0, tiled=False)
-    ends = gathered[:, :, : hdim * nstate].reshape(seq_count, heads, hdim, nstate)
-    totals = gathered[:, :, hdim * nstate]
+    ends = gathered[:, :, : hdim * nstate].astype(jnp.float32).reshape(seq_count, heads, hdim, nstate)
+    sent = gathered[:, :, hdim * nstate :].astype(jnp.float32)
+    totals = sent[:, :, 0] + (sent[:, :, 128] + sent[:, :, 256])
     entering = zero_state
     for turn in range(seq_count - 1):
         stepped = jnp.exp(totals[turn])[:, None, None] * entering + ends[turn]

time: 235 us -> 218 us (0.928)
  waiting for transfers between devices: 109 us -> 92.5 us
  matrix products: 32.8 us -> 29.2 us
  other arithmetic: 32.1 us -> 35.5 us
    all_gather x1, waiting for transfers between devices: 33.4 us -> 17.3 us  [local(): gathered = lax.all_gather(packed, 'seq', axis=0, tiled=False)]
    reduce_sum x1, other arithmetic: 4.53 us -> 1.41 us  [local(): scale = lax.rsqrt(jnp.mean(gated * gated, axis=1, keepdims=True) + 1e-05)]
    convert_element_type x0 -> x2, other arithmetic: none -> 2.91 us  [the longest x1 2 us: local(): gathered[:, :, :hdim * nstate].astype(jnp.float32)]
    unnamed x37 -> x48, local copies, waits for them, and re-layouts: 11.1 us -> 10.9 us
  transfers between devices with their start and end apart: 4 -> 4, of which waited for: 3 -> 2; matrix products, arithmetic and copies ran while one was open for 12% -> 18% of each run, Pallas kernels for 0% -> 0%
where the time goes in v5:
time: 218 us; the launch traced here: 217 us
  waiting for transfers between devices  92.5 us (42%)
  other arithmetic  35.5 us (16%)
  matrix products  29.2 us (13%)
  local copies, waits for them, and re-layouts  20 us (9%)
  between operations  15.9 us (7%)
  blocking collectives  12.8 us (6%)
  starting transfers between devices  11.1 us (5%)
    all_gather x1, waiting for transfers between devices, local(): lax.all_gather(wide_rows, 'req', axis=0, tiled=True)  75.2 us
    all_gather x1, waiting for transfers between devices, local(): gathered = lax.all_gather(packed, 'seq', axis=0, tiled=False)  17.3 us
    dot_general x1, matrix products, local(): jnp.dot(tok_rows, lax.all_gather(wide_rows, 'req', axis=0, tiled=True), p...  15.3 us
    all_gather x1, blocking collectives, local(): wide_rows = lax.all_gather(w_in, 'seq', axis=1, tiled=True)  12.8 us
    unnamed x48, local copies, waits for them, and re-layouts  10.9 us
    convert_element_type x1, other arithmetic, local(): conv_act = jax.nn.silu(accum).astype(jnp.bfloat16)  10.5 us
    dot_general x2, matrix products, block_step(): jnp.einsum('htu,uhp->thp', mixing, heads_x, preferred_element_type=jnp.fl...  8.76 us
    all_to_all x1, starting transfers between devices, local(): lax.all_to_all(share[None], 'req', split_axis=1, concat_axis=0, tiled=True)  7.77 us
  transfers between devices with their start and end apart: 4, of which 2 were waited for; matrix products, arithmetic and copies ran while one was open for 18% of the time, Pallas kernels for 0%

profile of v5, /device:TPU:1, one launch (start us, length us, event | category | flops | bytes accessed | tf_op | source)
XLA Modules:
  0.0 217.0 jit_solution(9497161019344867276)
XLA Ops:
  7.2 12.8 %all-gather.1 = bf16[4,1096,64]{1,2,0:T(8,128)(2,1)S(1)} all-gather(bf16[1,1096,64]{1,2,0:T(8,128)(2,1)} %bitcast.194), channel_id=1, replica_groups=mesh['req'=32,'seq'=4] {'seq'}, dimensions={0}, use_global_device_ids=true | all-gather | bytes 701440 | tf_op jit(solution)/shard_map/all_gather | solution.py:61
  20.5 1.2 reshape.358
  21.8 1.3 compare_select_fusion.1
  27.5 75.2 %all-gather.5.cloned.1.call-done = bf16[2048,4384]{1,0:T(8,128)(2,1)} async-done(((bf16[64,4384]{1,0:T(8,128)(2,1)}), bf16[2048,4384]{1,0:T(8,128)(2,1)}) %all-gather.5.cloned.1.call-update) | async-done | bytes 17956880 | tf_op jit(solution)/shard_map/all_gather | solution.py:64
  102.7 15.3 %convolution_convert_fusion = bf16[512,4384]{0,1:T(8,128)(2,1)} fusion(bf16[2048,4384]{1,0:T(8,128)(2,1)} %all-gather.5.cloned.1.call-done, bf16[1,1,512,2048]{3,2,1,0:T(8,128)(2,1)S(1)} %copy-done), kind=kOutput, calls=%fused_computation.3 | convolution fusion | flops 9196158976 | bytes 24543232 | tf_op jit(solution)/shard_map/dot_general | solution.py:62
  118.0 1.8 slice.193
  124.7 3.3 %collective-permute-start = (bf16[3,2304]{1,0:T(4,128)(2,1)S(1)}, bf16[3,2304]{1,0:T(4,128)(2,1)S(1)}, u32[]{:S(2)}, u32[]{:S(2)}) collective-permute-start(bf16[3,2304]{1,0:T(4,128)(2,1)S(1)} %copy.75), channel_id=1, source_target_pairs={{0,1},{1,2},{2,3},{4,5},{5,6},{6,7},{8,9},{9,10},{10,11},{12,13},{... | collective-permute-start | bytes 41480 | tf_op jit(solution)/shard_map/ppermute | solution.py:12
  128.5 1.2 reduce-window.26
  132.0 10.5 %multiply_convert_fusion.2 = bf16[512,2304]{0,1:T(8,128)(2,1)S(1)} fusion(bf16[512,2304]{0,1:T(8,128)(2,1)} %copy-done.2, bf16[3,2304]{0,1:T(8,128)(2,1)S(1)} %copy.76, f32[2304]{0:T(1024)S(1)} %get-tuple-element.17, f32[2304]{0:T(1024)S(1)} %get-tuple-element.18, f32[2304]{0:T(1024)S(1)} %get-tuple-element.16, f32[2304]{0:T(1024)S(1)} %get-tuple-element.15, ...), kind=kLoop, calls=%fused_computation.6 | loop fusion | flops 30670848 | bytes 4778496 | tf_op jit(solution)/shard_map/convert_element_type | solution.py:78
  145.7 1.4 slice.227
  149.7 4.4 %bitcast_add_fusion.1 = f32[256,32,64]{0,2,1:T(8,128)} fusion(f32[256,32,64]{0,2,1:T(8,128)S(1)} %fusion.29, bf16[256,32,64]{0,2,1:T(8,128)(2,1)S(1)} %bitcast.192, f32[32,256]{1,0:T(8,128)S(1)} %copy-done.8, f32[32,256]{1,0:T(8,128)S(1)} %copy-done.4, f32[256,256]{1,0:T(8,128)S(1)} %fusion.46, pred[256,256]{1,0:T(8,128)(4,1)S(1)} %iota_compare_fusion, ...), kind=kOutput, calls=%fused_computation.44 | convolution fusion | flops 282066944 | bytes 5668864 | tf_op jit(solution)/shard_map/htu,uhp->thp/dot_general | solution.py:27
  154.2 4.3 %bitcast_add_fusion = f32[256,32,64]{0,2,1:T(8,128)} fusion(f32[256,32,64]{0,2,1:T(8,128)S(1)} %fusion.37, bf16[256,32,64]{0,2,1:T(8,128)(2,1)S(1)} %bitcast.191, f32[32,256]{1,0:T(8,128)S(1)} %copy-done.6, f32[32,256]{1,0:T(8,128)S(1)} %copy-done.5, f32[256,256]{1,0:T(8,128)S(1)} %fusion.41, pred[256,256]{1,0:T(8,128)(4,1)S(1)} %iota_compare_fusion, ...), kind=kOutput, calls=%fused_computation.43 | convolution fusion | flops 282066944 | bytes 5668864 | tf_op jit(solution)/shard_map/htu,uhp->thp/dot_general | solution.py:27
  158.5 17.3 %all-gather.7.cloned.1.call-done = bf16[128,8576]{1,0:T(8,128)(2,1)} async-done(((bf16[32,8576]{1,0:T(8,128)(2,1)}), bf16[128,8576]{1,0:T(8,128)(2,1)}) %all-gather.7.cloned.1.call-update) | async-done | bytes 2195472 | tf_op jit(solution)/shard_map/all_gather | solution.py:114
  175.8 2.0 slice_convert_fusion
  178.7 1.6 slice_bitcast_fusion.2
  182.1 7.8 %all-to-all-start = ((f32[1,32,16,128]{3,2,0,1:T(8,128)}), f32[1,32,16,128]{3,2,0,1:T(8,128)}, u32[]{:S(2)}, u32[]{:S(2)}) async-start(f32[1,32,16,128]{3,2,0,1:T(8,128)} %bitcast.190), calls=%async_computation | async-start | bytes 524288 | tf_op jit(solution)/shard_map/all_to_all | solution.py:139
  189.9 1.4 copy.109
  191.3 1.4 copy.110
  193.9 1.9 fusion.32
  195.8 3.7 %fusion.6 = f32[512,32,64]{0,2,1:T(8,128)S(1)} fusion(f32[256,32,64]{0,2,1:T(8,128)} %bitcast_add_fusion, f32[256,32,64]{0,2,1:T(8,128)} %bitcast_add_fusion.1, bf16[512,32,64]{0,2,1:T(8,128)(2,1)S(1)} %bitcast.181, f32[512,32,64]{0,2,1:T(8,128)S(1)} %fusion.32, f32[32]{0:T(128)S(1)} %copy-done.13, f32[512,32]{0,1:T(8,128)S(1)} %fusion.59), kind=kLoop, calls=%fused_computation.14 | loop fusion | flops 6291456 | bytes 14745728 | tf_op jit(solution)/shard_map/add | solution.py:126
  199.6 1.4 multiply_reduce_fusion
  201.0 2.9 %fusion.21 = bf16[1,1,512,2048]{2,3,1,0:T(8,128)(2,1)} fusion(f32[2048]{0:T(1024)S(1)} %copy-done.11, f32[512]{0:T(512)S(1)} %add_rsqrt_fusion, pred[512]{0:T(512)(128)(4,1)S(1)} %iota_compare_fusion.2, bf16[512,4384]{0,1:T(8,128)(2,1)S(1)} %bitcast.180, f32[512,32,64]{0,2,1:T(8,128)S(1)} %fusion.6), kind=kLoop, calls=%fused_computation.37 | loop fusion | flops 10485760 | bytes 8399360 | tf_op jit(solution)/shard_map/reshape | solution.py:133
  203.9 3.9 %copy.89 = bf16[1,1,512,2048]{3,2,1,0:T(8,128)(2,1)} copy(bf16[1,1,512,2048]{2,3,1,0:T(8,128)(2,1)} %fusion.21) | data formatting | bytes 4194304
  207.9 1.5 gather_fusion
  (107 shorter events, 21.5 us)
Async XLA Ops:
  7.2 95.5 %copy-start = (bf16[1,1,512,2048]{3,2,1,0:T(8,128)(2,1)S(1)}, bf16[1,1,512,2048]{3,2,1,0:T(8,128)(2,1)}, u32[]{:S(2)}) copy-start(bf16[1,1,512,2048]{3,2,1,0:T(8,128)(2,1)} %param.10) | copy-start | bytes 6291460
  7.2 95.5 %all-gather.5.cloned.1.call-start = ((), (), s32[]{:S(2)}) async-start(), calls=%async_computation.1 | async-start | bytes 18923520 | tf_op jit(solution)/shard_map/all_gather | solution.py:64
  21.8 154.0 %all-gather.7.cloned.1.call-start = ((), (), s32[]{:S(2)}) async-start(), calls=%async_computation.2 | async-start | bytes 2744320 | tf_op jit(solution)/shard_map/all_gather | solution.py:114
  118.0 1.9 copy-start.12
  118.0 14.0 %copy-start.10 = (f32[2304]{0:T(1024)S(1)}, f32[2304]{0:T(1024)}, u32[]{:S(2)}) copy-start(f32[2304]{0:T(1024)} %param.13) | copy-start | bytes 27652
  119.9 12.1 %copy-start.2 = (bf16[512,2304]{0,1:T(8,128)(2,1)}, bf16[512,2304]{0,1:T(8,128)(2,1)S(1)}, u32[]{:S(2)}) copy-start(bf16[512,2304]{0,1:T(8,128)(2,1)S(1)} %slice.193) | copy-start | bytes 7077892
  124.7 6.9 %collective-permute-start = (bf16[3,2304]{1,0:T(4,128)(2,1)S(1)}, bf16[3,2304]{1,0:T(4,128)(2,1)S(1)}, u32[]{:S(2)}, u32[]{:S(2)}) collective-permute-start(bf16[3,2304]{1,0:T(4,128)(2,1)S(1)} %copy.75), channel_id=1, source_target_pairs={{0,1},{1,2},{2,3},{4,5},{5,6},{6,7},{8,9},{9,10},{10,11},{12,13},{... | collective-permute-start | bytes 41480 | tf_op jit(solution)/shard_map/ppermute | solution.py:12
  132.0 10.9 %copy-start.14 = (f32[32]{0:T(128)S(1)}, f32[32]{0:T(128)}, u32[]{:S(2)}) copy-start(f32[32]{0:T(128)} %exponential_multiply_fusion.2) | copy-start | bytes 388
  142.5 0.9 copy-start.15
  148.5 1.2 copy-start.4
  148.5 1.2 copy-start.8
  148.5 1.2 copy-start.9
  149.7 4.5 %copy-start.5 = (f32[32,256]{1,0:T(8,128)S(1)}, f32[32,256]{1,0:T(8,128)}, u32[]{:S(2)}) copy-start(f32[32,256]{1,0:T(8,128)} %get-tuple-element.40) | copy-start | bytes 98308
  149.7 4.4 %copy-start.6 = (f32[32,256]{1,0:T(8,128)S(1)}, f32[32,256]{1,0:T(8,128)}, u32[]{:S(2)}) copy-start(f32[32,256]{1,0:T(8,128)} %get-tuple-element.32) | copy-start | bytes 98308
  149.7 4.4 %copy-start.7 = (f32[256,32]{0,1:T(8,128)S(1)}, f32[256,32]{0,1:T(8,128)}, u32[]{:S(2)}) copy-start(f32[256,32]{0,1:T(8,128)} %get-tuple-element.38) | copy-start | bytes 98308
  180.2 0.8 copy-start.16
  182.1 25.7 %all-to-all-start = ((f32[1,32,16,128]{3,2,0,1:T(8,128)}), f32[1,32,16,128]{3,2,0,1:T(8,128)}, u32[]{:S(2)}, u32[]{:S(2)}) async-start(f32[1,32,16,128]{3,2,0,1:T(8,128)} %bitcast.190), calls=%async_computation | async-start | bytes 524288 | tf_op jit(solution)/shard_map/all_to_all | solution.py:139
  193.1 2.7 %copy-start.3 = (bf16[512,2048]{0,1:T(8,128)(2,1)S(1)}, bf16[512,2048]{0,1:T(8,128)(2,1)}, u32[]{:S(2)}) copy-start(bf16[512,2048]{0,1:T(8,128)(2,1)} %slice.227) | copy-start | bytes 6291460
  193.1 2.7 %copy-start.13 = (f32[32]{0:T(128)S(1)}, f32[32]{0:T(128)}, u32[]{:S(2)}) copy-start(f32[32]{0:T(128)} %param.16) | copy-start | bytes 388
  193.8 5.7 %slice-start = ((s8[4489216]{0:T(1024)(128)(4,1)}), s8[4194304]{0:T(1024)(128)(4,1)S(1)}, s32[]{:S(2)}) async-start(s8[4489216]{0:T(1024)(128)(4,1)} %bitcast.179), calls=%async_computation.3 | async-start | bytes 8388608
  195.8 3.8 %slice-start.1 = ((s8[4489216]{0:T(1024)(128)(4,1)}), s8[294912]{0:T(1024)(128)(4,1)S(1)}, s32[]{:S(2)}) async-start(s8[4489216]{0:T(1024)(128)(4,1)} %bitcast.179), calls=%async_computation.4 | async-start | bytes 589824
  199.6 1.4 copy-start.11
  201.0 9.2 %copy-start.1 = (bf16[1,1,512,2048]{3,2,1,0:T(8,128)(2,1)S(1)}, bf16[1,1,512,2048]{3,2,1,0:T(8,128)(2,1)}, u32[]{:S(2)}) copy-start(bf16[1,1,512,2048]{3,2,1,0:T(8,128)(2,1)} %param.10) | copy-start | bytes 6291460
Sparse Core Ops, SparseCore 0:
  21.9 80.7 all-gather.4
  145.2 30.5 all-gather.6

commit v6 on v5

--- a/solution.py
+++ b/solution.py
@@ -58,23 +58,32 @@
     my_block = lax.axis_index("seq")
     qlen = jnp.sum(jnp.where(prompt_group == my_group, lengths, 0))
     filled = jnp.arange(slots, dtype=jnp.int32) < qlen
+    edge_hidden = lax.dynamic_slice_in_dim(tok_rows, qlen - (taps - 1), taps - 1, 0)
+    prev_hidden = shifted(edge_hidden, "seq", 1)
     wide_rows = lax.all_gather(w_in, "seq", axis=1, tiled=True)
+    both_rows = jnp.concatenate([tok_rows, prev_hidden], axis=0)
     projected = jnp.dot(
-        tok_rows,
+        both_rows,
         lax.all_gather(wide_rows, "req", axis=0, tiled=True),
         preferred_element_type=jnp.float32,
     ).astype(jnp.bfloat16)
-    gate_z = projected[:, :inner]
-    conv_in = projected[:, inner : inner + convdim]
-    dt_raw = projected[:, inner + convdim :]
-    edge_rows = lax.dynamic_slice_in_dim(conv_in, qlen - (taps - 1), taps - 1, 0)
-    prev_edge = shifted(edge_rows, "seq", 1)
-    extended = jnp.concatenate([prev_edge, conv_in], axis=0)
+    gate_z = projected[:slots, :inner]
+    conv_in = projected[:slots, inner : inner + convdim]
+    prev_edge = projected[slots:, inner : inner + convdim].astype(jnp.float32)
+    dt_raw = projected[:slots, inner + convdim :]
     accum = jnp.zeros((slots, convdim), jnp.float32) + conv_bias[None, :]
     for tap_index in range(taps):
-        accum = accum + conv_weight[tap_index][None, :] * extended[
-            tap_index : tap_index + slots
-        ].astype(jnp.float32)
+        lag = taps - 1 - tap_index
+        taken = jnp.pad(conv_in[: slots - lag], ((lag, 0), (0, 0))).astype(jnp.float32)
+        accum = accum + conv_weight[tap_index][None, :] * taken
+    edge_terms = []
+    for row in range(taps - 1):
+        term = jnp.zeros((convdim,), jnp.float32)
+        for tap_index in range(taps - 1 - row):
+            term = term + conv_weight[tap_index] * prev_edge[row + tap_index]
+        edge_terms.append(term)
+    edge_fix = jnp.pad(jnp.stack(edge_terms), ((0, slots - (taps - 1)), (0, 0)))
+    accum = accum + edge_fix
     conv_act = jax.nn.silu(accum).astype(jnp.bfloat16)
     inputs_x = conv_act[:, :inner]
     b_rows = conv_act[:, inner : inner + nstate]
@@ -115,10 +124,11 @@
     ends = gathered[:, :, : hdim * nstate].astype(jnp.float32).reshape(seq_count, heads, hdim, nstate)
     sent = gathered[:, :, hdim * nstate :].astype(jnp.float32)
     totals = sent[:, :, 0] + (sent[:, :, 128] + sent[:, :, 256])
-    entering = zero_state
-    for turn in range(seq_count - 1):
-        stepped = jnp.exp(totals[turn])[:, None, None] * entering + ends[turn]
-        entering = jnp.where(turn < my_block, stepped, entering)
+    order = jnp.arange(seq_count)
+    between = (order[None, :] > order[:, None]) & (order[None, :] < my_block)
+    log_coef = jnp.sum(jnp.where(between[:, :, None], totals[None, :, :], 0.0), axis=1)
+    coef = jnp.where((order < my_block)[:, None], jnp.exp(log_coef), 0.0)
+    entering = jnp.sum(coef[:, :, None, None] * ends, axis=0)
     incoming = jnp.exp(through)[:, :, None] * jnp.einsum(
         "tn,hpn->thp", c_rows.astype(jnp.float32), entering, precision=lax.Precision.HIGHEST
     )

time: 218 us -> 228 us (1.046)
  other arithmetic: 35.5 us -> 42.2 us
  matrix products: 29.2 us -> 34.9 us
  waiting for transfers between devices: 92.5 us -> 87 us
  local copies, waits for them, and re-layouts: 20 us -> 24.6 us
    all_gather x1, waiting for transfers between devices: 75.2 us -> 67.7 us  [local(): lax.all_gather(wide_rows, 'req', axis=0, tiled=True)]
    another operation x10, other arithmetic: 3.96 us -> 10 us
    slice x3 -> x5, local copies, waits for them, and re-layouts: 3.05 us -> 8 us  [the longest x3 5.46 us: local(): conv_in[:slots - lag]]
    dot_general x1, matrix products: 15.3 us -> 18.8 us  [local(): jnp.dot(both_rows, lax.all_gather(wide_rows, 'req', axis=0, tiled=True),...]
    another operation x7, local copies, waits for them, and re-layouts: 0.35 us -> 3.66 us
    reduce_sum x0 -> x1, other arithmetic: none -> 2.39 us  [local(): entering = jnp.sum(coef[:, :, None, None] * ends, axis=0)]
    unnamed x48 -> x74, local copies, waits for them, and re-layouts: 10.9 us -> 9.57 us
  transfers between devices with their start and end apart: 4 -> 4, of which waited for: 2 -> 2; matrix products, arithmetic and copies ran while one was open for 18% -> 15% of each run, Pallas kernels for 0% -> 0%
where the time goes in v6:
time: 228 us; the launch traced here: 227 us
  waiting for transfers between devices  87 us (38%)
  other arithmetic  42.2 us (19%)
  matrix products  34.9 us (15%)
  local copies, waits for them, and re-layouts  24.6 us (11%)
  between operations  16 us (7%)
  blocking collectives  12.7 us (6%)
  starting transfers between devices  9.33 us (4%)
    all_gather x1, waiting for transfers between devices, local(): lax.all_gather(wide_rows, 'req', axis=0, tiled=True)  67.7 us
    all_gather x1, waiting for transfers between devices, local(): gathered = lax.all_gather(packed, 'seq', axis=0, tiled=False)  19.2 us
    dot_general x1, matrix products, local(): jnp.dot(both_rows, lax.all_gather(wide_rows, 'req', axis=0, tiled=True),...  18.8 us
    all_gather x1, blocking collectives, local(): wide_rows = lax.all_gather(w_in, 'seq', axis=1, tiled=True)  12.7 us
    another operation x10, other arithmetic  10 us
    unnamed x74, local copies, waits for them, and re-layouts  9.57 us
    dot_general x2, matrix products, block_step(): jnp.einsum('htu,uhp->thp', mixing, heads_x, preferred_element_type=jnp.fl...  8.72 us
    convert_element_type x1, other arithmetic, local(): conv_act = jax.nn.silu(accum).astype(jnp.bfloat16)  8.56 us
  transfers between devices with their start and end apart: 4, of which 2 were waited for; matrix products, arithmetic and copies ran while one was open for 15% of the time, Pallas kernels for 0%

profile of v6, /device:TPU:1, one launch (start us, length us, event | category | flops | bytes accessed | tf_op | source)
XLA Modules:
  0.0 226.7 jit_solution(524451668465215450)
XLA Ops:
  7.2 12.7 %all-gather.1 = bf16[4,1096,64]{1,2,0:T(8,128)(2,1)S(1)} all-gather(bf16[1,1096,64]{1,2,0:T(8,128)(2,1)} %bitcast.174), channel_id=1, replica_groups=mesh['req'=32,'seq'=4] {'seq'}, dimensions={0}, use_global_device_ids=true | all-gather | bytes 701440 | tf_op jit(solution)/shard_map/all_gather | solution.py:63
  21.7 1.8 compare_select_fusion.1
  25.7 1.5 collective-permute-start
  30.3 1.6 slice_reduce_fusion.9
  34.9 67.7 %all-gather.5.cloned.1.call-done = bf16[2048,4384]{1,0:T(8,128)(2,1)} async-done(((bf16[64,4384]{1,0:T(8,128)(2,1)}), bf16[2048,4384]{1,0:T(8,128)(2,1)}) %all-gather.5.cloned.1.call-update) | async-done | bytes 17956880 | tf_op jit(solution)/shard_map/all_gather | solution.py:67
  102.6 18.8 %convolution_convert_fusion = bf16[515,4384]{0,1:T(8,128)(2,1)S(1)} fusion(bf16[2048,4384]{1,0:T(8,128)(2,1)} %all-gather.5.cloned.1.call-done, bf16[3,2048]{1,0:T(4,128)(2,1)S(1)} %collective-permute-done, bf16[512,2048]{1,0:T(8,128)(2,1)} %bitcast.177), kind=kOutput, calls=%fused_computation.3 | convolution fusion | flops 9254261760 | bytes 24581824 | tf_op jit(solution)/shard_map/dot_general | solution.py:65
  121.5 1.8 slice.191
  123.4 2.0 slice.192
  125.4 1.6 slice.193
  128.4 1.9 reduce-window.20
  134.7 1.9 reduce-window.24
  142.3 1.5 exponential_multiply_fusion
  143.9 2.1 fusion.28
  147.3 8.6 %multiply_convert_fusion.2 = bf16[512,2304]{0,1:T(8,128)(2,1)S(1)} fusion(f32[1,2304]{0,1:T(8,128)S(1)} %get-tuple-element.29, f32[1,2304]{0,1:T(8,128)S(1)} %get-tuple-element.24, f32[1,2304]{0,1:T(8,128)S(1)} %get-tuple-element.23, bf16[515,4384]{0,1:T(8,128)(2,1)} %copy-done.2, f32[2304]{0:T(1024)S(1)} %copy-done.10, bf16[511,2304]{0,1:T(8,128)(2,1)S(1)} %copy-done.5, ...), kind=kLoop, calls=%fused_computation.10 | loop fusion | flops 28311552 | bytes 11842560 | tf_op jit(solution)/shard_map/convert_element_type | solution.py:87
  160.4 1.9 pad_maximum_fusion
  165.1 4.4 %bitcast_add_fusion.1 = f32[256,32,64]{0,2,1:T(8,128)} fusion(f32[256,32,64]{0,2,1:T(8,128)S(1)} %fusion.29, bf16[256,32,64]{0,2,1:T(8,128)(2,1)S(1)} %bitcast.172, f32[32,256]{1,0:T(8,128)S(1)} %copy-done.15, f32[32,256]{1,0:T(8,128)S(1)} %copy-done.11, f32[256,256]{1,0:T(8,128)S(1)} %fusion.46, pred[256,256]{1,0:T(8,128)(4,1)S(1)} %iota_compare_fusion.1, ...), kind=kOutput, calls=%fused_computation.45 | convolution fusion | flops 282066944 | bytes 5668864 | tf_op jit(solution)/shard_map/htu,uhp->thp/dot_general | solution.py:27
  169.5 4.3 %bitcast_add_fusion = f32[256,32,64]{0,2,1:T(8,128)} fusion(f32[256,32,64]{0,2,1:T(8,128)S(1)} %fusion.37, bf16[256,32,64]{0,2,1:T(8,128)(2,1)S(1)} %bitcast.171, f32[32,256]{1,0:T(8,128)S(1)} %copy-done.13, f32[32,256]{1,0:T(8,128)S(1)} %copy-done.12, f32[256,256]{1,0:T(8,128)S(1)} %fusion.41, pred[256,256]{1,0:T(8,128)(4,1)S(1)} %iota_compare_fusion.1, ...), kind=kOutput, calls=%fused_computation.44 | convolution fusion | flops 282066944 | bytes 5668864 | tf_op jit(solution)/shard_map/htu,uhp->thp/dot_general | solution.py:27
  173.9 19.2 %all-gather.7.cloned.1.call-done = bf16[128,8576]{1,0:T(8,128)(2,1)} async-done(((bf16[32,8576]{1,0:T(8,128)(2,1)}), bf16[128,8576]{1,0:T(8,128)(2,1)}) %all-gather.7.cloned.1.call-update) | async-done | bytes 2195472 | tf_op jit(solution)/shard_map/all_gather | solution.py:123
  193.1 2.0 slice_convert_fusion
  198.0 7.7 %all-to-all-start = ((f32[1,32,16,128]{3,2,0,1:T(8,128)}), f32[1,32,16,128]{3,2,0,1:T(8,128)S(1)}, u32[]{:S(2)}, u32[]{:S(2)}) async-start(f32[1,32,16,128]{3,2,0,1:T(8,128)} %bitcast.32), calls=%async_computation | async-start | bytes 524288 | tf_op jit(solution)/shard_map/all_to_all | solution.py:149
  205.8 2.4 %multiply_reduce_fusion.1 = f32[32,8192]{1,0:T(8,128)S(1)} fusion(f32[4,32]{1,0:T(4,128)S(1)} %exponential_select_fusion, bf16[4,32,8576]{2,1,0:T(8,128)(2,1)} %bitcast.161), kind=kLoop, calls=%fused_computation.22 | loop fusion | flops 2883584 | bytes 3146240 | tf_op jit(solution)/shard_map/reduce_sum | solution.py:131
  208.6 4.1 %fusion.7 = f32[512,32,64]{0,2,1:T(8,128)S(1)} fusion(f32[256,32,64]{0,2,1:T(8,128)} %bitcast_add_fusion, f32[256,32,64]{0,2,1:T(8,128)S(1)} %copy-done.6, bf16[512,32,64]{0,2,1:T(8,128)(2,1)S(1)} %bitcast.155, f32[32,64,128]{2,1,0:T(8,128)S(1)} %bitcast.163, f32[32]{0:T(128)S(1)} %copy-done.23, f32[512,32]{0,1:T(8,128)S(1)} %fusion.56, ...), kind=kOutput, calls=%fused_computation.18 | convolution fusion | flops 1616904192 | bytes 11731456 | tf_op jit(solution)/shard_map/tn,hpn->thp/dot_general | solution.py:132
  214.2 1.9 fusion.23
  216.1 2.4 %copy.221 = bf16[1,1,512,2048]{3,2,1,0:T(8,128)(2,1)} copy(bf16[1,1,512,2048]{2,3,1,0:T(8,128)(2,1)S(1)} %fusion.23) | data formatting | bytes 4194304
  (136 shorter events, 34.7 us)
Async XLA Ops:
  7.2 95.4 %all-gather.5.cloned.1.call-start = ((), (), s32[]{:S(2)}) async-start(), calls=%async_computation.1 | async-start | bytes 18923520 | tf_op jit(solution)/shard_map/all_gather | solution.py:67
  21.7 171.4 %all-gather.7.cloned.1.call-start = ((), (), s32[]{:S(2)}) async-start(), calls=%async_computation.2 | async-start | bytes 2744320 | tf_op jit(solution)/shard_map/all_gather | solution.py:123
  25.7 9.2 %collective-permute-start = (bf16[3,2048]{1,0:T(4,128)(2,1)S(1)}, bf16[3,2048]{1,0:T(4,128)(2,1)S(1)}, u32[]{:S(2)}, u32[]{:S(2)}) collective-permute-start(bf16[3,2048]{1,0:T(4,128)(2,1)S(1)} %dynamic-slice_bitcast_fusion), channel_id=1, source_target_pairs={{0,1},{1,2},{2,3},{4,5},{5,6},{6,7},{8,9},{9,10},{10,11},{12,13},{... | collective-permute-start | bytes 36872 | tf_op jit(solution)/shard_map/ppermute | solution.py:12
  27.3 5.3 %copy-start.28 = (pred[4]{0:T(512)(128)(4,1)}, pred[4]{0:T(512)(128)(4,1)S(1)}, u32[]{:S(2)}) copy-start(pred[4]{0:T(512)(128)(4,1)S(1)} %iota_compare_fusion.4) | copy-start | bytes 16
  32.6 94.4 %copy-start.19 = (pred[512]{0:T(512)(128)(4,1)}, pred[512]{0:T(512)(128)(4,1)S(1)}, u32[]{:S(2)}) copy-start(pred[512]{0:T(512)(128)(4,1)S(1)} %iota_compare_fusion.3) | copy-start | bytes 1540
  121.4 5.6 %copy-start.2 = (bf16[515,4384]{0,1:T(8,128)(2,1)}, bf16[515,4384]{0,1:T(8,128)(2,1)S(1)}, u32[]{:S(2)}) copy-start(bf16[515,4384]{0,1:T(8,128)(2,1)S(1)} %convolution_convert_fusion) | copy-start | bytes 13546564
  123.4 3.6 %copy-start.22 = (f32[32]{0:T(128)S(1)}, f32[32]{0:T(128)}, u32[]{:S(2)}) copy-start(f32[32]{0:T(128)} %param.14) | copy-start | bytes 388
  123.4 3.6 %copy-start.25 = (f32[32]{0:T(128)S(1)}, f32[32]{0:T(128)}, u32[]{:S(2)}) copy-start(f32[32]{0:T(128)} %exponential_negate_fusion) | copy-start | bytes 388
  143.8 3.4 %copy-start.5 = (bf16[511,2304]{0,1:T(8,128)(2,1)S(1)}, bf16[511,2304]{0,1:T(8,128)(2,1)}, u32[]{:S(2)}) copy-start(bf16[511,2304]{0,1:T(8,128)(2,1)} %slice.193) | copy-start | bytes 7064068
  143.8 3.4 %copy-start.8 = (f32[2304]{0:T(1024)S(1)}, f32[2304]{0:T(1024)}, u32[]{:S(2)}) copy-start(f32[2304]{0:T(1024)} %get-tuple-element.15) | copy-start | bytes 27652
  143.8 3.4 %copy-start.9 = (f32[2304]{0:T(1024)S(1)}, f32[2304]{0:T(1024)}, u32[]{:S(2)}) copy-start(f32[2304]{0:T(1024)} %get-tuple-element.16) | copy-start | bytes 27652
  143.8 3.4 %copy-start.10 = (f32[2304]{0:T(1024)S(1)}, f32[2304]{0:T(1024)}, u32[]{:S(2)}) copy-start(f32[2304]{0:T(1024)} %get-tuple-element.17) | copy-start | bytes 27652
  143.8 3.4 %copy-start.17 = (f32[2304]{0:T(1024)S(1)}, f32[2304]{0:T(1024)}, u32[]{:S(2)}) copy-start(f32[2304]{0:T(1024)} %param.13) | copy-start | bytes 27652
  155.8 9.1 %copy-start = (bf16[512,2304]{0,1:T(8,128)(2,1)}, bf16[512,2304]{0,1:T(8,128)(2,1)S(1)}, u32[]{:S(2)}) copy-start(bf16[512,2304]{0,1:T(8,128)(2,1)S(1)} %multiply_convert_fusion.2) | copy-start | bytes 7077892
  156.3 6.0 %copy-start.21 = (s32[32]{0:T(128)S(1)}, s32[32]{0:T(128)}, u32[]{:S(2)}) copy-start(s32[32]{0:T(128)} %get-tuple-element.45) | copy-start | bytes 388
  165.1 4.4 %copy-start.12 = (f32[32,256]{1,0:T(8,128)S(1)}, f32[32,256]{1,0:T(8,128)}, u32[]{:S(2)}) copy-start(f32[32,256]{1,0:T(8,128)} %get-tuple-element.42) | copy-start | bytes 98308
  165.1 4.4 %copy-start.13 = (f32[32,256]{1,0:T(8,128)S(1)}, f32[32,256]{1,0:T(8,128)}, u32[]{:S(2)}) copy-start(f32[32,256]{1,0:T(8,128)} %get-tuple-element.31) | copy-start | bytes 98308
  165.1 4.4 %copy-start.14 = (f32[256,32]{0,1:T(8,128)S(1)}, f32[256,32]{0,1:T(8,128)}, u32[]{:S(2)}) copy-start(f32[256,32]{0,1:T(8,128)} %get-tuple-element.40) | copy-start | bytes 98308
  196.0 9.6 %copy-start.29 = (pred[4]{0:T(512)(128)(4,1)S(1)}, pred[4]{0:T(512)(128)(4,1)}, u32[]{:S(2)}) copy-start(pred[4]{0:T(512)(128)(4,1)} %copy-done.28) | copy-start | bytes 16
  196.8 11.6 %slice-start = ((bf16[512,2304]{0,1:T(8,128)(2,1)}), bf16[512,2048]{0,1:T(8,128)(2,1)S(1)}, s32[]{:S(2)}) async-start(bf16[512,2304]{0,1:T(8,128)(2,1)} %copy-done), calls=%async_computation.3 | async-start | bytes 4194304 | tf_op jit(solution)/shard_map/slice | solution.py:88
  196.8 11.6 %copy-start.23 = (f32[32]{0:T(128)S(1)}, f32[32]{0:T(128)}, u32[]{:S(2)}) copy-start(f32[32]{0:T(128)} %param.16) | copy-start | bytes 388
  198.0 20.5 %all-to-all-start = ((f32[1,32,16,128]{3,2,0,1:T(8,128)}), f32[1,32,16,128]{3,2,0,1:T(8,128)S(1)}, u32[]{:S(2)}, u32[]{:S(2)}) async-start(f32[1,32,16,128]{3,2,0,1:T(8,128)} %bitcast.32), calls=%async_computation | async-start | bytes 524288 | tf_op jit(solution)/shard_map/all_to_all | solution.py:149
  208.2 4.5 %slice-start.1 = ((s8[5611520]{0:T(1024)(128)(4,1)}), s8[4194304]{0:T(1024)(128)(4,1)S(1)}, s32[]{:S(2)}) async-start(s8[5611520]{0:T(1024)(128)(4,1)} %bitcast.156), calls=%async_computation.4 | async-start | bytes 8388608
  208.6 4.1 %slice-start.2 = ((s8[5611520]{0:T(1024)(128)(4,1)}), s8[1417216]{0:T(1024)(128)(4,1)S(1)}, s32[]{:S(2)}) async-start(s8[5611520]{0:T(1024)(128)(4,1)} %bitcast.156), calls=%async_computation.5 | async-start | bytes 2834432
  (13 other events, 24.2 us)
Sparse Core Ops, SparseCore 0:
  21.8 80.7 all-gather.4
  162.5 30.5 all-gather.6

commit v7 on v6

--- a/solution.py
+++ b/solution.py
@@ -58,19 +58,17 @@
     my_block = lax.axis_index("seq")
     qlen = jnp.sum(jnp.where(prompt_group == my_group, lengths, 0))
     filled = jnp.arange(slots, dtype=jnp.int32) < qlen
-    edge_hidden = lax.dynamic_slice_in_dim(tok_rows, qlen - (taps - 1), taps - 1, 0)
-    prev_hidden = shifted(edge_hidden, "seq", 1)
     wide_rows = lax.all_gather(w_in, "seq", axis=1, tiled=True)
-    both_rows = jnp.concatenate([tok_rows, prev_hidden], axis=0)
     projected = jnp.dot(
-        both_rows,
+        tok_rows,
         lax.all_gather(wide_rows, "req", axis=0, tiled=True),
         preferred_element_type=jnp.float32,
     ).astype(jnp.bfloat16)
-    gate_z = projected[:slots, :inner]
-    conv_in = projected[:slots, inner : inner + convdim]
-    prev_edge = projected[slots:, inner : inner + convdim].astype(jnp.float32)
-    dt_raw = projected[:slots, inner + convdim :]
+    gate_z = projected[:, :inner]
+    conv_in = projected[:, inner : inner + convdim]
+    dt_raw = projected[:, inner + convdim :]
+    edge_rows = lax.dynamic_slice_in_dim(conv_in, qlen - (taps - 1), taps - 1, 0)
+    prev_edge = shifted(edge_rows, "seq", 1).astype(jnp.float32)
     accum = jnp.zeros((slots, convdim), jnp.float32) + conv_bias[None, :]
     for tap_index in range(taps):
         lag = taps - 1 - tap_index

time: 228 us -> 220 us (0.965)
  other arithmetic: 42.2 us -> 32 us
  waiting for transfers between devices: 87 us -> 94.2 us
  matrix products: 34.9 us -> 29.5 us
    all_gather x1, waiting for transfers between devices: 67.7 us -> 76.2 us  [local(): lax.all_gather(wide_rows, 'req', axis=0, tiled=True)]
    another operation x10 -> x11, other arithmetic: 10 us -> 2.74 us
    dot_general x1, matrix products: 18.8 us -> 15.3 us  [local(): jnp.dot(tok_rows, lax.all_gather(wide_rows, 'req', axis=0, tiled=True), p...]
    reduce_sum x1, other arithmetic: 1.39 us -> 4.53 us  [local(): scale = lax.rsqrt(jnp.mean(gated * gated, axis=1, keepdims=True) + 1e-05)]
    reshape x1, other arithmetic: 1.89 us -> 4.81 us  [local(): gated_out = normed.astype(jnp.bfloat16).reshape(1, 1, slots, inner)]
    another operation x7 -> x8, local copies, waits for them, and re-layouts: 3.66 us -> 0.74 us  [the longest x1 0.39 us: local(): edge_fix = jnp.pad(jnp.stack(edge_terms), ((0, slots - (taps - 1)), (0, 0)))]
    unnamed x74 -> x37, local copies, waits for them, and re-layouts: 9.57 us -> 8.87 us
  transfers between devices with their start and end apart: 4 -> 4, of which waited for: 2 -> 3; matrix products, arithmetic and copies ran while one was open for 15% -> 15% of each run, Pallas kernels for 0% -> 0%
where the time goes in v7:
time: 220 us; the launch traced here: 219 us
  waiting for transfers between devices  94.2 us (43%)
  other arithmetic  32 us (15%)
  matrix products  29.5 us (13%)
  local copies, waits for them, and re-layouts  23.9 us (11%)
  between operations  15.8 us (7%)
  blocking collectives  12.8 us (6%)
  starting transfers between devices  11.1 us (5%)
    all_gather x1, waiting for transfers between devices, local(): lax.all_gather(wide_rows, 'req', axis=0, tiled=True)  76.2 us
    all_gather x1, waiting for transfers between devices, local(): gathered = lax.all_gather(packed, 'seq', axis=0, tiled=False)  17.8 us
    dot_general x1, matrix products, local(): jnp.dot(tok_rows, lax.all_gather(wide_rows, 'req', axis=0, tiled=True), p...  15.3 us
    all_gather x1, blocking collectives, local(): wide_rows = lax.all_gather(w_in, 'seq', axis=1, tiled=True)  12.8 us
    unnamed x37, local copies, waits for them, and re-layouts  8.87 us
    dot_general x2, matrix products, block_step(): jnp.einsum('htu,uhp->thp', mixing, heads_x, preferred_element_type=jnp.fl...  8.73 us
    convert_element_type x1, other arithmetic, local(): conv_act = jax.nn.silu(accum).astype(jnp.bfloat16)  8.36 us
    all_to_all x1, starting transfers between devices, local(): lax.all_to_all(share[None], 'req', split_axis=1, concat_axis=0, tiled=True)  7.75 us
  transfers between devices with their start and end apart: 4, of which 3 were waited for; matrix products, arithmetic and copies ran while one was open for 15% of the time, Pallas kernels for 0%

profile of v7, /device:TPU:1, one launch (start us, length us, event | category | flops | bytes accessed | tf_op | source)
XLA Modules:
  0.0 219.4 jit_solution(2714784185225631095)
XLA Ops:
  7.2 12.8 %all-gather.1 = bf16[4,1096,64]{1,2,0:T(8,128)(2,1)S(1)} all-gather(bf16[1,1096,64]{1,2,0:T(8,128)(2,1)} %bitcast.172), channel_id=1, replica_groups=mesh['req'=32,'seq'=4] {'seq'}, dimensions={0}, use_global_device_ids=true | all-gather | bytes 701440 | tf_op jit(solution)/shard_map/all_gather | solution.py:61
  20.5 1.2 reshape.371
  21.8 1.3 compare_select_fusion.1
  26.5 76.2 %all-gather.5.cloned.1.call-done = bf16[2048,4384]{1,0:T(8,128)(2,1)} async-done(((bf16[64,4384]{1,0:T(8,128)(2,1)}), bf16[2048,4384]{1,0:T(8,128)(2,1)}) %all-gather.5.cloned.1.call-update) | async-done | bytes 17956880 | tf_op jit(solution)/shard_map/all_gather | solution.py:64
  102.7 15.3 %convolution_convert_fusion = bf16[512,4384]{0,1:T(8,128)(2,1)} fusion(bf16[2048,4384]{1,0:T(8,128)(2,1)} %all-gather.5.cloned.1.call-done, bf16[1,1,512,2048]{3,2,1,0:T(8,128)(2,1)S(1)} %copy-done), kind=kOutput, calls=%fused_computation.3 | convolution fusion | flops 9196158976 | bytes 24543232 | tf_op jit(solution)/shard_map/dot_general | solution.py:62
  118.0 3.2 %slice.190 = bf16[512,2304]{0,1:T(8,128)(2,1)} slice(bf16[512,4384]{0,1:T(8,128)(2,1)} %convolution_convert_fusion), slice={[0:512], [2048:4352]} | slice | bytes 4718592 | tf_op jit(solution)/shard_map/slice | solution.py:68
  124.3 1.5 constant_dynamic-slice_fusion
  126.1 3.3 %collective-permute-start = (bf16[3,2304]{1,0:T(4,128)(2,1)S(1)}, bf16[3,2304]{1,0:T(4,128)(2,1)S(1)}, u32[]{:S(2)}, u32[]{:S(2)}) collective-permute-start(bf16[3,2304]{1,0:T(4,128)(2,1)S(1)} %copy.81), channel_id=1, source_target_pairs={{0,1},{1,2},{2,3},{4,5},{5,6},{6,7},{8,9},{9,10},{10,11},{12,13},{... | collective-permute-start | bytes 41480 | tf_op jit(solution)/shard_map/ppermute | solution.py:12
  129.4 1.2 reduce-window.26
  131.2 3.4 %slice.189 = bf16[511,2304]{0,1:T(8,128)(2,1)} slice(bf16[512,4384]{0,1:T(8,128)(2,1)} %convolution_convert_fusion), slice={[0:511], [2048:4352]} | slice | bytes 4709376 | tf_op jit(solution)/shard_map/slice | solution.py:75
  134.6 1.5 slice.188
  136.2 1.6 slice.187
  138.6 8.4 %multiply_convert_fusion.2 = bf16[512,2304]{0,1:T(8,128)(2,1)S(1)} fusion(f32[3,2304]{0,1:T(8,128)S(1)} %copy.82, f32[2304]{0:T(1024)S(1)} %get-tuple-element.14, bf16[511,2304]{0,1:T(8,128)(2,1)} %slice.189, f32[2304]{0:T(1024)S(1)} %get-tuple-element.15, bf16[510,2304]{0,1:T(8,128)(2,1)} %slice.188, f32[2304]{0:T(1024)S(1)} %get-tuple-element.13, ...), kind=kLoop, calls=%fused_computation.6 | loop fusion | flops 21233664 | bytes 11842560 | tf_op jit(solution)/shard_map/convert_element_type | solution.py:85
  149.8 1.5 copy-done.5
  153.8 4.4 %bitcast_add_fusion = f32[256,32,64]{0,2,1:T(8,128)} fusion(f32[256,32,64]{0,2,1:T(8,128)S(1)} %fusion.32, bf16[256,32,64]{0,2,1:T(8,128)(2,1)S(1)} %bitcast.170, f32[32,256]{1,0:T(8,128)S(1)} %get-tuple-element.29, f32[32,256]{1,0:T(8,128)S(1)} %get-tuple-element.40, f32[256,256]{1,0:T(8,128)S(1)} %fusion.36, pred[256,256]{1,0:T(8,128)(4,1)S(1)} %iota_compare_fusion, ...), kind=kOutput, calls=%fused_computation.37 | convolution fusion | flops 282066944 | bytes 5668864 | tf_op jit(solution)/shard_map/htu,uhp->thp/dot_general | solution.py:27
  158.2 4.4 %bitcast_add_fusion.1 = f32[256,32,64]{0,2,1:T(8,128)} fusion(f32[256,32,64]{0,2,1:T(8,128)S(1)} %fusion.24, bf16[256,32,64]{0,2,1:T(8,128)(2,1)S(1)} %bitcast.169, f32[32,256]{1,0:T(8,128)S(1)} %get-tuple-element.30, f32[32,256]{1,0:T(8,128)S(1)} %get-tuple-element.41, f32[256,256]{1,0:T(8,128)S(1)} %fusion.41, pred[256,256]{1,0:T(8,128)(4,1)S(1)} %iota_compare_fusion, ...), kind=kOutput, calls=%fused_computation.38 | convolution fusion | flops 282066944 | bytes 5668864 | tf_op jit(solution)/shard_map/htu,uhp->thp/dot_general | solution.py:27
  162.6 17.8 %all-gather.7.cloned.1.call-done = bf16[128,8576]{1,0:T(8,128)(2,1)} async-done(((bf16[32,8576]{1,0:T(8,128)(2,1)}), bf16[128,8576]{1,0:T(8,128)(2,1)}) %all-gather.7.cloned.1.call-update) | async-done | bytes 2195472 | tf_op jit(solution)/shard_map/all_gather | solution.py:121
  180.3 1.1 slice_convert_fusion.1
  181.4 2.2 slice_convert_fusion
  186.0 2.2 %fusion.6 = f32[512,32,64]{0,2,1:T(8,128)S(1)} fusion(f32[256,32,64]{0,2,1:T(8,128)S(1)} %copy-done.8, f32[256,32,64]{0,2,1:T(8,128)S(1)} %copy-done.9, bf16[512,32,64]{0,2,1:T(8,128)(2,1)S(1)} %bitcast.155, f32[32,64,128]{2,1,0:T(8,128)S(1)} %bitcast.161, f32[32]{0:T(128)S(1)} %copy-done.14, f32[512,32]{0,1:T(8,128)S(1)} %fusion.52, ...), kind=kOutput, calls=%fused_computation.14 | convolution fusion | flops 1616904192 | bytes 11731456 | tf_op jit(solution)/shard_map/tn,hpn->thp/dot_general | solution.py:130
  188.3 4.5 %multiply_reduce_fusion = f32[512]{0:T(512)S(1)} fusion(bf16[512,4384]{0,1:T(8,128)(2,1)} %convolution_convert_fusion, f32[512,32,64]{0,2,1:T(8,128)S(1)} %fusion.6), kind=kLoop, calls=%fused_computation.17 | loop fusion | flops 8388096 | bytes 6293504 | tf_op jit(solution)/shard_map/reduce_sum | solution.py:139
  194.5 7.7 %all-to-all-start = ((f32[1,32,16,128]{3,2,0,1:T(8,128)}), f32[1,32,16,128]{3,2,0,1:T(8,128)S(1)}, u32[]{:S(2)}, u32[]{:S(2)}) async-start(f32[1,32,16,128]{3,2,0,1:T(8,128)} %bitcast.31), calls=%async_computation | async-start | bytes 524288 | tf_op jit(solution)/shard_map/all_to_all | solution.py:147
  202.3 4.8 %fusion.19 = bf16[1,1,512,2048]{2,3,1,0:T(8,128)(2,1)} fusion(f32[2048]{0:T(1024)S(1)} %copy-done.12, f32[512]{0:T(512)S(1)} %add_rsqrt_fusion, pred[512]{0:T(512)(128)(4,1)S(1)} %iota_compare_fusion.2, bf16[512,4384]{0,1:T(8,128)(2,1)} %convolution_convert_fusion, f32[512,32,64]{0,2,1:T(8,128)} %copy-done.3), kind=kLoop, calls=%fused_computation.31 | loop fusion | flops 10485760 | bytes 8399360 | tf_op jit(solution)/shard_map/reshape | solution.py:141
  207.1 3.9 %copy.95 = bf16[1,1,512,2048]{3,2,1,0:T(8,128)(2,1)} copy(bf16[1,1,512,2048]{2,3,1,0:T(8,128)(2,1)} %fusion.19) | data formatting | bytes 4194304
  (101 shorter events, 18.1 us)
Async XLA Ops:
  7.2 95.5 %copy-start = (bf16[1,1,512,2048]{3,2,1,0:T(8,128)(2,1)S(1)}, bf16[1,1,512,2048]{3,2,1,0:T(8,128)(2,1)}, u32[]{:S(2)}) copy-start(bf16[1,1,512,2048]{3,2,1,0:T(8,128)(2,1)} %param.10) | copy-start | bytes 6291460
  7.2 95.5 %all-gather.5.cloned.1.call-start = ((), (), s32[]{:S(2)}) async-start(), calls=%async_computation.1 | async-start | bytes 18923520 | tf_op jit(solution)/shard_map/all_gather | solution.py:64
  21.8 158.5 %all-gather.7.cloned.1.call-start = ((), (), s32[]{:S(2)}) async-start(), calls=%async_computation.2 | async-start | bytes 2744320 | tf_op jit(solution)/shard_map/all_gather | solution.py:121
  118.0 3.2 %copy-start.13 = (f32[32]{0:T(128)S(1)}, f32[32]{0:T(128)}, u32[]{:S(2)}) copy-start(f32[32]{0:T(128)} %param.14) | copy-start | bytes 388
  126.1 11.9 %collective-permute-start = (bf16[3,2304]{1,0:T(4,128)(2,1)S(1)}, bf16[3,2304]{1,0:T(4,128)(2,1)S(1)}, u32[]{:S(2)}, u32[]{:S(2)}) collective-permute-start(bf16[3,2304]{1,0:T(4,128)(2,1)S(1)} %copy.81), channel_id=1, source_target_pairs={{0,1},{1,2},{2,3},{4,5},{5,6},{6,7},{8,9},{9,10},{10,11},{12,13},{... | collective-permute-start | bytes 41480 | tf_op jit(solution)/shard_map/ppermute | solution.py:12
  130.8 3.9 %copy-start.2 = (bf16[512,4384]{0,1:T(8,128)(2,1)S(1)}, bf16[512,4384]{0,1:T(8,128)(2,1)}, u32[]{:S(2)}) copy-start(bf16[512,4384]{0,1:T(8,128)(2,1)} %convolution_convert_fusion) | copy-start | bytes 13467652
  134.6 3.4 %copy-start.10 = (f32[4,2304]{1,0:T(4,128)S(1)}, f32[4,2304]{1,0:T(4,128)}, u32[]{:S(2)}) copy-start(f32[4,2304]{1,0:T(4,128)} %param.12) | copy-start | bytes 110596
  136.2 2.4 %copy-start.11 = (f32[2304]{0:T(1024)S(1)}, f32[2304]{0:T(1024)}, u32[]{:S(2)}) copy-start(f32[2304]{0:T(1024)} %param.13) | copy-start | bytes 27652
  147.0 1.4 copy-start.4
  149.6 1.7 copy-start.5
  180.3 3.5 %copy-start.7 = (bf16[128,8576]{1,0:T(8,128)(2,1)S(1)}, bf16[128,8576]{1,0:T(8,128)(2,1)}, u32[]{:S(2)}) copy-start(bf16[128,8576]{1,0:T(8,128)(2,1)} %all-gather.7.cloned.1.call-done) | copy-start | bytes 6586372
  181.4 3.2 %copy-start.8 = (f32[256,32,64]{0,2,1:T(8,128)S(1)}, f32[256,32,64]{0,2,1:T(8,128)}, u32[]{:S(2)}) copy-start(f32[256,32,64]{0,2,1:T(8,128)} %bitcast_add_fusion) | copy-start | bytes 6291460
  181.4 3.2 %copy-start.9 = (f32[256,32,64]{0,2,1:T(8,128)S(1)}, f32[256,32,64]{0,2,1:T(8,128)}, u32[]{:S(2)}) copy-start(f32[256,32,64]{0,2,1:T(8,128)} %bitcast_add_fusion.1) | copy-start | bytes 6291460
  183.6 1.9 copy-start.6
  183.6 2.5 %slice-start = ((bf16[512,2304]{0,1:T(8,128)(2,1)}), bf16[512,2048]{0,1:T(8,128)(2,1)S(1)}, s32[]{:S(2)}) async-start(bf16[512,2304]{0,1:T(8,128)(2,1)} %copy-done.4), calls=%async_computation.3 | async-start | bytes 4194304 | tf_op jit(solution)/shard_map/slice | solution.py:86
  183.6 2.4 %copy-start.14 = (f32[32]{0:T(128)S(1)}, f32[32]{0:T(128)}, u32[]{:S(2)}) copy-start(f32[32]{0:T(128)} %param.16) | copy-start | bytes 388
  188.3 5.3 %copy-start.3 = (f32[512,32,64]{0,2,1:T(8,128)}, f32[512,32,64]{0,2,1:T(8,128)S(1)}, u32[]{:S(2)}) copy-start(f32[512,32,64]{0,2,1:T(8,128)S(1)} %fusion.6) | copy-start | bytes 12582916
  192.8 9.4 %copy-start.12 = (f32[2048]{0:T(1024)S(1)}, f32[2048]{0:T(1024)}, u32[]{:S(2)}) copy-start(f32[2048]{0:T(1024)} %param.17) | copy-start | bytes 24580
  194.5 16.7 %all-to-all-start = ((f32[1,32,16,128]{3,2,0,1:T(8,128)}), f32[1,32,16,128]{3,2,0,1:T(8,128)S(1)}, u32[]{:S(2)}, u32[]{:S(2)}) async-start(f32[1,32,16,128]{3,2,0,1:T(8,128)} %bitcast.31), calls=%async_computation | async-start | bytes 524288 | tf_op jit(solution)/shard_map/all_to_all | solution.py:147
  202.3 10.3 %copy-start.1 = (bf16[1,1,512,2048]{3,2,1,0:T(8,128)(2,1)S(1)}, bf16[1,1,512,2048]{3,2,1,0:T(8,128)(2,1)}, u32[]{:S(2)}) copy-start(bf16[1,1,512,2048]{3,2,1,0:T(8,128)(2,1)} %param.10) | copy-start | bytes 6291460
Sparse Core Ops, SparseCore 0:
  21.9 80.7 all-gather.4
  149.7 30.5 all-gather.6

commit v8 on v7

--- a/solution.py
+++ b/solution.py
@@ -118,15 +118,22 @@
         [local_end.reshape(heads, hdim * nstate).astype(jnp.bfloat16), parts.reshape(heads, 3 * 128)],
         axis=1,
     )
-    gathered = lax.all_gather(packed, "seq", axis=0, tiled=False)
+    arrived = [packed]
+    for distance in range(1, seq_count):
+        cycle = [(i, (i + distance) % seq_count) for i in range(seq_count)]
+        arrived.append(lax.ppermute(packed, "seq", cycle))
+    gathered = jnp.stack(arrived)
     ends = gathered[:, :, : hdim * nstate].astype(jnp.float32).reshape(seq_count, heads, hdim, nstate)
     sent = gathered[:, :, hdim * nstate :].astype(jnp.float32)
-    totals = sent[:, :, 0] + (sent[:, :, 128] + sent[:, :, 256])
+    by_distance = sent[:, :, 0] + (sent[:, :, 128] + sent[:, :, 256])
     order = jnp.arange(seq_count)
+    source = (my_block - order) % seq_count
+    totals = jnp.take(by_distance, (my_block - order) % seq_count, axis=0)
     between = (order[None, :] > order[:, None]) & (order[None, :] < my_block)
     log_coef = jnp.sum(jnp.where(between[:, :, None], totals[None, :, :], 0.0), axis=1)
     coef = jnp.where((order < my_block)[:, None], jnp.exp(log_coef), 0.0)
-    entering = jnp.sum(coef[:, :, None, None] * ends, axis=0)
+    coef_by_distance = jnp.take(coef, source, axis=0)
+    entering = jnp.sum(coef_by_distance[:, :, None, None] * ends, axis=0)
     incoming = jnp.exp(through)[:, :, None] * jnp.einsum(
         "tn,hpn->thp", c_rows.astype(jnp.float32), entering, precision=lax.Precision.HIGHEST
     )
@@ -139,11 +146,12 @@
     scale = lax.rsqrt(jnp.mean(gated * gated, axis=1, keepdims=True) + 1e-05)
     normed = jnp.where(filled[:, None], gated * scale * norm_weight[None, :], 0.0)
     gated_out = normed.astype(jnp.bfloat16).reshape(1, 1, slots, inner)
-    later_mask = jnp.arange(seq_count)[None, :] > jnp.arange(seq_count)[:, None]
+    later_mask = order[None, :] > order[:, None]
     after = jnp.sum(jnp.where(later_mask[:, :, None], totals[None, :, :], 0.0), axis=1)
+    after_by_distance = jnp.take(after, source, axis=0)
     piece = hdim // seq_count
     own_ends = lax.dynamic_slice_in_dim(ends, my_block * piece, piece, axis=2)
-    share = jnp.sum(jnp.exp(after)[:, :, None, None] * own_ends, axis=0)
+    share = jnp.sum(jnp.exp(after_by_distance)[:, :, None, None] * own_ends, axis=0)
     moved = lax.all_to_all(share[None], "req", split_axis=1, concat_axis=0, tiled=True)
     final_states = jnp.take(moved, prompt_group, axis=0)
     return (gated_out, final_states)

time: 220 us -> 221 us (level)
    all_gather x1 -> x0, waiting for transfers between devices: 17.8 us -> none  [local(): gathered = lax.all_gather(packed, 'seq', axis=0, tiled=False)]
    ppermute x0 -> x3, waiting for transfers between devices: none -> 16.3 us  [local(): arrived.append(lax.ppermute(packed, 'seq', cycle))]
    ppermute x0 -> x3, starting transfers between devices: none -> 3.33 us  [local(): arrived.append(lax.ppermute(packed, 'seq', cycle))]
    dot_general x1, matrix products: 2.23 us -> 4.46 us  [local(): jnp.einsum('tn,hpn->thp', c_rows.astype(jnp.float32), entering, precision...]
    unnamed x37 -> x34, local copies, waits for them, and re-layouts: 8.87 us -> 7.24 us
  transfers between devices with their start and end apart: 4 -> 6, of which waited for: 3 -> 5; matrix products, arithmetic and copies ran while one was open for 15% -> 13% of each run, Pallas kernels for 0% -> 0%
where the time goes in v8:
time: 221 us
  waiting for transfers between devices  92.6 us (42%)
  other arithmetic  32.1 us (15%)
  matrix products  31.7 us (14%)
  local copies, waits for them, and re-layouts  23.2 us (10%)
  between operations  15.8 us (7%)
  blocking collectives  12.8 us (6%)
  starting transfers between devices  12.5 us (6%)
    all_gather x1, waiting for transfers between devices, local(): lax.all_gather(wide_rows, 'req', axis=0, tiled=True)  76.2 us
    ppermute x3, waiting for transfers between devices, local(): arrived.append(lax.ppermute(packed, 'seq', cycle))  16.3 us
    dot_general x1, matrix products, local(): jnp.dot(tok_rows, lax.all_gather(wide_rows, 'req', axis=0, tiled=True), p...  15.3 us
    all_gather x1, blocking collectives, local(): wide_rows = lax.all_gather(w_in, 'seq', axis=1, tiled=True)  12.8 us
    dot_general x2, matrix products, block_step(): jnp.einsum('htu,uhp->thp', mixing, heads_x, preferred_element_type=jnp.fl...  8.73 us
    convert_element_type x1, other arithmetic, local(): conv_act = jax.nn.silu(accum).astype(jnp.bfloat16)  8.36 us
    unnamed x34, local copies, waits for them, and re-layouts  7.24 us
    slice x3, local copies, waits for them, and re-layouts, local(): conv_in[:slots - lag]  6.37 us
  transfers between devices with their start and end apart: 6, of which 5 were waited for; matrix products, arithmetic and copies ran while one was open for 13% of the time, Pallas kernels for 0%

profile of v8, /device:TPU:1, one launch (start us, length us, event | category | flops | bytes accessed | tf_op | source)
XLA Modules:
  0.0 220.7 jit_solution(9351436009000988413)
XLA Ops:
  7.2 12.8 %all-gather = bf16[4,1096,64]{1,2,0:T(8,128)(2,1)S(1)} all-gather(bf16[1,1096,64]{1,2,0:T(8,128)(2,1)} %bitcast.181), channel_id=1, replica_groups=mesh['req'=32,'seq'=4] {'seq'}, dimensions={0}, use_global_device_ids=true | all-gather | bytes 701440 | tf_op jit(solution)/shard_map/all_gather | solution.py:61
  21.8 1.3 compare_select_fusion.2
  26.5 76.2 %all-gather.3.cloned.1.call-done = bf16[2048,4384]{1,0:T(8,128)(2,1)} async-done(((bf16[64,4384]{1,0:T(8,128)(2,1)}), bf16[2048,4384]{1,0:T(8,128)(2,1)}) %all-gather.3.cloned.1.call-update) | async-done | bytes 17956880 | tf_op jit(solution)/shard_map/all_gather | solution.py:64
  102.7 15.3 %convolution_convert_fusion = bf16[512,4384]{0,1:T(8,128)(2,1)} fusion(bf16[2048,4384]{1,0:T(8,128)(2,1)} %all-gather.3.cloned.1.call-done, bf16[1,1,512,2048]{3,2,1,0:T(8,128)(2,1)S(1)} %copy-done), kind=kOutput, calls=%fused_computation.6 | convolution fusion | flops 9196158976 | bytes 24543232 | tf_op jit(solution)/shard_map/dot_general | solution.py:62
  118.0 3.2 %slice.196 = bf16[512,2304]{0,1:T(8,128)(2,1)} slice(bf16[512,4384]{0,1:T(8,128)(2,1)} %convolution_convert_fusion), slice={[0:512], [2048:4352]} | slice | bytes 4718592 | tf_op jit(solution)/shard_map/slice | solution.py:68
  125.9 1.5 constant_dynamic-slice_fusion
  127.7 3.5 %collective-permute-start = (bf16[3,2304]{1,0:T(4,128)(2,1)S(1)}, bf16[3,2304]{1,0:T(4,128)(2,1)S(1)}, u32[]{:S(2)}, u32[]{:S(2)}) collective-permute-start(bf16[3,2304]{1,0:T(4,128)(2,1)S(1)} %copy.83), channel_id=1, source_target_pairs={{0,1},{1,2},{2,3},{4,5},{5,6},{6,7},{8,9},{9,10},{10,11},{12,13},{... | collective-permute-start | bytes 41480 | tf_op jit(solution)/shard_map/ppermute | solution.py:12
  131.5 3.2 %slice.195 = bf16[511,2304]{0,1:T(8,128)(2,1)} slice(bf16[512,4384]{0,1:T(8,128)(2,1)} %convolution_convert_fusion), slice={[0:511], [2048:4352]} | slice | bytes 4709376 | tf_op jit(solution)/shard_map/slice | solution.py:75
  134.8 1.5 slice.194
  136.3 1.6 slice.193
  138.6 8.4 %multiply_convert_fusion.2 = bf16[512,2304]{0,1:T(8,128)(2,1)S(1)} fusion(f32[3,2304]{0,1:T(8,128)S(1)} %copy.84, f32[2304]{0:T(1024)S(1)} %get-tuple-element.15, bf16[511,2304]{0,1:T(8,128)(2,1)} %slice.195, f32[2304]{0:T(1024)S(1)} %get-tuple-element.16, bf16[510,2304]{0,1:T(8,128)(2,1)} %slice.194, f32[2304]{0:T(1024)S(1)} %get-tuple-element.14, ...), kind=kLoop, calls=%fused_computation.9 | loop fusion | flops 21233664 | bytes 11842560 | tf_op jit(solution)/shard_map/convert_element_type | solution.py:85
  152.1 2.4 %collective-permute-start.2 = (bf16[32,8576]{1,0:T(8,128)(2,1)S(1)}, bf16[32,8576]{1,0:T(8,128)(2,1)S(1)}, u32[]{:S(2)}, u32[]{:S(2)}) collective-permute-start(bf16[32,8576]{1,0:T(8,128)(2,1)S(1)} %bitcast_dynamic-update-slice_fusion.1), channel_id=1, source_target_pairs={{0,2},{1,3},{2,0},{3,1},{4,6},{5,7},{6,4},{7,5},{8,10},{9,11},{10,... | collective-permute-start | bytes 1646600 | tf_op jit(solution)/shard_map/ppermute | solution.py:124
  154.7 4.3 %bitcast_add_fusion = f32[256,32,64]{0,2,1:T(8,128)} fusion(f32[256,32,64]{0,2,1:T(8,128)S(1)} %fusion.33, bf16[256,32,64]{0,2,1:T(8,128)(2,1)S(1)} %bitcast.179, f32[32,256]{1,0:T(8,128)S(1)} %get-tuple-element.30, f32[32,256]{1,0:T(8,128)S(1)} %get-tuple-element.41, f32[256,256]{1,0:T(8,128)S(1)} %fusion.37, pred[256,256]{1,0:T(8,128)(4,1)S(1)} %iota_compare_fusion, ...), kind=kOutput, calls=%fused_computation.43 | convolution fusion | flops 282066944 | bytes 5668864 | tf_op jit(solution)/shard_map/htu,uhp->thp/dot_general | solution.py:27
  159.1 4.4 %bitcast_add_fusion.1 = f32[256,32,64]{0,2,1:T(8,128)} fusion(f32[256,32,64]{0,2,1:T(8,128)S(1)} %fusion.25, bf16[256,32,64]{0,2,1:T(8,128)(2,1)S(1)} %bitcast.178, f32[32,256]{1,0:T(8,128)S(1)} %get-tuple-element.31, f32[32,256]{1,0:T(8,128)S(1)} %get-tuple-element.42, f32[256,256]{1,0:T(8,128)S(1)} %fusion.42, pred[256,256]{1,0:T(8,128)(4,1)S(1)} %iota_compare_fusion, ...), kind=kOutput, calls=%fused_computation.44 | convolution fusion | flops 282066944 | bytes 5668864 | tf_op jit(solution)/shard_map/htu,uhp->thp/dot_general | solution.py:27
  163.4 1.7 collective-permute-done.3
  165.2 2.1 collective-permute-done.2
  167.3 12.4 %collective-permute-done.1 = bf16[32,8576]{1,0:T(8,128)(2,1)S(1)} collective-permute-done((bf16[32,8576]{1,0:T(8,128)(2,1)S(1)}, bf16[32,8576]{1,0:T(8,128)(2,1)S(1)}, u32[]{:S(2)}, u32[]{:S(2)}) %collective-permute-start.1) | collective-permute-done | bytes 548896 | tf_op jit(solution)/shard_map/ppermute | solution.py:124
  180.5 2.4 %fusion.20 = f32[4,32,8192]{2,1,0:T(8,128)} fusion(bf16[1,32,8576]{2,1,0:T(8,128)(2,1)S(1)} %bitcast.163, bf16[1,32,8576]{2,1,0:T(8,128)(2,1)S(1)} %bitcast.166, bf16[1,32,8576]{2,1,0:T(8,128)(2,1)S(1)} %bitcast.169, bf16[1,32,8576]{2,1,0:T(8,128)(2,1)S(1)} %bitcast.159), kind=kLoop, calls=%fused_computation.36 | loop fusion | flops 8388608 | bytes 6389760 | tf_op jit(solution)/shard_map/convert_element_type | solution.py:126
  185.0 2.0 multiply_reduce_fusion.1
  187.2 4.5 %fusion.6 = f32[512,32,64]{0,2,1:T(8,128)S(1)} fusion(f32[256,32,64]{0,2,1:T(8,128)} %bitcast_add_fusion, f32[256,32,64]{0,2,1:T(8,128)} %bitcast_add_fusion.1, bf16[512,32,64]{0,2,1:T(8,128)(2,1)S(1)} %bitcast.156, f32[32,64,128]{2,1,0:T(8,128)S(1)} %bitcast.171, f32[32]{0:T(128)S(1)} %copy-done.13, f32[512,32]{0,1:T(8,128)S(1)} %fusion.54, ...), kind=kOutput, calls=%fused_computation.17 | convolution fusion | flops 1616904192 | bytes 11731456 | tf_op jit(solution)/shard_map/tn,hpn->thp/dot_general | solution.py:137
  191.7 4.6 %multiply_reduce_fusion = f32[512]{0:T(512)S(1)} fusion(bf16[512,4384]{0,1:T(8,128)(2,1)} %convolution_convert_fusion, f32[512,32,64]{0,2,1:T(8,128)S(1)} %fusion.6), kind=kLoop, calls=%fused_computation.20 | loop fusion | flops 8388096 | bytes 6293504 | tf_op jit(solution)/shard_map/reduce_sum | solution.py:146
  198.0 5.6 %all-to-all-start = ((f32[1,32,16,128]{3,2,0,1:T(8,128)}), f32[1,32,16,128]{3,2,0,1:T(8,128)S(1)}, u32[]{:S(2)}, u32[]{:S(2)}) async-start(f32[1,32,16,128]{3,2,0,1:T(8,128)} %bitcast.34), calls=%async_computation | async-start | bytes 524288 | tf_op jit(solution)/shard_map/all_to_all | solution.py:155
  203.6 4.8 %fusion.19 = bf16[1,1,512,2048]{2,3,1,0:T(8,128)(2,1)} fusion(f32[2048]{0:T(1024)S(1)} %copy-done.11, f32[512]{0:T(512)S(1)} %add_rsqrt_fusion, pred[512]{0:T(512)(128)(4,1)S(1)} %iota_compare_fusion.2, bf16[512,4384]{0,1:T(8,128)(2,1)} %convolution_convert_fusion, f32[512,32,64]{0,2,1:T(8,128)} %copy-done.3), kind=kLoop, calls=%fused_computation.34 | loop fusion | flops 10485760 | bytes 8399360 | tf_op jit(solution)/shard_map/reshape | solution.py:148
  208.4 3.9 %copy.97 = bf16[1,1,512,2048]{3,2,1,0:T(8,128)(2,1)} copy(bf16[1,1,512,2048]{2,3,1,0:T(8,128)(2,1)} %fusion.19) | data formatting | bytes 4194304
  (108 shorter events, 21.2 us)
Async XLA Ops:
  7.2 95.5 %copy-start = (bf16[1,1,512,2048]{3,2,1,0:T(8,128)(2,1)S(1)}, bf16[1,1,512,2048]{3,2,1,0:T(8,128)(2,1)}, u32[]{:S(2)}) copy-start(bf16[1,1,512,2048]{3,2,1,0:T(8,128)(2,1)} %param.12) | copy-start | bytes 6291460
  7.2 95.5 %all-gather.3.cloned.1.call-start = ((), (), s32[]{:S(2)}) async-start(), calls=%async_computation.1 | async-start | bytes 18923520 | tf_op jit(solution)/shard_map/all_gather | solution.py:64
  118.0 3.2 %copy-start.12 = (f32[32]{0:T(128)S(1)}, f32[32]{0:T(128)}, u32[]{:S(2)}) copy-start(f32[32]{0:T(128)} %param.16) | copy-start | bytes 388
  127.7 7.1 %copy-start.2 = (bf16[512,4384]{0,1:T(8,128)(2,1)S(1)}, bf16[512,4384]{0,1:T(8,128)(2,1)}, u32[]{:S(2)}) copy-start(bf16[512,4384]{0,1:T(8,128)(2,1)} %convolution_convert_fusion) | copy-start | bytes 13467652
  127.7 10.4 %collective-permute-start = (bf16[3,2304]{1,0:T(4,128)(2,1)S(1)}, bf16[3,2304]{1,0:T(4,128)(2,1)S(1)}, u32[]{:S(2)}, u32[]{:S(2)}) collective-permute-start(bf16[3,2304]{1,0:T(4,128)(2,1)S(1)} %copy.83), channel_id=1, source_target_pairs={{0,1},{1,2},{2,3},{4,5},{5,6},{6,7},{8,9},{9,10},{10,11},{12,13},{... | collective-permute-start | bytes 41480 | tf_op jit(solution)/shard_map/ppermute | solution.py:12
  134.8 3.3 %copy-start.9 = (f32[4,2304]{1,0:T(4,128)S(1)}, f32[4,2304]{1,0:T(4,128)}, u32[]{:S(2)}) copy-start(f32[4,2304]{1,0:T(4,128)} %param.14) | copy-start | bytes 110596
  136.3 2.3 %copy-start.10 = (f32[2304]{0:T(1024)S(1)}, f32[2304]{0:T(1024)}, u32[]{:S(2)}) copy-start(f32[2304]{0:T(1024)} %param.15) | copy-start | bytes 27652
  147.0 3.5 %copy-start.4 = (bf16[512,2304]{0,1:T(8,128)(2,1)}, bf16[512,2304]{0,1:T(8,128)(2,1)S(1)}, u32[]{:S(2)}) copy-start(bf16[512,2304]{0,1:T(8,128)(2,1)S(1)} %multiply_convert_fusion.2) | copy-start | bytes 7077892
  151.4 13.8 %collective-permute-start.3 = (bf16[32,8576]{1,0:T(8,128)(2,1)S(1)}, bf16[32,8576]{1,0:T(8,128)(2,1)S(1)}, u32[]{:S(2)}, u32[]{:S(2)}) collective-permute-start(bf16[32,8576]{1,0:T(8,128)(2,1)S(1)} %bitcast_dynamic-update-slice_fusion.1), channel_id=1, source_target_pairs={{0,3},{1,0},{2,1},{3,2},{4,7},{5,4},{6,5},{7,6},{8,11},{9,8},{10,9... | collective-permute-start | bytes 1646600 | tf_op jit(solution)/shard_map/ppermute | solution.py:124
  152.1 15.3 %collective-permute-start.2 = (bf16[32,8576]{1,0:T(8,128)(2,1)S(1)}, bf16[32,8576]{1,0:T(8,128)(2,1)S(1)}, u32[]{:S(2)}, u32[]{:S(2)}) collective-permute-start(bf16[32,8576]{1,0:T(8,128)(2,1)S(1)} %bitcast_dynamic-update-slice_fusion.1), channel_id=1, source_target_pairs={{0,2},{1,3},{2,0},{3,1},{4,6},{5,7},{6,4},{7,5},{8,10},{9,11},{10,... | collective-permute-start | bytes 1646600 | tf_op jit(solution)/shard_map/ppermute | solution.py:124
  154.4 25.3 %collective-permute-start.1 = (bf16[32,8576]{1,0:T(8,128)(2,1)S(1)}, bf16[32,8576]{1,0:T(8,128)(2,1)S(1)}, u32[]{:S(2)}, u32[]{:S(2)}) collective-permute-start(bf16[32,8576]{1,0:T(8,128)(2,1)S(1)} %bitcast_dynamic-update-slice_fusion.1), channel_id=1, source_target_pairs={{0,1},{1,2},{2,3},{3,0},{4,5},{5,6},{6,7},{7,4},{8,9},{9,10},{10,1... | collective-permute-start | bytes 1646600 | tf_op jit(solution)/shard_map/ppermute | solution.py:124
  167.3 12.4 %copy-start.7 = (bf16[32,8576]{1,0:T(8,128)(2,1)}, bf16[32,8576]{1,0:T(8,128)(2,1)S(1)}, u32[]{:S(2)}) copy-start(bf16[32,8576]{1,0:T(8,128)(2,1)S(1)} %collective-permute-done.2) | copy-start | bytes 1646596
  179.7 0.8 copy-start.8
  182.9 4.3 %slice-start = ((bf16[512,2304]{0,1:T(8,128)(2,1)}), bf16[512,2048]{0,1:T(8,128)(2,1)S(1)}, s32[]{:S(2)}) async-start(bf16[512,2304]{0,1:T(8,128)(2,1)} %copy-done.4), calls=%async_computation.2 | async-start | bytes 4194304 | tf_op jit(solution)/shard_map/slice | solution.py:86
  182.9 4.3 %copy-start.13 = (f32[32]{0:T(128)S(1)}, f32[32]{0:T(128)}, u32[]{:S(2)}) copy-start(f32[32]{0:T(128)} %param.18) | copy-start | bytes 388
  184.9 2.3 %copy-start.5 = (bf16[512,2304]{0,1:T(8,128)(2,1)S(1)}, bf16[512,2304]{0,1:T(8,128)(2,1)}, u32[]{:S(2)}) copy-start(bf16[512,2304]{0,1:T(8,128)(2,1)} %copy-done.4) | copy-start | bytes 7077892
  191.7 5.4 %copy-start.3 = (f32[512,32,64]{0,2,1:T(8,128)}, f32[512,32,64]{0,2,1:T(8,128)S(1)}, u32[]{:S(2)}) copy-start(f32[512,32,64]{0,2,1:T(8,128)S(1)} %fusion.6) | copy-start | bytes 12582916
  191.7 4.6 %copy-start.6 = (f32[4,32,8192]{2,1,0:T(8,128)S(1)}, f32[4,32,8192]{2,1,0:T(8,128)}, u32[]{:S(2)}) copy-start(f32[4,32,8192]{2,1,0:T(8,128)} %fusion.20) | copy-start | bytes 12582916
  196.3 7.3 %copy-start.11 = (f32[2048]{0:T(1024)S(1)}, f32[2048]{0:T(1024)}, u32[]{:S(2)}) copy-start(f32[2048]{0:T(1024)} %param.19) | copy-start | bytes 24580
  198.0 14.5 %all-to-all-start = ((f32[1,32,16,128]{3,2,0,1:T(8,128)}), f32[1,32,16,128]{3,2,0,1:T(8,128)S(1)}, u32[]{:S(2)}, u32[]{:S(2)}) async-start(f32[1,32,16,128]{3,2,0,1:T(8,128)} %bitcast.34), calls=%async_computation | async-start | bytes 524288 | tf_op jit(solution)/shard_map/all_to_all | solution.py:155
  203.6 10.3 %copy-start.1 = (bf16[1,1,512,2048]{3,2,1,0:T(8,128)(2,1)S(1)}, bf16[1,1,512,2048]{3,2,1,0:T(8,128)(2,1)}, u32[]{:S(2)}) copy-start(bf16[1,1,512,2048]{3,2,1,0:T(8,128)(2,1)} %param.12) | copy-start | bytes 6291460
Sparse Core Ops, SparseCore 0:
  21.9 80.7 all-gather.2

commit v9 on v7

--- a/solution.py
+++ b/solution.py
@@ -58,7 +58,8 @@
     my_block = lax.axis_index("seq")
     qlen = jnp.sum(jnp.where(prompt_group == my_group, lengths, 0))
     filled = jnp.arange(slots, dtype=jnp.int32) < qlen
-    wide_rows = lax.all_gather(w_in, "seq", axis=1, tiled=True)
+    stacked = lax.all_gather(w_in, "seq", axis=0, tiled=False)
+    wide_rows = jnp.transpose(stacked, (1, 0, 2)).reshape(w_in.shape[0], -1)
     projected = jnp.dot(
         tok_rows,
         lax.all_gather(wide_rows, "req", axis=0, tiled=True),

time: 220 us -> 220 us (level)
    unnamed x37 -> x36, local copies, waits for them, and re-layouts: 8.87 us -> 7.62 us
where the time goes in v9:
time: 220 us; the launch traced here: 219 us
  waiting for transfers between devices  94.2 us (43%)
  other arithmetic  32 us (15%)
  matrix products  29.5 us (13%)
  local copies, waits for them, and re-layouts  23.9 us (11%)
  between operations  15.8 us (7%)
  blocking collectives  12.8 us (6%)
  starting transfers between devices  11.1 us (5%)
    all_gather x1, waiting for transfers between devices, local(): lax.all_gather(wide_rows, 'req', axis=0, tiled=True)  76.2 us
    all_gather x1, waiting for transfers between devices, local(): gathered = lax.all_gather(packed, 'seq', axis=0, tiled=False)  17.8 us
    dot_general x1, matrix products, local(): jnp.dot(tok_rows, lax.all_gather(wide_rows, 'req', axis=0, tiled=True), p...  15.3 us
    all_gather x1, blocking collectives, local(): stacked = lax.all_gather(w_in, 'seq', axis=0, tiled=False)  12.8 us
    dot_general x2, matrix products, block_step(): jnp.einsum('htu,uhp->thp', mixing, heads_x, preferred_element_type=jnp.fl...  8.73 us
    convert_element_type x1, other arithmetic, local(): conv_act = jax.nn.silu(accum).astype(jnp.bfloat16)  8.36 us
    all_to_all x1, starting transfers between devices, local(): lax.all_to_all(share[None], 'req', split_axis=1, concat_axis=0, tiled=True)  7.75 us
    unnamed x36, local copies, waits for them, and re-layouts  7.62 us
  transfers between devices with their start and end apart: 4, of which 3 were waited for; matrix products, arithmetic and copies ran while one was open for 15% of the time, Pallas kernels for 0%

profile of v9, /device:TPU:1, one launch (start us, length us, event | category | flops | bytes accessed | tf_op | source)
XLA Modules:
  0.0 219.4 jit_solution(4030392255377088037)
XLA Ops:
  7.2 12.8 %all-gather = bf16[256,1096]{1,0:T(8,128)(2,1)S(1)} all-gather(bf16[64,1096]{1,0:T(8,128)(2,1)} %param.11), channel_id=2, replica_groups=mesh['req'=32,'seq'=4] {'seq'}, dimensions={0}, use_global_device_ids=true | all-gather | bytes 701440 | tf_op jit(solution)/shard_map/all_gather | solution.py:61
  20.5 1.2 reshape.346
  21.8 1.3 compare_select_fusion.1
  26.5 76.2 %all-gather.5.cloned.1.call-done = bf16[2048,4384]{1,0:T(8,128)(2,1)} async-done(((bf16[64,4384]{1,0:T(8,128)(2,1)}), bf16[2048,4384]{1,0:T(8,128)(2,1)}) %all-gather.5.cloned.1.call-update) | async-done | bytes 17956880 | tf_op jit(solution)/shard_map/all_gather | solution.py:65
  102.7 15.3 %convolution_convert_fusion = bf16[512,4384]{0,1:T(8,128)(2,1)} fusion(bf16[2048,4384]{1,0:T(8,128)(2,1)} %all-gather.5.cloned.1.call-done, bf16[1,1,512,2048]{3,2,1,0:T(8,128)(2,1)S(1)} %copy-done), kind=kOutput, calls=%fused_computation.3 | convolution fusion | flops 9196158976 | bytes 24543232 | tf_op jit(solution)/shard_map/dot_general | solution.py:63
  118.0 3.2 %slice.190 = bf16[512,2304]{0,1:T(8,128)(2,1)} slice(bf16[512,4384]{0,1:T(8,128)(2,1)} %convolution_convert_fusion), slice={[0:512], [2048:4352]} | slice | bytes 4718592 | tf_op jit(solution)/shard_map/slice | solution.py:69
  124.3 1.5 constant_dynamic-slice_fusion
  126.1 3.3 %collective-permute-start = (bf16[3,2304]{1,0:T(4,128)(2,1)S(1)}, bf16[3,2304]{1,0:T(4,128)(2,1)S(1)}, u32[]{:S(2)}, u32[]{:S(2)}) collective-permute-start(bf16[3,2304]{1,0:T(4,128)(2,1)S(1)} %copy.81), channel_id=1, source_target_pairs={{0,1},{1,2},{2,3},{4,5},{5,6},{6,7},{8,9},{9,10},{10,11},{12,13},{... | collective-permute-start | bytes 41480 | tf_op jit(solution)/shard_map/ppermute | solution.py:12
  129.4 1.2 reduce-window.26
  131.2 3.4 %slice.189 = bf16[511,2304]{0,1:T(8,128)(2,1)} slice(bf16[512,4384]{0,1:T(8,128)(2,1)} %convolution_convert_fusion), slice={[0:511], [2048:4352]} | slice | bytes 4709376 | tf_op jit(solution)/shard_map/slice | solution.py:76
  134.6 1.5 slice.188
  136.2 1.6 slice.187
  138.6 8.4 %multiply_convert_fusion.2 = bf16[512,2304]{0,1:T(8,128)(2,1)S(1)} fusion(f32[3,2304]{0,1:T(8,128)S(1)} %copy.82, f32[2304]{0:T(1024)S(1)} %get-tuple-element.14, bf16[511,2304]{0,1:T(8,128)(2,1)} %slice.189, f32[2304]{0:T(1024)S(1)} %get-tuple-element.15, bf16[510,2304]{0,1:T(8,128)(2,1)} %slice.188, f32[2304]{0:T(1024)S(1)} %get-tuple-element.13, ...), kind=kLoop, calls=%fused_computation.6 | loop fusion | flops 21233664 | bytes 11842560 | tf_op jit(solution)/shard_map/convert_element_type | solution.py:86
  149.8 1.5 copy-done.5
  153.8 4.4 %bitcast_add_fusion = f32[256,32,64]{0,2,1:T(8,128)} fusion(f32[256,32,64]{0,2,1:T(8,128)S(1)} %fusion.32, bf16[256,32,64]{0,2,1:T(8,128)(2,1)S(1)} %bitcast.169, f32[32,256]{1,0:T(8,128)S(1)} %get-tuple-element.29, f32[32,256]{1,0:T(8,128)S(1)} %get-tuple-element.40, f32[256,256]{1,0:T(8,128)S(1)} %fusion.36, pred[256,256]{1,0:T(8,128)(4,1)S(1)} %iota_compare_fusion, ...), kind=kOutput, calls=%fused_computation.37 | convolution fusion | flops 282066944 | bytes 5668864 | tf_op jit(solution)/shard_map/htu,uhp->thp/dot_general | solution.py:27
  158.2 4.4 %bitcast_add_fusion.1 = f32[256,32,64]{0,2,1:T(8,128)} fusion(f32[256,32,64]{0,2,1:T(8,128)S(1)} %fusion.24, bf16[256,32,64]{0,2,1:T(8,128)(2,1)S(1)} %bitcast.168, f32[32,256]{1,0:T(8,128)S(1)} %get-tuple-element.30, f32[32,256]{1,0:T(8,128)S(1)} %get-tuple-element.41, f32[256,256]{1,0:T(8,128)S(1)} %fusion.41, pred[256,256]{1,0:T(8,128)(4,1)S(1)} %iota_compare_fusion, ...), kind=kOutput, calls=%fused_computation.38 | convolution fusion | flops 282066944 | bytes 5668864 | tf_op jit(solution)/shard_map/htu,uhp->thp/dot_general | solution.py:27
  162.6 17.8 %all-gather.7.cloned.1.call-done = bf16[128,8576]{1,0:T(8,128)(2,1)} async-done(((bf16[32,8576]{1,0:T(8,128)(2,1)}), bf16[128,8576]{1,0:T(8,128)(2,1)}) %all-gather.7.cloned.1.call-update) | async-done | bytes 2195472 | tf_op jit(solution)/shard_map/all_gather | solution.py:122
  180.3 1.1 slice_convert_fusion.1
  181.4 2.2 slice_convert_fusion
  186.0 2.2 %fusion.6 = f32[512,32,64]{0,2,1:T(8,128)S(1)} fusion(f32[256,32,64]{0,2,1:T(8,128)S(1)} %copy-done.8, f32[256,32,64]{0,2,1:T(8,128)S(1)} %copy-done.9, bf16[512,32,64]{0,2,1:T(8,128)(2,1)S(1)} %bitcast.153, f32[32,64,128]{2,1,0:T(8,128)S(1)} %bitcast.159, f32[32]{0:T(128)S(1)} %copy-done.14, f32[512,32]{0,1:T(8,128)S(1)} %fusion.52, ...), kind=kOutput, calls=%fused_computation.14 | convolution fusion | flops 1616904192 | bytes 11731456 | tf_op jit(solution)/shard_map/tn,hpn->thp/dot_general | solution.py:131
  188.3 4.5 %multiply_reduce_fusion = f32[512]{0:T(512)S(1)} fusion(bf16[512,4384]{0,1:T(8,128)(2,1)} %convolution_convert_fusion, f32[512,32,64]{0,2,1:T(8,128)S(1)} %fusion.6), kind=kLoop, calls=%fused_computation.17 | loop fusion | flops 8388096 | bytes 6293504 | tf_op jit(solution)/shard_map/reduce_sum | solution.py:140
  194.5 7.7 %all-to-all-start = ((f32[1,32,16,128]{3,2,0,1:T(8,128)}), f32[1,32,16,128]{3,2,0,1:T(8,128)S(1)}, u32[]{:S(2)}, u32[]{:S(2)}) async-start(f32[1,32,16,128]{3,2,0,1:T(8,128)} %bitcast.30), calls=%async_computation | async-start | bytes 524288 | tf_op jit(solution)/shard_map/all_to_all | solution.py:148
  202.3 4.8 %fusion.19 = bf16[1,1,512,2048]{2,3,1,0:T(8,128)(2,1)} fusion(f32[2048]{0:T(1024)S(1)} %copy-done.12, f32[512]{0:T(512)S(1)} %add_rsqrt_fusion, pred[512]{0:T(512)(128)(4,1)S(1)} %iota_compare_fusion.2, bf16[512,4384]{0,1:T(8,128)(2,1)} %convolution_convert_fusion, f32[512,32,64]{0,2,1:T(8,128)} %copy-done.3), kind=kLoop, calls=%fused_computation.31 | loop fusion | flops 10485760 | bytes 8399360 | tf_op jit(solution)/shard_map/reshape | solution.py:142
  207.1 3.9 %copy.95 = bf16[1,1,512,2048]{3,2,1,0:T(8,128)(2,1)} copy(bf16[1,1,512,2048]{2,3,1,0:T(8,128)(2,1)} %fusion.19) | data formatting | bytes 4194304
  (101 shorter events, 18.1 us)
Async XLA Ops:
  7.2 95.5 %copy-start = (bf16[1,1,512,2048]{3,2,1,0:T(8,128)(2,1)S(1)}, bf16[1,1,512,2048]{3,2,1,0:T(8,128)(2,1)}, u32[]{:S(2)}) copy-start(bf16[1,1,512,2048]{3,2,1,0:T(8,128)(2,1)} %param.10) | copy-start | bytes 6291460
  7.2 95.5 %all-gather.5.cloned.1.call-start = ((), (), s32[]{:S(2)}) async-start(), calls=%async_computation.1 | async-start | bytes 18923520 | tf_op jit(solution)/shard_map/all_gather | solution.py:65
  21.8 158.5 %all-gather.7.cloned.1.call-start = ((), (), s32[]{:S(2)}) async-start(), calls=%async_computation.2 | async-start | bytes 2744320 | tf_op jit(solution)/shard_map/all_gather | solution.py:122
  118.0 3.2 %copy-start.13 = (f32[32]{0:T(128)S(1)}, f32[32]{0:T(128)}, u32[]{:S(2)}) copy-start(f32[32]{0:T(128)} %param.14) | copy-start | bytes 388
  126.1 11.9 %collective-permute-start = (bf16[3,2304]{1,0:T(4,128)(2,1)S(1)}, bf16[3,2304]{1,0:T(4,128)(2,1)S(1)}, u32[]{:S(2)}, u32[]{:S(2)}) collective-permute-start(bf16[3,2304]{1,0:T(4,128)(2,1)S(1)} %copy.81), channel_id=1, source_target_pairs={{0,1},{1,2},{2,3},{4,5},{5,6},{6,7},{8,9},{9,10},{10,11},{12,13},{... | collective-permute-start | bytes 41480 | tf_op jit(solution)/shard_map/ppermute | solution.py:12
  130.8 3.9 %copy-start.2 = (bf16[512,4384]{0,1:T(8,128)(2,1)S(1)}, bf16[512,4384]{0,1:T(8,128)(2,1)}, u32[]{:S(2)}) copy-start(bf16[512,4384]{0,1:T(8,128)(2,1)} %convolution_convert_fusion) | copy-start | bytes 13467652
  134.6 3.4 %copy-start.10 = (f32[4,2304]{1,0:T(4,128)S(1)}, f32[4,2304]{1,0:T(4,128)}, u32[]{:S(2)}) copy-start(f32[4,2304]{1,0:T(4,128)} %param.12) | copy-start | bytes 110596
  136.2 2.4 %copy-start.11 = (f32[2304]{0:T(1024)S(1)}, f32[2304]{0:T(1024)}, u32[]{:S(2)}) copy-start(f32[2304]{0:T(1024)} %param.13) | copy-start | bytes 27652
  147.0 1.4 copy-start.4
  149.6 1.7 copy-start.5
  180.3 3.5 %copy-start.7 = (bf16[128,8576]{1,0:T(8,128)(2,1)S(1)}, bf16[128,8576]{1,0:T(8,128)(2,1)}, u32[]{:S(2)}) copy-start(bf16[128,8576]{1,0:T(8,128)(2,1)} %all-gather.7.cloned.1.call-done) | copy-start | bytes 6586372
  181.4 3.2 %copy-start.8 = (f32[256,32,64]{0,2,1:T(8,128)S(1)}, f32[256,32,64]{0,2,1:T(8,128)}, u32[]{:S(2)}) copy-start(f32[256,32,64]{0,2,1:T(8,128)} %bitcast_add_fusion) | copy-start | bytes 6291460
  181.4 3.2 %copy-start.9 = (f32[256,32,64]{0,2,1:T(8,128)S(1)}, f32[256,32,64]{0,2,1:T(8,128)}, u32[]{:S(2)}) copy-start(f32[256,32,64]{0,2,1:T(8,128)} %bitcast_add_fusion.1) | copy-start | bytes 6291460
  183.6 1.9 copy-start.6
  183.6 2.5 %slice-start = ((bf16[512,2304]{0,1:T(8,128)(2,1)}), bf16[512,2048]{0,1:T(8,128)(2,1)S(1)}, s32[]{:S(2)}) async-start(bf16[512,2304]{0,1:T(8,128)(2,1)} %copy-done.4), calls=%async_computation.3 | async-start | bytes 4194304 | tf_op jit(solution)/shard_map/slice | solution.py:87
  183.6 2.4 %copy-start.14 = (f32[32]{0:T(128)S(1)}, f32[32]{0:T(128)}, u32[]{:S(2)}) copy-start(f32[32]{0:T(128)} %param.16) | copy-start | bytes 388
  188.3 5.3 %copy-start.3 = (f32[512,32,64]{0,2,1:T(8,128)}, f32[512,32,64]{0,2,1:T(8,128)S(1)}, u32[]{:S(2)}) copy-start(f32[512,32,64]{0,2,1:T(8,128)S(1)} %fusion.6) | copy-start | bytes 12582916
  192.8 9.4 %copy-start.12 = (f32[2048]{0:T(1024)S(1)}, f32[2048]{0:T(1024)}, u32[]{:S(2)}) copy-start(f32[2048]{0:T(1024)} %param.17) | copy-start | bytes 24580
  194.5 16.7 %all-to-all-start = ((f32[1,32,16,128]{3,2,0,1:T(8,128)}), f32[1,32,16,128]{3,2,0,1:T(8,128)S(1)}, u32[]{:S(2)}, u32[]{:S(2)}) async-start(f32[1,32,16,128]{3,2,0,1:T(8,128)} %bitcast.30), calls=%async_computation | async-start | bytes 524288 | tf_op jit(solution)/shard_map/all_to_all | solution.py:148
  202.3 10.3 %copy-start.1 = (bf16[1,1,512,2048]{3,2,1,0:T(8,128)(2,1)S(1)}, bf16[1,1,512,2048]{3,2,1,0:T(8,128)(2,1)}, u32[]{:S(2)}) copy-start(bf16[1,1,512,2048]{3,2,1,0:T(8,128)(2,1)} %param.10) | copy-start | bytes 6291460
Sparse Core Ops, SparseCore 0:
  21.9 80.7 all-gather.4
  149.7 30.5 all-gather.6

commit v10 on v5

--- a/solution.py
+++ b/solution.py
@@ -1,6 +1,8 @@
 import jax
 import jax.numpy as jnp
 from jax import lax
+from jax.experimental import pallas as pl
+from jax.experimental.pallas import tpu as pltpu
 from jax.sharding import PartitionSpec as P
 
 BLOCK = 256
@@ -10,6 +12,44 @@
     devices = range(lax.axis_size(axis))
     route = [(i - distance, i) for i in devices if i - distance in devices]
     return lax.ppermute(block, axis, route)
+
+
+def conv_kernel(x_ref, edge_ref, w_ref, b_ref, o_ref):
+    x = x_ref[...].astype(jnp.float32)
+    edge = edge_ref[...].astype(jnp.float32)
+    w = w_ref[...]
+    taps = w.shape[1]
+    lane = lax.broadcasted_iota(jnp.int32, x.shape, 1)
+    acc = jnp.broadcast_to(b_ref[...], x.shape)
+    for tap in range(taps):
+        lag = taps - 1 - tap
+        moved = x
+        if lag > 0:
+            moved = pltpu.roll(x, lag, 1)
+            for t in range(lag):
+                moved = jnp.where(lane == t, edge[:, taps - 1 - lag + t][:, None], moved)
+        acc = acc + w[:, tap][:, None] * moved
+    o_ref[...] = (acc * (1.0 / (1.0 + jnp.exp(-acc)))).astype(o_ref.dtype)
+
+
+def conv_silu(conv_t, edge_t, weight_t, bias_t, rows=256):
+    feats, slots = conv_t.shape
+    taps = weight_t.shape[1]
+    return pl.pallas_call(
+        conv_kernel,
+        grid=(feats // rows,),
+        in_specs=[
+            pl.BlockSpec((rows, slots), lambda i: (i, 0)),
+            pl.BlockSpec((rows, taps - 1), lambda i: (i, 0)),
+            pl.BlockSpec((rows, taps), lambda i: (i, 0)),
+            pl.BlockSpec((rows, 1), lambda i: (i, 0)),
+        ],
+        out_specs=pl.BlockSpec((rows, slots), lambda i: (i, 0)),
+        out_shape=jax.ShapeDtypeStruct((feats, slots), jnp.bfloat16),
+        cost_estimate=pl.CostEstimate(
+            flops=feats * slots * 14, transcendentals=feats * slots, bytes_accessed=feats * slots * 4
+        ),
+    )(conv_t, edge_t, weight_t, bias_t)
 
 
 def block_step(state, pieces):
@@ -69,13 +109,7 @@
     dt_raw = projected[:, inner + convdim :]
     edge_rows = lax.dynamic_slice_in_dim(conv_in, qlen - (taps - 1), taps - 1, 0)
     prev_edge = shifted(edge_rows, "seq", 1)
-    extended = jnp.concatenate([prev_edge, conv_in], axis=0)
-    accum = jnp.zeros((slots, convdim), jnp.float32) + conv_bias[None, :]
-    for tap_index in range(taps):
-        accum = accum + conv_weight[tap_index][None, :] * extended[
-            tap_index : tap_index + slots
-        ].astype(jnp.float32)
-    conv_act = jax.nn.silu(accum).astype(jnp.bfloat16)
+    conv_act = conv_silu(conv_in.T, prev_edge.T, conv_weight.T, conv_bias[:, None]).T
     inputs_x = conv_act[:, :inner]
     b_rows = conv_act[:, inner : inner + nstate]
     c_rows = conv_act[:, inner + nstate :]

time: 218 us -> 219 us (level)
  other arithmetic: 35.5 us -> 21.6 us
  Pallas kernels: 0 us -> 10.2 us
  local copies, waits for them, and re-layouts: 20 us -> 25.7 us
    convert_element_type x1 -> x0, other arithmetic: 10.5 us -> none  [local(): conv_act = jax.nn.silu(accum).astype(jnp.bfloat16)]
    pallas_call x0 -> x1, Pallas kernels: none -> 10.2 us  [conv_silu(): pl.pallas_call(conv_kernel, grid=(feats // rows,), in_specs=[pl.BlockSpec...]
    add x1 -> x0, other arithmetic: 3.73 us -> none  [local(): outputs.reshape(slots, heads, hdim) + incoming]
    unnamed x48 -> x57, local copies, waits for them, and re-layouts: 10.9 us -> 13.9 us
  transfers between devices with their start and end apart: 4 -> 4, of which waited for: 2 -> 2; matrix products, arithmetic and copies ran while one was open for 18% -> 17% of each run, Pallas kernels for 0% -> 0%
where the time goes in v10:
time: 219 us; the launch traced here: 218 us
  waiting for transfers between devices  91.3 us (42%)
  matrix products  29.5 us (13%)
  local copies, waits for them, and re-layouts  25.7 us (12%)
  other arithmetic  21.6 us (10%)
  between operations  15.9 us (7%)
  blocking collectives  12.8 us (6%)
  starting transfers between devices  11.1 us (5%)
  Pallas kernels  10.2 us (5%)
    all_gather x1, waiting for transfers between devices, local(): lax.all_gather(wide_rows, 'req', axis=0, tiled=True)  73.9 us
    all_gather x1, waiting for transfers between devices, local(): gathered = lax.all_gather(packed, 'seq', axis=0, tiled=False)  17.3 us
    dot_general x1, matrix products, local(): jnp.dot(tok_rows, lax.all_gather(wide_rows, 'req', axis=0, tiled=True), p...  15.3 us
    unnamed x57, local copies, waits for them, and re-layouts  13.9 us
    all_gather x1, blocking collectives, local(): wide_rows = lax.all_gather(w_in, 'seq', axis=1, tiled=True)  12.8 us
    pallas_call x1, Pallas kernels, conv_silu(): pl.pallas_call(conv_kernel, grid=(feats // rows,), in_specs=[pl.BlockSpec...  10.2 us
    dot_general x2, matrix products, block_step(): jnp.einsum('htu,uhp->thp', mixing, heads_x, preferred_element_type=jnp.fl...  8.76 us
    all_to_all x1, starting transfers between devices, local(): lax.all_to_all(share[None], 'req', split_axis=1, concat_axis=0, tiled=True)  7.77 us
  transfers between devices with their start and end apart: 4, of which 2 were waited for; matrix products, arithmetic and copies ran while one was open for 17% of the time, Pallas kernels for 0%

profile of v10, /device:TPU:1, one launch (start us, length us, event | category | flops | bytes accessed | tf_op | source)
XLA Modules:
  0.0 218.1 jit_solution(757172048434146206)
XLA Ops:
  7.3 12.8 %all-gather.1 = bf16[4,1096,64]{1,2,0:T(8,128)(2,1)S(1)} all-gather(bf16[1,1096,64]{1,2,0:T(8,128)(2,1)} %bitcast.211), channel_id=1, replica_groups=mesh['req'=32,'seq'=4] {'seq'}, dimensions={0}, use_global_device_ids=true | all-gather | bytes 701440 | tf_op jit(solution)/shard_map/all_gather | solution.py:101
  21.9 1.3 compare_select_fusion.1
  24.5 2.2 %copy.84 = f32[4,2304]{0,1:T(8,128)} copy(f32[4,2304]{1,0:T(4,128)} %param.12) | data formatting | bytes 73728 | tf_op args[2]
  26.7 1.4 broadcast_in_dim.163.b_ref
  28.8 73.9 %all-gather.5.cloned.1.call-done = bf16[2048,4384]{1,0:T(8,128)(2,1)} async-done(((bf16[64,4384]{1,0:T(8,128)(2,1)}), bf16[2048,4384]{1,0:T(8,128)(2,1)}) %all-gather.5.cloned.1.call-update) | async-done | bytes 17956880 | tf_op jit(solution)/shard_map/all_gather | solution.py:104
  102.8 15.3 %convolution_convert_fusion = bf16[512,4384]{0,1:T(8,128)(2,1)} fusion(bf16[2048,4384]{1,0:T(8,128)(2,1)} %all-gather.5.cloned.1.call-done, bf16[1,1,512,2048]{3,2,1,0:T(8,128)(2,1)S(1)} %copy-done), kind=kOutput, calls=%fused_computation.3 | convolution fusion | flops 9196158976 | bytes 24543232 | tf_op jit(solution)/shard_map/dot_general | solution.py:102
  118.1 3.4 %fusion.62 = (bf16[512,2304]{0,1:T(8,128)(2,1)S(1)}, bf16[2304,512]{1,0:T(8,128)(2,1)}) fusion(bf16[512,4384]{0,1:T(8,128)(2,1)} %convolution_convert_fusion), kind=kLoop, calls=%fused_computation.138 | loop fusion | bytes 7077888 | tf_op jit(solution)/shard_map/slice | solution.py:108
  126.2 3.3 %collective-permute-start = (bf16[3,2304]{1,0:T(4,128)(2,1)S(1)}, bf16[3,2304]{1,0:T(4,128)(2,1)S(1)}, u32[]{:S(2)}, u32[]{:S(2)}) collective-permute-start(bf16[3,2304]{1,0:T(4,128)(2,1)S(1)} %copy.82), channel_id=1, source_target_pairs={{0,1},{1,2},{2,3},{4,5},{5,6},{6,7},{8,9},{9,10},{10,11},{12,13},{... | collective-permute-start | bytes 41480 | tf_op jit(solution)/shard_map/ppermute | solution.py:14
  134.4 10.2 %shard_map.113 = bf16[2304,512]{1,0:T(8,128)(2,1)} custom-call(bf16[2304,512]{1,0:T(8,128)(2,1)} %get-tuple-element.21.x_ref, bf16[2304,3]{1,0:T(8,128)(2,1)} %bitcast.201, f32[2304,4]{1,0:T(8,128)} %bitcast.198, f32[2304,1]{1,0:T(8,128)} %broadcast_in_dim.163.b_ref), custom_call_target="tpu_custom_call" | custom-call | flops 16515072 | bytes 4718592 | tf_op jit(solution)/shard_map/pallas_call | solution.py:38
  144.5 2.1 fusion.20
  149.5 1.4 slice.195
  153.6 4.4 %bitcast_add_fusion.1 = f32[256,32,64]{0,2,1:T(8,128)} fusion(f32[256,32,64]{0,2,1:T(8,128)S(1)} %fusion.27, bf16[256,32,64]{0,2,1:T(8,128)(2,1)S(1)} %bitcast.209, f32[32,256]{1,0:T(8,128)S(1)} %copy-done.10, f32[32,256]{1,0:T(8,128)S(1)} %copy-done.6, f32[256,256]{1,0:T(8,128)S(1)} %fusion.43, pred[256,256]{1,0:T(8,128)(4,1)S(1)} %iota_compare_fusion, ...), kind=kOutput, calls=%fused_computation.36 | convolution fusion | flops 282066944 | bytes 5668864 | tf_op jit(solution)/shard_map/htu,uhp->thp/dot_general | solution.py:67
  158.0 4.3 %bitcast_add_fusion = f32[256,32,64]{0,2,1:T(8,128)} fusion(f32[256,32,64]{0,2,1:T(8,128)S(1)} %fusion.34, bf16[256,32,64]{0,2,1:T(8,128)(2,1)S(1)} %bitcast.208, f32[32,256]{1,0:T(8,128)S(1)} %copy-done.8, f32[32,256]{1,0:T(8,128)S(1)} %copy-done.7, f32[256,256]{1,0:T(8,128)S(1)} %fusion.38, pred[256,256]{1,0:T(8,128)(4,1)S(1)} %iota_compare_fusion, ...), kind=kOutput, calls=%fused_computation.35 | convolution fusion | flops 282066944 | bytes 5668864 | tf_op jit(solution)/shard_map/htu,uhp->thp/dot_general | solution.py:67
  162.4 17.3 %all-gather.7.cloned.1.call-done = bf16[128,8576]{1,0:T(8,128)(2,1)} async-done(((bf16[32,8576]{1,0:T(8,128)(2,1)}), bf16[128,8576]{1,0:T(8,128)(2,1)}) %all-gather.7.cloned.1.call-update) | async-done | bytes 2195472 | tf_op jit(solution)/shard_map/all_gather | solution.py:148
  179.7 2.0 slice_convert_fusion
  182.6 1.6 slice_bitcast_fusion.2
  186.0 7.8 %all-to-all-start = ((f32[1,32,16,128]{3,2,0,1:T(8,128)}), f32[1,32,16,128]{3,2,0,1:T(8,128)}, u32[]{:S(2)}, u32[]{:S(2)}) async-start(f32[1,32,16,128]{3,2,0,1:T(8,128)} %bitcast.207), calls=%async_computation | async-start | bytes 524288 | tf_op jit(solution)/shard_map/all_to_all | solution.py:173
  193.8 1.4 copy.118
  195.2 1.6 copy.119
  198.4 2.2 %fusion.6 = f32[512,32,64]{0,2,1:T(8,128)S(1)} fusion(f32[256,32,64]{0,2,1:T(8,128)S(1)} %copy-done.5, f32[256,32,64]{0,2,1:T(8,128)S(1)} %copy-done.4, bf16[512,32,64]{0,2,1:T(8,128)(2,1)S(1)} %bitcast.196, f32[32,64,128]{2,1,0:T(8,128)S(1)} %fusion.24, f32[32]{0:T(128)S(1)} %copy-done.15, f32[512,32]{0,1:T(8,128)S(1)} %fusion.56, ...), kind=kOutput, calls=%fused_computation.13 | convolution fusion | flops 1616904192 | bytes 11731456 | tf_op jit(solution)/shard_map/tn,hpn->thp/dot_general | solution.py:156
  200.7 1.4 multiply_reduce_fusion
  202.1 2.9 %fusion.19 = bf16[1,1,512,2048]{2,3,1,0:T(8,128)(2,1)} fusion(f32[2048]{0:T(1024)S(1)} %copy-done.13, f32[512]{0:T(512)S(1)} %add_rsqrt_fusion, pred[512]{0:T(512)(128)(4,1)S(1)} %iota_compare_fusion.2, bf16[512,4384]{0,1:T(8,128)(2,1)S(1)} %bitcast.195, f32[512,32,64]{0,2,1:T(8,128)S(1)} %fusion.6), kind=kLoop, calls=%fused_computation.29 | loop fusion | flops 10485760 | bytes 8399360 | tf_op jit(solution)/shard_map/reshape | solution.py:167
  205.0 3.9 %copy.98 = bf16[1,1,512,2048]{3,2,1,0:T(8,128)(2,1)} copy(bf16[1,1,512,2048]{2,3,1,0:T(8,128)(2,1)} %fusion.19) | data formatting | bytes 4194304
  208.9 1.5 gather_fusion
  (115 shorter events, 22.6 us)
Async XLA Ops:
  7.2 95.6 %copy-start = (bf16[1,1,512,2048]{3,2,1,0:T(8,128)(2,1)S(1)}, bf16[1,1,512,2048]{3,2,1,0:T(8,128)(2,1)}, u32[]{:S(2)}) copy-start(bf16[1,1,512,2048]{3,2,1,0:T(8,128)(2,1)} %param.10) | copy-start | bytes 6291460
  7.2 21.6 %copy-start.18 = (s32[32]{0:T(128)S(1)}, s32[32]{0:T(128)}, u32[]{:S(2)}) copy-start(s32[32]{0:T(128)} %param.19) | copy-start | bytes 388
  7.2 19.5 %copy-start.12 = (f32[2304]{0:T(1024)S(1)}, f32[2304]{0:T(1024)}, u32[]{:S(2)}) copy-start(f32[2304]{0:T(1024)} %param.13) | copy-start | bytes 27652
  7.2 21.6 %copy-start.20 = (f32[32]{0:T(128)S(1)}, f32[32]{0:T(128)}, u32[]{:S(2)}) copy-start(f32[32]{0:T(128)} %param.15) | copy-start | bytes 388
  7.2 95.5 %all-gather.5.cloned.1.call-start = ((), (), s32[]{:S(2)}) async-start(), calls=%async_computation.1 | async-start | bytes 18923520 | tf_op jit(solution)/shard_map/all_gather | solution.py:104
  21.8 157.8 %all-gather.7.cloned.1.call-start = ((), (), s32[]{:S(2)}) async-start(), calls=%async_computation.2 | async-start | bytes 2744320 | tf_op jit(solution)/shard_map/all_gather | solution.py:148
  118.1 3.4 %copy-start.14 = (f32[32]{0:T(128)S(1)}, f32[32]{0:T(128)}, u32[]{:S(2)}) copy-start(f32[32]{0:T(128)} %param.14) | copy-start | bytes 388
  126.2 7.0 %collective-permute-start = (bf16[3,2304]{1,0:T(4,128)(2,1)S(1)}, bf16[3,2304]{1,0:T(4,128)(2,1)S(1)}, u32[]{:S(2)}, u32[]{:S(2)}) collective-permute-start(bf16[3,2304]{1,0:T(4,128)(2,1)S(1)} %copy.82), channel_id=1, source_target_pairs={{0,1},{1,2},{2,3},{4,5},{5,6},{6,7},{8,9},{9,10},{10,11},{12,13},{... | collective-permute-start | bytes 41480 | tf_op jit(solution)/shard_map/ppermute | solution.py:14
  134.4 12.3 %copy-start.16 = (f32[32]{0:T(128)S(1)}, f32[32]{0:T(128)}, u32[]{:S(2)}) copy-start(f32[32]{0:T(128)} %exponential_multiply_fusion.2) | copy-start | bytes 388
  144.5 2.3 %copy-start.2 = (bf16[2304,512]{1,0:T(8,128)(2,1)S(1)}, bf16[2304,512]{1,0:T(8,128)(2,1)}, u32[]{:S(2)}) copy-start(bf16[2304,512]{1,0:T(8,128)(2,1)} %shard_map.113) | copy-start | bytes 7077892
  144.5 2.7 %copy-start.17 = (f32[32]{0:T(128)S(1)}, f32[32]{0:T(128)}, u32[]{:S(2)}) copy-start(f32[32]{0:T(128)} %exp.93) | copy-start | bytes 388
  152.4 1.2 copy-start.6
  153.6 4.5 %copy-start.7 = (f32[32,256]{1,0:T(8,128)S(1)}, f32[32,256]{1,0:T(8,128)}, u32[]{:S(2)}) copy-start(f32[32,256]{1,0:T(8,128)} %get-tuple-element.38) | copy-start | bytes 98308
  153.6 4.4 %copy-start.8 = (f32[32,256]{1,0:T(8,128)S(1)}, f32[32,256]{1,0:T(8,128)}, u32[]{:S(2)}) copy-start(f32[32,256]{1,0:T(8,128)} %get-tuple-element.30) | copy-start | bytes 98308
  153.6 4.4 %copy-start.9 = (f32[256,32]{0,1:T(8,128)S(1)}, f32[256,32]{0,1:T(8,128)}, u32[]{:S(2)}) copy-start(f32[256,32]{0,1:T(8,128)} %get-tuple-element.36) | copy-start | bytes 98308
  186.0 22.9 %all-to-all-start = ((f32[1,32,16,128]{3,2,0,1:T(8,128)}), f32[1,32,16,128]{3,2,0,1:T(8,128)}, u32[]{:S(2)}, u32[]{:S(2)}) async-start(f32[1,32,16,128]{3,2,0,1:T(8,128)} %bitcast.207), calls=%async_computation | async-start | bytes 524288 | tf_op jit(solution)/shard_map/all_to_all | solution.py:173
  195.2 2.7 %copy-start.3 = (bf16[512,2048]{0,1:T(8,128)(2,1)S(1)}, bf16[512,2048]{0,1:T(8,128)(2,1)}, u32[]{:S(2)}) copy-start(bf16[512,2048]{0,1:T(8,128)(2,1)} %slice.195) | copy-start | bytes 6291460
  195.2 2.7 %copy-start.4 = (f32[256,32,64]{0,2,1:T(8,128)S(1)}, f32[256,32,64]{0,2,1:T(8,128)}, u32[]{:S(2)}) copy-start(f32[256,32,64]{0,2,1:T(8,128)} %bitcast_add_fusion.1) | copy-start | bytes 6291460
  195.2 3.2 %copy-start.5 = (f32[256,32,64]{0,2,1:T(8,128)S(1)}, f32[256,32,64]{0,2,1:T(8,128)}, u32[]{:S(2)}) copy-start(f32[256,32,64]{0,2,1:T(8,128)} %bitcast_add_fusion) | copy-start | bytes 6291460
  195.2 3.2 %copy-start.15 = (f32[32]{0:T(128)S(1)}, f32[32]{0:T(128)}, u32[]{:S(2)}) copy-start(f32[32]{0:T(128)} %param.16) | copy-start | bytes 388
  197.2 3.5 %slice-start = ((s8[4489216]{0:T(1024)(128)(4,1)}), s8[4194304]{0:T(1024)(128)(4,1)S(1)}, s32[]{:S(2)}) async-start(s8[4489216]{0:T(1024)(128)(4,1)} %bitcast.194), calls=%async_computation.3 | async-start | bytes 8388608
  198.4 2.3 %slice-start.1 = ((s8[4489216]{0:T(1024)(128)(4,1)}), s8[294912]{0:T(1024)(128)(4,1)S(1)}, s32[]{:S(2)}) async-start(s8[4489216]{0:T(1024)(128)(4,1)} %bitcast.194), calls=%async_computation.4 | async-start | bytes 589824
  200.7 1.4 copy-start.13
  202.1 9.2 %copy-start.1 = (bf16[1,1,512,2048]{3,2,1,0:T(8,128)(2,1)S(1)}, bf16[1,1,512,2048]{3,2,1,0:T(8,128)(2,1)}, u32[]{:S(2)}) copy-start(bf16[1,1,512,2048]{3,2,1,0:T(8,128)(2,1)} %param.10) | copy-start | bytes 6291460
  (3 other events, 3.2 us)
Sparse Core Ops, SparseCore 0:
  22.0 80.7 all-gather.4
  149.1 30.5 all-gather.6

commit v11 on v10

--- a/solution.py
+++ b/solution.py
@@ -29,7 +29,7 @@
             for t in range(lag):
                 moved = jnp.where(lane == t, edge[:, taps - 1 - lag + t][:, None], moved)
         acc = acc + w[:, tap][:, None] * moved
-    o_ref[...] = (acc * (1.0 / (1.0 + jnp.exp(-acc)))).astype(o_ref.dtype)
+    o_ref[...] = (acc * (0.5 + 0.5 * jnp.tanh(0.5 * acc))).astype(o_ref.dtype)
 
 
 def conv_silu(conv_t, edge_t, weight_t, bias_t, rows=256):
@@ -161,7 +161,8 @@
         + incoming
         + d_skip[None, :, None] * inputs_x.astype(jnp.float32).reshape(slots, heads, hdim)
     )
-    gated = heads_y.reshape(slots, inner) * jax.nn.silu(gate_z.astype(jnp.float32))
+    gate = gate_z.astype(jnp.float32)
+    gated = heads_y.reshape(slots, inner) * (gate * (0.5 + 0.5 * jnp.tanh(0.5 * gate)))
     scale = lax.rsqrt(jnp.mean(gated * gated, axis=1, keepdims=True) + 1e-05)
     normed = jnp.where(filled[:, None], gated * scale * norm_weight[None, :], 0.0)
     gated_out = normed.astype(jnp.bfloat16).reshape(1, 1, slots, inner)

time: 219 us -> 219 us (level)
  no operation moved by 1% of the time
where the time goes in v11:
time: 219 us; the launch traced here: 218 us
  waiting for transfers between devices  91.3 us (42%)
  matrix products  29.5 us (13%)
  local copies, waits for them, and re-layouts  25.7 us (12%)
  other arithmetic  21.4 us (10%)
  between operations  15.9 us (7%)
  blocking collectives  12.8 us (6%)
  starting transfers between devices  11.1 us (5%)
  Pallas kernels  10.1 us (5%)
    all_gather x1, waiting for transfers between devices, local(): lax.all_gather(wide_rows, 'req', axis=0, tiled=True)  73.9 us
    all_gather x1, waiting for transfers between devices, local(): gathered = lax.all_gather(packed, 'seq', axis=0, tiled=False)  17.3 us
    dot_general x1, matrix products, local(): jnp.dot(tok_rows, lax.all_gather(wide_rows, 'req', axis=0, tiled=True), p...  15.3 us
    unnamed x57, local copies, waits for them, and re-layouts  13.9 us
    all_gather x1, blocking collectives, local(): wide_rows = lax.all_gather(w_in, 'seq', axis=1, tiled=True)  12.8 us
    pallas_call x1, Pallas kernels, conv_silu(): pl.pallas_call(conv_kernel, grid=(feats // rows,), in_specs=[pl.BlockSpec...  10.1 us
    dot_general x2, matrix products, block_step(): jnp.einsum('htu,uhp->thp', mixing, heads_x, preferred_element_type=jnp.fl...  8.76 us
    all_to_all x1, starting transfers between devices, local(): lax.all_to_all(share[None], 'req', split_axis=1, concat_axis=0, tiled=True)  7.77 us
  transfers between devices with their start and end apart: 4, of which 2 were waited for; matrix products, arithmetic and copies ran while one was open for 17% of the time, Pallas kernels for 0%

profile of v11, /device:TPU:1, one launch (start us, length us, event | category | flops | bytes accessed | tf_op | source)
XLA Modules:
  0.0 217.8 jit_solution(16590999386424380085)
XLA Ops:
  7.3 12.8 %all-gather.1 = bf16[4,1096,64]{1,2,0:T(8,128)(2,1)S(1)} all-gather(bf16[1,1096,64]{1,2,0:T(8,128)(2,1)} %bitcast.211), channel_id=1, replica_groups=mesh['req'=32,'seq'=4] {'seq'}, dimensions={0}, use_global_device_ids=true | all-gather | bytes 701440 | tf_op jit(solution)/shard_map/all_gather | solution.py:101
  20.6 1.3 reshape.357
  21.9 1.3 compare_select_fusion.1
  24.5 2.2 %copy.84 = f32[4,2304]{0,1:T(8,128)} copy(f32[4,2304]{1,0:T(4,128)} %param.12) | data formatting | bytes 73728 | tf_op args[2]
  26.7 1.4 broadcast_in_dim.163.b_ref
  28.8 73.9 %all-gather.5.cloned.1.call-done = bf16[2048,4384]{1,0:T(8,128)(2,1)} async-done(((bf16[64,4384]{1,0:T(8,128)(2,1)}), bf16[2048,4384]{1,0:T(8,128)(2,1)}) %all-gather.5.cloned.1.call-update) | async-done | bytes 17956880 | tf_op jit(solution)/shard_map/all_gather | solution.py:104
  102.8 15.3 %convolution_convert_fusion = bf16[512,4384]{0,1:T(8,128)(2,1)} fusion(bf16[2048,4384]{1,0:T(8,128)(2,1)} %all-gather.5.cloned.1.call-done, bf16[1,1,512,2048]{3,2,1,0:T(8,128)(2,1)S(1)} %copy-done), kind=kOutput, calls=%fused_computation.3 | convolution fusion | flops 9196158976 | bytes 24543232 | tf_op jit(solution)/shard_map/dot_general | solution.py:102
  118.1 3.4 %fusion.62 = (bf16[512,2304]{0,1:T(8,128)(2,1)S(1)}, bf16[2304,512]{1,0:T(8,128)(2,1)}) fusion(bf16[512,4384]{0,1:T(8,128)(2,1)} %convolution_convert_fusion), kind=kLoop, calls=%fused_computation.138 | loop fusion | bytes 7077888 | tf_op jit(solution)/shard_map/slice | solution.py:108
  126.2 3.3 %collective-permute-start = (bf16[3,2304]{1,0:T(4,128)(2,1)S(1)}, bf16[3,2304]{1,0:T(4,128)(2,1)S(1)}, u32[]{:S(2)}, u32[]{:S(2)}) collective-permute-start(bf16[3,2304]{1,0:T(4,128)(2,1)S(1)} %copy.82), channel_id=1, source_target_pairs={{0,1},{1,2},{2,3},{4,5},{5,6},{6,7},{8,9},{9,10},{10,11},{12,13},{... | collective-permute-start | bytes 41480 | tf_op jit(solution)/shard_map/ppermute | solution.py:14
  134.4 10.1 %shard_map.113 = bf16[2304,512]{1,0:T(8,128)(2,1)} custom-call(bf16[2304,512]{1,0:T(8,128)(2,1)} %get-tuple-element.21.x_ref, bf16[2304,3]{1,0:T(8,128)(2,1)} %bitcast.201, f32[2304,4]{1,0:T(8,128)} %bitcast.198, f32[2304,1]{1,0:T(8,128)} %broadcast_in_dim.163.b_ref), custom_call_target="tpu_custom_call" | custom-call | flops 16515072 | bytes 4718592 | tf_op jit(solution)/shard_map/pallas_call | solution.py:38
  144.4 2.1 fusion.20
  149.5 1.4 slice.195
  153.5 4.4 %bitcast_add_fusion.1 = f32[256,32,64]{0,2,1:T(8,128)} fusion(f32[256,32,64]{0,2,1:T(8,128)S(1)} %fusion.27, bf16[256,32,64]{0,2,1:T(8,128)(2,1)S(1)} %bitcast.209, f32[32,256]{1,0:T(8,128)S(1)} %copy-done.10, f32[32,256]{1,0:T(8,128)S(1)} %copy-done.6, f32[256,256]{1,0:T(8,128)S(1)} %fusion.43, pred[256,256]{1,0:T(8,128)(4,1)S(1)} %iota_compare_fusion, ...), kind=kOutput, calls=%fused_computation.36 | convolution fusion | flops 282066944 | bytes 5668864 | tf_op jit(solution)/shard_map/htu,uhp->thp/dot_general | solution.py:67
  157.9 4.3 %bitcast_add_fusion = f32[256,32,64]{0,2,1:T(8,128)} fusion(f32[256,32,64]{0,2,1:T(8,128)S(1)} %fusion.34, bf16[256,32,64]{0,2,1:T(8,128)(2,1)S(1)} %bitcast.208, f32[32,256]{1,0:T(8,128)S(1)} %copy-done.8, f32[32,256]{1,0:T(8,128)S(1)} %copy-done.7, f32[256,256]{1,0:T(8,128)S(1)} %fusion.38, pred[256,256]{1,0:T(8,128)(4,1)S(1)} %iota_compare_fusion, ...), kind=kOutput, calls=%fused_computation.35 | convolution fusion | flops 282066944 | bytes 5668864 | tf_op jit(solution)/shard_map/htu,uhp->thp/dot_general | solution.py:67
  162.3 17.3 %all-gather.7.cloned.1.call-done = bf16[128,8576]{1,0:T(8,128)(2,1)} async-done(((bf16[32,8576]{1,0:T(8,128)(2,1)}), bf16[128,8576]{1,0:T(8,128)(2,1)}) %all-gather.7.cloned.1.call-update) | async-done | bytes 2195472 | tf_op jit(solution)/shard_map/all_gather | solution.py:148
  179.6 2.0 slice_convert_fusion
  182.5 1.6 slice_bitcast_fusion.2
  185.9 7.8 %all-to-all-start = ((f32[1,32,16,128]{3,2,0,1:T(8,128)}), f32[1,32,16,128]{3,2,0,1:T(8,128)}, u32[]{:S(2)}, u32[]{:S(2)}) async-start(f32[1,32,16,128]{3,2,0,1:T(8,128)} %bitcast.207), calls=%async_computation | async-start | bytes 524288 | tf_op jit(solution)/shard_map/all_to_all | solution.py:174
  193.7 1.4 copy.118
  195.2 1.6 copy.119
  198.3 2.2 %fusion.6 = f32[512,32,64]{0,2,1:T(8,128)S(1)} fusion(f32[256,32,64]{0,2,1:T(8,128)S(1)} %copy-done.5, f32[256,32,64]{0,2,1:T(8,128)S(1)} %copy-done.4, bf16[512,32,64]{0,2,1:T(8,128)(2,1)S(1)} %bitcast.196, f32[32,64,128]{2,1,0:T(8,128)S(1)} %fusion.24, f32[32]{0:T(128)S(1)} %copy-done.15, f32[512,32]{0,1:T(8,128)S(1)} %fusion.56, ...), kind=kOutput, calls=%fused_computation.13 | convolution fusion | flops 1616904192 | bytes 11731456 | tf_op jit(solution)/shard_map/tn,hpn->thp/dot_general | solution.py:156
  201.8 2.8 %fusion.19 = bf16[1,1,512,2048]{2,3,1,0:T(8,128)(2,1)} fusion(f32[2048]{0:T(1024)S(1)} %copy-done.13, f32[512]{0:T(512)S(1)} %add_rsqrt_fusion, pred[512]{0:T(512)(128)(4,1)S(1)} %iota_compare_fusion.2, bf16[512,4384]{0,1:T(8,128)(2,1)S(1)} %bitcast.195, f32[512,32,64]{0,2,1:T(8,128)S(1)} %fusion.6), kind=kLoop, calls=%fused_computation.29 | loop fusion | flops 10485760 | bytes 8399360 | tf_op jit(solution)/shard_map/reshape | solution.py:168
  204.7 3.9 %copy.98 = bf16[1,1,512,2048]{3,2,1,0:T(8,128)(2,1)} copy(bf16[1,1,512,2048]{2,3,1,0:T(8,128)(2,1)} %fusion.19) | data formatting | bytes 4194304
  208.6 1.5 gather_fusion
  (115 shorter events, 22.6 us)
Async XLA Ops:
  7.2 95.6 %copy-start = (bf16[1,1,512,2048]{3,2,1,0:T(8,128)(2,1)S(1)}, bf16[1,1,512,2048]{3,2,1,0:T(8,128)(2,1)}, u32[]{:S(2)}) copy-start(bf16[1,1,512,2048]{3,2,1,0:T(8,128)(2,1)} %param.10) | copy-start | bytes 6291460
  7.2 21.6 %copy-start.18 = (s32[32]{0:T(128)S(1)}, s32[32]{0:T(128)}, u32[]{:S(2)}) copy-start(s32[32]{0:T(128)} %param.19) | copy-start | bytes 388
  7.2 19.5 %copy-start.12 = (f32[2304]{0:T(1024)S(1)}, f32[2304]{0:T(1024)}, u32[]{:S(2)}) copy-start(f32[2304]{0:T(1024)} %param.13) | copy-start | bytes 27652
  7.2 21.6 %copy-start.20 = (f32[32]{0:T(128)S(1)}, f32[32]{0:T(128)}, u32[]{:S(2)}) copy-start(f32[32]{0:T(128)} %param.15) | copy-start | bytes 388
  7.2 95.5 %all-gather.5.cloned.1.call-start = ((), (), s32[]{:S(2)}) async-start(), calls=%async_computation.1 | async-start | bytes 18923520 | tf_op jit(solution)/shard_map/all_gather | solution.py:104
  21.8 157.7 %all-gather.7.cloned.1.call-start = ((), (), s32[]{:S(2)}) async-start(), calls=%async_computation.2 | async-start | bytes 2744320 | tf_op jit(solution)/shard_map/all_gather | solution.py:148
  118.1 3.4 %copy-start.14 = (f32[32]{0:T(128)S(1)}, f32[32]{0:T(128)}, u32[]{:S(2)}) copy-start(f32[32]{0:T(128)} %param.14) | copy-start | bytes 388
  126.2 7.0 %collective-permute-start = (bf16[3,2304]{1,0:T(4,128)(2,1)S(1)}, bf16[3,2304]{1,0:T(4,128)(2,1)S(1)}, u32[]{:S(2)}, u32[]{:S(2)}) collective-permute-start(bf16[3,2304]{1,0:T(4,128)(2,1)S(1)} %copy.82), channel_id=1, source_target_pairs={{0,1},{1,2},{2,3},{4,5},{5,6},{6,7},{8,9},{9,10},{10,11},{12,13},{... | collective-permute-start | bytes 41480 | tf_op jit(solution)/shard_map/ppermute | solution.py:14
  134.4 12.2 %copy-start.16 = (f32[32]{0:T(128)S(1)}, f32[32]{0:T(128)}, u32[]{:S(2)}) copy-start(f32[32]{0:T(128)} %exponential_multiply_fusion.2) | copy-start | bytes 388
  144.4 2.3 %copy-start.2 = (bf16[2304,512]{1,0:T(8,128)(2,1)S(1)}, bf16[2304,512]{1,0:T(8,128)(2,1)}, u32[]{:S(2)}) copy-start(bf16[2304,512]{1,0:T(8,128)(2,1)} %shard_map.113) | copy-start | bytes 7077892
  144.4 2.7 %copy-start.17 = (f32[32]{0:T(128)S(1)}, f32[32]{0:T(128)}, u32[]{:S(2)}) copy-start(f32[32]{0:T(128)} %exp.89) | copy-start | bytes 388
  152.3 1.2 copy-start.6
  153.5 4.5 %copy-start.7 = (f32[32,256]{1,0:T(8,128)S(1)}, f32[32,256]{1,0:T(8,128)}, u32[]{:S(2)}) copy-start(f32[32,256]{1,0:T(8,128)} %get-tuple-element.38) | copy-start | bytes 98308
  153.5 4.4 %copy-start.8 = (f32[32,256]{1,0:T(8,128)S(1)}, f32[32,256]{1,0:T(8,128)}, u32[]{:S(2)}) copy-start(f32[32,256]{1,0:T(8,128)} %get-tuple-element.30) | copy-start | bytes 98308
  153.5 4.4 %copy-start.9 = (f32[256,32]{0,1:T(8,128)S(1)}, f32[256,32]{0,1:T(8,128)}, u32[]{:S(2)}) copy-start(f32[256,32]{0,1:T(8,128)} %get-tuple-element.36) | copy-start | bytes 98308
  185.9 22.7 %all-to-all-start = ((f32[1,32,16,128]{3,2,0,1:T(8,128)}), f32[1,32,16,128]{3,2,0,1:T(8,128)}, u32[]{:S(2)}, u32[]{:S(2)}) async-start(f32[1,32,16,128]{3,2,0,1:T(8,128)} %bitcast.207), calls=%async_computation | async-start | bytes 524288 | tf_op jit(solution)/shard_map/all_to_all | solution.py:174
  195.1 2.7 %copy-start.3 = (bf16[512,2048]{0,1:T(8,128)(2,1)S(1)}, bf16[512,2048]{0,1:T(8,128)(2,1)}, u32[]{:S(2)}) copy-start(bf16[512,2048]{0,1:T(8,128)(2,1)} %slice.195) | copy-start | bytes 6291460
  195.1 2.7 %copy-start.4 = (f32[256,32,64]{0,2,1:T(8,128)S(1)}, f32[256,32,64]{0,2,1:T(8,128)}, u32[]{:S(2)}) copy-start(f32[256,32,64]{0,2,1:T(8,128)} %bitcast_add_fusion.1) | copy-start | bytes 6291460
  195.1 3.2 %copy-start.5 = (f32[256,32,64]{0,2,1:T(8,128)S(1)}, f32[256,32,64]{0,2,1:T(8,128)}, u32[]{:S(2)}) copy-start(f32[256,32,64]{0,2,1:T(8,128)} %bitcast_add_fusion) | copy-start | bytes 6291460
  195.1 3.2 %copy-start.15 = (f32[32]{0:T(128)S(1)}, f32[32]{0:T(128)}, u32[]{:S(2)}) copy-start(f32[32]{0:T(128)} %param.16) | copy-start | bytes 388
  197.1 3.5 %slice-start = ((s8[4489216]{0:T(1024)(128)(4,1)}), s8[4194304]{0:T(1024)(128)(4,1)S(1)}, s32[]{:S(2)}) async-start(s8[4489216]{0:T(1024)(128)(4,1)} %bitcast.194), calls=%async_computation.3 | async-start | bytes 8388608
  198.3 2.3 %slice-start.1 = ((s8[4489216]{0:T(1024)(128)(4,1)}), s8[294912]{0:T(1024)(128)(4,1)S(1)}, s32[]{:S(2)}) async-start(s8[4489216]{0:T(1024)(128)(4,1)} %bitcast.194), calls=%async_computation.4 | async-start | bytes 589824
  200.6 1.3 copy-start.13
  201.8 9.1 %copy-start.1 = (bf16[1,1,512,2048]{3,2,1,0:T(8,128)(2,1)S(1)}, bf16[1,1,512,2048]{3,2,1,0:T(8,128)(2,1)}, u32[]{:S(2)}) copy-start(bf16[1,1,512,2048]{3,2,1,0:T(8,128)(2,1)} %param.10) | copy-start | bytes 6291460
  (3 other events, 3.2 us)
Sparse Core Ops, SparseCore 0:
  22.0 80.7 all-gather.4
  149.0 30.5 all-gather.6

commit v12 on v11

--- a/solution.py
+++ b/solution.py
@@ -18,21 +18,25 @@
     x = x_ref[...].astype(jnp.float32)
     edge = edge_ref[...].astype(jnp.float32)
     w = w_ref[...]
+    b = b_ref[...]
     taps = w.shape[1]
-    lane = lax.broadcasted_iota(jnp.int32, x.shape, 1)
-    acc = jnp.broadcast_to(b_ref[...], x.shape)
-    for tap in range(taps):
+    acc = b + w[:, taps - 1 : taps] * x
+    for tap in range(taps - 1):
+        acc = acc + w[:, tap : tap + 1] * pltpu.roll(x, taps - 1 - tap, 1)
+    o_ref[...] = (acc * (0.5 + 0.5 * jnp.tanh(0.5 * acc))).astype(o_ref.dtype)
+    head = x[:, :128]
+    lane = lax.broadcasted_iota(jnp.int32, head.shape, 1)
+    first = b + w[:, taps - 1 : taps] * head
+    for tap in range(taps - 1):
         lag = taps - 1 - tap
-        moved = x
-        if lag > 0:
-            moved = pltpu.roll(x, lag, 1)
-            for t in range(lag):
-                moved = jnp.where(lane == t, edge[:, taps - 1 - lag + t][:, None], moved)
-        acc = acc + w[:, tap][:, None] * moved
-    o_ref[...] = (acc * (0.5 + 0.5 * jnp.tanh(0.5 * acc))).astype(o_ref.dtype)
+        moved = pltpu.roll(head, lag, 1)
+        for t in range(lag):
+            moved = jnp.where(lane == t, edge[:, tap + t : tap + t + 1], moved)
+        first = first + w[:, tap : tap + 1] * moved
+    o_ref[:, :128] = (first * (0.5 + 0.5 * jnp.tanh(0.5 * first))).astype(o_ref.dtype)
 
 
-def conv_silu(conv_t, edge_t, weight_t, bias_t, rows=256):
+def conv_silu(conv_t, edge_t, weight_t, bias_t, rows=768):
     feats, slots = conv_t.shape
     taps = weight_t.shape[1]
     return pl.pallas_call(

time: 219 us -> 218 us (level)
  no operation moved by 1% of the time
where the time goes in v12:
time: 218 us; the launch traced here: 217 us
  waiting for transfers between devices  91.3 us (42%)
  matrix products  29.5 us (14%)
  local copies, waits for them, and re-layouts  25.7 us (12%)
  other arithmetic  21.4 us (10%)
  between operations  15.9 us (7%)
  blocking collectives  12.8 us (6%)
  starting transfers between devices  11.1 us (5%)
  Pallas kernels  9.19 us (4%)
    all_gather x1, waiting for transfers between devices, local(): lax.all_gather(wide_rows, 'req', axis=0, tiled=True)  73.9 us
    all_gather x1, waiting for transfers between devices, local(): gathered = lax.all_gather(packed, 'seq', axis=0, tiled=False)  17.3 us
    dot_general x1, matrix products, local(): jnp.dot(tok_rows, lax.all_gather(wide_rows, 'req', axis=0, tiled=True), p...  15.3 us
    unnamed x57, local copies, waits for them, and re-layouts  13.9 us
    all_gather x1, blocking collectives, local(): wide_rows = lax.all_gather(w_in, 'seq', axis=1, tiled=True)  12.8 us
    pallas_call x1, Pallas kernels, conv_silu(): pl.pallas_call(conv_kernel, grid=(feats // rows,), in_specs=[pl.BlockSpec...  9.19 us
    dot_general x2, matrix products, block_step(): jnp.einsum('htu,uhp->thp', mixing, heads_x, preferred_element_type=jnp.fl...  8.76 us
    all_to_all x1, starting transfers between devices, local(): lax.all_to_all(share[None], 'req', split_axis=1, concat_axis=0, tiled=True)  7.77 us
  transfers between devices with their start and end apart: 4, of which 2 were waited for; matrix products, arithmetic and copies ran while one was open for 17% of the time, Pallas kernels for 0%

profile of v12, /device:TPU:1, one launch (start us, length us, event | category | flops | bytes accessed | tf_op | source)
XLA Modules:
  0.0 216.9 jit_solution(12757663741536623835)
XLA Ops:
  7.3 12.8 %all-gather.1 = bf16[4,1096,64]{1,2,0:T(8,128)(2,1)S(1)} all-gather(bf16[1,1096,64]{1,2,0:T(8,128)(2,1)} %bitcast.211), channel_id=1, replica_groups=mesh['req'=32,'seq'=4] {'seq'}, dimensions={0}, use_global_device_ids=true | all-gather | bytes 701440 | tf_op jit(solution)/shard_map/all_gather | solution.py:105
  20.6 1.3 reshape.357
  21.9 1.3 compare_select_fusion.1
  24.5 2.2 %copy.84 = f32[4,2304]{0,1:T(8,128)} copy(f32[4,2304]{1,0:T(4,128)} %param.12) | data formatting | bytes 73728 | tf_op args[2]
  26.7 1.4 broadcast_in_dim.163.b_ref
  28.8 73.9 %all-gather.5.cloned.1.call-done = bf16[2048,4384]{1,0:T(8,128)(2,1)} async-done(((bf16[64,4384]{1,0:T(8,128)(2,1)}), bf16[2048,4384]{1,0:T(8,128)(2,1)}) %all-gather.5.cloned.1.call-update) | async-done | bytes 17956880 | tf_op jit(solution)/shard_map/all_gather | solution.py:108
  102.8 15.3 %convolution_convert_fusion = bf16[512,4384]{0,1:T(8,128)(2,1)} fusion(bf16[2048,4384]{1,0:T(8,128)(2,1)} %all-gather.5.cloned.1.call-done, bf16[1,1,512,2048]{3,2,1,0:T(8,128)(2,1)S(1)} %copy-done), kind=kOutput, calls=%fused_computation.3 | convolution fusion | flops 9196158976 | bytes 24543232 | tf_op jit(solution)/shard_map/dot_general | solution.py:106
  118.1 3.4 %fusion.62 = (bf16[512,2304]{0,1:T(8,128)(2,1)S(1)}, bf16[2304,512]{1,0:T(8,128)(2,1)}) fusion(bf16[512,4384]{0,1:T(8,128)(2,1)} %convolution_convert_fusion), kind=kLoop, calls=%fused_computation.138 | loop fusion | bytes 7077888 | tf_op jit(solution)/shard_map/slice | solution.py:112
  126.2 3.3 %collective-permute-start = (bf16[3,2304]{1,0:T(4,128)(2,1)S(1)}, bf16[3,2304]{1,0:T(4,128)(2,1)S(1)}, u32[]{:S(2)}, u32[]{:S(2)}) collective-permute-start(bf16[3,2304]{1,0:T(4,128)(2,1)S(1)} %copy.82), channel_id=1, source_target_pairs={{0,1},{1,2},{2,3},{4,5},{5,6},{6,7},{8,9},{9,10},{10,11},{12,13},{... | collective-permute-start | bytes 41480 | tf_op jit(solution)/shard_map/ppermute | solution.py:14
  134.4 9.2 %shard_map.113 = bf16[2304,512]{1,0:T(8,128)(2,1)} custom-call(bf16[2304,512]{1,0:T(8,128)(2,1)} %get-tuple-element.21.x_ref, bf16[2304,3]{1,0:T(8,128)(2,1)} %bitcast.201, f32[2304,4]{1,0:T(8,128)} %bitcast.198, f32[2304,1]{1,0:T(8,128)} %broadcast_in_dim.163.b_ref), custom_call_target="tpu_custom_call" | custom-call | flops 16515072 | bytes 4718592 | tf_op jit(solution)/shard_map/pallas_call | solution.py:42
  143.6 2.1 fusion.20
  148.6 1.4 slice.195
  152.6 4.4 %bitcast_add_fusion.1 = f32[256,32,64]{0,2,1:T(8,128)} fusion(f32[256,32,64]{0,2,1:T(8,128)S(1)} %fusion.27, bf16[256,32,64]{0,2,1:T(8,128)(2,1)S(1)} %bitcast.209, f32[32,256]{1,0:T(8,128)S(1)} %copy-done.10, f32[32,256]{1,0:T(8,128)S(1)} %copy-done.6, f32[256,256]{1,0:T(8,128)S(1)} %fusion.43, pred[256,256]{1,0:T(8,128)(4,1)S(1)} %iota_compare_fusion, ...), kind=kOutput, calls=%fused_computation.36 | convolution fusion | flops 282066944 | bytes 5668864 | tf_op jit(solution)/shard_map/htu,uhp->thp/dot_general | solution.py:71
  157.1 4.3 %bitcast_add_fusion = f32[256,32,64]{0,2,1:T(8,128)} fusion(f32[256,32,64]{0,2,1:T(8,128)S(1)} %fusion.34, bf16[256,32,64]{0,2,1:T(8,128)(2,1)S(1)} %bitcast.208, f32[32,256]{1,0:T(8,128)S(1)} %copy-done.8, f32[32,256]{1,0:T(8,128)S(1)} %copy-done.7, f32[256,256]{1,0:T(8,128)S(1)} %fusion.38, pred[256,256]{1,0:T(8,128)(4,1)S(1)} %iota_compare_fusion, ...), kind=kOutput, calls=%fused_computation.35 | convolution fusion | flops 282066944 | bytes 5668864 | tf_op jit(solution)/shard_map/htu,uhp->thp/dot_general | solution.py:71
  161.4 17.3 %all-gather.7.cloned.1.call-done = bf16[128,8576]{1,0:T(8,128)(2,1)} async-done(((bf16[32,8576]{1,0:T(8,128)(2,1)}), bf16[128,8576]{1,0:T(8,128)(2,1)}) %all-gather.7.cloned.1.call-update) | async-done | bytes 2195472 | tf_op jit(solution)/shard_map/all_gather | solution.py:152
  178.7 2.0 slice_convert_fusion
  181.6 1.6 slice_bitcast_fusion.2
  185.1 7.8 %all-to-all-start = ((f32[1,32,16,128]{3,2,0,1:T(8,128)}), f32[1,32,16,128]{3,2,0,1:T(8,128)}, u32[]{:S(2)}, u32[]{:S(2)}) async-start(f32[1,32,16,128]{3,2,0,1:T(8,128)} %bitcast.207), calls=%async_computation | async-start | bytes 524288 | tf_op jit(solution)/shard_map/all_to_all | solution.py:178
  192.8 1.4 copy.118
  194.3 1.6 copy.119
  197.4 2.2 %fusion.6 = f32[512,32,64]{0,2,1:T(8,128)S(1)} fusion(f32[256,32,64]{0,2,1:T(8,128)S(1)} %copy-done.5, f32[256,32,64]{0,2,1:T(8,128)S(1)} %copy-done.4, bf16[512,32,64]{0,2,1:T(8,128)(2,1)S(1)} %bitcast.196, f32[32,64,128]{2,1,0:T(8,128)S(1)} %fusion.24, f32[32]{0:T(128)S(1)} %copy-done.15, f32[512,32]{0,1:T(8,128)S(1)} %fusion.56, ...), kind=kOutput, calls=%fused_computation.13 | convolution fusion | flops 1616904192 | bytes 11731456 | tf_op jit(solution)/shard_map/tn,hpn->thp/dot_general | solution.py:160
  201.0 2.8 %fusion.19 = bf16[1,1,512,2048]{2,3,1,0:T(8,128)(2,1)} fusion(f32[2048]{0:T(1024)S(1)} %copy-done.13, f32[512]{0:T(512)S(1)} %add_rsqrt_fusion, pred[512]{0:T(512)(128)(4,1)S(1)} %iota_compare_fusion.2, bf16[512,4384]{0,1:T(8,128)(2,1)S(1)} %bitcast.195, f32[512,32,64]{0,2,1:T(8,128)S(1)} %fusion.6), kind=kLoop, calls=%fused_computation.29 | loop fusion | flops 10485760 | bytes 8399360 | tf_op jit(solution)/shard_map/reshape | solution.py:172
  203.8 3.9 %copy.98 = bf16[1,1,512,2048]{3,2,1,0:T(8,128)(2,1)} copy(bf16[1,1,512,2048]{2,3,1,0:T(8,128)(2,1)} %fusion.19) | data formatting | bytes 4194304
  207.7 1.5 gather_fusion
  (115 shorter events, 22.6 us)
Async XLA Ops:
  7.2 95.6 %copy-start = (bf16[1,1,512,2048]{3,2,1,0:T(8,128)(2,1)S(1)}, bf16[1,1,512,2048]{3,2,1,0:T(8,128)(2,1)}, u32[]{:S(2)}) copy-start(bf16[1,1,512,2048]{3,2,1,0:T(8,128)(2,1)} %param.10) | copy-start | bytes 6291460
  7.2 21.6 %copy-start.18 = (s32[32]{0:T(128)S(1)}, s32[32]{0:T(128)}, u32[]{:S(2)}) copy-start(s32[32]{0:T(128)} %param.19) | copy-start | bytes 388
  7.2 19.5 %copy-start.12 = (f32[2304]{0:T(1024)S(1)}, f32[2304]{0:T(1024)}, u32[]{:S(2)}) copy-start(f32[2304]{0:T(1024)} %param.13) | copy-start | bytes 27652
  7.2 21.6 %copy-start.20 = (f32[32]{0:T(128)S(1)}, f32[32]{0:T(128)}, u32[]{:S(2)}) copy-start(f32[32]{0:T(128)} %param.15) | copy-start | bytes 388
  7.2 95.5 %all-gather.5.cloned.1.call-start = ((), (), s32[]{:S(2)}) async-start(), calls=%async_computation.1 | async-start | bytes 18923520 | tf_op jit(solution)/shard_map/all_gather | solution.py:108
  21.8 156.9 %all-gather.7.cloned.1.call-start = ((), (), s32[]{:S(2)}) async-start(), calls=%async_computation.2 | async-start | bytes 2744320 | tf_op jit(solution)/shard_map/all_gather | solution.py:152
  118.1 3.4 %copy-start.14 = (f32[32]{0:T(128)S(1)}, f32[32]{0:T(128)}, u32[]{:S(2)}) copy-start(f32[32]{0:T(128)} %param.14) | copy-start | bytes 388
  126.2 7.0 %collective-permute-start = (bf16[3,2304]{1,0:T(4,128)(2,1)S(1)}, bf16[3,2304]{1,0:T(4,128)(2,1)S(1)}, u32[]{:S(2)}, u32[]{:S(2)}) collective-permute-start(bf16[3,2304]{1,0:T(4,128)(2,1)S(1)} %copy.82), channel_id=1, source_target_pairs={{0,1},{1,2},{2,3},{4,5},{5,6},{6,7},{8,9},{9,10},{10,11},{12,13},{... | collective-permute-start | bytes 41480 | tf_op jit(solution)/shard_map/ppermute | solution.py:14
  134.4 11.3 %copy-start.16 = (f32[32]{0:T(128)S(1)}, f32[32]{0:T(128)}, u32[]{:S(2)}) copy-start(f32[32]{0:T(128)} %exponential_multiply_fusion.2) | copy-start | bytes 388
  143.6 2.3 %copy-start.2 = (bf16[2304,512]{1,0:T(8,128)(2,1)S(1)}, bf16[2304,512]{1,0:T(8,128)(2,1)}, u32[]{:S(2)}) copy-start(bf16[2304,512]{1,0:T(8,128)(2,1)} %shard_map.113) | copy-start | bytes 7077892
  143.6 2.7 %copy-start.17 = (f32[32]{0:T(128)S(1)}, f32[32]{0:T(128)}, u32[]{:S(2)}) copy-start(f32[32]{0:T(128)} %exp.89) | copy-start | bytes 388
  151.4 1.2 copy-start.6
  152.6 4.5 %copy-start.7 = (f32[32,256]{1,0:T(8,128)S(1)}, f32[32,256]{1,0:T(8,128)}, u32[]{:S(2)}) copy-start(f32[32,256]{1,0:T(8,128)} %get-tuple-element.38) | copy-start | bytes 98308
  152.6 4.4 %copy-start.8 = (f32[32,256]{1,0:T(8,128)S(1)}, f32[32,256]{1,0:T(8,128)}, u32[]{:S(2)}) copy-start(f32[32,256]{1,0:T(8,128)} %get-tuple-element.30) | copy-start | bytes 98308
  152.6 4.4 %copy-start.9 = (f32[256,32]{0,1:T(8,128)S(1)}, f32[256,32]{0,1:T(8,128)}, u32[]{:S(2)}) copy-start(f32[256,32]{0,1:T(8,128)} %get-tuple-element.36) | copy-start | bytes 98308
  185.1 22.7 %all-to-all-start = ((f32[1,32,16,128]{3,2,0,1:T(8,128)}), f32[1,32,16,128]{3,2,0,1:T(8,128)}, u32[]{:S(2)}, u32[]{:S(2)}) async-start(f32[1,32,16,128]{3,2,0,1:T(8,128)} %bitcast.207), calls=%async_computation | async-start | bytes 524288 | tf_op jit(solution)/shard_map/all_to_all | solution.py:178
  194.2 2.7 %copy-start.3 = (bf16[512,2048]{0,1:T(8,128)(2,1)S(1)}, bf16[512,2048]{0,1:T(8,128)(2,1)}, u32[]{:S(2)}) copy-start(bf16[512,2048]{0,1:T(8,128)(2,1)} %slice.195) | copy-start | bytes 6291460
  194.3 2.7 %copy-start.4 = (f32[256,32,64]{0,2,1:T(8,128)S(1)}, f32[256,32,64]{0,2,1:T(8,128)}, u32[]{:S(2)}) copy-start(f32[256,32,64]{0,2,1:T(8,128)} %bitcast_add_fusion.1) | copy-start | bytes 6291460
  194.3 3.2 %copy-start.5 = (f32[256,32,64]{0,2,1:T(8,128)S(1)}, f32[256,32,64]{0,2,1:T(8,128)}, u32[]{:S(2)}) copy-start(f32[256,32,64]{0,2,1:T(8,128)} %bitcast_add_fusion) | copy-start | bytes 6291460
  194.3 3.2 %copy-start.15 = (f32[32]{0:T(128)S(1)}, f32[32]{0:T(128)}, u32[]{:S(2)}) copy-start(f32[32]{0:T(128)} %param.16) | copy-start | bytes 388
  196.2 3.5 %slice-start = ((s8[4489216]{0:T(1024)(128)(4,1)}), s8[4194304]{0:T(1024)(128)(4,1)S(1)}, s32[]{:S(2)}) async-start(s8[4489216]{0:T(1024)(128)(4,1)} %bitcast.194), calls=%async_computation.3 | async-start | bytes 8388608
  197.4 2.3 %slice-start.1 = ((s8[4489216]{0:T(1024)(128)(4,1)}), s8[294912]{0:T(1024)(128)(4,1)S(1)}, s32[]{:S(2)}) async-start(s8[4489216]{0:T(1024)(128)(4,1)} %bitcast.194), calls=%async_computation.4 | async-start | bytes 589824
  199.7 1.3 copy-start.13
  201.0 9.1 %copy-start.1 = (bf16[1,1,512,2048]{3,2,1,0:T(8,128)(2,1)S(1)}, bf16[1,1,512,2048]{3,2,1,0:T(8,128)(2,1)}, u32[]{:S(2)}) copy-start(bf16[1,1,512,2048]{3,2,1,0:T(8,128)(2,1)} %param.10) | copy-start | bytes 6291460
  (3 other events, 3.2 us)
Sparse Core Ops, SparseCore 0:
  22.0 80.7 all-gather.4
  148.1 30.5 all-gather.6

commit v13 on v12

--- a/solution.py
+++ b/solution.py
@@ -54,6 +54,34 @@
             flops=feats * slots * 14, transcendentals=feats * slots, bytes_accessed=feats * slots * 4
         ),
     )(conv_t, edge_t, weight_t, bias_t)
+
+
+def norm_kernel(y_ref, z_ref, w_ref, mask_ref, o_ref):
+    z = z_ref[...].astype(jnp.float32)
+    gated = y_ref[...] * (z * (0.5 + 0.5 * jnp.tanh(0.5 * z)))
+    mean = jnp.sum(gated * gated, axis=0, keepdims=True) * (1.0 / gated.shape[0])
+    normed = gated * lax.rsqrt(mean + 1e-05) * w_ref[...]
+    normed = jnp.where(mask_ref[...] > 0.5, normed, 0.0)
+    o_ref[...] = normed.T.astype(o_ref.dtype)
+
+
+def gate_norm(y_t, z_t, weight, mask, cols=128):
+    units, slots = y_t.shape
+    return pl.pallas_call(
+        norm_kernel,
+        grid=(slots // cols,),
+        in_specs=[
+            pl.BlockSpec((units, cols), lambda i: (0, i)),
+            pl.BlockSpec((units, cols), lambda i: (0, i)),
+            pl.BlockSpec((units, 1), lambda i: (0, 0)),
+            pl.BlockSpec((1, cols), lambda i: (0, i)),
+        ],
+        out_specs=pl.BlockSpec((cols, units), lambda i: (i, 0)),
+        out_shape=jax.ShapeDtypeStruct((slots, units), jnp.bfloat16),
+        cost_estimate=pl.CostEstimate(
+            flops=units * slots * 12, transcendentals=units * slots, bytes_accessed=units * slots * 8
+        ),
+    )(y_t, z_t, weight, mask)
 
 
 def block_step(state, pieces):
@@ -165,11 +193,12 @@
         + incoming
         + d_skip[None, :, None] * inputs_x.astype(jnp.float32).reshape(slots, heads, hdim)
     )
-    gate = gate_z.astype(jnp.float32)
-    gated = heads_y.reshape(slots, inner) * (gate * (0.5 + 0.5 * jnp.tanh(0.5 * gate)))
-    scale = lax.rsqrt(jnp.mean(gated * gated, axis=1, keepdims=True) + 1e-05)
-    normed = jnp.where(filled[:, None], gated * scale * norm_weight[None, :], 0.0)
-    gated_out = normed.astype(jnp.bfloat16).reshape(1, 1, slots, inner)
+    gated_out = gate_norm(
+        heads_y.reshape(slots, inner).T,
+        gate_z.T,
+        norm_weight[:, None],
+        filled.astype(jnp.float32)[None, :],
+    ).reshape(1, 1, slots, inner)
     later_mask = jnp.arange(seq_count)[None, :] > jnp.arange(seq_count)[:, None]
     after = jnp.sum(jnp.where(later_mask[:, :, None], totals[None, :, :], 0.0), axis=1)
     piece = hdim // seq_count

time: 218 us -> 218 us (level)
  Pallas kernels: 9.19 us -> 15.8 us
  waiting for transfers between devices: 91.3 us -> 85.7 us
  other arithmetic: 21.4 us -> 18 us
  matrix products: 29.5 us -> 31.7 us
    pallas_call x0 -> x1, Pallas kernels: none -> 6.59 us  [gate_norm(): pl.pallas_call(norm_kernel, grid=(slots // cols,), in_specs=[pl.BlockSpec...]
    unnamed x57 -> x58, local copies, waits for them, and re-layouts: 13.9 us -> 9.93 us
    all_gather x1, waiting for transfers between devices: 17.3 us -> 14 us  [local(): gathered = lax.all_gather(packed, 'seq', axis=0, tiled=False)]
    transpose x0 -> x1, local copies, waits for them, and re-layouts: none -> 3.06 us  [local(): gated_out = gate_norm(heads_y.reshape(slots, inner).T, gate_z.T, norm_wei...]
    reshape x1 -> x0, other arithmetic: 2.82 us -> none  [local(): gated_out = normed.astype(jnp.bfloat16).reshape(1, 1, slots, inner)]
    all_gather x1, waiting for transfers between devices: 73.9 us -> 71.6 us  [local(): lax.all_gather(wide_rows, 'req', axis=0, tiled=True)]
  transfers between devices with their start and end apart: 4 -> 4, of which waited for: 2 -> 2; matrix products, arithmetic and copies ran while one was open for 17% -> 16% of each run, Pallas kernels for 0% -> 3%
where the time goes in v13:
time: 218 us; the launch traced here: 217 us
  waiting for transfers between devices  85.7 us (39%)
  matrix products  31.7 us (15%)
  local copies, waits for them, and re-layouts  26.2 us (12%)
  other arithmetic  18 us (8%)
  Pallas kernels  15.8 us (7%)
  between operations  15.8 us (7%)
  blocking collectives  12.8 us (6%)
  starting transfers between devices  11.1 us (5%)
    all_gather x1, waiting for transfers between devices, local(): lax.all_gather(wide_rows, 'req', axis=0, tiled=True)  71.6 us
    dot_general x1, matrix products, local(): jnp.dot(tok_rows, lax.all_gather(wide_rows, 'req', axis=0, tiled=True), p...  15.3 us
    all_gather x1, waiting for transfers between devices, local(): gathered = lax.all_gather(packed, 'seq', axis=0, tiled=False)  14 us
    all_gather x1, blocking collectives, local(): wide_rows = lax.all_gather(w_in, 'seq', axis=1, tiled=True)  12.8 us
    unnamed x58, local copies, waits for them, and re-layouts  9.93 us
    pallas_call x1, Pallas kernels, conv_silu(): pl.pallas_call(conv_kernel, grid=(feats // rows,), in_specs=[pl.BlockSpec...  9.19 us
    dot_general x2, matrix products, block_step(): jnp.einsum('htu,uhp->thp', mixing, heads_x, preferred_element_type=jnp.fl...  8.78 us
    all_to_all x1, starting transfers between devices, local(): lax.all_to_all(share[None], 'req', split_axis=1, concat_axis=0, tiled=True)  7.78 us
  transfers between devices with their start and end apart: 4, of which 2 were waited for; matrix products, arithmetic and copies ran while one was open for 16% of the time, Pallas kernels for 3%

profile of v13, /device:TPU:1, one launch (start us, length us, event | category | flops | bytes accessed | tf_op | source)
XLA Modules:
  0.0 217.1 jit_solution(5357791486943199093)
XLA Ops:
  7.3 12.8 %all-gather.1 = bf16[4,1096,64]{1,2,0:T(8,128)(2,1)S(1)} all-gather(bf16[1,1096,64]{1,2,0:T(8,128)(2,1)} %bitcast.210), channel_id=1, replica_groups=mesh['req'=32,'seq'=4] {'seq'}, dimensions={0}, use_global_device_ids=true | all-gather | bytes 701440 | tf_op jit(solution)/shard_map/all_gather | solution.py:133
  20.6 1.3 reshape.358
  23.9 1.4 copy.83
  25.3 1.4 broadcast_in_dim.151.b_ref
  26.7 1.4 copy.97.w_ref
  29.3 1.2 compare_convert_fusion.mask_ref
  31.2 71.6 %all-gather.5.cloned.1.call-done = bf16[2048,4384]{1,0:T(8,128)(2,1)} async-done(((bf16[64,4384]{1,0:T(8,128)(2,1)}), bf16[2048,4384]{1,0:T(8,128)(2,1)}) %all-gather.5.cloned.1.call-update) | async-done | bytes 17956880 | tf_op jit(solution)/shard_map/all_gather | solution.py:136
  102.8 15.3 %convolution_convert_fusion = bf16[512,4384]{0,1:T(8,128)(2,1)} fusion(bf16[2048,4384]{1,0:T(8,128)(2,1)} %all-gather.5.cloned.1.call-done, bf16[1,1,512,2048]{3,2,1,0:T(8,128)(2,1)S(1)} %copy-done), kind=kOutput, calls=%fused_computation.3 | convolution fusion | flops 9196158976 | bytes 24543232 | tf_op jit(solution)/shard_map/dot_general | solution.py:134
  118.1 3.4 %fusion.57 = (bf16[512,2304]{0,1:T(8,128)(2,1)S(1)}, bf16[2304,512]{1,0:T(8,128)(2,1)}) fusion(bf16[512,4384]{0,1:T(8,128)(2,1)} %convolution_convert_fusion), kind=kLoop, calls=%fused_computation.130 | loop fusion | bytes 7077888 | tf_op jit(solution)/shard_map/slice | solution.py:140
  126.2 3.3 %collective-permute-start = (bf16[3,2304]{1,0:T(4,128)(2,1)S(1)}, bf16[3,2304]{1,0:T(4,128)(2,1)S(1)}, u32[]{:S(2)}, u32[]{:S(2)}) collective-permute-start(bf16[3,2304]{1,0:T(4,128)(2,1)S(1)} %copy.81), channel_id=1, source_target_pairs={{0,1},{1,2},{2,3},{4,5},{5,6},{6,7},{8,9},{9,10},{10,11},{12,13},{... | collective-permute-start | bytes 41480 | tf_op jit(solution)/shard_map/ppermute | solution.py:14
  133.9 9.2 %shard_map.113 = bf16[2304,512]{1,0:T(8,128)(2,1)} custom-call(bf16[2304,512]{1,0:T(8,128)(2,1)} %get-tuple-element.15.x_ref, bf16[2304,3]{1,0:T(8,128)(2,1)} %bitcast.199, f32[2304,4]{1,0:T(8,128)} %bitcast.196, f32[2304,1]{1,0:T(8,128)} %broadcast_in_dim.151.b_ref), custom_call_target="tpu_custom_call" | custom-call | flops 16515072 | bytes 4718592 | tf_op jit(solution)/shard_map/pallas_call | solution.py:42
  143.1 2.1 fusion.15
  147.5 3.1 %slice_bitcast_fusion.z_ref = bf16[2048,512]{1,0:T(8,128)(2,1)} fusion(bf16[512,4384]{0,1:T(8,128)(2,1)} %convolution_convert_fusion), kind=kLoop, calls=%fused_computation.21 | loop fusion | bytes 4194304 | tf_op jit(solution)/shard_map/transpose | solution.py:198
  150.6 1.5 slice.195
  155.4 4.4 %bitcast_add_fusion.1 = f32[256,32,64]{0,2,1:T(8,128)} fusion(f32[256,32,64]{0,2,1:T(8,128)S(1)} %fusion.22, bf16[256,32,64]{0,2,1:T(8,128)(2,1)S(1)} %bitcast.208, f32[32,256]{1,0:T(8,128)S(1)} %copy-done.13, f32[32,256]{1,0:T(8,128)S(1)} %copy-done.9, f32[256,256]{1,0:T(8,128)S(1)} %fusion.38, pred[256,256]{1,0:T(8,128)(4,1)S(1)} %copy-done.7, ...), kind=kOutput, calls=%fused_computation.28 | convolution fusion | flops 282066944 | bytes 5668864 | tf_op jit(solution)/shard_map/htu,uhp->thp/dot_general | solution.py:99
  159.8 4.3 %bitcast_add_fusion = f32[256,32,64]{0,2,1:T(8,128)} fusion(f32[256,32,64]{0,2,1:T(8,128)S(1)} %fusion.29, bf16[256,32,64]{0,2,1:T(8,128)(2,1)S(1)} %bitcast.207, f32[32,256]{1,0:T(8,128)S(1)} %copy-done.11, f32[32,256]{1,0:T(8,128)S(1)} %copy-done.10, f32[256,256]{1,0:T(8,128)S(1)} %fusion.33, pred[256,256]{1,0:T(8,128)(4,1)S(1)} %copy-done.7, ...), kind=kOutput, calls=%fused_computation.27 | convolution fusion | flops 282066944 | bytes 5668864 | tf_op jit(solution)/shard_map/htu,uhp->thp/dot_general | solution.py:99
  164.2 14.0 %all-gather.7.cloned.1.call-done = bf16[128,8576]{1,0:T(8,128)(2,1)} async-done(((bf16[32,8576]{1,0:T(8,128)(2,1)}), bf16[128,8576]{1,0:T(8,128)(2,1)}) %all-gather.7.cloned.1.call-update) | async-done | bytes 2195472 | tf_op jit(solution)/shard_map/all_gather | solution.py:180
  178.2 2.0 slice_convert_fusion
  181.1 1.6 slice_bitcast_fusion.3
  184.5 7.8 %all-to-all-start = ((f32[1,32,16,128]{3,2,0,1:T(8,128)}), f32[1,32,16,128]{3,2,0,1:T(8,128)}, u32[]{:S(2)}, u32[]{:S(2)}) async-start(f32[1,32,16,128]{3,2,0,1:T(8,128)} %bitcast.206), calls=%async_computation | async-start | bytes 524288 | tf_op jit(solution)/shard_map/all_to_all | solution.py:207
  192.3 1.5 copy.117
  197.0 4.3 %fusion.2 = f32[512,32,64]{0,2,1:T(8,128)} fusion(f32[256,32,64]{0,2,1:T(8,128)S(1)} %copy-done.6, f32[256,32,64]{0,2,1:T(8,128)S(1)} %copy-done.5, bf16[512,32,64]{0,2,1:T(8,128)(2,1)S(1)} %bitcast.194, f32[32,64,128]{2,1,0:T(8,128)S(1)} %fusion.19, f32[32]{0:T(128)S(1)} %copy-done.18, f32[512,32]{0,1:T(8,128)S(1)} %fusion.51, ...), kind=kOutput, calls=%fused_computation.7 | convolution fusion | flops 1616904192 | bytes 11731456 | tf_op jit(solution)/shard_map/tn,hpn->thp/dot_general | solution.py:188
  201.3 6.6 %shard_map.114 = bf16[512,2048]{1,0:T(8,128)(2,1)} custom-call(f32[2048,512]{1,0:T(8,128)} %bitcast.193, bf16[2048,512]{1,0:T(8,128)(2,1)} %slice_bitcast_fusion.z_ref, f32[2048,1]{1,0:T(8,128)} %copy.97.w_ref, f32[1,512]{1,0:T(1,128)} %compare_convert_fusion.mask_ref), custom_call_target="tpu_custom_call" | custom-call | flops 12582912 | bytes 8388608 | tf_op jit(solution)/shard_map/pallas_call | solution.py:70
  207.9 1.5 gather_fusion
  (116 shorter events, 24.3 us)
Async XLA Ops:
  7.2 95.6 %copy-start = (bf16[1,1,512,2048]{3,2,1,0:T(8,128)(2,1)S(1)}, bf16[1,1,512,2048]{3,2,1,0:T(8,128)(2,1)}, u32[]{:S(2)}) copy-start(bf16[1,1,512,2048]{3,2,1,0:T(8,128)(2,1)} %param.10) | copy-start | bytes 6291460
  7.2 14.7 %copy-start.20 = (s32[32]{0:T(128)S(1)}, s32[32]{0:T(128)}, u32[]{:S(2)}) copy-start(s32[32]{0:T(128)} %param.18) | copy-start | bytes 388
  7.2 14.7 %copy-start.21 = (s32[32]{0:T(128)S(1)}, s32[32]{0:T(128)}, u32[]{:S(2)}) copy-start(s32[32]{0:T(128)} %param.19) | copy-start | bytes 388
  7.2 16.7 %copy-start.8 = (f32[4,2304]{1,0:T(4,128)S(1)}, f32[4,2304]{1,0:T(4,128)}, u32[]{:S(2)}) copy-start(f32[4,2304]{1,0:T(4,128)} %param.12) | copy-start | bytes 110596
  7.2 95.6 %all-gather.5.cloned.1.call-start = ((), (), s32[]{:S(2)}) async-start(), calls=%async_computation.1 | async-start | bytes 18923520 | tf_op jit(solution)/shard_map/all_gather | solution.py:136
  7.3 18.0 %copy-start.15 = (f32[2304]{0:T(1024)S(1)}, f32[2304]{0:T(1024)}, u32[]{:S(2)}) copy-start(f32[2304]{0:T(1024)} %param.13) | copy-start | bytes 27652
  20.6 6.2 %copy-start.16 = (f32[2048]{0:T(1024)S(1)}, f32[2048]{0:T(1024)}, u32[]{:S(2)}) copy-start(f32[2048]{0:T(1024)} %param.17) | copy-start | bytes 24580
  21.8 9.3 %copy-start.23 = (f32[32]{0:T(128)S(1)}, f32[32]{0:T(128)}, u32[]{:S(2)}) copy-start(f32[32]{0:T(128)} %param.15) | copy-start | bytes 388
  21.9 156.3 %all-gather.7.cloned.1.call-start = ((), (), s32[]{:S(2)}) async-start(), calls=%async_computation.2 | async-start | bytes 2744320 | tf_op jit(solution)/shard_map/all_gather | solution.py:180
  118.1 3.4 %copy-start.17 = (f32[32]{0:T(128)S(1)}, f32[32]{0:T(128)}, u32[]{:S(2)}) copy-start(f32[32]{0:T(128)} %param.14) | copy-start | bytes 388
  126.2 6.5 %collective-permute-start = (bf16[3,2304]{1,0:T(4,128)(2,1)S(1)}, bf16[3,2304]{1,0:T(4,128)(2,1)S(1)}, u32[]{:S(2)}, u32[]{:S(2)}) collective-permute-start(bf16[3,2304]{1,0:T(4,128)(2,1)S(1)} %copy.81), channel_id=1, source_target_pairs={{0,1},{1,2},{2,3},{4,5},{5,6},{6,7},{8,9},{9,10},{10,11},{12,13},{... | collective-permute-start | bytes 41480 | tf_op jit(solution)/shard_map/ppermute | solution.py:14
  143.1 2.3 %copy-start.2 = (bf16[2304,512]{1,0:T(8,128)(2,1)S(1)}, bf16[2304,512]{1,0:T(8,128)(2,1)}, u32[]{:S(2)}) copy-start(bf16[2304,512]{1,0:T(8,128)(2,1)} %shard_map.113) | copy-start | bytes 7077892
  143.1 2.7 %copy-start.19 = (f32[32]{0:T(128)S(1)}, f32[32]{0:T(128)}, u32[]{:S(2)}) copy-start(f32[32]{0:T(128)} %exp.89) | copy-start | bytes 388
  154.5 0.8 copy-start.7
  155.4 4.5 %copy-start.10 = (f32[32,256]{1,0:T(8,128)S(1)}, f32[32,256]{1,0:T(8,128)}, u32[]{:S(2)}) copy-start(f32[32,256]{1,0:T(8,128)} %get-tuple-element.32) | copy-start | bytes 98308
  155.4 4.5 %copy-start.11 = (f32[32,256]{1,0:T(8,128)S(1)}, f32[32,256]{1,0:T(8,128)}, u32[]{:S(2)}) copy-start(f32[32,256]{1,0:T(8,128)} %get-tuple-element.24) | copy-start | bytes 98308
  155.4 4.5 %copy-start.12 = (f32[256,32]{0,1:T(8,128)S(1)}, f32[256,32]{0,1:T(8,128)}, u32[]{:S(2)}) copy-start(f32[256,32]{0,1:T(8,128)} %get-tuple-element.30) | copy-start | bytes 98308
  184.5 23.4 %all-to-all-start = ((f32[1,32,16,128]{3,2,0,1:T(8,128)}), f32[1,32,16,128]{3,2,0,1:T(8,128)}, u32[]{:S(2)}, u32[]{:S(2)}) async-start(f32[1,32,16,128]{3,2,0,1:T(8,128)} %bitcast.206), calls=%async_computation | async-start | bytes 524288 | tf_op jit(solution)/shard_map/all_to_all | solution.py:207
  192.3 1.5 copy-start.4
  194.0 1.6 copy-start.6
  194.2 2.1 copy-start.3
  194.3 2.7 %copy-start.5 = (f32[256,32,64]{0,2,1:T(8,128)S(1)}, f32[256,32,64]{0,2,1:T(8,128)}, u32[]{:S(2)}) copy-start(f32[256,32,64]{0,2,1:T(8,128)} %bitcast_add_fusion.1) | copy-start | bytes 6291460
  194.3 2.7 %copy-start.18 = (f32[32]{0:T(128)S(1)}, f32[32]{0:T(128)}, u32[]{:S(2)}) copy-start(f32[32]{0:T(128)} %param.16) | copy-start | bytes 388
  201.3 8.9 %copy-start.1 = (bf16[1,1,512,2048]{3,2,1,0:T(8,128)(2,1)S(1)}, bf16[1,1,512,2048]{3,2,1,0:T(8,128)(2,1)}, u32[]{:S(2)}) copy-start(bf16[1,1,512,2048]{3,2,1,0:T(8,128)(2,1)} %param.10) | copy-start | bytes 6291460
  (4 other events, 3.3 us)
Sparse Core Ops, SparseCore 0:
  22.0 80.7 all-gather.4
  147.6 30.5 all-gather.6

commit v14 on v13

--- a/solution.py
+++ b/solution.py
@@ -130,7 +130,14 @@
     my_block = lax.axis_index("seq")
     qlen = jnp.sum(jnp.where(prompt_group == my_group, lengths, 0))
     filled = jnp.arange(slots, dtype=jnp.int32) < qlen
-    wide_rows = lax.all_gather(w_in, "seq", axis=1, tiled=True)
+    column_blocks = [w_in]
+    for distance in range(1, seq_count):
+        cycle = [(i, (i + distance) % seq_count) for i in range(seq_count)]
+        column_blocks.append(lax.ppermute(w_in, "seq", cycle))
+    by_distance = jnp.stack(column_blocks)
+    from_block = (my_block - jnp.arange(seq_count)) % seq_count
+    in_order = jnp.take(by_distance, from_block, axis=0)
+    wide_rows = jnp.transpose(in_order, (1, 0, 2)).reshape(w_in.shape[0], -1)
     projected = jnp.dot(
         tok_rows,
         lax.all_gather(wide_rows, "req", axis=0, tiled=True),

time: 218 us -> 214 us (0.982)
  blocking collectives: 12.8 us -> 0 us
  starting transfers between devices: 11.1 us -> 16.8 us
  waiting for transfers between devices: 85.7 us -> 89.9 us
    all_gather x1 -> x0, blocking collectives: 12.8 us -> none  [local(): wide_rows = lax.all_gather(w_in, 'seq', axis=1, tiled=True)]
    ppermute x0 -> x3, starting transfers between devices: none -> 5.71 us  [local(): column_blocks.append(lax.ppermute(w_in, 'seq', cycle))]
    ppermute x0 -> x3, waiting for transfers between devices: none -> 5.42 us  [local(): column_blocks.append(lax.ppermute(w_in, 'seq', cycle))]
    another operation x10 -> x11, other arithmetic: 3.94 us -> 4.96 us
    unnamed x58 -> x59, local copies, waits for them, and re-layouts: 9.93 us -> 9.4 us
  transfers between devices with their start and end apart: 4 -> 7, of which waited for: 2 -> 4; matrix products, arithmetic and copies ran while one was open for 16% -> 16% of each run, Pallas kernels for 3% -> 3%
where the time goes in v14:
time: 214 us; the launch traced here: 213 us
  waiting for transfers between devices  89.9 us (42%)
  matrix products  30.3 us (14%)
  local copies, waits for them, and re-layouts  26.1 us (12%)
  other arithmetic  18.6 us (9%)
  starting transfers between devices  16.8 us (8%)
  Pallas kernels  15.8 us (7%)
  between operations  15.8 us (7%)
    all_gather x1, waiting for transfers between devices, local(): lax.all_gather(wide_rows, 'req', axis=0, tiled=True)  70.4 us
    all_gather x1, waiting for transfers between devices, local(): gathered = lax.all_gather(packed, 'seq', axis=0, tiled=False)  14 us
    dot_general x1, matrix products, local(): jnp.dot(tok_rows, lax.all_gather(wide_rows, 'req', axis=0, tiled=True), p...  14 us
    unnamed x59, local copies, waits for them, and re-layouts  9.4 us
    pallas_call x1, Pallas kernels, conv_silu(): pl.pallas_call(conv_kernel, grid=(feats // rows,), in_specs=[pl.BlockSpec...  9.25 us
    dot_general x2, matrix products, block_step(): jnp.einsum('htu,uhp->thp', mixing, heads_x, preferred_element_type=jnp.fl...  8.72 us
    all_to_all x1, starting transfers between devices, local(): lax.all_to_all(share[None], 'req', split_axis=1, concat_axis=0, tiled=True)  7.77 us
    pallas_call x1, Pallas kernels, gate_norm(): pl.pallas_call(norm_kernel, grid=(slots // cols,), in_specs=[pl.BlockSpec...  6.59 us
  transfers between devices with their start and end apart: 7, of which 4 were waited for; matrix products, arithmetic and copies ran while one was open for 16% of the time, Pallas kernels for 3%

profile of v14, /device:TPU:1, one launch (start us, length us, event | category | flops | bytes accessed | tf_op | source)
XLA Modules:
  0.0 213.4 jit_solution(10217066982892926466)
XLA Ops:
  7.2 2.1 collective-permute-start
  9.3 2.5 %collective-permute-start.1 = (bf16[64,1096]{1,0:T(8,128)(2,1)}, bf16[64,1096]{1,0:T(8,128)(2,1)S(1)}, u32[]{:S(2)}, u32[]{:S(2)}) collective-permute-start(bf16[64,1096]{1,0:T(8,128)(2,1)} %param.11), channel_id=1, source_target_pairs={{0,2},{1,3},{2,0},{3,1},{4,6},{5,7},{6,4},{7,5},{8,10},{9,11},{10,... | collective-permute-start | bytes 420872 | tf_op jit(solution)/shard_map/ppermute | solution.py:136
  13.9 4.5 %collective-permute-done.1 = bf16[64,1096]{1,0:T(8,128)(2,1)S(1)} collective-permute-done((bf16[64,1096]{1,0:T(8,128)(2,1)}, bf16[64,1096]{1,0:T(8,128)(2,1)S(1)}, u32[]{:S(2)}, u32[]{:S(2)}) %collective-permute-start.1) | collective-permute-done | bytes 140320 | tf_op jit(solution)/shard_map/ppermute | solution.py:136
  24.0 1.4 copy.83
  25.4 1.4 broadcast_in_dim.163.b_ref
  26.8 1.4 copy.97.w_ref
  31.4 70.4 %all-gather.4.cloned.1.call-done = bf16[2048,4384]{1,0:T(8,128)(2,1)} async-done(((bf16[64,4384]{1,0:T(8,128)(2,1)}), bf16[2048,4384]{1,0:T(8,128)(2,1)}) %all-gather.4.cloned.1.call-update) | async-done | bytes 17956880 | tf_op jit(solution)/shard_map/all_gather | solution.py:143
  101.8 14.0 %fusion = bf16[512,4384]{0,1:T(8,128)(2,1)S(1)} fusion(bf16[2048,4384]{1,0:T(8,128)(2,1)} %all-gather.4.cloned.1.call-done, bf16[1,1,512,2048]{3,2,1,0:T(8,128)(2,1)S(1)} %copy-done), kind=kOutput, calls=%fused_computation.5 | convolution fusion | flops 9196158976 | bytes 24543232 | tf_op jit(solution)/shard_map/dot_general | solution.py:141
  115.8 2.0 fusion.61
  122.5 3.3 %collective-permute-start.3 = (bf16[3,2304]{1,0:T(4,128)(2,1)S(1)}, bf16[3,2304]{1,0:T(4,128)(2,1)S(1)}, u32[]{:S(2)}, u32[]{:S(2)}) collective-permute-start(bf16[3,2304]{1,0:T(4,128)(2,1)S(1)} %copy.81), channel_id=1, source_target_pairs={{0,1},{1,2},{2,3},{4,5},{5,6},{6,7},{8,9},{9,10},{10,11},{12,13},{... | collective-permute-start | bytes 41480 | tf_op jit(solution)/shard_map/ppermute | solution.py:14
  130.1 9.2 %shard_map.113 = bf16[2304,512]{1,0:T(8,128)(2,1)} custom-call(bf16[2304,512]{1,0:T(8,128)(2,1)} %get-tuple-element.15.x_ref, bf16[2304,3]{1,0:T(8,128)(2,1)} %bitcast.203, f32[2304,4]{1,0:T(8,128)} %bitcast.200, f32[2304,1]{1,0:T(8,128)} %broadcast_in_dim.163.b_ref), custom_call_target="tpu_custom_call" | custom-call | flops 16515072 | bytes 4718592 | tf_op jit(solution)/shard_map/pallas_call | solution.py:42
  139.4 2.1 fusion.16
  143.9 3.1 %slice_bitcast_fusion.z_ref = bf16[2048,512]{1,0:T(8,128)(2,1)} fusion(bf16[512,4384]{0,1:T(8,128)(2,1)} %copy-done.4), kind=kLoop, calls=%fused_computation.23 | loop fusion | bytes 4194304 | tf_op jit(solution)/shard_map/transpose | solution.py:205
  147.1 1.5 slice.197
  151.8 4.4 %bitcast_add_fusion.1 = f32[256,32,64]{0,2,1:T(8,128)} fusion(f32[256,32,64]{0,2,1:T(8,128)S(1)} %fusion.23, bf16[256,32,64]{0,2,1:T(8,128)(2,1)S(1)} %bitcast.211, f32[32,256]{1,0:T(8,128)S(1)} %copy-done.14, f32[32,256]{1,0:T(8,128)S(1)} %copy-done.10, f32[256,256]{1,0:T(8,128)S(1)} %fusion.39, pred[256,256]{1,0:T(8,128)(4,1)S(1)} %copy-done.8, ...), kind=kOutput, calls=%fused_computation.30 | convolution fusion | flops 282066944 | bytes 5668864 | tf_op jit(solution)/shard_map/htu,uhp->thp/dot_general | solution.py:99
  156.2 4.3 %bitcast_add_fusion = f32[256,32,64]{0,2,1:T(8,128)} fusion(f32[256,32,64]{0,2,1:T(8,128)S(1)} %fusion.30, bf16[256,32,64]{0,2,1:T(8,128)(2,1)S(1)} %bitcast.210, f32[32,256]{1,0:T(8,128)S(1)} %copy-done.12, f32[32,256]{1,0:T(8,128)S(1)} %copy-done.11, f32[256,256]{1,0:T(8,128)S(1)} %fusion.34, pred[256,256]{1,0:T(8,128)(4,1)S(1)} %copy-done.8, ...), kind=kOutput, calls=%fused_computation.29 | convolution fusion | flops 282066944 | bytes 5668864 | tf_op jit(solution)/shard_map/htu,uhp->thp/dot_general | solution.py:99
  160.5 14.0 %all-gather.6.cloned.1.call-done = bf16[128,8576]{1,0:T(8,128)(2,1)} async-done(((bf16[32,8576]{1,0:T(8,128)(2,1)}), bf16[128,8576]{1,0:T(8,128)(2,1)}) %all-gather.6.cloned.1.call-update) | async-done | bytes 2195472 | tf_op jit(solution)/shard_map/all_gather | solution.py:187
  174.6 2.0 slice_convert_fusion
  177.5 1.5 slice_bitcast_fusion.3
  180.9 7.8 %all-to-all-start = ((f32[1,32,16,128]{3,2,0,1:T(8,128)}), f32[1,32,16,128]{3,2,0,1:T(8,128)}, u32[]{:S(2)}, u32[]{:S(2)}) async-start(f32[1,32,16,128]{3,2,0,1:T(8,128)} %bitcast.209), calls=%async_computation | async-start | bytes 524288 | tf_op jit(solution)/shard_map/all_to_all | solution.py:214
  188.7 1.5 copy.117
  193.3 4.3 %fusion.3 = f32[512,32,64]{0,2,1:T(8,128)} fusion(f32[256,32,64]{0,2,1:T(8,128)S(1)} %copy-done.7, f32[256,32,64]{0,2,1:T(8,128)S(1)} %copy-done.6, bf16[512,32,64]{0,2,1:T(8,128)(2,1)S(1)} %bitcast.198, f32[32,64,128]{2,1,0:T(8,128)S(1)} %fusion.20, f32[32]{0:T(128)S(1)} %copy-done.19, f32[512,32]{0,1:T(8,128)S(1)} %fusion.55, ...), kind=kOutput, calls=%fused_computation.9 | convolution fusion | flops 1616904192 | bytes 11731456 | tf_op jit(solution)/shard_map/tn,hpn->thp/dot_general | solution.py:195
  197.7 6.6 %shard_map.114 = bf16[512,2048]{1,0:T(8,128)(2,1)} custom-call(f32[2048,512]{1,0:T(8,128)} %bitcast.197, bf16[2048,512]{1,0:T(8,128)(2,1)} %slice_bitcast_fusion.z_ref, f32[2048,1]{1,0:T(8,128)} %copy.97.w_ref, f32[1,512]{1,0:T(1,128)} %compare_convert_fusion.mask_ref), custom_call_target="tpu_custom_call" | custom-call | flops 12582912 | bytes 8388608 | tf_op jit(solution)/shard_map/pallas_call | solution.py:70
  204.3 1.5 gather_fusion.1
  (129 shorter events, 30.8 us)
Async XLA Ops:
  7.2 94.6 %copy-start = (bf16[1,1,512,2048]{3,2,1,0:T(8,128)(2,1)S(1)}, bf16[1,1,512,2048]{3,2,1,0:T(8,128)(2,1)}, u32[]{:S(2)}) copy-start(bf16[1,1,512,2048]{3,2,1,0:T(8,128)(2,1)} %param.10) | copy-start | bytes 6291460
  7.2 94.6 %all-gather.4.cloned.1.call-start = ((), (), s32[]{:S(2)}) async-start(), calls=%async_computation.1 | async-start | bytes 18923520 | tf_op jit(solution)/shard_map/all_gather | solution.py:143
  7.2 6.7 %collective-permute-start = (bf16[64,1096]{1,0:T(8,128)(2,1)}, bf16[64,1096]{1,0:T(8,128)(2,1)S(1)}, u32[]{:S(2)}, u32[]{:S(2)}) collective-permute-start(bf16[64,1096]{1,0:T(8,128)(2,1)} %param.11), channel_id=1, source_target_pairs={{0,1},{1,2},{2,3},{3,0},{4,5},{5,6},{6,7},{7,4},{8,9},{9,10},{10,1... | collective-permute-start | bytes 420872 | tf_op jit(solution)/shard_map/ppermute | solution.py:136
  9.3 9.1 %collective-permute-start.1 = (bf16[64,1096]{1,0:T(8,128)(2,1)}, bf16[64,1096]{1,0:T(8,128)(2,1)S(1)}, u32[]{:S(2)}, u32[]{:S(2)}) collective-permute-start(bf16[64,1096]{1,0:T(8,128)(2,1)} %param.11), channel_id=1, source_target_pairs={{0,2},{1,3},{2,0},{3,1},{4,6},{5,7},{6,4},{7,5},{8,10},{9,11},{10,... | collective-permute-start | bytes 420872 | tf_op jit(solution)/shard_map/ppermute | solution.py:136
  11.8 6.6 %collective-permute-start.2 = (bf16[64,1096]{1,0:T(8,128)(2,1)}, bf16[64,1096]{1,0:T(8,128)(2,1)S(1)}, u32[]{:S(2)}, u32[]{:S(2)}) collective-permute-start(bf16[64,1096]{1,0:T(8,128)(2,1)} %param.11), channel_id=1, source_target_pairs={{0,3},{1,0},{2,1},{3,2},{4,7},{5,4},{6,5},{7,6},{8,11},{9,8},{10,9... | collective-permute-start | bytes 420872 | tf_op jit(solution)/shard_map/ppermute | solution.py:136
  19.4 2.6 %copy-start.21 = (s32[32]{0:T(128)S(1)}, s32[32]{0:T(128)}, u32[]{:S(2)}) copy-start(s32[32]{0:T(128)} %param.18) | copy-start | bytes 388
  19.4 2.6 %copy-start.22 = (s32[32]{0:T(128)S(1)}, s32[32]{0:T(128)}, u32[]{:S(2)}) copy-start(s32[32]{0:T(128)} %param.19) | copy-start | bytes 388
  19.4 4.6 %copy-start.9 = (f32[4,2304]{1,0:T(4,128)S(1)}, f32[4,2304]{1,0:T(4,128)}, u32[]{:S(2)}) copy-start(f32[4,2304]{1,0:T(4,128)} %param.12) | copy-start | bytes 110596
  20.2 5.2 %copy-start.16 = (f32[2304]{0:T(1024)S(1)}, f32[2304]{0:T(1024)}, u32[]{:S(2)}) copy-start(f32[2304]{0:T(1024)} %param.13) | copy-start | bytes 27652
  20.7 6.1 %copy-start.17 = (f32[2048]{0:T(1024)S(1)}, f32[2048]{0:T(1024)}, u32[]{:S(2)}) copy-start(f32[2048]{0:T(1024)} %param.17) | copy-start | bytes 24580
  22.0 9.4 %copy-start.24 = (f32[32]{0:T(128)S(1)}, f32[32]{0:T(128)}, u32[]{:S(2)}) copy-start(f32[32]{0:T(128)} %param.15) | copy-start | bytes 388
  22.0 152.6 %all-gather.6.cloned.1.call-start = ((), (), s32[]{:S(2)}) async-start(), calls=%async_computation.2 | async-start | bytes 2744320 | tf_op jit(solution)/shard_map/all_gather | solution.py:187
  115.8 2.8 %copy-start.4 = (bf16[512,4384]{0,1:T(8,128)(2,1)}, bf16[512,4384]{0,1:T(8,128)(2,1)S(1)}, u32[]{:S(2)}) copy-start(bf16[512,4384]{0,1:T(8,128)(2,1)S(1)} %fusion) | copy-start | bytes 13467652
  115.8 2.8 %copy-start.18 = (f32[32]{0:T(128)S(1)}, f32[32]{0:T(128)}, u32[]{:S(2)}) copy-start(f32[32]{0:T(128)} %param.14) | copy-start | bytes 388
  122.5 6.5 %collective-permute-start.3 = (bf16[3,2304]{1,0:T(4,128)(2,1)S(1)}, bf16[3,2304]{1,0:T(4,128)(2,1)S(1)}, u32[]{:S(2)}, u32[]{:S(2)}) collective-permute-start(bf16[3,2304]{1,0:T(4,128)(2,1)S(1)} %copy.81), channel_id=1, source_target_pairs={{0,1},{1,2},{2,3},{4,5},{5,6},{6,7},{8,9},{9,10},{10,11},{12,13},{... | collective-permute-start | bytes 41480 | tf_op jit(solution)/shard_map/ppermute | solution.py:14
  139.4 2.3 %copy-start.2 = (bf16[2304,512]{1,0:T(8,128)(2,1)S(1)}, bf16[2304,512]{1,0:T(8,128)(2,1)}, u32[]{:S(2)}) copy-start(bf16[2304,512]{1,0:T(8,128)(2,1)} %shard_map.113) | copy-start | bytes 7077892
  139.4 2.7 %copy-start.20 = (f32[32]{0:T(128)S(1)}, f32[32]{0:T(128)}, u32[]{:S(2)}) copy-start(f32[32]{0:T(128)} %exp.89) | copy-start | bytes 388
  151.8 4.4 %copy-start.11 = (f32[32,256]{1,0:T(8,128)S(1)}, f32[32,256]{1,0:T(8,128)}, u32[]{:S(2)}) copy-start(f32[32,256]{1,0:T(8,128)} %get-tuple-element.32) | copy-start | bytes 98308
  151.8 4.4 %copy-start.12 = (f32[32,256]{1,0:T(8,128)S(1)}, f32[32,256]{1,0:T(8,128)}, u32[]{:S(2)}) copy-start(f32[32,256]{1,0:T(8,128)} %get-tuple-element.24) | copy-start | bytes 98308
  151.8 4.4 %copy-start.13 = (f32[256,32]{0,1:T(8,128)S(1)}, f32[256,32]{0,1:T(8,128)}, u32[]{:S(2)}) copy-start(f32[256,32]{0,1:T(8,128)} %get-tuple-element.30) | copy-start | bytes 98308
  180.9 23.4 %all-to-all-start = ((f32[1,32,16,128]{3,2,0,1:T(8,128)}), f32[1,32,16,128]{3,2,0,1:T(8,128)}, u32[]{:S(2)}, u32[]{:S(2)}) async-start(f32[1,32,16,128]{3,2,0,1:T(8,128)} %bitcast.209), calls=%async_computation | async-start | bytes 524288 | tf_op jit(solution)/shard_map/all_to_all | solution.py:214
  190.6 2.7 %copy-start.6 = (f32[256,32,64]{0,2,1:T(8,128)S(1)}, f32[256,32,64]{0,2,1:T(8,128)}, u32[]{:S(2)}) copy-start(f32[256,32,64]{0,2,1:T(8,128)} %bitcast_add_fusion.1) | copy-start | bytes 6291460
  190.6 2.7 %copy-start.19 = (f32[32]{0:T(128)S(1)}, f32[32]{0:T(128)}, u32[]{:S(2)}) copy-start(f32[32]{0:T(128)} %param.16) | copy-start | bytes 388
  197.7 8.9 %copy-start.1 = (bf16[1,1,512,2048]{3,2,1,0:T(8,128)(2,1)S(1)}, bf16[1,1,512,2048]{3,2,1,0:T(8,128)(2,1)}, u32[]{:S(2)}) copy-start(bf16[1,1,512,2048]{3,2,1,0:T(8,128)(2,1)} %param.10) | copy-start | bytes 6291460
  (8 other events, 9.4 us)
Sparse Core Ops, SparseCore 0:
  22.1 79.5 all-gather.3
  144.0 30.5 all-gather.5

commit v15 on v14

--- a/solution.py
+++ b/solution.py
@@ -134,10 +134,14 @@
     for distance in range(1, seq_count):
         cycle = [(i, (i + distance) % seq_count) for i in range(seq_count)]
         column_blocks.append(lax.ppermute(w_in, "seq", cycle))
-    by_distance = jnp.stack(column_blocks)
-    from_block = (my_block - jnp.arange(seq_count)) % seq_count
-    in_order = jnp.take(by_distance, from_block, axis=0)
-    wide_rows = jnp.transpose(in_order, (1, 0, 2)).reshape(w_in.shape[0], -1)
+    ordered = []
+    for block in range(seq_count):
+        distance_of = (my_block - block) % seq_count
+        chosen = column_blocks[0]
+        for distance in range(1, seq_count):
+            chosen = jnp.where(distance_of == distance, column_blocks[distance], chosen)
+        ordered.append(chosen)
+    wide_rows = jnp.concatenate(ordered, axis=1)
     projected = jnp.dot(
         tok_rows,
         lax.all_gather(wide_rows, "req", axis=0, tiled=True),

time: 214 us -> 214 us (level)
    ppermute x3, waiting for transfers between devices: 5.42 us -> 9.5 us  [local(): column_blocks.append(lax.ppermute(w_in, 'seq', cycle))]
    all_gather x1, waiting for transfers between devices: 70.4 us -> 67.5 us  [local(): lax.all_gather(wide_rows, 'req', axis=0, tiled=True)]
    another operation x11 -> x10, other arithmetic: 4.96 us -> 3.95 us
  transfers between devices with their start and end apart: 7 -> 7, of which waited for: 4 -> 5; matrix products, arithmetic and copies ran while one was open for 16% -> 18% of each run, Pallas kernels for 3% -> 3%
where the time goes in v15:
time: 214 us
  waiting for transfers between devices  91.1 us (43%)
  matrix products  30.3 us (14%)
  local copies, waits for them, and re-layouts  26 us (12%)
  other arithmetic  19.2 us (9%)
  Pallas kernels  15.8 us (7%)
  between operations  15.8 us (7%)
  starting transfers between devices  15.6 us (7%)
    all_gather x1, waiting for transfers between devices, local(): lax.all_gather(wide_rows, 'req', axis=0, tiled=True)  67.5 us
    all_gather x1, waiting for transfers between devices, local(): gathered = lax.all_gather(packed, 'seq', axis=0, tiled=False)  14 us
    dot_general x1, matrix products, local(): jnp.dot(tok_rows, lax.all_gather(wide_rows, 'req', axis=0, tiled=True), p...  14 us
    unnamed x59, local copies, waits for them, and re-layouts  10.7 us
    ppermute x3, waiting for transfers between devices, local(): column_blocks.append(lax.ppermute(w_in, 'seq', cycle))  9.5 us
    pallas_call x1, Pallas kernels, conv_silu(): pl.pallas_call(conv_kernel, grid=(feats // rows,), in_specs=[pl.BlockSpec...  9.25 us
    dot_general x2, matrix products, block_step(): jnp.einsum('htu,uhp->thp', mixing, heads_x, preferred_element_type=jnp.fl...  8.72 us
    all_to_all x1, starting transfers between devices, local(): lax.all_to_all(share[None], 'req', split_axis=1, concat_axis=0, tiled=True)  7.77 us
  transfers between devices with their start and end apart: 7, of which 5 were waited for; matrix products, arithmetic and copies ran while one was open for 18% of the time, Pallas kernels for 3%

profile of v15, /device:TPU:1, one launch (start us, length us, event | category | flops | bytes accessed | tf_op | source)
XLA Modules:
  0.0 213.8 jit_solution(16857829004412913150)
XLA Ops:
  7.3 3.4 %collective-permute-start = (bf16[64,1096]{1,0:T(8,128)(2,1)}, bf16[64,1096]{1,0:T(8,128)(2,1)S(1)}, u32[]{:S(2)}, u32[]{:S(2)}) collective-permute-start(bf16[64,1096]{1,0:T(8,128)(2,1)} %param.11), channel_id=1, source_target_pairs={{0,3},{1,0},{2,1},{3,2},{4,7},{5,4},{6,5},{7,6},{8,11},{9,8},{10,9... | collective-permute-start | bytes 420872 | tf_op jit(solution)/shard_map/ppermute | solution.py:136
  11.8 4.9 %collective-permute-done = bf16[64,1096]{1,0:T(8,128)(2,1)S(1)} collective-permute-done((bf16[64,1096]{1,0:T(8,128)(2,1)}, bf16[64,1096]{1,0:T(8,128)(2,1)S(1)}, u32[]{:S(2)}, u32[]{:S(2)}) %collective-permute-start) | collective-permute-done | bytes 140320 | tf_op jit(solution)/shard_map/ppermute | solution.py:136
  16.8 4.5 %collective-permute-done.2 = bf16[64,1096]{1,0:T(8,128)(2,1)S(1)} collective-permute-done((bf16[64,1096]{1,0:T(8,128)(2,1)}, bf16[64,1096]{1,0:T(8,128)(2,1)S(1)}, u32[]{:S(2)}, u32[]{:S(2)}) %collective-permute-start.2) | collective-permute-done | bytes 140320 | tf_op jit(solution)/shard_map/ppermute | solution.py:136
  25.5 1.4 copy.79
  26.9 1.4 broadcast_in_dim.151.b_ref
  32.9 67.5 %all-gather.4.cloned.1.call-done = bf16[2048,4384]{1,0:T(8,128)(2,1)} async-done(((bf16[64,4384]{1,0:T(8,128)(2,1)}), bf16[2048,4384]{1,0:T(8,128)(2,1)}) %all-gather.4.cloned.1.call-update) | async-done | bytes 17956880 | tf_op jit(solution)/shard_map/all_gather | solution.py:147
  100.4 14.0 %fusion = bf16[512,4384]{0,1:T(8,128)(2,1)S(1)} fusion(bf16[2048,4384]{1,0:T(8,128)(2,1)} %all-gather.4.cloned.1.call-done, bf16[1,1,512,2048]{3,2,1,0:T(8,128)(2,1)S(1)} %copy-done), kind=kOutput, calls=%fused_computation.4 | convolution fusion | flops 9196158976 | bytes 24543232 | tf_op jit(solution)/shard_map/dot_general | solution.py:145
  114.4 2.0 copy-done.4
  116.4 1.8 fusion.58
  118.7 3.3 %collective-permute-start.3 = (bf16[3,2304]{1,0:T(4,128)(2,1)S(1)}, bf16[3,2304]{1,0:T(4,128)(2,1)S(1)}, u32[]{:S(2)}, u32[]{:S(2)}) collective-permute-start(bf16[3,2304]{1,0:T(4,128)(2,1)S(1)} %copy.77), channel_id=1, source_target_pairs={{0,1},{1,2},{2,3},{4,5},{5,6},{6,7},{8,9},{9,10},{10,11},{12,13},{... | collective-permute-start | bytes 41480 | tf_op jit(solution)/shard_map/ppermute | solution.py:14
  130.6 9.2 %shard_map.113 = bf16[2304,512]{1,0:T(8,128)(2,1)} custom-call(bf16[2304,512]{1,0:T(8,128)(2,1)} %get-tuple-element.15.x_ref, bf16[2304,3]{1,0:T(8,128)(2,1)} %bitcast.195, f32[2304,4]{1,0:T(8,128)} %bitcast.192, f32[2304,1]{1,0:T(8,128)} %broadcast_in_dim.151.b_ref), custom_call_target="tpu_custom_call" | custom-call | flops 16515072 | bytes 4718592 | tf_op jit(solution)/shard_map/pallas_call | solution.py:42
  139.8 2.1 fusion.16
  144.3 3.1 %slice_bitcast_fusion.z_ref = bf16[2048,512]{1,0:T(8,128)(2,1)} fusion(bf16[512,4384]{0,1:T(8,128)(2,1)} %copy-done.4), kind=kLoop, calls=%fused_computation.22 | loop fusion | bytes 4194304 | tf_op jit(solution)/shard_map/transpose | solution.py:209
  147.5 1.5 slice.195
  152.2 4.4 %bitcast_add_fusion.1 = f32[256,32,64]{0,2,1:T(8,128)} fusion(f32[256,32,64]{0,2,1:T(8,128)S(1)} %fusion.23, bf16[256,32,64]{0,2,1:T(8,128)(2,1)S(1)} %bitcast.203, f32[32,256]{1,0:T(8,128)S(1)} %copy-done.14, f32[32,256]{1,0:T(8,128)S(1)} %copy-done.10, f32[256,256]{1,0:T(8,128)S(1)} %fusion.39, pred[256,256]{1,0:T(8,128)(4,1)S(1)} %copy-done.8, ...), kind=kOutput, calls=%fused_computation.29 | convolution fusion | flops 282066944 | bytes 5668864 | tf_op jit(solution)/shard_map/htu,uhp->thp/dot_general | solution.py:99
  156.6 4.3 %bitcast_add_fusion = f32[256,32,64]{0,2,1:T(8,128)} fusion(f32[256,32,64]{0,2,1:T(8,128)S(1)} %fusion.30, bf16[256,32,64]{0,2,1:T(8,128)(2,1)S(1)} %bitcast.202, f32[32,256]{1,0:T(8,128)S(1)} %copy-done.12, f32[32,256]{1,0:T(8,128)S(1)} %copy-done.11, f32[256,256]{1,0:T(8,128)S(1)} %fusion.34, pred[256,256]{1,0:T(8,128)(4,1)S(1)} %copy-done.8, ...), kind=kOutput, calls=%fused_computation.28 | convolution fusion | flops 282066944 | bytes 5668864 | tf_op jit(solution)/shard_map/htu,uhp->thp/dot_general | solution.py:99
  161.0 14.0 %all-gather.6.cloned.1.call-done = bf16[128,8576]{1,0:T(8,128)(2,1)} async-done(((bf16[32,8576]{1,0:T(8,128)(2,1)}), bf16[128,8576]{1,0:T(8,128)(2,1)}) %all-gather.6.cloned.1.call-update) | async-done | bytes 2195472 | tf_op jit(solution)/shard_map/all_gather | solution.py:191
  175.0 2.0 slice_convert_fusion
  177.9 1.5 slice_bitcast_fusion.3
  181.3 7.8 %all-to-all-start = ((f32[1,32,16,128]{3,2,0,1:T(8,128)}), f32[1,32,16,128]{3,2,0,1:T(8,128)}, u32[]{:S(2)}, u32[]{:S(2)}) async-start(f32[1,32,16,128]{3,2,0,1:T(8,128)} %bitcast.201), calls=%async_computation | async-start | bytes 524288 | tf_op jit(solution)/shard_map/all_to_all | solution.py:218
  189.1 1.5 copy.113
  193.7 4.3 %fusion.3 = f32[512,32,64]{0,2,1:T(8,128)} fusion(f32[256,32,64]{0,2,1:T(8,128)S(1)} %copy-done.7, f32[256,32,64]{0,2,1:T(8,128)S(1)} %copy-done.6, bf16[512,32,64]{0,2,1:T(8,128)(2,1)S(1)} %bitcast.190, f32[32,64,128]{2,1,0:T(8,128)S(1)} %fusion.20, f32[32]{0:T(128)S(1)} %copy-done.19, f32[512,32]{0,1:T(8,128)S(1)} %fusion.52, ...), kind=kOutput, calls=%fused_computation.8 | convolution fusion | flops 1616904192 | bytes 11731456 | tf_op jit(solution)/shard_map/tn,hpn->thp/dot_general | solution.py:199
  198.1 6.6 %shard_map.114 = bf16[512,2048]{1,0:T(8,128)(2,1)} custom-call(f32[2048,512]{1,0:T(8,128)} %bitcast.189, bf16[2048,512]{1,0:T(8,128)(2,1)} %slice_bitcast_fusion.z_ref, f32[2048,1]{1,0:T(8,128)} %copy.93.w_ref, f32[1,512]{1,0:T(1,128)} %compare_convert_fusion.mask_ref), custom_call_target="tpu_custom_call" | custom-call | flops 12582912 | bytes 8388608 | tf_op jit(solution)/shard_map/pallas_call | solution.py:70
  204.7 1.5 gather_fusion
  (123 shorter events, 29.9 us)
Async XLA Ops:
  7.2 93.2 %copy-start = (bf16[1,1,512,2048]{3,2,1,0:T(8,128)(2,1)S(1)}, bf16[1,1,512,2048]{3,2,1,0:T(8,128)(2,1)}, u32[]{:S(2)}) copy-start(bf16[1,1,512,2048]{3,2,1,0:T(8,128)(2,1)} %param.10) | copy-start | bytes 6291460
  7.2 16.4 %copy-start.21 = (s32[32]{0:T(128)S(1)}, s32[32]{0:T(128)}, u32[]{:S(2)}) copy-start(s32[32]{0:T(128)} %param.18) | copy-start | bytes 388
  7.2 16.4 %copy-start.22 = (s32[32]{0:T(128)S(1)}, s32[32]{0:T(128)}, u32[]{:S(2)}) copy-start(s32[32]{0:T(128)} %param.19) | copy-start | bytes 388
  7.2 18.3 %copy-start.9 = (f32[4,2304]{1,0:T(4,128)S(1)}, f32[4,2304]{1,0:T(4,128)}, u32[]{:S(2)}) copy-start(f32[4,2304]{1,0:T(4,128)} %param.12) | copy-start | bytes 110596
  7.2 19.7 %copy-start.16 = (f32[2304]{0:T(1024)S(1)}, f32[2304]{0:T(1024)}, u32[]{:S(2)}) copy-start(f32[2304]{0:T(1024)} %param.13) | copy-start | bytes 27652
  7.2 93.1 %all-gather.4.cloned.1.call-start = ((), (), s32[]{:S(2)}) async-start(), calls=%async_computation.1 | async-start | bytes 18923520 | tf_op jit(solution)/shard_map/all_gather | solution.py:147
  7.3 9.4 %collective-permute-start = (bf16[64,1096]{1,0:T(8,128)(2,1)}, bf16[64,1096]{1,0:T(8,128)(2,1)S(1)}, u32[]{:S(2)}, u32[]{:S(2)}) collective-permute-start(bf16[64,1096]{1,0:T(8,128)(2,1)} %param.11), channel_id=1, source_target_pairs={{0,3},{1,0},{2,1},{3,2},{4,7},{5,4},{6,5},{7,6},{8,11},{9,8},{10,9... | collective-permute-start | bytes 420872 | tf_op jit(solution)/shard_map/ppermute | solution.py:136
  10.6 6.1 %collective-permute-start.1 = (bf16[64,1096]{1,0:T(8,128)(2,1)}, bf16[64,1096]{1,0:T(8,128)(2,1)S(1)}, u32[]{:S(2)}, u32[]{:S(2)}) collective-permute-start(bf16[64,1096]{1,0:T(8,128)(2,1)} %param.11), channel_id=1, source_target_pairs={{0,2},{1,3},{2,0},{3,1},{4,6},{5,7},{6,4},{7,5},{8,10},{9,11},{10,... | collective-permute-start | bytes 420872 | tf_op jit(solution)/shard_map/ppermute | solution.py:136
  11.2 10.1 %collective-permute-start.2 = (bf16[64,1096]{1,0:T(8,128)(2,1)}, bf16[64,1096]{1,0:T(8,128)(2,1)S(1)}, u32[]{:S(2)}, u32[]{:S(2)}) collective-permute-start(bf16[64,1096]{1,0:T(8,128)(2,1)} %param.11), channel_id=1, source_target_pairs={{0,1},{1,2},{2,3},{3,0},{4,5},{5,6},{6,7},{7,4},{8,9},{9,10},{10,1... | collective-permute-start | bytes 420872 | tf_op jit(solution)/shard_map/ppermute | solution.py:136
  22.3 6.0 %copy-start.17 = (f32[2048]{0:T(1024)S(1)}, f32[2048]{0:T(1024)}, u32[]{:S(2)}) copy-start(f32[2048]{0:T(1024)} %param.17) | copy-start | bytes 24580
  23.5 9.4 %copy-start.24 = (f32[32]{0:T(128)S(1)}, f32[32]{0:T(128)}, u32[]{:S(2)}) copy-start(f32[32]{0:T(128)} %param.15) | copy-start | bytes 388
  23.5 151.5 %all-gather.6.cloned.1.call-start = ((), (), s32[]{:S(2)}) async-start(), calls=%async_computation.2 | async-start | bytes 2744320 | tf_op jit(solution)/shard_map/all_gather | solution.py:191
  116.4 5.6 %copy-start.18 = (f32[32]{0:T(128)S(1)}, f32[32]{0:T(128)}, u32[]{:S(2)}) copy-start(f32[32]{0:T(128)} %param.14) | copy-start | bytes 388
  118.7 10.7 %collective-permute-start.3 = (bf16[3,2304]{1,0:T(4,128)(2,1)S(1)}, bf16[3,2304]{1,0:T(4,128)(2,1)S(1)}, u32[]{:S(2)}, u32[]{:S(2)}) collective-permute-start(bf16[3,2304]{1,0:T(4,128)(2,1)S(1)} %copy.77), channel_id=1, source_target_pairs={{0,1},{1,2},{2,3},{4,5},{5,6},{6,7},{8,9},{9,10},{10,11},{12,13},{... | collective-permute-start | bytes 41480 | tf_op jit(solution)/shard_map/ppermute | solution.py:14
  139.8 2.3 %copy-start.2 = (bf16[2304,512]{1,0:T(8,128)(2,1)S(1)}, bf16[2304,512]{1,0:T(8,128)(2,1)}, u32[]{:S(2)}) copy-start(bf16[2304,512]{1,0:T(8,128)(2,1)} %shard_map.113) | copy-start | bytes 7077892
  139.8 2.7 %copy-start.20 = (f32[32]{0:T(128)S(1)}, f32[32]{0:T(128)}, u32[]{:S(2)}) copy-start(f32[32]{0:T(128)} %exp.89) | copy-start | bytes 388
  152.2 4.4 %copy-start.11 = (f32[32,256]{1,0:T(8,128)S(1)}, f32[32,256]{1,0:T(8,128)}, u32[]{:S(2)}) copy-start(f32[32,256]{1,0:T(8,128)} %get-tuple-element.36) | copy-start | bytes 98308
  152.2 4.4 %copy-start.12 = (f32[32,256]{1,0:T(8,128)S(1)}, f32[32,256]{1,0:T(8,128)}, u32[]{:S(2)}) copy-start(f32[32,256]{1,0:T(8,128)} %get-tuple-element.28) | copy-start | bytes 98308
  152.2 4.4 %copy-start.13 = (f32[256,32]{0,1:T(8,128)S(1)}, f32[256,32]{0,1:T(8,128)}, u32[]{:S(2)}) copy-start(f32[256,32]{0,1:T(8,128)} %get-tuple-element.34) | copy-start | bytes 98308
  181.3 23.4 %all-to-all-start = ((f32[1,32,16,128]{3,2,0,1:T(8,128)}), f32[1,32,16,128]{3,2,0,1:T(8,128)}, u32[]{:S(2)}, u32[]{:S(2)}) async-start(f32[1,32,16,128]{3,2,0,1:T(8,128)} %bitcast.201), calls=%async_computation | async-start | bytes 524288 | tf_op jit(solution)/shard_map/all_to_all | solution.py:218
  191.0 2.1 copy-start.3
  191.0 2.7 %copy-start.6 = (f32[256,32,64]{0,2,1:T(8,128)S(1)}, f32[256,32,64]{0,2,1:T(8,128)}, u32[]{:S(2)}) copy-start(f32[256,32,64]{0,2,1:T(8,128)} %bitcast_add_fusion.1) | copy-start | bytes 6291460
  191.0 2.7 %copy-start.19 = (f32[32]{0:T(128)S(1)}, f32[32]{0:T(128)}, u32[]{:S(2)}) copy-start(f32[32]{0:T(128)} %param.16) | copy-start | bytes 388
  198.1 8.9 %copy-start.1 = (bf16[1,1,512,2048]{3,2,1,0:T(8,128)(2,1)S(1)}, bf16[1,1,512,2048]{3,2,1,0:T(8,128)(2,1)}, u32[]{:S(2)}) copy-start(bf16[1,1,512,2048]{3,2,1,0:T(8,128)(2,1)} %param.10) | copy-start | bytes 6291460
  (8 other events, 9.4 us)
Sparse Core Ops, SparseCore 0:
  23.6 76.6 all-gather.3
  144.4 30.5 all-gather.5

commit v16 on v14

--- a/solution.py
+++ b/solution.py
@@ -212,7 +212,10 @@
     own_ends = lax.dynamic_slice_in_dim(ends, my_block * piece, piece, axis=2)
     share = jnp.sum(jnp.exp(after)[:, :, None, None] * own_ends, axis=0)
     moved = lax.all_to_all(share[None], "req", split_axis=1, concat_axis=0, tiled=True)
-    final_states = jnp.take(moved, prompt_group, axis=0)
+    pick = (prompt_group[:, None] == jnp.arange(moved.shape[0])[None, :]).astype(jnp.float32)
+    final_states = jnp.einsum(
+        "pg,gabc->pabc", pick, moved, precision=lax.Precision.HIGHEST
+    )
     return (gated_out, final_states)
 
 

time: 214 us -> 213 us (level)
    unnamed x59 -> x58, local copies, waits for them, and re-layouts: 9.4 us -> 10.3 us
where the time goes in v16:
time: 213 us
  waiting for transfers between devices  89.9 us (42%)
  matrix products  31.6 us (15%)
  local copies, waits for them, and re-layouts  24.9 us (12%)
  other arithmetic  17.8 us (8%)
  starting transfers between devices  16.9 us (8%)
  Pallas kernels  15.8 us (7%)
  between operations  15.8 us (7%)
    all_gather x1, waiting for transfers between devices, local(): lax.all_gather(wide_rows, 'req', axis=0, tiled=True)  70.4 us
    all_gather x1, waiting for transfers between devices, local(): gathered = lax.all_gather(packed, 'seq', axis=0, tiled=False)  14 us
    dot_general x1, matrix products, local(): jnp.dot(tok_rows, lax.all_gather(wide_rows, 'req', axis=0, tiled=True), p...  14 us
    unnamed x58, local copies, waits for them, and re-layouts  10.3 us
    pallas_call x1, Pallas kernels, conv_silu(): pl.pallas_call(conv_kernel, grid=(feats // rows,), in_specs=[pl.BlockSpec...  9.25 us
    dot_general x2, matrix products, block_step(): jnp.einsum('htu,uhp->thp', mixing, heads_x, preferred_element_type=jnp.fl...  8.72 us
    all_to_all x1, starting transfers between devices, local(): lax.all_to_all(share[None], 'req', split_axis=1, concat_axis=0, tiled=True)  7.8 us
    pallas_call x1, Pallas kernels, gate_norm(): pl.pallas_call(norm_kernel, grid=(slots // cols,), in_specs=[pl.BlockSpec...  6.59 us
  transfers between devices with their start and end apart: 7, of which 4 were waited for; matrix products, arithmetic and copies ran while one was open for 16% of the time, Pallas kernels for 3%

profile of v16, /device:TPU:1, one launch (start us, length us, event | category | flops | bytes accessed | tf_op | source)
XLA Modules:
  0.0 212.7 jit_solution(11448974472803133246)
XLA Ops:
  7.2 2.1 collective-permute-start
  9.3 2.5 %collective-permute-start.1 = (bf16[64,1096]{1,0:T(8,128)(2,1)}, bf16[64,1096]{1,0:T(8,128)(2,1)S(1)}, u32[]{:S(2)}, u32[]{:S(2)}) collective-permute-start(bf16[64,1096]{1,0:T(8,128)(2,1)} %param.11), channel_id=1, source_target_pairs={{0,2},{1,3},{2,0},{3,1},{4,6},{5,7},{6,4},{7,5},{8,10},{9,11},{10,... | collective-permute-start | bytes 420872 | tf_op jit(solution)/shard_map/ppermute | solution.py:136
  13.9 4.5 %collective-permute-done.1 = bf16[64,1096]{1,0:T(8,128)(2,1)S(1)} collective-permute-done((bf16[64,1096]{1,0:T(8,128)(2,1)}, bf16[64,1096]{1,0:T(8,128)(2,1)S(1)}, u32[]{:S(2)}, u32[]{:S(2)}) %collective-permute-start.1) | collective-permute-done | bytes 140320 | tf_op jit(solution)/shard_map/ppermute | solution.py:136
  24.0 1.4 copy.88
  25.4 1.4 broadcast_in_dim.150.b_ref
  26.8 1.4 copy.102.w_ref
  31.3 70.4 %all-gather.4.cloned.1.call-done = bf16[2048,4384]{1,0:T(8,128)(2,1)} async-done(((bf16[64,4384]{1,0:T(8,128)(2,1)}), bf16[2048,4384]{1,0:T(8,128)(2,1)}) %all-gather.4.cloned.1.call-update) | async-done | bytes 17956880 | tf_op jit(solution)/shard_map/all_gather | solution.py:143
  101.8 14.0 %fusion = bf16[512,4384]{0,1:T(8,128)(2,1)S(1)} fusion(bf16[2048,4384]{1,0:T(8,128)(2,1)} %all-gather.4.cloned.1.call-done, bf16[1,1,512,2048]{3,2,1,0:T(8,128)(2,1)S(1)} %copy-done), kind=kOutput, calls=%fused_computation.4 | convolution fusion | flops 9196158976 | bytes 24543232 | tf_op jit(solution)/shard_map/dot_general | solution.py:141
  115.8 2.0 fusion.65
  122.5 3.3 %collective-permute-start.3 = (bf16[3,2304]{1,0:T(4,128)(2,1)S(1)}, bf16[3,2304]{1,0:T(4,128)(2,1)S(1)}, u32[]{:S(2)}, u32[]{:S(2)}) collective-permute-start(bf16[3,2304]{1,0:T(4,128)(2,1)S(1)} %copy.86), channel_id=1, source_target_pairs={{0,1},{1,2},{2,3},{4,5},{5,6},{6,7},{8,9},{9,10},{10,11},{12,13},{... | collective-permute-start | bytes 41480 | tf_op jit(solution)/shard_map/ppermute | solution.py:14
  129.6 9.2 %shard_map.113 = bf16[2304,512]{1,0:T(8,128)(2,1)} custom-call(bf16[2304,512]{1,0:T(8,128)(2,1)} %get-tuple-element.21.x_ref, bf16[2304,3]{1,0:T(8,128)(2,1)} %bitcast.206, f32[2304,4]{1,0:T(8,128)} %bitcast.203, f32[2304,1]{1,0:T(8,128)} %broadcast_in_dim.150.b_ref), custom_call_target="tpu_custom_call" | custom-call | flops 16515072 | bytes 4718592 | tf_op jit(solution)/shard_map/pallas_call | solution.py:42
  138.9 2.1 fusion.16
  143.3 3.1 %slice_bitcast_fusion.z_ref = bf16[2048,512]{1,0:T(8,128)(2,1)} fusion(bf16[512,4384]{0,1:T(8,128)(2,1)} %copy-done.4), kind=kLoop, calls=%fused_computation.22 | loop fusion | bytes 4194304 | tf_op jit(solution)/shard_map/transpose | solution.py:205
  146.5 1.5 slice.195
  151.3 4.4 %bitcast_add_fusion.1 = f32[256,32,64]{0,2,1:T(8,128)} fusion(f32[256,32,64]{0,2,1:T(8,128)S(1)} %fusion.23, bf16[256,32,64]{0,2,1:T(8,128)(2,1)S(1)} %bitcast.214, f32[32,256]{1,0:T(8,128)S(1)} %copy-done.14, f32[32,256]{1,0:T(8,128)S(1)} %copy-done.10, f32[256,256]{1,0:T(8,128)S(1)} %fusion.40, pred[256,256]{1,0:T(8,128)(4,1)S(1)} %copy-done.8, ...), kind=kOutput, calls=%fused_computation.29 | convolution fusion | flops 282066944 | bytes 5668864 | tf_op jit(solution)/shard_map/htu,uhp->thp/dot_general | solution.py:99
  155.7 4.3 %bitcast_add_fusion = f32[256,32,64]{0,2,1:T(8,128)} fusion(f32[256,32,64]{0,2,1:T(8,128)S(1)} %fusion.31, bf16[256,32,64]{0,2,1:T(8,128)(2,1)S(1)} %bitcast.213, f32[32,256]{1,0:T(8,128)S(1)} %copy-done.12, f32[32,256]{1,0:T(8,128)S(1)} %copy-done.11, f32[256,256]{1,0:T(8,128)S(1)} %fusion.35, pred[256,256]{1,0:T(8,128)(4,1)S(1)} %copy-done.8, ...), kind=kOutput, calls=%fused_computation.28 | convolution fusion | flops 282066944 | bytes 5668864 | tf_op jit(solution)/shard_map/htu,uhp->thp/dot_general | solution.py:99
  160.0 14.0 %all-gather.6.cloned.1.call-done = bf16[128,8576]{1,0:T(8,128)(2,1)} async-done(((bf16[32,8576]{1,0:T(8,128)(2,1)}), bf16[128,8576]{1,0:T(8,128)(2,1)}) %all-gather.6.cloned.1.call-update) | async-done | bytes 2195472 | tf_op jit(solution)/shard_map/all_gather | solution.py:187
  174.0 2.0 slice_convert_fusion
  176.9 1.5 slice_bitcast_fusion.3
  180.3 7.8 %all-to-all-start = ((f32[1,32,16,128]{3,2,0,1:T(8,128)}), f32[1,32,16,128]{3,2,0,1:T(8,128)}, u32[]{:S(2)}, u32[]{:S(2)}) async-start(f32[1,32,16,128]{3,2,0,1:T(8,128)} %bitcast.212), calls=%async_computation | async-start | bytes 524288 | tf_op jit(solution)/shard_map/all_to_all | solution.py:214
  188.2 1.5 copy.124
  192.8 4.4 %fusion.3 = f32[512,32,64]{0,2,1:T(8,128)} fusion(f32[256,32,64]{0,2,1:T(8,128)S(1)} %copy-done.7, f32[256,32,64]{0,2,1:T(8,128)S(1)} %copy-done.6, bf16[512,32,64]{0,2,1:T(8,128)(2,1)S(1)} %bitcast.201, f32[32,64,128]{2,1,0:T(8,128)S(1)} %fusion.20, f32[32]{0:T(128)S(1)} %copy-done.20, f32[512,32]{0,1:T(8,128)S(1)} %fusion.59, ...), kind=kOutput, calls=%fused_computation.8 | convolution fusion | flops 1616904192 | bytes 11731456 | tf_op jit(solution)/shard_map/tn,hpn->thp/dot_general | solution.py:195
  197.2 6.6 %shard_map.114 = bf16[512,2048]{1,0:T(8,128)(2,1)} custom-call(f32[2048,512]{1,0:T(8,128)} %bitcast.200, bf16[2048,512]{1,0:T(8,128)(2,1)} %slice_bitcast_fusion.z_ref, f32[2048,1]{1,0:T(8,128)} %copy.102.w_ref, f32[1,512]{1,0:T(1,128)} %compare_convert_fusion.mask_ref), custom_call_target="tpu_custom_call" | custom-call | flops 12582912 | bytes 8388608 | tf_op jit(solution)/shard_map/pallas_call | solution.py:70
  203.7 1.3 convolution_bitcast_fusion
  (125 shorter events, 30.3 us)
Async XLA Ops:
  7.2 94.6 %copy-start = (bf16[1,1,512,2048]{3,2,1,0:T(8,128)(2,1)S(1)}, bf16[1,1,512,2048]{3,2,1,0:T(8,128)(2,1)}, u32[]{:S(2)}) copy-start(bf16[1,1,512,2048]{3,2,1,0:T(8,128)(2,1)} %param.10) | copy-start | bytes 6291460
  7.2 94.6 %all-gather.4.cloned.1.call-start = ((), (), s32[]{:S(2)}) async-start(), calls=%async_computation.1 | async-start | bytes 18923520 | tf_op jit(solution)/shard_map/all_gather | solution.py:143
  7.2 6.7 %collective-permute-start = (bf16[64,1096]{1,0:T(8,128)(2,1)}, bf16[64,1096]{1,0:T(8,128)(2,1)S(1)}, u32[]{:S(2)}, u32[]{:S(2)}) collective-permute-start(bf16[64,1096]{1,0:T(8,128)(2,1)} %param.11), channel_id=1, source_target_pairs={{0,1},{1,2},{2,3},{3,0},{4,5},{5,6},{6,7},{7,4},{8,9},{9,10},{10,1... | collective-permute-start | bytes 420872 | tf_op jit(solution)/shard_map/ppermute | solution.py:136
  9.3 9.1 %collective-permute-start.1 = (bf16[64,1096]{1,0:T(8,128)(2,1)}, bf16[64,1096]{1,0:T(8,128)(2,1)S(1)}, u32[]{:S(2)}, u32[]{:S(2)}) collective-permute-start(bf16[64,1096]{1,0:T(8,128)(2,1)} %param.11), channel_id=1, source_target_pairs={{0,2},{1,3},{2,0},{3,1},{4,6},{5,7},{6,4},{7,5},{8,10},{9,11},{10,... | collective-permute-start | bytes 420872 | tf_op jit(solution)/shard_map/ppermute | solution.py:136
  11.8 6.6 %collective-permute-start.2 = (bf16[64,1096]{1,0:T(8,128)(2,1)}, bf16[64,1096]{1,0:T(8,128)(2,1)S(1)}, u32[]{:S(2)}, u32[]{:S(2)}) collective-permute-start(bf16[64,1096]{1,0:T(8,128)(2,1)} %param.11), channel_id=1, source_target_pairs={{0,3},{1,0},{2,1},{3,2},{4,7},{5,4},{6,5},{7,6},{8,11},{9,8},{10,9... | collective-permute-start | bytes 420872 | tf_op jit(solution)/shard_map/ppermute | solution.py:136
  19.4 2.6 %copy-start.18 = (s32[32]{0:T(128)S(1)}, s32[32]{0:T(128)}, u32[]{:S(2)}) copy-start(s32[32]{0:T(128)} %param.19) | copy-start | bytes 388
  19.4 2.6 %copy-start.22 = (s32[32]{0:T(128)S(1)}, s32[32]{0:T(128)}, u32[]{:S(2)}) copy-start(s32[32]{0:T(128)} %param.18) | copy-start | bytes 388
  19.4 4.6 %copy-start.9 = (f32[4,2304]{1,0:T(4,128)S(1)}, f32[4,2304]{1,0:T(4,128)}, u32[]{:S(2)}) copy-start(f32[4,2304]{1,0:T(4,128)} %param.12) | copy-start | bytes 110596
  20.2 5.2 %copy-start.16 = (f32[2304]{0:T(1024)S(1)}, f32[2304]{0:T(1024)}, u32[]{:S(2)}) copy-start(f32[2304]{0:T(1024)} %param.13) | copy-start | bytes 27652
  20.7 6.1 %copy-start.17 = (f32[2048]{0:T(1024)S(1)}, f32[2048]{0:T(1024)}, u32[]{:S(2)}) copy-start(f32[2048]{0:T(1024)} %param.17) | copy-start | bytes 24580
  22.0 9.4 %copy-start.23 = (f32[32]{0:T(128)S(1)}, f32[32]{0:T(128)}, u32[]{:S(2)}) copy-start(f32[32]{0:T(128)} %param.15) | copy-start | bytes 388
  22.0 152.0 %all-gather.6.cloned.1.call-start = ((), (), s32[]{:S(2)}) async-start(), calls=%async_computation.2 | async-start | bytes 2744320 | tf_op jit(solution)/shard_map/all_gather | solution.py:187
  115.8 2.8 %copy-start.4 = (bf16[512,4384]{0,1:T(8,128)(2,1)}, bf16[512,4384]{0,1:T(8,128)(2,1)S(1)}, u32[]{:S(2)}) copy-start(bf16[512,4384]{0,1:T(8,128)(2,1)S(1)} %fusion) | copy-start | bytes 13467652
  115.8 2.8 %copy-start.19 = (f32[32]{0:T(128)S(1)}, f32[32]{0:T(128)}, u32[]{:S(2)}) copy-start(f32[32]{0:T(128)} %param.14) | copy-start | bytes 388
  122.5 5.9 %collective-permute-start.3 = (bf16[3,2304]{1,0:T(4,128)(2,1)S(1)}, bf16[3,2304]{1,0:T(4,128)(2,1)S(1)}, u32[]{:S(2)}, u32[]{:S(2)}) collective-permute-start(bf16[3,2304]{1,0:T(4,128)(2,1)S(1)} %copy.86), channel_id=1, source_target_pairs={{0,1},{1,2},{2,3},{4,5},{5,6},{6,7},{8,9},{9,10},{10,11},{12,13},{... | collective-permute-start | bytes 41480 | tf_op jit(solution)/shard_map/ppermute | solution.py:14
  138.9 2.3 %copy-start.2 = (bf16[2304,512]{1,0:T(8,128)(2,1)S(1)}, bf16[2304,512]{1,0:T(8,128)(2,1)}, u32[]{:S(2)}) copy-start(bf16[2304,512]{1,0:T(8,128)(2,1)} %shard_map.113) | copy-start | bytes 7077892
  151.3 4.4 %copy-start.11 = (f32[32,256]{1,0:T(8,128)S(1)}, f32[32,256]{1,0:T(8,128)}, u32[]{:S(2)}) copy-start(f32[32,256]{1,0:T(8,128)} %get-tuple-element.38) | copy-start | bytes 98308
  151.3 4.4 %copy-start.12 = (f32[32,256]{1,0:T(8,128)S(1)}, f32[32,256]{1,0:T(8,128)}, u32[]{:S(2)}) copy-start(f32[32,256]{1,0:T(8,128)} %get-tuple-element.30) | copy-start | bytes 98308
  151.3 4.4 %copy-start.13 = (f32[256,32]{0,1:T(8,128)S(1)}, f32[256,32]{0,1:T(8,128)}, u32[]{:S(2)}) copy-start(f32[256,32]{0,1:T(8,128)} %get-tuple-element.36) | copy-start | bytes 98308
  180.3 23.4 %all-to-all-start = ((f32[1,32,16,128]{3,2,0,1:T(8,128)}), f32[1,32,16,128]{3,2,0,1:T(8,128)}, u32[]{:S(2)}, u32[]{:S(2)}) async-start(f32[1,32,16,128]{3,2,0,1:T(8,128)} %bitcast.212), calls=%async_computation | async-start | bytes 524288 | tf_op jit(solution)/shard_map/all_to_all | solution.py:214
  190.1 2.1 copy-start.3
  190.1 2.7 %copy-start.6 = (f32[256,32,64]{0,2,1:T(8,128)S(1)}, f32[256,32,64]{0,2,1:T(8,128)}, u32[]{:S(2)}) copy-start(f32[256,32,64]{0,2,1:T(8,128)} %bitcast_add_fusion.1) | copy-start | bytes 6291460
  190.1 2.7 %copy-start.20 = (f32[32]{0:T(128)S(1)}, f32[32]{0:T(128)}, u32[]{:S(2)}) copy-start(f32[32]{0:T(128)} %param.16) | copy-start | bytes 388
  197.1 8.7 %copy-start.1 = (bf16[1,1,512,2048]{3,2,1,0:T(8,128)(2,1)S(1)}, bf16[1,1,512,2048]{3,2,1,0:T(8,128)(2,1)}, u32[]{:S(2)}) copy-start(bf16[1,1,512,2048]{3,2,1,0:T(8,128)(2,1)} %param.10) | copy-start | bytes 6291460
  (7 other events, 7.3 us)
Sparse Core Ops, SparseCore 0:
  22.1 79.5 all-gather.3
  143.4 30.5 all-gather.5

commit v17 on v14

--- a/solution.py
+++ b/solution.py
@@ -184,6 +184,18 @@
         [local_end.reshape(heads, hdim * nstate).astype(jnp.bfloat16), parts.reshape(heads, 3 * 128)],
         axis=1,
     )
+    piece = hdim // seq_count
+    slices = local_end.reshape(heads, seq_count, piece, nstate)
+    own_total = jnp.broadcast_to(block_total[:, None, None, None], (heads, seq_count, 1, nstate))
+    payload = jnp.concatenate([slices, own_total], axis=2).reshape(heads * seq_count, piece + 1, nstate)
+    received = lax.all_to_all(payload, ("req", "seq"), split_axis=0, concat_axis=0, tiled=True)
+    received = received.reshape(-1, seq_count, piece + 1, nstate)
+    group_totals = received[:, :, piece, 0]
+    later_mask = jnp.arange(seq_count)[None, :] > jnp.arange(seq_count)[:, None]
+    group_after = jnp.sum(
+        jnp.where(later_mask[None, :, :], group_totals[:, None, :], 0.0), axis=2
+    )
+    group_final = jnp.sum(jnp.exp(group_after)[:, :, None, None] * received[:, :, :piece, :], axis=1)
     gathered = lax.all_gather(packed, "seq", axis=0, tiled=False)
     ends = gathered[:, :, : hdim * nstate].astype(jnp.float32).reshape(seq_count, heads, hdim, nstate)
     sent = gathered[:, :, hdim * nstate :].astype(jnp.float32)
@@ -206,13 +218,10 @@
         norm_weight[:, None],
         filled.astype(jnp.float32)[None, :],
     ).reshape(1, 1, slots, inner)
-    later_mask = jnp.arange(seq_count)[None, :] > jnp.arange(seq_count)[:, None]
-    after = jnp.sum(jnp.where(later_mask[:, :, None], totals[None, :, :], 0.0), axis=1)
-    piece = hdim // seq_count
-    own_ends = lax.dynamic_slice_in_dim(ends, my_block * piece, piece, axis=2)
-    share = jnp.sum(jnp.exp(after)[:, :, None, None] * own_ends, axis=0)
-    moved = lax.all_to_all(share[None], "req", split_axis=1, concat_axis=0, tiled=True)
-    final_states = jnp.take(moved, prompt_group, axis=0)
+    pick = (prompt_group[:, None] == jnp.arange(group_final.shape[0])[None, :]).astype(jnp.float32)
+    final_states = jnp.einsum(
+        "pg,gbc->pbc", pick, group_final, precision=lax.Precision.HIGHEST
+    )[:, None]
     return (gated_out, final_states)
 
 

time: 214 us -> 220 us (1.028)
  local copies, waits for them, and re-layouts: 26.1 us -> 29.6 us
  waiting for transfers between devices: 89.9 us -> 92.6 us
  other arithmetic: 18.6 us -> 16.4 us
    all_to_all x1, waiting for transfers between devices: 0.01 us -> 13 us  [local(): lax.all_to_all(payload, ('req', 'seq'), split_axis=0, concat_axis=0, tile...]
    all_gather x1, waiting for transfers between devices: 14 us -> 3.03 us  [local(): gathered = lax.all_gather(packed, 'seq', axis=0, tiled=False)]
    unnamed x59 -> x55, local copies, waits for them, and re-layouts: 9.4 us -> 8.3 us
  transfers between devices with their start and end apart: 7 -> 7, of which waited for: 4 -> 5; matrix products, arithmetic and copies ran while one was open for 16% -> 14% of each run, Pallas kernels for 3% -> 0%
where the time goes in v17:
time: 220 us; the launch traced here: 219 us
  waiting for transfers between devices  92.6 us (42%)
  matrix products  32.1 us (15%)
  local copies, waits for them, and re-layouts  29.6 us (13%)
  starting transfers between devices  17.1 us (8%)
  other arithmetic  16.4 us (7%)
  Pallas kernels  15.8 us (7%)
  between operations  15.8 us (7%)
    all_gather x1, waiting for transfers between devices, local(): lax.all_gather(wide_rows, 'req', axis=0, tiled=True)  71 us
    dot_general x1, matrix products, local(): jnp.dot(tok_rows, lax.all_gather(wide_rows, 'req', axis=0, tiled=True), p...  14 us
    all_to_all x1, waiting for transfers between devices, local(): lax.all_to_all(payload, ('req', 'seq'), split_axis=0, concat_axis=0, tile...  13 us
    pallas_call x1, Pallas kernels, conv_silu(): pl.pallas_call(conv_kernel, grid=(feats // rows,), in_specs=[pl.BlockSpec...  9.2 us
    dot_general x2, matrix products, block_step(): jnp.einsum('htu,uhp->thp', mixing, heads_x, preferred_element_type=jnp.fl...  8.75 us
    unnamed x55, local copies, waits for them, and re-layouts  8.3 us
    all_to_all x1, starting transfers between devices, local(): lax.all_to_all(payload, ('req', 'seq'), split_axis=0, concat_axis=0, tile...  8.06 us
    pallas_call x1, Pallas kernels, gate_norm(): pl.pallas_call(norm_kernel, grid=(slots // cols,), in_specs=[pl.BlockSpec...  6.59 us
  transfers between devices with their start and end apart: 7, of which 5 were waited for; matrix products, arithmetic and copies ran while one was open for 14% of the time, Pallas kernels for 0%

profile of v17, /device:TPU:1, one launch (start us, length us, event | category | flops | bytes accessed | tf_op | source)
XLA Modules:
  0.0 219.5 jit_solution(5157390003627572978)
XLA Ops:
  7.2 2.1 collective-permute-start
  9.3 2.5 %collective-permute-start.1 = (bf16[64,1096]{1,0:T(8,128)(2,1)}, bf16[64,1096]{1,0:T(8,128)(2,1)S(1)}, u32[]{:S(2)}, u32[]{:S(2)}) collective-permute-start(bf16[64,1096]{1,0:T(8,128)(2,1)} %param.11), channel_id=1, source_target_pairs={{0,2},{1,3},{2,0},{3,1},{4,6},{5,7},{6,4},{7,5},{8,10},{9,11},{10,... | collective-permute-start | bytes 420872 | tf_op jit(solution)/shard_map/ppermute | solution.py:136
  13.9 4.5 %collective-permute-done.1 = bf16[64,1096]{1,0:T(8,128)(2,1)S(1)} collective-permute-done((bf16[64,1096]{1,0:T(8,128)(2,1)}, bf16[64,1096]{1,0:T(8,128)(2,1)S(1)}, u32[]{:S(2)}, u32[]{:S(2)}) %collective-permute-start.1) | collective-permute-done | bytes 140320 | tf_op jit(solution)/shard_map/ppermute | solution.py:136
  24.0 1.4 copy.95
  25.4 1.4 broadcast_in_dim.167.b_ref
  26.8 1.4 copy.109.w_ref
  30.7 71.0 %all-gather.4.cloned.1.call-done = bf16[2048,4384]{1,0:T(8,128)(2,1)} async-done(((bf16[64,4384]{1,0:T(8,128)(2,1)}), bf16[2048,4384]{1,0:T(8,128)(2,1)}) %all-gather.4.cloned.1.call-update) | async-done | bytes 17956880 | tf_op jit(solution)/shard_map/all_gather | solution.py:143
  101.8 14.0 %fusion = bf16[512,4384]{0,1:T(8,128)(2,1)S(1)} fusion(bf16[2048,4384]{1,0:T(8,128)(2,1)} %all-gather.4.cloned.1.call-done, bf16[1,1,512,2048]{3,2,1,0:T(8,128)(2,1)S(1)} %copy-done), kind=kOutput, calls=%fused_computation.4 | convolution fusion | flops 9196158976 | bytes 24543232 | tf_op jit(solution)/shard_map/dot_general | solution.py:141
  115.8 2.0 fusion.61
  120.2 3.1 %slice_bitcast_fusion.z_ref = bf16[2048,512]{1,0:T(8,128)(2,1)} fusion(bf16[512,4384]{0,1:T(8,128)(2,1)} %copy-done.4), kind=kLoop, calls=%fused_computation.22 | loop fusion | bytes 4194304 | tf_op jit(solution)/shard_map/transpose | solution.py:217
  127.2 3.3 %collective-permute-start.3 = (bf16[3,2304]{1,0:T(4,128)(2,1)S(1)}, bf16[3,2304]{1,0:T(4,128)(2,1)S(1)}, u32[]{:S(2)}, u32[]{:S(2)}) collective-permute-start(bf16[3,2304]{1,0:T(4,128)(2,1)S(1)} %copy.93), channel_id=1, source_target_pairs={{0,1},{1,2},{2,3},{4,5},{5,6},{6,7},{8,9},{9,10},{10,11},{12,13},{... | collective-permute-start | bytes 41480 | tf_op jit(solution)/shard_map/ppermute | solution.py:14
  133.6 9.2 %shard_map.113 = bf16[2304,512]{1,0:T(8,128)(2,1)} custom-call(bf16[2304,512]{1,0:T(8,128)(2,1)} %get-tuple-element.19.x_ref, bf16[2304,3]{1,0:T(8,128)(2,1)} %bitcast.203, f32[2304,4]{1,0:T(8,128)} %bitcast.197, f32[2304,1]{1,0:T(8,128)} %broadcast_in_dim.167.b_ref), custom_call_target="tpu_custom_call" | custom-call | flops 16515072 | bytes 4718592 | tf_op jit(solution)/shard_map/pallas_call | solution.py:42
  142.8 3.2 %slice.203 = bf16[512,2048]{0,1:T(8,128)(2,1)} slice(bf16[512,2304]{0,1:T(8,128)(2,1)} %bitcast.185), slice={[0:512], [0:2048]} | slice | bytes 4194304 | tf_op jit(solution)/shard_map/slice | solution.py:152
  148.3 1.3 pad_maximum_fusion
  149.6 8.1 %all-to-all-start = ((f32[128,17,128]{2,1,0:T(8,128)}), f32[128,17,128]{2,1,0:T(8,128)}, u32[]{:S(2)}, u32[]{:S(2)}) async-start(f32[128,17,128]{2,1,0:T(8,128)} %pad_maximum_fusion), calls=%async_computation | async-start | bytes 3145728 | tf_op jit(solution)/shard_map/all_to_all | solution.py:191
  157.7 1.4 copy.157
  162.0 4.4 %bitcast_add_fusion.1 = f32[256,32,64]{0,2,1:T(8,128)} fusion(f32[256,32,64]{0,2,1:T(8,128)S(1)} %fusion.23, bf16[256,32,64]{0,2,1:T(8,128)(2,1)S(1)} %bitcast.210, f32[32,256]{1,0:T(8,128)S(1)} %copy-done.14, f32[32,256]{1,0:T(8,128)S(1)} %copy-done.10, f32[256,256]{1,0:T(8,128)S(1)} %fusion.38, pred[256,256]{1,0:T(8,128)(4,1)S(1)} %copy-done.8, ...), kind=kOutput, calls=%fused_computation.29 | convolution fusion | flops 282066944 | bytes 5668864 | tf_op jit(solution)/shard_map/htu,uhp->thp/dot_general | solution.py:99
  167.6 4.3 %bitcast_add_fusion = f32[256,32,64]{0,2,1:T(8,128)} fusion(f32[256,32,64]{0,2,1:T(8,128)S(1)} %fusion.29, bf16[256,32,64]{0,2,1:T(8,128)(2,1)S(1)} %bitcast.209, f32[32,256]{1,0:T(8,128)S(1)} %copy-done.12, f32[32,256]{1,0:T(8,128)S(1)} %copy-done.11, f32[256,256]{1,0:T(8,128)S(1)} %fusion.33, pred[256,256]{1,0:T(8,128)(4,1)S(1)} %copy-done.8, ...), kind=kOutput, calls=%fused_computation.28 | convolution fusion | flops 282066944 | bytes 5668864 | tf_op jit(solution)/shard_map/htu,uhp->thp/dot_general | solution.py:99
  172.0 13.0 %all-to-all-done = f32[128,17,128]{2,1,0:T(8,128)} async-done(((f32[128,17,128]{2,1,0:T(8,128)}), f32[128,17,128]{2,1,0:T(8,128)}, u32[]{:S(2)}, u32[]{:S(2)}) %all-to-all-start) | async-done | bytes 1114144 | tf_op jit(solution)/shard_map/all_to_all | solution.py:191
  185.0 1.7 copy.110
  192.2 3.0 %all-gather.6.cloned.1.call-done = bf16[128,8576]{1,0:T(8,128)(2,1)} async-done(((bf16[32,8576]{1,0:T(8,128)(2,1)}), bf16[128,8576]{1,0:T(8,128)(2,1)}) %all-gather.6.cloned.1.call-update) | async-done | bytes 2195472 | tf_op jit(solution)/shard_map/all_gather | solution.py:199
  195.2 2.0 slice_convert_fusion
  201.7 4.3 %fusion.3 = f32[512,32,64]{0,2,1:T(8,128)} fusion(f32[256,32,64]{0,2,1:T(8,128)S(1)} %copy-done.6, f32[256,32,64]{0,2,1:T(8,128)S(1)} %copy-done.5, bf16[512,32,64]{0,2,1:T(8,128)(2,1)S(1)} %bitcast.196, f32[32,64,128]{2,1,0:T(8,128)S(1)} %fusion.19, f32[32]{0:T(128)S(1)} %copy-done.20, f32[512,32]{0,1:T(8,128)S(1)} %fusion.57, ...), kind=kOutput, calls=%fused_computation.8 | convolution fusion | flops 1616904192 | bytes 11731456 | tf_op jit(solution)/shard_map/tn,hpn->thp/dot_general | solution.py:207
  206.0 6.6 %shard_map.114 = bf16[512,2048]{1,0:T(8,128)(2,1)} custom-call(f32[2048,512]{1,0:T(8,128)} %bitcast.195, bf16[2048,512]{1,0:T(8,128)(2,1)} %slice_bitcast_fusion.z_ref, f32[2048,1]{1,0:T(8,128)} %copy.109.w_ref, f32[1,512]{1,0:T(1,128)} %compare_convert_fusion.mask_ref), custom_call_target="tpu_custom_call" | custom-call | flops 12582912 | bytes 8388608 | tf_op jit(solution)/shard_map/pallas_call | solution.py:70
  (130 shorter events, 34.5 us)
Async XLA Ops:
  7.2 94.6 %copy-start = (bf16[1,1,512,2048]{3,2,1,0:T(8,128)(2,1)S(1)}, bf16[1,1,512,2048]{3,2,1,0:T(8,128)(2,1)}, u32[]{:S(2)}) copy-start(bf16[1,1,512,2048]{3,2,1,0:T(8,128)(2,1)} %param.10) | copy-start | bytes 6291460
  7.2 94.6 %all-gather.4.cloned.1.call-start = ((), (), s32[]{:S(2)}) async-start(), calls=%async_computation.1 | async-start | bytes 18923520 | tf_op jit(solution)/shard_map/all_gather | solution.py:143
  7.2 6.7 %collective-permute-start = (bf16[64,1096]{1,0:T(8,128)(2,1)}, bf16[64,1096]{1,0:T(8,128)(2,1)S(1)}, u32[]{:S(2)}, u32[]{:S(2)}) collective-permute-start(bf16[64,1096]{1,0:T(8,128)(2,1)} %param.11), channel_id=1, source_target_pairs={{0,1},{1,2},{2,3},{3,0},{4,5},{5,6},{6,7},{7,4},{8,9},{9,10},{10,1... | collective-permute-start | bytes 420872 | tf_op jit(solution)/shard_map/ppermute | solution.py:136
  9.3 9.1 %collective-permute-start.1 = (bf16[64,1096]{1,0:T(8,128)(2,1)}, bf16[64,1096]{1,0:T(8,128)(2,1)S(1)}, u32[]{:S(2)}, u32[]{:S(2)}) collective-permute-start(bf16[64,1096]{1,0:T(8,128)(2,1)} %param.11), channel_id=1, source_target_pairs={{0,2},{1,3},{2,0},{3,1},{4,6},{5,7},{6,4},{7,5},{8,10},{9,11},{10,... | collective-permute-start | bytes 420872 | tf_op jit(solution)/shard_map/ppermute | solution.py:136
  11.8 6.6 %collective-permute-start.2 = (bf16[64,1096]{1,0:T(8,128)(2,1)}, bf16[64,1096]{1,0:T(8,128)(2,1)S(1)}, u32[]{:S(2)}, u32[]{:S(2)}) collective-permute-start(bf16[64,1096]{1,0:T(8,128)(2,1)} %param.11), channel_id=1, source_target_pairs={{0,3},{1,0},{2,1},{3,2},{4,7},{5,4},{6,5},{7,6},{8,11},{9,8},{10,9... | collective-permute-start | bytes 420872 | tf_op jit(solution)/shard_map/ppermute | solution.py:136
  19.4 2.6 %copy-start.18 = (s32[32]{0:T(128)S(1)}, s32[32]{0:T(128)}, u32[]{:S(2)}) copy-start(s32[32]{0:T(128)} %param.19) | copy-start | bytes 388
  19.4 2.6 %copy-start.21 = (s32[32]{0:T(128)S(1)}, s32[32]{0:T(128)}, u32[]{:S(2)}) copy-start(s32[32]{0:T(128)} %param.18) | copy-start | bytes 388
  19.4 4.5 %copy-start.9 = (f32[4,2304]{1,0:T(4,128)S(1)}, f32[4,2304]{1,0:T(4,128)}, u32[]{:S(2)}) copy-start(f32[4,2304]{1,0:T(4,128)} %param.12) | copy-start | bytes 110596
  20.2 5.1 %copy-start.16 = (f32[2304]{0:T(1024)S(1)}, f32[2304]{0:T(1024)}, u32[]{:S(2)}) copy-start(f32[2304]{0:T(1024)} %param.13) | copy-start | bytes 27652
  20.7 6.1 %copy-start.17 = (f32[2048]{0:T(1024)S(1)}, f32[2048]{0:T(1024)}, u32[]{:S(2)}) copy-start(f32[2048]{0:T(1024)} %param.17) | copy-start | bytes 24580
  22.0 8.7 %copy-start.22 = (f32[32]{0:T(128)S(1)}, f32[32]{0:T(128)}, u32[]{:S(2)}) copy-start(f32[32]{0:T(128)} %param.15) | copy-start | bytes 388
  115.8 2.8 %copy-start.4 = (bf16[512,4384]{0,1:T(8,128)(2,1)}, bf16[512,4384]{0,1:T(8,128)(2,1)S(1)}, u32[]{:S(2)}) copy-start(bf16[512,4384]{0,1:T(8,128)(2,1)S(1)} %fusion) | copy-start | bytes 13467652
  115.8 2.8 %copy-start.19 = (f32[32]{0:T(128)S(1)}, f32[32]{0:T(128)}, u32[]{:S(2)}) copy-start(f32[32]{0:T(128)} %param.14) | copy-start | bytes 388
  127.2 5.2 %collective-permute-start.3 = (bf16[3,2304]{1,0:T(4,128)(2,1)S(1)}, bf16[3,2304]{1,0:T(4,128)(2,1)S(1)}, u32[]{:S(2)}, u32[]{:S(2)}) collective-permute-start(bf16[3,2304]{1,0:T(4,128)(2,1)S(1)} %copy.93), channel_id=1, source_target_pairs={{0,1},{1,2},{2,3},{4,5},{5,6},{6,7},{8,9},{9,10},{10,11},{12,13},{... | collective-permute-start | bytes 41480 | tf_op jit(solution)/shard_map/ppermute | solution.py:14
  142.8 3.2 %copy-start.2 = (bf16[2304,512]{1,0:T(8,128)(2,1)S(1)}, bf16[2304,512]{1,0:T(8,128)(2,1)}, u32[]{:S(2)}) copy-start(bf16[2304,512]{1,0:T(8,128)(2,1)} %shard_map.113) | copy-start | bytes 7077892
  149.6 9.5 %copy-start.7 = (bf16[4,8,3,128]{3,1,2,0:T(8,128)(2,1)S(1)}, bf16[4,8,3,128]{3,1,2,0:T(8,128)(2,1)}, u32[]{:S(2)}) copy-start(bf16[4,8,3,128]{3,1,2,0:T(8,128)(2,1)} %copy.159) | copy-start | bytes 73732
  149.6 35.4 %all-to-all-start = ((f32[128,17,128]{2,1,0:T(8,128)}), f32[128,17,128]{2,1,0:T(8,128)}, u32[]{:S(2)}, u32[]{:S(2)}) async-start(f32[128,17,128]{2,1,0:T(8,128)} %pad_maximum_fusion), calls=%async_computation | async-start | bytes 3145728 | tf_op jit(solution)/shard_map/all_to_all | solution.py:191
  157.6 37.6 %all-gather.6.cloned.1.call-start = ((), (), s32[]{:S(2)}) async-start(), calls=%async_computation.2 | async-start | bytes 2744320 | tf_op jit(solution)/shard_map/all_gather | solution.py:199
  166.4 1.2 copy-start.13
  198.8 1.6 copy-start.6
  199.0 2.1 copy-start.3
  199.0 2.7 %copy-start.5 = (f32[256,32,64]{0,2,1:T(8,128)S(1)}, f32[256,32,64]{0,2,1:T(8,128)}, u32[]{:S(2)}) copy-start(f32[256,32,64]{0,2,1:T(8,128)} %bitcast_add_fusion.1) | copy-start | bytes 6291460
  199.0 2.7 %copy-start.20 = (f32[32]{0:T(128)S(1)}, f32[32]{0:T(128)}, u32[]{:S(2)}) copy-start(f32[32]{0:T(128)} %param.16) | copy-start | bytes 388
  206.0 6.6 %copy-start.1 = (bf16[1,1,512,2048]{3,2,1,0:T(8,128)(2,1)S(1)}, bf16[1,1,512,2048]{3,2,1,0:T(8,128)(2,1)}, u32[]{:S(2)}) copy-start(bf16[1,1,512,2048]{3,2,1,0:T(8,128)(2,1)} %param.10) | copy-start | bytes 6291460
  (6 other events, 5.8 us)
Sparse Core Ops, SparseCore 0:
  22.1 79.5 all-gather.3
  160.1 35.0 all-gather.5

commit v18 on v16

--- a/solution.py
+++ b/solution.py
@@ -211,7 +211,9 @@
     piece = hdim // seq_count
     own_ends = lax.dynamic_slice_in_dim(ends, my_block * piece, piece, axis=2)
     share = jnp.sum(jnp.exp(after)[:, :, None, None] * own_ends, axis=0)
-    moved = lax.all_to_all(share[None], "req", split_axis=1, concat_axis=0, tiled=True)
+    moved = lax.all_to_all(
+        share[None].astype(jnp.bfloat16), "req", split_axis=1, concat_axis=0, tiled=True
+    ).astype(jnp.float32)
     pick = (prompt_group[:, None] == jnp.arange(moved.shape[0])[None, :]).astype(jnp.float32)
     final_states = jnp.einsum(
         "pg,gabc->pabc", pick, moved, precision=lax.Precision.HIGHEST

time: 213 us -> 212 us (level)
  no operation moved by 1% of the time
where the time goes in v18:
time: 212 us; the launch traced here: 211 us
  waiting for transfers between devices  89.9 us (42%)
  matrix products  30.5 us (14%)
  local copies, waits for them, and re-layouts  25 us (12%)
  other arithmetic  17.7 us (8%)
  starting transfers between devices  16.8 us (8%)
  Pallas kernels  15.8 us (7%)
  between operations  15.8 us (7%)
    all_gather x1, waiting for transfers between devices, local(): lax.all_gather(wide_rows, 'req', axis=0, tiled=True)  71 us
    dot_general x1, matrix products, local(): jnp.dot(tok_rows, lax.all_gather(wide_rows, 'req', axis=0, tiled=True), p...  14 us
    all_gather x1, waiting for transfers between devices, local(): gathered = lax.all_gather(packed, 'seq', axis=0, tiled=False)  13.4 us
    unnamed x58, local copies, waits for them, and re-layouts  10.3 us
    pallas_call x1, Pallas kernels, conv_silu(): pl.pallas_call(conv_kernel, grid=(feats // rows,), in_specs=[pl.BlockSpec...  9.25 us
    dot_general x2, matrix products, block_step(): jnp.einsum('htu,uhp->thp', mixing, heads_x, preferred_element_type=jnp.fl...  8.74 us
    all_to_all x1, starting transfers between devices, local(): lax.all_to_all(share[None].astype(jnp.bfloat16), 'req', split_axis=1, con...  7.71 us
    pallas_call x1, Pallas kernels, gate_norm(): pl.pallas_call(norm_kernel, grid=(slots // cols,), in_specs=[pl.BlockSpec...  6.59 us
  transfers between devices with their start and end apart: 7, of which 4 were waited for; matrix products, arithmetic and copies ran while one was open for 16% of the time, Pallas kernels for 3%

profile of v18, /device:TPU:1, one launch (start us, length us, event | category | flops | bytes accessed | tf_op | source)
XLA Modules:
  0.0 211.5 jit_solution(6416176909525175191)
XLA Ops:
  7.2 2.1 collective-permute-start
  9.3 2.5 %collective-permute-start.1 = (bf16[64,1096]{1,0:T(8,128)(2,1)}, bf16[64,1096]{1,0:T(8,128)(2,1)S(1)}, u32[]{:S(2)}, u32[]{:S(2)}) collective-permute-start(bf16[64,1096]{1,0:T(8,128)(2,1)} %param.11), channel_id=1, source_target_pairs={{0,2},{1,3},{2,0},{3,1},{4,6},{5,7},{6,4},{7,5},{8,10},{9,11},{10,... | collective-permute-start | bytes 420872 | tf_op jit(solution)/shard_map/ppermute | solution.py:136
  13.9 4.5 %collective-permute-done.1 = bf16[64,1096]{1,0:T(8,128)(2,1)S(1)} collective-permute-done((bf16[64,1096]{1,0:T(8,128)(2,1)}, bf16[64,1096]{1,0:T(8,128)(2,1)S(1)}, u32[]{:S(2)}, u32[]{:S(2)}) %collective-permute-start.1) | collective-permute-done | bytes 140320 | tf_op jit(solution)/shard_map/ppermute | solution.py:136
  24.0 1.4 copy.88
  25.4 1.4 broadcast_in_dim.147.b_ref
  26.8 1.4 copy.102.w_ref
  28.8 1.2 compare_convert_fusion.mask_ref
  30.8 71.0 %all-gather.4.cloned.1.call-done = bf16[2048,4384]{1,0:T(8,128)(2,1)} async-done(((bf16[64,4384]{1,0:T(8,128)(2,1)}), bf16[2048,4384]{1,0:T(8,128)(2,1)}) %all-gather.4.cloned.1.call-update) | async-done | bytes 17956880 | tf_op jit(solution)/shard_map/all_gather | solution.py:143
  101.8 14.0 %fusion = bf16[512,4384]{0,1:T(8,128)(2,1)S(1)} fusion(bf16[2048,4384]{1,0:T(8,128)(2,1)} %all-gather.4.cloned.1.call-done, bf16[1,1,512,2048]{3,2,1,0:T(8,128)(2,1)S(1)} %copy-done), kind=kOutput, calls=%fused_computation.4 | convolution fusion | flops 9196158976 | bytes 24543232 | tf_op jit(solution)/shard_map/dot_general | solution.py:141
  115.8 2.0 fusion.65
  121.9 3.3 %collective-permute-start.3 = (bf16[3,2304]{1,0:T(4,128)(2,1)S(1)}, bf16[3,2304]{1,0:T(4,128)(2,1)S(1)}, u32[]{:S(2)}, u32[]{:S(2)}) collective-permute-start(bf16[3,2304]{1,0:T(4,128)(2,1)S(1)} %copy.86), channel_id=1, source_target_pairs={{0,1},{1,2},{2,3},{4,5},{5,6},{6,7},{8,9},{9,10},{10,11},{12,13},{... | collective-permute-start | bytes 41480 | tf_op jit(solution)/shard_map/ppermute | solution.py:14
  129.0 9.2 %shard_map.113 = bf16[2304,512]{1,0:T(8,128)(2,1)} custom-call(bf16[2304,512]{1,0:T(8,128)(2,1)} %get-tuple-element.21.x_ref, bf16[2304,3]{1,0:T(8,128)(2,1)} %bitcast.208, f32[2304,4]{1,0:T(8,128)} %bitcast.205, f32[2304,1]{1,0:T(8,128)} %broadcast_in_dim.147.b_ref), custom_call_target="tpu_custom_call" | custom-call | flops 16515072 | bytes 4718592 | tf_op jit(solution)/shard_map/pallas_call | solution.py:42
  138.3 2.1 fusion.16
  142.7 3.1 %slice_bitcast_fusion.z_ref = bf16[2048,512]{1,0:T(8,128)(2,1)} fusion(bf16[512,4384]{0,1:T(8,128)(2,1)} %copy-done.4), kind=kLoop, calls=%fused_computation.22 | loop fusion | bytes 4194304 | tf_op jit(solution)/shard_map/transpose | solution.py:205
  146.5 1.5 slice.195
  151.3 4.4 %bitcast_add_fusion.1 = f32[256,32,64]{0,2,1:T(8,128)} fusion(f32[256,32,64]{0,2,1:T(8,128)S(1)} %fusion.23, bf16[256,32,64]{0,2,1:T(8,128)(2,1)S(1)} %bitcast.215, f32[32,256]{1,0:T(8,128)S(1)} %copy-done.15, f32[32,256]{1,0:T(8,128)S(1)} %get-tuple-element.39, f32[256,256]{1,0:T(8,128)S(1)} %fusion.40, pred[256,256]{1,0:T(8,128)(4,1)S(1)} %copy-done.10, ...), kind=kOutput, calls=%fused_computation.29 | convolution fusion | flops 282066944 | bytes 5668864 | tf_op jit(solution)/shard_map/htu,uhp->thp/dot_general | solution.py:99
  155.7 4.3 %bitcast_add_fusion = f32[256,32,64]{0,2,1:T(8,128)} fusion(f32[256,32,64]{0,2,1:T(8,128)S(1)} %fusion.31, bf16[256,32,64]{0,2,1:T(8,128)(2,1)S(1)} %bitcast.214, f32[32,256]{1,0:T(8,128)S(1)} %copy-done.13, f32[32,256]{1,0:T(8,128)S(1)} %copy-done.12, f32[256,256]{1,0:T(8,128)S(1)} %fusion.35, pred[256,256]{1,0:T(8,128)(4,1)S(1)} %copy-done.10, ...), kind=kOutput, calls=%fused_computation.28 | convolution fusion | flops 282066944 | bytes 5668864 | tf_op jit(solution)/shard_map/htu,uhp->thp/dot_general | solution.py:99
  160.0 13.4 %all-gather.6.cloned.1.call-done = bf16[128,8576]{1,0:T(8,128)(2,1)} async-done(((bf16[32,8576]{1,0:T(8,128)(2,1)}), bf16[128,8576]{1,0:T(8,128)(2,1)}) %all-gather.6.cloned.1.call-update) | async-done | bytes 2195472 | tf_op jit(solution)/shard_map/all_gather | solution.py:187
  173.5 2.0 slice_convert_fusion
  176.4 1.5 slice_bitcast_fusion.3
  180.2 7.7 %all-to-all-start = ((bf16[1,32,16,128]{3,2,0,1:T(8,128)(2,1)}), bf16[1,32,16,128]{3,2,0,1:T(8,128)(2,1)S(1)}, u32[]{:S(2)}, u32[]{:S(2)}) async-start(bf16[1,32,16,128]{3,2,0,1:T(8,128)(2,1)} %bitcast.174), calls=%async_computation | async-start | bytes 262144 | tf_op jit(solution)/shard_map/all_to_all | solution.py:214
  188.0 1.5 copy.124
  192.6 4.3 %fusion.3 = f32[512,32,64]{0,2,1:T(8,128)} fusion(f32[256,32,64]{0,2,1:T(8,128)S(1)} %copy-done.7, f32[256,32,64]{0,2,1:T(8,128)S(1)} %copy-done.6, bf16[512,32,64]{0,2,1:T(8,128)(2,1)S(1)} %bitcast.203, f32[32,64,128]{2,1,0:T(8,128)S(1)} %fusion.20, f32[32]{0:T(128)S(1)} %copy-done.21, f32[512,32]{0,1:T(8,128)S(1)} %copy-done.8, ...), kind=kOutput, calls=%fused_computation.8 | convolution fusion | flops 1616904192 | bytes 11731456 | tf_op jit(solution)/shard_map/tn,hpn->thp/dot_general | solution.py:195
  197.0 6.6 %shard_map.114 = bf16[512,2048]{1,0:T(8,128)(2,1)} custom-call(f32[2048,512]{1,0:T(8,128)} %bitcast.202, bf16[2048,512]{1,0:T(8,128)(2,1)} %slice_bitcast_fusion.z_ref, f32[2048,1]{1,0:T(8,128)} %copy.102.w_ref, f32[1,512]{1,0:T(1,128)} %compare_convert_fusion.mask_ref), custom_call_target="tpu_custom_call" | custom-call | flops 12582912 | bytes 8388608 | tf_op jit(solution)/shard_map/pallas_call | solution.py:70
  (125 shorter events, 29.2 us)
Async XLA Ops:
  7.2 94.6 %copy-start = (bf16[1,1,512,2048]{3,2,1,0:T(8,128)(2,1)S(1)}, bf16[1,1,512,2048]{3,2,1,0:T(8,128)(2,1)}, u32[]{:S(2)}) copy-start(bf16[1,1,512,2048]{3,2,1,0:T(8,128)(2,1)} %param.10) | copy-start | bytes 6291460
  7.2 94.6 %all-gather.4.cloned.1.call-start = ((), (), s32[]{:S(2)}) async-start(), calls=%async_computation.1 | async-start | bytes 18923520 | tf_op jit(solution)/shard_map/all_gather | solution.py:143
  7.2 6.7 %collective-permute-start = (bf16[64,1096]{1,0:T(8,128)(2,1)}, bf16[64,1096]{1,0:T(8,128)(2,1)S(1)}, u32[]{:S(2)}, u32[]{:S(2)}) collective-permute-start(bf16[64,1096]{1,0:T(8,128)(2,1)} %param.11), channel_id=1, source_target_pairs={{0,1},{1,2},{2,3},{3,0},{4,5},{5,6},{6,7},{7,4},{8,9},{9,10},{10,1... | collective-permute-start | bytes 420872 | tf_op jit(solution)/shard_map/ppermute | solution.py:136
  9.3 9.1 %collective-permute-start.1 = (bf16[64,1096]{1,0:T(8,128)(2,1)}, bf16[64,1096]{1,0:T(8,128)(2,1)S(1)}, u32[]{:S(2)}, u32[]{:S(2)}) collective-permute-start(bf16[64,1096]{1,0:T(8,128)(2,1)} %param.11), channel_id=1, source_target_pairs={{0,2},{1,3},{2,0},{3,1},{4,6},{5,7},{6,4},{7,5},{8,10},{9,11},{10,... | collective-permute-start | bytes 420872 | tf_op jit(solution)/shard_map/ppermute | solution.py:136
  11.8 6.6 %collective-permute-start.2 = (bf16[64,1096]{1,0:T(8,128)(2,1)}, bf16[64,1096]{1,0:T(8,128)(2,1)S(1)}, u32[]{:S(2)}, u32[]{:S(2)}) collective-permute-start(bf16[64,1096]{1,0:T(8,128)(2,1)} %param.11), channel_id=1, source_target_pairs={{0,3},{1,0},{2,1},{3,2},{4,7},{5,4},{6,5},{7,6},{8,11},{9,8},{10,9... | collective-permute-start | bytes 420872 | tf_op jit(solution)/shard_map/ppermute | solution.py:136
  19.4 2.6 %copy-start.19 = (s32[32]{0:T(128)S(1)}, s32[32]{0:T(128)}, u32[]{:S(2)}) copy-start(s32[32]{0:T(128)} %param.19) | copy-start | bytes 388
  19.4 2.6 %copy-start.22 = (s32[32]{0:T(128)S(1)}, s32[32]{0:T(128)}, u32[]{:S(2)}) copy-start(s32[32]{0:T(128)} %param.18) | copy-start | bytes 388
  19.4 4.6 %copy-start.11 = (f32[4,2304]{1,0:T(4,128)S(1)}, f32[4,2304]{1,0:T(4,128)}, u32[]{:S(2)}) copy-start(f32[4,2304]{1,0:T(4,128)} %param.12) | copy-start | bytes 110596
  20.2 5.2 %copy-start.17 = (f32[2304]{0:T(1024)S(1)}, f32[2304]{0:T(1024)}, u32[]{:S(2)}) copy-start(f32[2304]{0:T(1024)} %param.13) | copy-start | bytes 27652
  20.7 6.1 %copy-start.18 = (f32[2048]{0:T(1024)S(1)}, f32[2048]{0:T(1024)}, u32[]{:S(2)}) copy-start(f32[2048]{0:T(1024)} %param.17) | copy-start | bytes 24580
  22.0 8.8 %copy-start.23 = (f32[32]{0:T(128)S(1)}, f32[32]{0:T(128)}, u32[]{:S(2)}) copy-start(f32[32]{0:T(128)} %param.15) | copy-start | bytes 388
  22.0 151.5 %all-gather.6.cloned.1.call-start = ((), (), s32[]{:S(2)}) async-start(), calls=%async_computation.2 | async-start | bytes 2744320 | tf_op jit(solution)/shard_map/all_gather | solution.py:187
  115.8 2.8 %copy-start.4 = (bf16[512,4384]{0,1:T(8,128)(2,1)}, bf16[512,4384]{0,1:T(8,128)(2,1)S(1)}, u32[]{:S(2)}) copy-start(bf16[512,4384]{0,1:T(8,128)(2,1)S(1)} %fusion) | copy-start | bytes 13467652
  115.8 2.8 %copy-start.20 = (f32[32]{0:T(128)S(1)}, f32[32]{0:T(128)}, u32[]{:S(2)}) copy-start(f32[32]{0:T(128)} %param.14) | copy-start | bytes 388
  121.9 6.0 %collective-permute-start.3 = (bf16[3,2304]{1,0:T(4,128)(2,1)S(1)}, bf16[3,2304]{1,0:T(4,128)(2,1)S(1)}, u32[]{:S(2)}, u32[]{:S(2)}) collective-permute-start(bf16[3,2304]{1,0:T(4,128)(2,1)S(1)} %copy.86), channel_id=1, source_target_pairs={{0,1},{1,2},{2,3},{4,5},{5,6},{6,7},{8,9},{9,10},{10,11},{12,13},{... | collective-permute-start | bytes 41480 | tf_op jit(solution)/shard_map/ppermute | solution.py:14
  138.3 2.3 %copy-start.2 = (bf16[2304,512]{1,0:T(8,128)(2,1)S(1)}, bf16[2304,512]{1,0:T(8,128)(2,1)}, u32[]{:S(2)}) copy-start(bf16[2304,512]{1,0:T(8,128)(2,1)} %shard_map.113) | copy-start | bytes 7077892
  151.3 4.4 %copy-start.12 = (f32[32,256]{1,0:T(8,128)S(1)}, f32[32,256]{1,0:T(8,128)}, u32[]{:S(2)}) copy-start(f32[32,256]{1,0:T(8,128)} %get-tuple-element.38) | copy-start | bytes 98308
  151.3 4.4 %copy-start.13 = (f32[32,256]{1,0:T(8,128)S(1)}, f32[32,256]{1,0:T(8,128)}, u32[]{:S(2)}) copy-start(f32[32,256]{1,0:T(8,128)} %get-tuple-element.30) | copy-start | bytes 98308
  151.3 4.4 %copy-start.14 = (f32[256,32]{0,1:T(8,128)S(1)}, f32[256,32]{0,1:T(8,128)}, u32[]{:S(2)}) copy-start(f32[256,32]{0,1:T(8,128)} %get-tuple-element.36) | copy-start | bytes 98308
  180.2 23.3 %all-to-all-start = ((bf16[1,32,16,128]{3,2,0,1:T(8,128)(2,1)}), bf16[1,32,16,128]{3,2,0,1:T(8,128)(2,1)S(1)}, u32[]{:S(2)}, u32[]{:S(2)}) async-start(bf16[1,32,16,128]{3,2,0,1:T(8,128)(2,1)} %bitcast.174), calls=%async_computation | async-start | bytes 262144 | tf_op jit(solution)/shard_map/all_to_all | solution.py:214
  189.9 2.1 copy-start.3
  189.9 2.7 %copy-start.6 = (f32[256,32,64]{0,2,1:T(8,128)S(1)}, f32[256,32,64]{0,2,1:T(8,128)}, u32[]{:S(2)}) copy-start(f32[256,32,64]{0,2,1:T(8,128)} %bitcast_add_fusion.1) | copy-start | bytes 6291460
  189.9 2.7 %copy-start.21 = (f32[32]{0:T(128)S(1)}, f32[32]{0:T(128)}, u32[]{:S(2)}) copy-start(f32[32]{0:T(128)} %param.16) | copy-start | bytes 388
  197.0 7.7 %copy-start.1 = (bf16[1,1,512,2048]{3,2,1,0:T(8,128)(2,1)S(1)}, bf16[1,1,512,2048]{3,2,1,0:T(8,128)(2,1)}, u32[]{:S(2)}) copy-start(bf16[1,1,512,2048]{3,2,1,0:T(8,128)(2,1)} %param.10) | copy-start | bytes 6291460
  (7 other events, 8.2 us)
Sparse Core Ops, SparseCore 0:
  22.1 79.5 all-gather.3
  142.8 30.5 all-gather.5

commit v19 on v16

--- a/solution.py
+++ b/solution.py
@@ -56,22 +56,26 @@
     )(conv_t, edge_t, weight_t, bias_t)
 
 
-def norm_kernel(y_ref, z_ref, w_ref, mask_ref, o_ref):
+def norm_kernel(out_ref, inc_ref, x_ref, skip_ref, z_ref, w_ref, mask_ref, o_ref):
     z = z_ref[...].astype(jnp.float32)
-    gated = y_ref[...] * (z * (0.5 + 0.5 * jnp.tanh(0.5 * z)))
+    y = out_ref[...] + inc_ref[...] + skip_ref[...] * x_ref[...].astype(jnp.float32)
+    gated = y * (z * (0.5 + 0.5 * jnp.tanh(0.5 * z)))
     mean = jnp.sum(gated * gated, axis=0, keepdims=True) * (1.0 / gated.shape[0])
     normed = gated * lax.rsqrt(mean + 1e-05) * w_ref[...]
     normed = jnp.where(mask_ref[...] > 0.5, normed, 0.0)
     o_ref[...] = normed.T.astype(o_ref.dtype)
 
 
-def gate_norm(y_t, z_t, weight, mask, cols=128):
-    units, slots = y_t.shape
+def gate_norm(out_t, inc_t, x_t, skip, z_t, weight, mask, cols=128):
+    units, slots = out_t.shape
     return pl.pallas_call(
         norm_kernel,
         grid=(slots // cols,),
         in_specs=[
             pl.BlockSpec((units, cols), lambda i: (0, i)),
+            pl.BlockSpec((units, cols), lambda i: (0, i)),
+            pl.BlockSpec((units, cols), lambda i: (0, i)),
+            pl.BlockSpec((units, 1), lambda i: (0, 0)),
             pl.BlockSpec((units, cols), lambda i: (0, i)),
             pl.BlockSpec((units, 1), lambda i: (0, 0)),
             pl.BlockSpec((1, cols), lambda i: (0, i)),
@@ -81,7 +85,7 @@
         cost_estimate=pl.CostEstimate(
             flops=units * slots * 12, transcendentals=units * slots, bytes_accessed=units * slots * 8
         ),
-    )(y_t, z_t, weight, mask)
+    )(out_t, inc_t, x_t, skip, z_t, weight, mask)
 
 
 def block_step(state, pieces):
@@ -195,13 +199,11 @@
     incoming = jnp.exp(through)[:, :, None] * jnp.einsum(
         "tn,hpn->thp", c_rows.astype(jnp.float32), entering, precision=lax.Precision.HIGHEST
     )
-    heads_y = (
-        outputs.reshape(slots, heads, hdim)
-        + incoming
-        + d_skip[None, :, None] * inputs_x.astype(jnp.float32).reshape(slots, heads, hdim)
-    )
     gated_out = gate_norm(
-        heads_y.reshape(slots, inner).T,
+        outputs.reshape(slots, inner).T,
+        incoming.reshape(slots, inner).T,
+        inputs_x.T,
+        jnp.repeat(d_skip, hdim)[:, None],
         gate_z.T,
         norm_weight[:, None],
         filled.astype(jnp.float32)[None, :],

time: 213 us -> 218 us (1.023)
  Pallas kernels: 15.8 us -> 19.3 us
    pallas_call x1, Pallas kernels: 6.59 us -> 10 us  [gate_norm(): pl.pallas_call(norm_kernel, grid=(slots // cols,), in_specs=[pl.BlockSpec...]
    dot_general x2, matrix products: 8.72 us -> 5.42 us  [block_step(): jnp.einsum('htu,uhp->thp', mixing, heads_x, preferred_element_type=jnp.fl...]
    all_gather x1, waiting for transfers between devices: 14 us -> 17 us  [local(): gathered = lax.all_gather(packed, 'seq', axis=0, tiled=False)]
    transpose x0 -> x1, other arithmetic: none -> 2.51 us  [local(): outputs.reshape(slots, inner)]
    dot_general x2, matrix products: 1.95 us -> 4.26 us  [block_step(): jnp.einsum('tn,hpn->thp', c_rows.astype(jnp.float32), state, precision=la...]
    unnamed x58 -> x52, local copies, waits for them, and re-layouts: 10.3 us -> 9.11 us
  transfers between devices with their start and end apart: 7 -> 7, of which waited for: 4 -> 4; matrix products, arithmetic and copies ran while one was open for 16% -> 14% of each run, Pallas kernels for 3% -> 5%
where the time goes in v19:
time: 218 us
  waiting for transfers between devices  91.4 us (42%)
  matrix products  31.6 us (14%)
  local copies, waits for them, and re-layouts  25.4 us (12%)
  Pallas kernels  19.3 us (9%)
  other arithmetic  17.3 us (8%)
  starting transfers between devices  16.8 us (8%)
  between operations  15.8 us (7%)
    all_gather x1, waiting for transfers between devices, local(): lax.all_gather(wide_rows, 'req', axis=0, tiled=True)  68.9 us
    all_gather x1, waiting for transfers between devices, local(): gathered = lax.all_gather(packed, 'seq', axis=0, tiled=False)  17 us
    dot_general x1, matrix products, local(): jnp.dot(tok_rows, lax.all_gather(wide_rows, 'req', axis=0, tiled=True), p...  14 us
    pallas_call x1, Pallas kernels, gate_norm(): pl.pallas_call(norm_kernel, grid=(slots // cols,), in_specs=[pl.BlockSpec...  10 us
    pallas_call x1, Pallas kernels, conv_silu(): pl.pallas_call(conv_kernel, grid=(feats // rows,), in_specs=[pl.BlockSpec...  9.25 us
    unnamed x52, local copies, waits for them, and re-layouts  9.11 us
    all_to_all x1, starting transfers between devices, local(): lax.all_to_all(share[None], 'req', split_axis=1, concat_axis=0, tiled=True)  7.77 us
    ppermute x3, starting transfers between devices, local(): column_blocks.append(lax.ppermute(w_in, 'seq', cycle))  5.71 us
  transfers between devices with their start and end apart: 7, of which 4 were waited for; matrix products, arithmetic and copies ran while one was open for 14% of the time, Pallas kernels for 5%

profile of v19, /device:TPU:1, one launch (start us, length us, event | category | flops | bytes accessed | tf_op | source)
XLA Modules:
  0.0 217.6 jit_solution(10914015791718095128)
XLA Ops:
  7.2 2.1 collective-permute-start
  9.3 2.5 %collective-permute-start.1 = (bf16[64,1096]{1,0:T(8,128)(2,1)}, bf16[64,1096]{1,0:T(8,128)(2,1)S(1)}, u32[]{:S(2)}, u32[]{:S(2)}) collective-permute-start(bf16[64,1096]{1,0:T(8,128)(2,1)} %param.11), channel_id=1, source_target_pairs={{0,2},{1,3},{2,0},{3,1},{4,6},{5,7},{6,4},{7,5},{8,10},{9,11},{10,... | collective-permute-start | bytes 420872 | tf_op jit(solution)/shard_map/ppermute | solution.py:140
  13.9 4.5 %collective-permute-done.1 = bf16[64,1096]{1,0:T(8,128)(2,1)S(1)} collective-permute-done((bf16[64,1096]{1,0:T(8,128)(2,1)}, bf16[64,1096]{1,0:T(8,128)(2,1)S(1)}, u32[]{:S(2)}, u32[]{:S(2)}) %collective-permute-start.1) | collective-permute-done | bytes 140320 | tf_op jit(solution)/shard_map/ppermute | solution.py:140
  24.1 1.4 copy.91
  26.9 2.0 broadcast_in_dim_reshape.4.skip_ref
  32.9 68.9 %all-gather.4.cloned.1.call-done = bf16[2048,4384]{1,0:T(8,128)(2,1)} async-done(((bf16[64,4384]{1,0:T(8,128)(2,1)}), bf16[2048,4384]{1,0:T(8,128)(2,1)}) %all-gather.4.cloned.1.call-update) | async-done | bytes 17956880 | tf_op jit(solution)/shard_map/all_gather | solution.py:147
  101.8 14.0 %fusion = bf16[512,4384]{0,1:T(8,128)(2,1)S(1)} fusion(bf16[2048,4384]{1,0:T(8,128)(2,1)} %all-gather.4.cloned.1.call-done, bf16[1,1,512,2048]{3,2,1,0:T(8,128)(2,1)S(1)} %copy-done), kind=kOutput, calls=%fused_computation.4 | convolution fusion | flops 9196158976 | bytes 24543232 | tf_op jit(solution)/shard_map/dot_general | solution.py:145
  115.8 2.0 fusion.64
  123.6 3.3 %collective-permute-start.3 = (bf16[3,2304]{1,0:T(4,128)(2,1)S(1)}, bf16[3,2304]{1,0:T(4,128)(2,1)S(1)}, u32[]{:S(2)}, u32[]{:S(2)}) collective-permute-start(bf16[3,2304]{1,0:T(4,128)(2,1)S(1)} %copy.89), channel_id=1, source_target_pairs={{0,1},{1,2},{2,3},{4,5},{5,6},{6,7},{8,9},{9,10},{10,11},{12,13},{... | collective-permute-start | bytes 41480 | tf_op jit(solution)/shard_map/ppermute | solution.py:14
  129.1 9.2 %shard_map.113 = bf16[2304,512]{1,0:T(8,128)(2,1)} custom-call(bf16[2304,512]{1,0:T(8,128)(2,1)} %get-tuple-element.21.x_ref, bf16[2304,3]{1,0:T(8,128)(2,1)} %bitcast.209, f32[2304,4]{1,0:T(8,128)} %bitcast.206, f32[2304,1]{1,0:T(8,128)} %broadcast_in_dim.153.b_ref), custom_call_target="tpu_custom_call" | custom-call | flops 16515072 | bytes 4718592 | tf_op jit(solution)/shard_map/pallas_call | solution.py:42
  138.4 3.3 %fusion.22 = f32[256,32,64]{0,2,1:T(8,128)} fusion(bf16[512,2304]{0,1:T(8,128)(2,1)} %bitcast.193), kind=kOutput, calls=%fused_computation.49 | convolution fusion | flops 805306368 | bytes 2162688 | tf_op jit(solution)/shard_map/tn,hpn->thp/dot_general | solution.py:104
  141.7 1.8 fusion.39
  147.4 1.4 copy-done.5
  148.8 2.7 %bitcast_add_fusion.1 = f32[256,32,64]{0,2,1:T(8,128)S(1)} fusion(f32[256,32,64]{0,2,1:T(8,128)S(1)} %copy-done.5, bf16[256,32,64]{0,2,1:T(8,128)(2,1)S(1)} %bitcast.219, f32[32,256]{1,0:T(8,128)S(1)} %copy-done.12, f32[32,256]{1,0:T(8,128)S(1)} %get-tuple-element.39, f32[256,256]{1,0:T(8,128)S(1)} %copy-done.6, pred[256,256]{1,0:T(8,128)(4,1)S(1)} %copy-done.7, ...), kind=kOutput, calls=%fused_computation.29 | convolution fusion | flops 282066944 | bytes 5668864 | tf_op jit(solution)/shard_map/htu,uhp->thp/dot_general | solution.py:103
  151.6 2.7 %bitcast_add_fusion = f32[256,32,64]{0,2,1:T(8,128)S(1)} fusion(f32[256,32,64]{0,2,1:T(8,128)S(1)} %fusion.30, bf16[256,32,64]{0,2,1:T(8,128)(2,1)S(1)} %bitcast.218, f32[32,256]{1,0:T(8,128)S(1)} %copy-done.10, f32[32,256]{1,0:T(8,128)S(1)} %copy-done.9, f32[256,256]{1,0:T(8,128)S(1)} %fusion.34, pred[256,256]{1,0:T(8,128)(4,1)S(1)} %copy-done.7, ...), kind=kOutput, calls=%fused_computation.28 | convolution fusion | flops 282066944 | bytes 5668864 | tf_op jit(solution)/shard_map/htu,uhp->thp/dot_general | solution.py:103
  154.3 2.5 %maximum_bitcast_fusion.out_ref = f32[2048,512]{1,0:T(8,128)} fusion(f32[256,2048]{0,1:T(8,128)S(1)} %bitcast.216, f32[256,2048]{0,1:T(8,128)S(1)} %bitcast.215), kind=kLoop, calls=%fused_computation.7 | loop fusion | flops 1048576 | bytes 8388608 | tf_op jit(solution)/shard_map/transpose | solution.py:203
  156.8 4.1 %slice_bitcast_fusion = (bf16[2048,512]{1,0:T(8,128)(2,1)}, bf16[2048,512]{1,0:T(8,128)(2,1)}) fusion(bf16[512,4384]{0,1:T(8,128)(2,1)} %copy-done.3, bf16[512,2304]{0,1:T(8,128)(2,1)S(1)} %bitcast.201), kind=kLoop, calls=%fused_computation.21 | loop fusion | bytes 8388608 | tf_op jit(solution)/shard_map/transpose | solution.py:207
  160.9 17.0 %all-gather.6.cloned.1.call-done = bf16[128,8576]{1,0:T(8,128)(2,1)} async-done(((bf16[32,8576]{1,0:T(8,128)(2,1)}), bf16[128,8576]{1,0:T(8,128)(2,1)}) %all-gather.6.cloned.1.call-update) | async-done | bytes 2195472 | tf_op jit(solution)/shard_map/all_gather | solution.py:191
  177.9 2.0 slice_convert_fusion
  180.8 1.6 slice_bitcast_fusion.4
  184.3 7.8 %all-to-all-start = ((f32[1,32,16,128]{3,2,0,1:T(8,128)}), f32[1,32,16,128]{3,2,0,1:T(8,128)}, u32[]{:S(2)}, u32[]{:S(2)}) async-start(f32[1,32,16,128]{3,2,0,1:T(8,128)} %bitcast.217), calls=%async_computation | async-start | bytes 524288 | tf_op jit(solution)/shard_map/all_to_all | solution.py:216
  192.1 1.5 copy.128
  194.9 3.7 %convolution_multiply_fusion = f32[512,32,64]{0,2,1:T(8,128)} fusion(f32[32,64,128]{2,1,0:T(8,128)S(1)} %fusion.19, f32[512,32]{0,1:T(8,128)S(1)} %fusion.58, bf16[512,2304]{0,1:T(8,128)(2,1)S(1)} %bitcast.202), kind=kOutput, calls=%fused_computation.20 | convolution fusion | flops 1611661312 | bytes 5439488 | tf_op jit(solution)/shard_map/tn,hpn->thp/dot_general | solution.py:199
  198.6 10.0 %shard_map.114 = bf16[512,2048]{1,0:T(8,128)(2,1)} custom-call(f32[2048,512]{1,0:T(8,128)} %maximum_bitcast_fusion.out_ref, f32[2048,512]{1,0:T(8,128)} %bitcast.204, bf16[2048,512]{1,0:T(8,128)(2,1)} %get-tuple-element.47.x_ref, f32[2048,1]{1,0:T(8,128)} %broadcast_in_dim_reshape.4.skip_ref, bf16[2048,512]{1,0:T(8,128)(2,1)} %get-tuple-element.46.z_ref, ...), custom_call_target="tpu_custom_call" | custom-call | flops 12582912 | bytes 8388608 | tf_op jit(solution)/shard_map/pallas_call | solution.py:71
  (121 shorter events, 29.8 us)
Async XLA Ops:
  7.2 94.6 %copy-start = (bf16[1,1,512,2048]{3,2,1,0:T(8,128)(2,1)S(1)}, bf16[1,1,512,2048]{3,2,1,0:T(8,128)(2,1)}, u32[]{:S(2)}) copy-start(bf16[1,1,512,2048]{3,2,1,0:T(8,128)(2,1)} %param.10) | copy-start | bytes 6291460
  7.2 94.6 %all-gather.4.cloned.1.call-start = ((), (), s32[]{:S(2)}) async-start(), calls=%async_computation.1 | async-start | bytes 18923520 | tf_op jit(solution)/shard_map/all_gather | solution.py:147
  7.2 6.7 %collective-permute-start = (bf16[64,1096]{1,0:T(8,128)(2,1)}, bf16[64,1096]{1,0:T(8,128)(2,1)S(1)}, u32[]{:S(2)}, u32[]{:S(2)}) collective-permute-start(bf16[64,1096]{1,0:T(8,128)(2,1)} %param.11), channel_id=1, source_target_pairs={{0,1},{1,2},{2,3},{3,0},{4,5},{5,6},{6,7},{7,4},{8,9},{9,10},{10,1... | collective-permute-start | bytes 420872 | tf_op jit(solution)/shard_map/ppermute | solution.py:140
  9.3 9.1 %collective-permute-start.1 = (bf16[64,1096]{1,0:T(8,128)(2,1)}, bf16[64,1096]{1,0:T(8,128)(2,1)S(1)}, u32[]{:S(2)}, u32[]{:S(2)}) collective-permute-start(bf16[64,1096]{1,0:T(8,128)(2,1)} %param.11), channel_id=1, source_target_pairs={{0,2},{1,3},{2,0},{3,1},{4,6},{5,7},{6,4},{7,5},{8,10},{9,11},{10,... | collective-permute-start | bytes 420872 | tf_op jit(solution)/shard_map/ppermute | solution.py:140
  11.8 6.6 %collective-permute-start.2 = (bf16[64,1096]{1,0:T(8,128)(2,1)}, bf16[64,1096]{1,0:T(8,128)(2,1)S(1)}, u32[]{:S(2)}, u32[]{:S(2)}) collective-permute-start(bf16[64,1096]{1,0:T(8,128)(2,1)} %param.11), channel_id=1, source_target_pairs={{0,3},{1,0},{2,1},{3,2},{4,7},{5,4},{6,5},{7,6},{8,11},{9,8},{10,9... | collective-permute-start | bytes 420872 | tf_op jit(solution)/shard_map/ppermute | solution.py:140
  19.4 2.7 %copy-start.16 = (s32[32]{0:T(128)S(1)}, s32[32]{0:T(128)}, u32[]{:S(2)}) copy-start(s32[32]{0:T(128)} %param.19) | copy-start | bytes 388
  19.4 2.7 %copy-start.19 = (s32[32]{0:T(128)S(1)}, s32[32]{0:T(128)}, u32[]{:S(2)}) copy-start(s32[32]{0:T(128)} %param.18) | copy-start | bytes 388
  19.4 4.6 %copy-start.8 = (f32[4,2304]{1,0:T(4,128)S(1)}, f32[4,2304]{1,0:T(4,128)}, u32[]{:S(2)}) copy-start(f32[4,2304]{1,0:T(4,128)} %param.12) | copy-start | bytes 110596
  20.2 5.2 %copy-start.14 = (f32[2304]{0:T(1024)S(1)}, f32[2304]{0:T(1024)}, u32[]{:S(2)}) copy-start(f32[2304]{0:T(1024)} %param.13) | copy-start | bytes 27652
  20.7 6.1 %copy-start.18 = (f32[32]{0:T(128)S(1)}, f32[32]{0:T(128)}, u32[]{:S(2)}) copy-start(f32[32]{0:T(128)} %param.16) | copy-start | bytes 388
  20.7 8.2 %copy-start.15 = (f32[2048]{0:T(1024)S(1)}, f32[2048]{0:T(1024)}, u32[]{:S(2)}) copy-start(f32[2048]{0:T(1024)} %param.17) | copy-start | bytes 24580
  22.0 10.8 %copy-start.20 = (f32[32]{0:T(128)S(1)}, f32[32]{0:T(128)}, u32[]{:S(2)}) copy-start(f32[32]{0:T(128)} %param.15) | copy-start | bytes 388
  22.0 155.9 %all-gather.6.cloned.1.call-start = ((), (), s32[]{:S(2)}) async-start(), calls=%async_computation.2 | async-start | bytes 2744320 | tf_op jit(solution)/shard_map/all_gather | solution.py:191
  115.8 2.8 %copy-start.3 = (bf16[512,4384]{0,1:T(8,128)(2,1)}, bf16[512,4384]{0,1:T(8,128)(2,1)S(1)}, u32[]{:S(2)}) copy-start(bf16[512,4384]{0,1:T(8,128)(2,1)S(1)} %fusion) | copy-start | bytes 13467652
  115.8 2.8 %copy-start.17 = (f32[32]{0:T(128)S(1)}, f32[32]{0:T(128)}, u32[]{:S(2)}) copy-start(f32[32]{0:T(128)} %param.14) | copy-start | bytes 388
  123.6 4.5 %collective-permute-start.3 = (bf16[3,2304]{1,0:T(4,128)(2,1)S(1)}, bf16[3,2304]{1,0:T(4,128)(2,1)S(1)}, u32[]{:S(2)}, u32[]{:S(2)}) collective-permute-start(bf16[3,2304]{1,0:T(4,128)(2,1)S(1)} %copy.89), channel_id=1, source_target_pairs={{0,1},{1,2},{2,3},{4,5},{5,6},{6,7},{8,9},{9,10},{10,11},{12,13},{... | collective-permute-start | bytes 41480 | tf_op jit(solution)/shard_map/ppermute | solution.py:14
  138.4 5.1 %copy-start.2 = (bf16[2304,512]{1,0:T(8,128)(2,1)S(1)}, bf16[2304,512]{1,0:T(8,128)(2,1)}, u32[]{:S(2)}) copy-start(bf16[2304,512]{1,0:T(8,128)(2,1)} %shard_map.113) | copy-start | bytes 7077892
  147.2 1.6 copy-start.5
  147.2 1.6 copy-start.6
  148.8 2.7 %copy-start.9 = (f32[32,256]{1,0:T(8,128)S(1)}, f32[32,256]{1,0:T(8,128)}, u32[]{:S(2)}) copy-start(f32[32,256]{1,0:T(8,128)} %get-tuple-element.38) | copy-start | bytes 98308
  148.8 2.7 %copy-start.10 = (f32[32,256]{1,0:T(8,128)S(1)}, f32[32,256]{1,0:T(8,128)}, u32[]{:S(2)}) copy-start(f32[32,256]{1,0:T(8,128)} %get-tuple-element.30) | copy-start | bytes 98308
  148.8 2.7 %copy-start.11 = (f32[256,32]{0,1:T(8,128)S(1)}, f32[256,32]{0,1:T(8,128)}, u32[]{:S(2)}) copy-start(f32[256,32]{0,1:T(8,128)} %get-tuple-element.36) | copy-start | bytes 98308
  184.3 24.4 %all-to-all-start = ((f32[1,32,16,128]{3,2,0,1:T(8,128)}), f32[1,32,16,128]{3,2,0,1:T(8,128)}, u32[]{:S(2)}, u32[]{:S(2)}) async-start(f32[1,32,16,128]{3,2,0,1:T(8,128)} %bitcast.217), calls=%async_computation | async-start | bytes 524288 | tf_op jit(solution)/shard_map/all_to_all | solution.py:216
  198.6 12.2 %copy-start.1 = (bf16[1,1,512,2048]{3,2,1,0:T(8,128)(2,1)S(1)}, bf16[1,1,512,2048]{3,2,1,0:T(8,128)(2,1)}, u32[]{:S(2)}) copy-start(bf16[1,1,512,2048]{3,2,1,0:T(8,128)(2,1)} %param.10) | copy-start | bytes 6291460
  (4 other events, 6.2 us)
Sparse Core Ops, SparseCore 0:
  22.1 79.5 all-gather.3
  146.1 31.7 all-gather.5

commit v20 on v16

--- a/solution.py
+++ b/solution.py
@@ -65,7 +65,7 @@
     o_ref[...] = normed.T.astype(o_ref.dtype)
 
 
-def gate_norm(y_t, z_t, weight, mask, cols=128):
+def gate_norm(y_t, z_t, weight, mask, cols=256):
     units, slots = y_t.shape
     return pl.pallas_call(
         norm_kernel,

time: 213 us -> 213 us (level)
  no operation moved by 1% of the time
where the time goes in v20:
time: 213 us
  waiting for transfers between devices  89.9 us (42%)
  matrix products  31.6 us (15%)
  local copies, waits for them, and re-layouts  24.9 us (12%)
  other arithmetic  17.8 us (8%)
  starting transfers between devices  16.9 us (8%)
  between operations  15.8 us (7%)
  Pallas kernels  15.7 us (7%)
    all_gather x1, waiting for transfers between devices, local(): lax.all_gather(wide_rows, 'req', axis=0, tiled=True)  70.4 us
    all_gather x1, waiting for transfers between devices, local(): gathered = lax.all_gather(packed, 'seq', axis=0, tiled=False)  14 us
    dot_general x1, matrix products, local(): jnp.dot(tok_rows, lax.all_gather(wide_rows, 'req', axis=0, tiled=True), p...  14 us
    unnamed x58, local copies, waits for them, and re-layouts  10.3 us
    pallas_call x1, Pallas kernels, conv_silu(): pl.pallas_call(conv_kernel, grid=(feats // rows,), in_specs=[pl.BlockSpec...  9.25 us
    dot_general x2, matrix products, block_step(): jnp.einsum('htu,uhp->thp', mixing, heads_x, preferred_element_type=jnp.fl...  8.72 us
    all_to_all x1, starting transfers between devices, local(): lax.all_to_all(share[None], 'req', split_axis=1, concat_axis=0, tiled=True)  7.8 us
    pallas_call x1, Pallas kernels, gate_norm(): pl.pallas_call(norm_kernel, grid=(slots // cols,), in_specs=[pl.BlockSpec...  6.42 us
  transfers between devices with their start and end apart: 7, of which 4 were waited for; matrix products, arithmetic and copies ran while one was open for 16% of the time, Pallas kernels for 3%

profile of v20, /device:TPU:1, one launch (start us, length us, event | category | flops | bytes accessed | tf_op | source)
XLA Modules:
  0.0 212.6 jit_solution(16625959378990747048)
XLA Ops:
  7.2 2.1 collective-permute-start
  9.3 2.5 %collective-permute-start.1 = (bf16[64,1096]{1,0:T(8,128)(2,1)}, bf16[64,1096]{1,0:T(8,128)(2,1)S(1)}, u32[]{:S(2)}, u32[]{:S(2)}) collective-permute-start(bf16[64,1096]{1,0:T(8,128)(2,1)} %param.11), channel_id=1, source_target_pairs={{0,2},{1,3},{2,0},{3,1},{4,6},{5,7},{6,4},{7,5},{8,10},{9,11},{10,... | collective-permute-start | bytes 420872 | tf_op jit(solution)/shard_map/ppermute | solution.py:136
  13.9 4.5 %collective-permute-done.1 = bf16[64,1096]{1,0:T(8,128)(2,1)S(1)} collective-permute-done((bf16[64,1096]{1,0:T(8,128)(2,1)}, bf16[64,1096]{1,0:T(8,128)(2,1)S(1)}, u32[]{:S(2)}, u32[]{:S(2)}) %collective-permute-start.1) | collective-permute-done | bytes 140320 | tf_op jit(solution)/shard_map/ppermute | solution.py:136
  24.0 1.4 copy.88
  25.4 1.4 broadcast_in_dim.150.b_ref
  26.8 1.4 copy.102.w_ref
  31.3 70.4 %all-gather.4.cloned.1.call-done = bf16[2048,4384]{1,0:T(8,128)(2,1)} async-done(((bf16[64,4384]{1,0:T(8,128)(2,1)}), bf16[2048,4384]{1,0:T(8,128)(2,1)}) %all-gather.4.cloned.1.call-update) | async-done | bytes 17956880 | tf_op jit(solution)/shard_map/all_gather | solution.py:143
  101.8 14.0 %fusion = bf16[512,4384]{0,1:T(8,128)(2,1)S(1)} fusion(bf16[2048,4384]{1,0:T(8,128)(2,1)} %all-gather.4.cloned.1.call-done, bf16[1,1,512,2048]{3,2,1,0:T(8,128)(2,1)S(1)} %copy-done), kind=kOutput, calls=%fused_computation.4 | convolution fusion | flops 9196158976 | bytes 24543232 | tf_op jit(solution)/shard_map/dot_general | solution.py:141
  115.8 2.0 fusion.65
  122.5 3.3 %collective-permute-start.3 = (bf16[3,2304]{1,0:T(4,128)(2,1)S(1)}, bf16[3,2304]{1,0:T(4,128)(2,1)S(1)}, u32[]{:S(2)}, u32[]{:S(2)}) collective-permute-start(bf16[3,2304]{1,0:T(4,128)(2,1)S(1)} %copy.86), channel_id=1, source_target_pairs={{0,1},{1,2},{2,3},{4,5},{5,6},{6,7},{8,9},{9,10},{10,11},{12,13},{... | collective-permute-start | bytes 41480 | tf_op jit(solution)/shard_map/ppermute | solution.py:14
  129.6 9.2 %shard_map.113 = bf16[2304,512]{1,0:T(8,128)(2,1)} custom-call(bf16[2304,512]{1,0:T(8,128)(2,1)} %get-tuple-element.21.x_ref, bf16[2304,3]{1,0:T(8,128)(2,1)} %bitcast.206, f32[2304,4]{1,0:T(8,128)} %bitcast.203, f32[2304,1]{1,0:T(8,128)} %broadcast_in_dim.150.b_ref), custom_call_target="tpu_custom_call" | custom-call | flops 16515072 | bytes 4718592 | tf_op jit(solution)/shard_map/pallas_call | solution.py:42
  138.9 2.1 fusion.16
  143.3 3.1 %slice_bitcast_fusion.z_ref = bf16[2048,512]{1,0:T(8,128)(2,1)} fusion(bf16[512,4384]{0,1:T(8,128)(2,1)} %copy-done.4), kind=kLoop, calls=%fused_computation.22 | loop fusion | bytes 4194304 | tf_op jit(solution)/shard_map/transpose | solution.py:205
  146.5 1.5 slice.195
  151.3 4.4 %bitcast_add_fusion.1 = f32[256,32,64]{0,2,1:T(8,128)} fusion(f32[256,32,64]{0,2,1:T(8,128)S(1)} %fusion.23, bf16[256,32,64]{0,2,1:T(8,128)(2,1)S(1)} %bitcast.214, f32[32,256]{1,0:T(8,128)S(1)} %copy-done.14, f32[32,256]{1,0:T(8,128)S(1)} %copy-done.10, f32[256,256]{1,0:T(8,128)S(1)} %fusion.40, pred[256,256]{1,0:T(8,128)(4,1)S(1)} %copy-done.8, ...), kind=kOutput, calls=%fused_computation.29 | convolution fusion | flops 282066944 | bytes 5668864 | tf_op jit(solution)/shard_map/htu,uhp->thp/dot_general | solution.py:99
  155.7 4.3 %bitcast_add_fusion = f32[256,32,64]{0,2,1:T(8,128)} fusion(f32[256,32,64]{0,2,1:T(8,128)S(1)} %fusion.31, bf16[256,32,64]{0,2,1:T(8,128)(2,1)S(1)} %bitcast.213, f32[32,256]{1,0:T(8,128)S(1)} %copy-done.12, f32[32,256]{1,0:T(8,128)S(1)} %copy-done.11, f32[256,256]{1,0:T(8,128)S(1)} %fusion.35, pred[256,256]{1,0:T(8,128)(4,1)S(1)} %copy-done.8, ...), kind=kOutput, calls=%fused_computation.28 | convolution fusion | flops 282066944 | bytes 5668864 | tf_op jit(solution)/shard_map/htu,uhp->thp/dot_general | solution.py:99
  160.0 14.0 %all-gather.6.cloned.1.call-done = bf16[128,8576]{1,0:T(8,128)(2,1)} async-done(((bf16[32,8576]{1,0:T(8,128)(2,1)}), bf16[128,8576]{1,0:T(8,128)(2,1)}) %all-gather.6.cloned.1.call-update) | async-done | bytes 2195472 | tf_op jit(solution)/shard_map/all_gather | solution.py:187
  174.0 2.0 slice_convert_fusion
  176.9 1.5 slice_bitcast_fusion.3
  180.3 7.8 %all-to-all-start = ((f32[1,32,16,128]{3,2,0,1:T(8,128)}), f32[1,32,16,128]{3,2,0,1:T(8,128)}, u32[]{:S(2)}, u32[]{:S(2)}) async-start(f32[1,32,16,128]{3,2,0,1:T(8,128)} %bitcast.212), calls=%async_computation | async-start | bytes 524288 | tf_op jit(solution)/shard_map/all_to_all | solution.py:214
  188.2 1.5 copy.124
  192.8 4.4 %fusion.3 = f32[512,32,64]{0,2,1:T(8,128)} fusion(f32[256,32,64]{0,2,1:T(8,128)S(1)} %copy-done.7, f32[256,32,64]{0,2,1:T(8,128)S(1)} %copy-done.6, bf16[512,32,64]{0,2,1:T(8,128)(2,1)S(1)} %bitcast.201, f32[32,64,128]{2,1,0:T(8,128)S(1)} %fusion.20, f32[32]{0:T(128)S(1)} %copy-done.20, f32[512,32]{0,1:T(8,128)S(1)} %fusion.59, ...), kind=kOutput, calls=%fused_computation.8 | convolution fusion | flops 1616904192 | bytes 11731456 | tf_op jit(solution)/shard_map/tn,hpn->thp/dot_general | solution.py:195
  197.2 6.4 %shard_map.114 = bf16[512,2048]{1,0:T(8,128)(2,1)} custom-call(f32[2048,512]{1,0:T(8,128)} %bitcast.200, bf16[2048,512]{1,0:T(8,128)(2,1)} %slice_bitcast_fusion.z_ref, f32[2048,1]{1,0:T(8,128)} %copy.102.w_ref, f32[1,512]{1,0:T(1,128)} %compare_convert_fusion.mask_ref), custom_call_target="tpu_custom_call" | custom-call | flops 12582912 | bytes 8388608 | tf_op jit(solution)/shard_map/pallas_call | solution.py:70
  203.6 1.3 convolution_bitcast_fusion
  (125 shorter events, 30.3 us)
Async XLA Ops:
  7.2 94.6 %copy-start = (bf16[1,1,512,2048]{3,2,1,0:T(8,128)(2,1)S(1)}, bf16[1,1,512,2048]{3,2,1,0:T(8,128)(2,1)}, u32[]{:S(2)}) copy-start(bf16[1,1,512,2048]{3,2,1,0:T(8,128)(2,1)} %param.10) | copy-start | bytes 6291460
  7.2 94.6 %all-gather.4.cloned.1.call-start = ((), (), s32[]{:S(2)}) async-start(), calls=%async_computation.1 | async-start | bytes 18923520 | tf_op jit(solution)/shard_map/all_gather | solution.py:143
  7.2 6.7 %collective-permute-start = (bf16[64,1096]{1,0:T(8,128)(2,1)}, bf16[64,1096]{1,0:T(8,128)(2,1)S(1)}, u32[]{:S(2)}, u32[]{:S(2)}) collective-permute-start(bf16[64,1096]{1,0:T(8,128)(2,1)} %param.11), channel_id=1, source_target_pairs={{0,1},{1,2},{2,3},{3,0},{4,5},{5,6},{6,7},{7,4},{8,9},{9,10},{10,1... | collective-permute-start | bytes 420872 | tf_op jit(solution)/shard_map/ppermute | solution.py:136
  9.3 9.1 %collective-permute-start.1 = (bf16[64,1096]{1,0:T(8,128)(2,1)}, bf16[64,1096]{1,0:T(8,128)(2,1)S(1)}, u32[]{:S(2)}, u32[]{:S(2)}) collective-permute-start(bf16[64,1096]{1,0:T(8,128)(2,1)} %param.11), channel_id=1, source_target_pairs={{0,2},{1,3},{2,0},{3,1},{4,6},{5,7},{6,4},{7,5},{8,10},{9,11},{10,... | collective-permute-start | bytes 420872 | tf_op jit(solution)/shard_map/ppermute | solution.py:136
  11.8 6.6 %collective-permute-start.2 = (bf16[64,1096]{1,0:T(8,128)(2,1)}, bf16[64,1096]{1,0:T(8,128)(2,1)S(1)}, u32[]{:S(2)}, u32[]{:S(2)}) collective-permute-start(bf16[64,1096]{1,0:T(8,128)(2,1)} %param.11), channel_id=1, source_target_pairs={{0,3},{1,0},{2,1},{3,2},{4,7},{5,4},{6,5},{7,6},{8,11},{9,8},{10,9... | collective-permute-start | bytes 420872 | tf_op jit(solution)/shard_map/ppermute | solution.py:136
  19.4 2.6 %copy-start.18 = (s32[32]{0:T(128)S(1)}, s32[32]{0:T(128)}, u32[]{:S(2)}) copy-start(s32[32]{0:T(128)} %param.19) | copy-start | bytes 388
  19.4 2.6 %copy-start.22 = (s32[32]{0:T(128)S(1)}, s32[32]{0:T(128)}, u32[]{:S(2)}) copy-start(s32[32]{0:T(128)} %param.18) | copy-start | bytes 388
  19.4 4.6 %copy-start.9 = (f32[4,2304]{1,0:T(4,128)S(1)}, f32[4,2304]{1,0:T(4,128)}, u32[]{:S(2)}) copy-start(f32[4,2304]{1,0:T(4,128)} %param.12) | copy-start | bytes 110596
  20.2 5.2 %copy-start.16 = (f32[2304]{0:T(1024)S(1)}, f32[2304]{0:T(1024)}, u32[]{:S(2)}) copy-start(f32[2304]{0:T(1024)} %param.13) | copy-start | bytes 27652
  20.7 6.1 %copy-start.17 = (f32[2048]{0:T(1024)S(1)}, f32[2048]{0:T(1024)}, u32[]{:S(2)}) copy-start(f32[2048]{0:T(1024)} %param.17) | copy-start | bytes 24580
  22.0 9.4 %copy-start.23 = (f32[32]{0:T(128)S(1)}, f32[32]{0:T(128)}, u32[]{:S(2)}) copy-start(f32[32]{0:T(128)} %param.15) | copy-start | bytes 388
  22.0 152.0 %all-gather.6.cloned.1.call-start = ((), (), s32[]{:S(2)}) async-start(), calls=%async_computation.2 | async-start | bytes 2744320 | tf_op jit(solution)/shard_map/all_gather | solution.py:187
  115.8 2.8 %copy-start.4 = (bf16[512,4384]{0,1:T(8,128)(2,1)}, bf16[512,4384]{0,1:T(8,128)(2,1)S(1)}, u32[]{:S(2)}) copy-start(bf16[512,4384]{0,1:T(8,128)(2,1)S(1)} %fusion) | copy-start | bytes 13467652
  115.8 2.8 %copy-start.19 = (f32[32]{0:T(128)S(1)}, f32[32]{0:T(128)}, u32[]{:S(2)}) copy-start(f32[32]{0:T(128)} %param.14) | copy-start | bytes 388
  122.5 5.9 %collective-permute-start.3 = (bf16[3,2304]{1,0:T(4,128)(2,1)S(1)}, bf16[3,2304]{1,0:T(4,128)(2,1)S(1)}, u32[]{:S(2)}, u32[]{:S(2)}) collective-permute-start(bf16[3,2304]{1,0:T(4,128)(2,1)S(1)} %copy.86), channel_id=1, source_target_pairs={{0,1},{1,2},{2,3},{4,5},{5,6},{6,7},{8,9},{9,10},{10,11},{12,13},{... | collective-permute-start | bytes 41480 | tf_op jit(solution)/shard_map/ppermute | solution.py:14
  138.9 2.3 %copy-start.2 = (bf16[2304,512]{1,0:T(8,128)(2,1)S(1)}, bf16[2304,512]{1,0:T(8,128)(2,1)}, u32[]{:S(2)}) copy-start(bf16[2304,512]{1,0:T(8,128)(2,1)} %shard_map.113) | copy-start | bytes 7077892
  151.3 4.4 %copy-start.11 = (f32[32,256]{1,0:T(8,128)S(1)}, f32[32,256]{1,0:T(8,128)}, u32[]{:S(2)}) copy-start(f32[32,256]{1,0:T(8,128)} %get-tuple-element.38) | copy-start | bytes 98308
  151.3 4.4 %copy-start.12 = (f32[32,256]{1,0:T(8,128)S(1)}, f32[32,256]{1,0:T(8,128)}, u32[]{:S(2)}) copy-start(f32[32,256]{1,0:T(8,128)} %get-tuple-element.30) | copy-start | bytes 98308
  151.3 4.4 %copy-start.13 = (f32[256,32]{0,1:T(8,128)S(1)}, f32[256,32]{0,1:T(8,128)}, u32[]{:S(2)}) copy-start(f32[256,32]{0,1:T(8,128)} %get-tuple-element.36) | copy-start | bytes 98308
  180.3 23.2 %all-to-all-start = ((f32[1,32,16,128]{3,2,0,1:T(8,128)}), f32[1,32,16,128]{3,2,0,1:T(8,128)}, u32[]{:S(2)}, u32[]{:S(2)}) async-start(f32[1,32,16,128]{3,2,0,1:T(8,128)} %bitcast.212), calls=%async_computation | async-start | bytes 524288 | tf_op jit(solution)/shard_map/all_to_all | solution.py:214
  190.1 2.1 copy-start.3
  190.1 2.7 %copy-start.6 = (f32[256,32,64]{0,2,1:T(8,128)S(1)}, f32[256,32,64]{0,2,1:T(8,128)}, u32[]{:S(2)}) copy-start(f32[256,32,64]{0,2,1:T(8,128)} %bitcast_add_fusion.1) | copy-start | bytes 6291460
  190.1 2.7 %copy-start.20 = (f32[32]{0:T(128)S(1)}, f32[32]{0:T(128)}, u32[]{:S(2)}) copy-start(f32[32]{0:T(128)} %param.16) | copy-start | bytes 388
  197.1 8.6 %copy-start.1 = (bf16[1,1,512,2048]{3,2,1,0:T(8,128)(2,1)S(1)}, bf16[1,1,512,2048]{3,2,1,0:T(8,128)(2,1)}, u32[]{:S(2)}) copy-start(bf16[1,1,512,2048]{3,2,1,0:T(8,128)(2,1)} %param.10) | copy-start | bytes 6291460
  (7 other events, 7.3 us)
Sparse Core Ops, SparseCore 0:
  22.1 79.5 all-gather.3
  143.4 30.5 all-gather.5

commit v21 on v16

--- a/solution.py
+++ b/solution.py
@@ -36,7 +36,7 @@
     o_ref[:, :128] = (first * (0.5 + 0.5 * jnp.tanh(0.5 * first))).astype(o_ref.dtype)
 
 
-def conv_silu(conv_t, edge_t, weight_t, bias_t, rows=768):
+def conv_silu(conv_t, edge_t, weight_t, bias_t, rows=1152):
     feats, slots = conv_t.shape
     taps = weight_t.shape[1]
     return pl.pallas_call(

time: 213 us -> 214 us (level)
  no operation moved by 1% of the time
where the time goes in v21:
time: 214 us; the launch traced here: 213 us
  waiting for transfers between devices  89.9 us (42%)
  matrix products  31.6 us (15%)
  local copies, waits for them, and re-layouts  24.9 us (12%)
  other arithmetic  17.8 us (8%)
  starting transfers between devices  16.9 us (8%)
  Pallas kernels  16.2 us (8%)
  between operations  15.8 us (7%)
    all_gather x1, waiting for transfers between devices, local(): lax.all_gather(wide_rows, 'req', axis=0, tiled=True)  70.4 us
    all_gather x1, waiting for transfers between devices, local(): gathered = lax.all_gather(packed, 'seq', axis=0, tiled=False)  14 us
    dot_general x1, matrix products, local(): jnp.dot(tok_rows, lax.all_gather(wide_rows, 'req', axis=0, tiled=True), p...  14 us
    unnamed x58, local copies, waits for them, and re-layouts  10.3 us
    pallas_call x1, Pallas kernels, conv_silu(): pl.pallas_call(conv_kernel, grid=(feats // rows,), in_specs=[pl.BlockSpec...  9.58 us
    dot_general x2, matrix products, block_step(): jnp.einsum('htu,uhp->thp', mixing, heads_x, preferred_element_type=jnp.fl...  8.72 us
    all_to_all x1, starting transfers between devices, local(): lax.all_to_all(share[None], 'req', split_axis=1, concat_axis=0, tiled=True)  7.79 us
    pallas_call x1, Pallas kernels, gate_norm(): pl.pallas_call(norm_kernel, grid=(slots // cols,), in_specs=[pl.BlockSpec...  6.59 us
  transfers between devices with their start and end apart: 7, of which 4 were waited for; matrix products, arithmetic and copies ran while one was open for 16% of the time, Pallas kernels for 3%

profile of v21, /device:TPU:1, one launch (start us, length us, event | category | flops | bytes accessed | tf_op | source)
XLA Modules:
  0.0 213.1 jit_solution(1494582003962407681)
XLA Ops:
  7.2 2.1 collective-permute-start
  9.3 2.5 %collective-permute-start.1 = (bf16[64,1096]{1,0:T(8,128)(2,1)}, bf16[64,1096]{1,0:T(8,128)(2,1)S(1)}, u32[]{:S(2)}, u32[]{:S(2)}) collective-permute-start(bf16[64,1096]{1,0:T(8,128)(2,1)} %param.11), channel_id=1, source_target_pairs={{0,2},{1,3},{2,0},{3,1},{4,6},{5,7},{6,4},{7,5},{8,10},{9,11},{10,... | collective-permute-start | bytes 420872 | tf_op jit(solution)/shard_map/ppermute | solution.py:136
  13.9 4.5 %collective-permute-done.1 = bf16[64,1096]{1,0:T(8,128)(2,1)S(1)} collective-permute-done((bf16[64,1096]{1,0:T(8,128)(2,1)}, bf16[64,1096]{1,0:T(8,128)(2,1)S(1)}, u32[]{:S(2)}, u32[]{:S(2)}) %collective-permute-start.1) | collective-permute-done | bytes 140320 | tf_op jit(solution)/shard_map/ppermute | solution.py:136
  24.0 1.4 copy.88
  25.4 1.4 broadcast_in_dim.150.b_ref
  26.8 1.4 copy.102.w_ref
  31.3 70.4 %all-gather.4.cloned.1.call-done = bf16[2048,4384]{1,0:T(8,128)(2,1)} async-done(((bf16[64,4384]{1,0:T(8,128)(2,1)}), bf16[2048,4384]{1,0:T(8,128)(2,1)}) %all-gather.4.cloned.1.call-update) | async-done | bytes 17956880 | tf_op jit(solution)/shard_map/all_gather | solution.py:143
  101.8 14.0 %fusion = bf16[512,4384]{0,1:T(8,128)(2,1)S(1)} fusion(bf16[2048,4384]{1,0:T(8,128)(2,1)} %all-gather.4.cloned.1.call-done, bf16[1,1,512,2048]{3,2,1,0:T(8,128)(2,1)S(1)} %copy-done), kind=kOutput, calls=%fused_computation.4 | convolution fusion | flops 9196158976 | bytes 24543232 | tf_op jit(solution)/shard_map/dot_general | solution.py:141
  115.8 2.0 fusion.65
  122.5 3.3 %collective-permute-start.3 = (bf16[3,2304]{1,0:T(4,128)(2,1)S(1)}, bf16[3,2304]{1,0:T(4,128)(2,1)S(1)}, u32[]{:S(2)}, u32[]{:S(2)}) collective-permute-start(bf16[3,2304]{1,0:T(4,128)(2,1)S(1)} %copy.86), channel_id=1, source_target_pairs={{0,1},{1,2},{2,3},{4,5},{5,6},{6,7},{8,9},{9,10},{10,11},{12,13},{... | collective-permute-start | bytes 41480 | tf_op jit(solution)/shard_map/ppermute | solution.py:14
  129.6 9.6 %shard_map.113 = bf16[2304,512]{1,0:T(8,128)(2,1)} custom-call(bf16[2304,512]{1,0:T(8,128)(2,1)} %get-tuple-element.21.x_ref, bf16[2304,3]{1,0:T(8,128)(2,1)} %bitcast.206, f32[2304,4]{1,0:T(8,128)} %bitcast.203, f32[2304,1]{1,0:T(8,128)} %broadcast_in_dim.150.b_ref), custom_call_target="tpu_custom_call" | custom-call | flops 16515072 | bytes 4718592 | tf_op jit(solution)/shard_map/pallas_call | solution.py:42
  139.2 2.1 fusion.16
  143.7 3.1 %slice_bitcast_fusion.z_ref = bf16[2048,512]{1,0:T(8,128)(2,1)} fusion(bf16[512,4384]{0,1:T(8,128)(2,1)} %copy-done.4), kind=kLoop, calls=%fused_computation.22 | loop fusion | bytes 4194304 | tf_op jit(solution)/shard_map/transpose | solution.py:205
  146.9 1.5 slice.195
  151.6 4.4 %bitcast_add_fusion.1 = f32[256,32,64]{0,2,1:T(8,128)} fusion(f32[256,32,64]{0,2,1:T(8,128)S(1)} %fusion.23, bf16[256,32,64]{0,2,1:T(8,128)(2,1)S(1)} %bitcast.214, f32[32,256]{1,0:T(8,128)S(1)} %copy-done.14, f32[32,256]{1,0:T(8,128)S(1)} %copy-done.10, f32[256,256]{1,0:T(8,128)S(1)} %fusion.40, pred[256,256]{1,0:T(8,128)(4,1)S(1)} %copy-done.8, ...), kind=kOutput, calls=%fused_computation.29 | convolution fusion | flops 282066944 | bytes 5668864 | tf_op jit(solution)/shard_map/htu,uhp->thp/dot_general | solution.py:99
  156.0 4.3 %bitcast_add_fusion = f32[256,32,64]{0,2,1:T(8,128)} fusion(f32[256,32,64]{0,2,1:T(8,128)S(1)} %fusion.31, bf16[256,32,64]{0,2,1:T(8,128)(2,1)S(1)} %bitcast.213, f32[32,256]{1,0:T(8,128)S(1)} %copy-done.12, f32[32,256]{1,0:T(8,128)S(1)} %copy-done.11, f32[256,256]{1,0:T(8,128)S(1)} %fusion.35, pred[256,256]{1,0:T(8,128)(4,1)S(1)} %copy-done.8, ...), kind=kOutput, calls=%fused_computation.28 | convolution fusion | flops 282066944 | bytes 5668864 | tf_op jit(solution)/shard_map/htu,uhp->thp/dot_general | solution.py:99
  160.3 14.0 %all-gather.6.cloned.1.call-done = bf16[128,8576]{1,0:T(8,128)(2,1)} async-done(((bf16[32,8576]{1,0:T(8,128)(2,1)}), bf16[128,8576]{1,0:T(8,128)(2,1)}) %all-gather.6.cloned.1.call-update) | async-done | bytes 2195472 | tf_op jit(solution)/shard_map/all_gather | solution.py:187
  174.4 2.0 slice_convert_fusion
  177.3 1.5 slice_bitcast_fusion.3
  180.7 7.8 %all-to-all-start = ((f32[1,32,16,128]{3,2,0,1:T(8,128)}), f32[1,32,16,128]{3,2,0,1:T(8,128)}, u32[]{:S(2)}, u32[]{:S(2)}) async-start(f32[1,32,16,128]{3,2,0,1:T(8,128)} %bitcast.212), calls=%async_computation | async-start | bytes 524288 | tf_op jit(solution)/shard_map/all_to_all | solution.py:214
  188.5 1.5 copy.124
  193.1 4.4 %fusion.3 = f32[512,32,64]{0,2,1:T(8,128)} fusion(f32[256,32,64]{0,2,1:T(8,128)S(1)} %copy-done.7, f32[256,32,64]{0,2,1:T(8,128)S(1)} %copy-done.6, bf16[512,32,64]{0,2,1:T(8,128)(2,1)S(1)} %bitcast.201, f32[32,64,128]{2,1,0:T(8,128)S(1)} %fusion.20, f32[32]{0:T(128)S(1)} %copy-done.20, f32[512,32]{0,1:T(8,128)S(1)} %fusion.59, ...), kind=kOutput, calls=%fused_computation.8 | convolution fusion | flops 1616904192 | bytes 11731456 | tf_op jit(solution)/shard_map/tn,hpn->thp/dot_general | solution.py:195
  197.5 6.6 %shard_map.114 = bf16[512,2048]{1,0:T(8,128)(2,1)} custom-call(f32[2048,512]{1,0:T(8,128)} %bitcast.200, bf16[2048,512]{1,0:T(8,128)(2,1)} %slice_bitcast_fusion.z_ref, f32[2048,1]{1,0:T(8,128)} %copy.102.w_ref, f32[1,512]{1,0:T(1,128)} %compare_convert_fusion.mask_ref), custom_call_target="tpu_custom_call" | custom-call | flops 12582912 | bytes 8388608 | tf_op jit(solution)/shard_map/pallas_call | solution.py:70
  204.1 1.3 convolution_bitcast_fusion
  (125 shorter events, 30.3 us)
Async XLA Ops:
  7.2 94.6 %copy-start = (bf16[1,1,512,2048]{3,2,1,0:T(8,128)(2,1)S(1)}, bf16[1,1,512,2048]{3,2,1,0:T(8,128)(2,1)}, u32[]{:S(2)}) copy-start(bf16[1,1,512,2048]{3,2,1,0:T(8,128)(2,1)} %param.10) | copy-start | bytes 6291460
  7.2 94.6 %all-gather.4.cloned.1.call-start = ((), (), s32[]{:S(2)}) async-start(), calls=%async_computation.1 | async-start | bytes 18923520 | tf_op jit(solution)/shard_map/all_gather | solution.py:143
  7.2 6.7 %collective-permute-start = (bf16[64,1096]{1,0:T(8,128)(2,1)}, bf16[64,1096]{1,0:T(8,128)(2,1)S(1)}, u32[]{:S(2)}, u32[]{:S(2)}) collective-permute-start(bf16[64,1096]{1,0:T(8,128)(2,1)} %param.11), channel_id=1, source_target_pairs={{0,1},{1,2},{2,3},{3,0},{4,5},{5,6},{6,7},{7,4},{8,9},{9,10},{10,1... | collective-permute-start | bytes 420872 | tf_op jit(solution)/shard_map/ppermute | solution.py:136
  9.3 9.1 %collective-permute-start.1 = (bf16[64,1096]{1,0:T(8,128)(2,1)}, bf16[64,1096]{1,0:T(8,128)(2,1)S(1)}, u32[]{:S(2)}, u32[]{:S(2)}) collective-permute-start(bf16[64,1096]{1,0:T(8,128)(2,1)} %param.11), channel_id=1, source_target_pairs={{0,2},{1,3},{2,0},{3,1},{4,6},{5,7},{6,4},{7,5},{8,10},{9,11},{10,... | collective-permute-start | bytes 420872 | tf_op jit(solution)/shard_map/ppermute | solution.py:136
  11.8 6.6 %collective-permute-start.2 = (bf16[64,1096]{1,0:T(8,128)(2,1)}, bf16[64,1096]{1,0:T(8,128)(2,1)S(1)}, u32[]{:S(2)}, u32[]{:S(2)}) collective-permute-start(bf16[64,1096]{1,0:T(8,128)(2,1)} %param.11), channel_id=1, source_target_pairs={{0,3},{1,0},{2,1},{3,2},{4,7},{5,4},{6,5},{7,6},{8,11},{9,8},{10,9... | collective-permute-start | bytes 420872 | tf_op jit(solution)/shard_map/ppermute | solution.py:136
  19.4 2.6 %copy-start.18 = (s32[32]{0:T(128)S(1)}, s32[32]{0:T(128)}, u32[]{:S(2)}) copy-start(s32[32]{0:T(128)} %param.19) | copy-start | bytes 388
  19.4 2.6 %copy-start.22 = (s32[32]{0:T(128)S(1)}, s32[32]{0:T(128)}, u32[]{:S(2)}) copy-start(s32[32]{0:T(128)} %param.18) | copy-start | bytes 388
  19.4 4.6 %copy-start.9 = (f32[4,2304]{1,0:T(4,128)S(1)}, f32[4,2304]{1,0:T(4,128)}, u32[]{:S(2)}) copy-start(f32[4,2304]{1,0:T(4,128)} %param.12) | copy-start | bytes 110596
  20.2 5.2 %copy-start.16 = (f32[2304]{0:T(1024)S(1)}, f32[2304]{0:T(1024)}, u32[]{:S(2)}) copy-start(f32[2304]{0:T(1024)} %param.13) | copy-start | bytes 27652
  20.7 6.1 %copy-start.17 = (f32[2048]{0:T(1024)S(1)}, f32[2048]{0:T(1024)}, u32[]{:S(2)}) copy-start(f32[2048]{0:T(1024)} %param.17) | copy-start | bytes 24580
  22.0 9.4 %copy-start.23 = (f32[32]{0:T(128)S(1)}, f32[32]{0:T(128)}, u32[]{:S(2)}) copy-start(f32[32]{0:T(128)} %param.15) | copy-start | bytes 388
  22.0 152.4 %all-gather.6.cloned.1.call-start = ((), (), s32[]{:S(2)}) async-start(), calls=%async_computation.2 | async-start | bytes 2744320 | tf_op jit(solution)/shard_map/all_gather | solution.py:187
  115.8 2.8 %copy-start.4 = (bf16[512,4384]{0,1:T(8,128)(2,1)}, bf16[512,4384]{0,1:T(8,128)(2,1)S(1)}, u32[]{:S(2)}) copy-start(bf16[512,4384]{0,1:T(8,128)(2,1)S(1)} %fusion) | copy-start | bytes 13467652
  115.8 2.8 %copy-start.19 = (f32[32]{0:T(128)S(1)}, f32[32]{0:T(128)}, u32[]{:S(2)}) copy-start(f32[32]{0:T(128)} %param.14) | copy-start | bytes 388
  122.5 5.9 %collective-permute-start.3 = (bf16[3,2304]{1,0:T(4,128)(2,1)S(1)}, bf16[3,2304]{1,0:T(4,128)(2,1)S(1)}, u32[]{:S(2)}, u32[]{:S(2)}) collective-permute-start(bf16[3,2304]{1,0:T(4,128)(2,1)S(1)} %copy.86), channel_id=1, source_target_pairs={{0,1},{1,2},{2,3},{4,5},{5,6},{6,7},{8,9},{9,10},{10,11},{12,13},{... | collective-permute-start | bytes 41480 | tf_op jit(solution)/shard_map/ppermute | solution.py:14
  139.2 2.3 %copy-start.2 = (bf16[2304,512]{1,0:T(8,128)(2,1)S(1)}, bf16[2304,512]{1,0:T(8,128)(2,1)}, u32[]{:S(2)}) copy-start(bf16[2304,512]{1,0:T(8,128)(2,1)} %shard_map.113) | copy-start | bytes 7077892
  151.6 4.4 %copy-start.11 = (f32[32,256]{1,0:T(8,128)S(1)}, f32[32,256]{1,0:T(8,128)}, u32[]{:S(2)}) copy-start(f32[32,256]{1,0:T(8,128)} %get-tuple-element.38) | copy-start | bytes 98308
  151.6 4.4 %copy-start.12 = (f32[32,256]{1,0:T(8,128)S(1)}, f32[32,256]{1,0:T(8,128)}, u32[]{:S(2)}) copy-start(f32[32,256]{1,0:T(8,128)} %get-tuple-element.30) | copy-start | bytes 98308
  151.6 4.4 %copy-start.13 = (f32[256,32]{0,1:T(8,128)S(1)}, f32[256,32]{0,1:T(8,128)}, u32[]{:S(2)}) copy-start(f32[256,32]{0,1:T(8,128)} %get-tuple-element.36) | copy-start | bytes 98308
  180.7 23.4 %all-to-all-start = ((f32[1,32,16,128]{3,2,0,1:T(8,128)}), f32[1,32,16,128]{3,2,0,1:T(8,128)}, u32[]{:S(2)}, u32[]{:S(2)}) async-start(f32[1,32,16,128]{3,2,0,1:T(8,128)} %bitcast.212), calls=%async_computation | async-start | bytes 524288 | tf_op jit(solution)/shard_map/all_to_all | solution.py:214
  190.4 2.1 copy-start.3
  190.4 2.7 %copy-start.6 = (f32[256,32,64]{0,2,1:T(8,128)S(1)}, f32[256,32,64]{0,2,1:T(8,128)}, u32[]{:S(2)}) copy-start(f32[256,32,64]{0,2,1:T(8,128)} %bitcast_add_fusion.1) | copy-start | bytes 6291460
  190.5 2.7 %copy-start.20 = (f32[32]{0:T(128)S(1)}, f32[32]{0:T(128)}, u32[]{:S(2)}) copy-start(f32[32]{0:T(128)} %param.16) | copy-start | bytes 388
  197.5 8.7 %copy-start.1 = (bf16[1,1,512,2048]{3,2,1,0:T(8,128)(2,1)S(1)}, bf16[1,1,512,2048]{3,2,1,0:T(8,128)(2,1)}, u32[]{:S(2)}) copy-start(bf16[1,1,512,2048]{3,2,1,0:T(8,128)(2,1)} %param.10) | copy-start | bytes 6291460
  (7 other events, 7.3 us)
Sparse Core Ops, SparseCore 0:
  22.1 79.5 all-gather.3
  143.8 30.5 all-gather.5

commit v22 on v16

--- a/solution.py
+++ b/solution.py
@@ -179,15 +179,15 @@
     total_mid = lax.reduce_precision(total_rest, exponent_bits=8, mantissa_bits=7)
     total_lo = total_rest - total_mid
     parts = jnp.stack([total_hi, total_mid, total_lo], axis=1).astype(jnp.bfloat16)
-    parts = jnp.broadcast_to(parts[:, :, None], (heads, 3, 128))
+    parts = jnp.pad(parts, ((0, 0), (0, 128 - 3)))
     packed = jnp.concatenate(
-        [local_end.reshape(heads, hdim * nstate).astype(jnp.bfloat16), parts.reshape(heads, 3 * 128)],
+        [local_end.reshape(heads, hdim * nstate).astype(jnp.bfloat16), parts],
         axis=1,
     )
     gathered = lax.all_gather(packed, "seq", axis=0, tiled=False)
     ends = gathered[:, :, : hdim * nstate].astype(jnp.float32).reshape(seq_count, heads, hdim, nstate)
     sent = gathered[:, :, hdim * nstate :].astype(jnp.float32)
-    totals = sent[:, :, 0] + (sent[:, :, 128] + sent[:, :, 256])
+    totals = sent[:, :, 0] + (sent[:, :, 1] + sent[:, :, 2])
     entering = zero_state
     for turn in range(seq_count - 1):
         stepped = jnp.exp(totals[turn])[:, None, None] * entering + ends[turn]

time: 213 us -> 213 us (level)
    unnamed x58 -> x56, local copies, waits for them, and re-layouts: 10.3 us -> 10.3 us
where the time goes in v22:
time: 213 us; the launch traced here: 212 us
  waiting for transfers between devices  90 us (42%)
  matrix products  31.6 us (15%)
  local copies, waits for them, and re-layouts  24.8 us (12%)
  other arithmetic  17.1 us (8%)
  starting transfers between devices  16.8 us (8%)
  Pallas kernels  15.8 us (7%)
  between operations  15.8 us (7%)
    all_gather x1, waiting for transfers between devices, local(): lax.all_gather(wide_rows, 'req', axis=0, tiled=True)  71 us
    dot_general x1, matrix products, local(): jnp.dot(tok_rows, lax.all_gather(wide_rows, 'req', axis=0, tiled=True), p...  14 us
    all_gather x1, waiting for transfers between devices, local(): gathered = lax.all_gather(packed, 'seq', axis=0, tiled=False)  13.5 us
    unnamed x56, local copies, waits for them, and re-layouts  10.3 us
    pallas_call x1, Pallas kernels, conv_silu(): pl.pallas_call(conv_kernel, grid=(feats // rows,), in_specs=[pl.BlockSpec...  9.25 us
    dot_general x2, matrix products, block_step(): jnp.einsum('htu,uhp->thp', mixing, heads_x, preferred_element_type=jnp.fl...  8.71 us
    all_to_all x1, starting transfers between devices, local(): lax.all_to_all(share[None], 'req', split_axis=1, concat_axis=0, tiled=True)  7.77 us
    pallas_call x1, Pallas kernels, gate_norm(): pl.pallas_call(norm_kernel, grid=(slots // cols,), in_specs=[pl.BlockSpec...  6.59 us
  transfers between devices with their start and end apart: 7, of which 4 were waited for; matrix products, arithmetic and copies ran while one was open for 16% of the time, Pallas kernels for 3%

profile of v22, /device:TPU:1, one launch (start us, length us, event | category | flops | bytes accessed | tf_op | source)
XLA Modules:
  0.0 212.0 jit_solution(18090841293774328938)
XLA Ops:
  7.2 2.1 collective-permute-start
  9.3 2.5 %collective-permute-start.1 = (bf16[64,1096]{1,0:T(8,128)(2,1)}, bf16[64,1096]{1,0:T(8,128)(2,1)S(1)}, u32[]{:S(2)}, u32[]{:S(2)}) collective-permute-start(bf16[64,1096]{1,0:T(8,128)(2,1)} %param.11), channel_id=1, source_target_pairs={{0,2},{1,3},{2,0},{3,1},{4,6},{5,7},{6,4},{7,5},{8,10},{9,11},{10,... | collective-permute-start | bytes 420872 | tf_op jit(solution)/shard_map/ppermute | solution.py:136
  13.9 4.5 %collective-permute-done.1 = bf16[64,1096]{1,0:T(8,128)(2,1)S(1)} collective-permute-done((bf16[64,1096]{1,0:T(8,128)(2,1)}, bf16[64,1096]{1,0:T(8,128)(2,1)S(1)}, u32[]{:S(2)}, u32[]{:S(2)}) %collective-permute-start.1) | collective-permute-done | bytes 140320 | tf_op jit(solution)/shard_map/ppermute | solution.py:136
  24.0 1.4 copy.88
  25.4 1.4 broadcast_in_dim.143.b_ref
  26.8 1.4 copy.102.w_ref
  30.8 71.0 %all-gather.4.cloned.1.call-done = bf16[2048,4384]{1,0:T(8,128)(2,1)} async-done(((bf16[64,4384]{1,0:T(8,128)(2,1)}), bf16[2048,4384]{1,0:T(8,128)(2,1)}) %all-gather.4.cloned.1.call-update) | async-done | bytes 17956880 | tf_op jit(solution)/shard_map/all_gather | solution.py:143
  101.8 14.0 %fusion = bf16[512,4384]{0,1:T(8,128)(2,1)S(1)} fusion(bf16[2048,4384]{1,0:T(8,128)(2,1)} %all-gather.4.cloned.1.call-done, bf16[1,1,512,2048]{3,2,1,0:T(8,128)(2,1)S(1)} %copy-done), kind=kOutput, calls=%fused_computation.4 | convolution fusion | flops 9196158976 | bytes 24543232 | tf_op jit(solution)/shard_map/dot_general | solution.py:141
  115.8 2.0 fusion.67
  122.5 3.3 %collective-permute-start.3 = (bf16[3,2304]{1,0:T(4,128)(2,1)S(1)}, bf16[3,2304]{1,0:T(4,128)(2,1)S(1)}, u32[]{:S(2)}, u32[]{:S(2)}) collective-permute-start(bf16[3,2304]{1,0:T(4,128)(2,1)S(1)} %copy.86), channel_id=1, source_target_pairs={{0,1},{1,2},{2,3},{4,5},{5,6},{6,7},{8,9},{9,10},{10,11},{12,13},{... | collective-permute-start | bytes 41480 | tf_op jit(solution)/shard_map/ppermute | solution.py:14
  129.5 9.2 %shard_map.113 = bf16[2304,512]{1,0:T(8,128)(2,1)} custom-call(bf16[2304,512]{1,0:T(8,128)(2,1)} %get-tuple-element.21.x_ref, bf16[2304,3]{1,0:T(8,128)(2,1)} %bitcast.202, f32[2304,4]{1,0:T(8,128)} %bitcast.199, f32[2304,1]{1,0:T(8,128)} %broadcast_in_dim.143.b_ref), custom_call_target="tpu_custom_call" | custom-call | flops 16515072 | bytes 4718592 | tf_op jit(solution)/shard_map/pallas_call | solution.py:42
  138.7 2.1 fusion.16
  143.2 3.1 %slice_bitcast_fusion.z_ref = bf16[2048,512]{1,0:T(8,128)(2,1)} fusion(bf16[512,4384]{0,1:T(8,128)(2,1)} %copy-done.4), kind=kLoop, calls=%fused_computation.22 | loop fusion | bytes 4194304 | tf_op jit(solution)/shard_map/transpose | solution.py:205
  146.3 1.5 slice.195
  151.1 4.4 %bitcast_add_fusion.1 = f32[256,32,64]{0,2,1:T(8,128)} fusion(f32[256,32,64]{0,2,1:T(8,128)S(1)} %fusion.25, bf16[256,32,64]{0,2,1:T(8,128)(2,1)S(1)} %bitcast.210, f32[32,256]{1,0:T(8,128)S(1)} %copy-done.14, f32[32,256]{1,0:T(8,128)S(1)} %copy-done.10, f32[256,256]{1,0:T(8,128)S(1)} %fusion.42, pred[256,256]{1,0:T(8,128)(4,1)S(1)} %copy-done.8, ...), kind=kOutput, calls=%fused_computation.29 | convolution fusion | flops 282066944 | bytes 5668864 | tf_op jit(solution)/shard_map/htu,uhp->thp/dot_general | solution.py:99
  155.5 4.3 %bitcast_add_fusion = f32[256,32,64]{0,2,1:T(8,128)} fusion(f32[256,32,64]{0,2,1:T(8,128)S(1)} %fusion.33, bf16[256,32,64]{0,2,1:T(8,128)(2,1)S(1)} %bitcast.209, f32[32,256]{1,0:T(8,128)S(1)} %copy-done.12, f32[32,256]{1,0:T(8,128)S(1)} %copy-done.11, f32[256,256]{1,0:T(8,128)S(1)} %fusion.37, pred[256,256]{1,0:T(8,128)(4,1)S(1)} %copy-done.8, ...), kind=kOutput, calls=%fused_computation.28 | convolution fusion | flops 282066944 | bytes 5668864 | tf_op jit(solution)/shard_map/htu,uhp->thp/dot_general | solution.py:99
  159.8 13.5 %all-gather.6.cloned.1.call-done = bf16[128,8320]{1,0:T(8,128)(2,1)} async-done(((bf16[32,8320]{1,0:T(8,128)(2,1)}), bf16[128,8320]{1,0:T(8,128)(2,1)}) %all-gather.6.cloned.1.call-update) | async-done | bytes 2129936 | tf_op jit(solution)/shard_map/all_gather | solution.py:187
  173.3 2.0 slice_convert_fusion
  176.1 1.5 slice_bitcast_fusion.3
  179.6 7.8 %all-to-all-start = ((f32[1,32,16,128]{3,2,0,1:T(8,128)}), f32[1,32,16,128]{3,2,0,1:T(8,128)}, u32[]{:S(2)}, u32[]{:S(2)}) async-start(f32[1,32,16,128]{3,2,0,1:T(8,128)} %bitcast.208), calls=%async_computation | async-start | bytes 524288 | tf_op jit(solution)/shard_map/all_to_all | solution.py:214
  187.4 1.5 copy.124
  192.0 4.4 %fusion.3 = f32[512,32,64]{0,2,1:T(8,128)} fusion(f32[256,32,64]{0,2,1:T(8,128)S(1)} %copy-done.7, f32[256,32,64]{0,2,1:T(8,128)S(1)} %copy-done.6, bf16[512,32,64]{0,2,1:T(8,128)(2,1)S(1)} %bitcast.197, f32[32,64,128]{2,1,0:T(8,128)S(1)} %fusion.21, f32[32]{0:T(128)S(1)} %copy-done.20, f32[512,32]{0,1:T(8,128)S(1)} %fusion.61, ...), kind=kOutput, calls=%fused_computation.8 | convolution fusion | flops 1616904192 | bytes 11731456 | tf_op jit(solution)/shard_map/tn,hpn->thp/dot_general | solution.py:195
  196.4 6.6 %shard_map.114 = bf16[512,2048]{1,0:T(8,128)(2,1)} custom-call(f32[2048,512]{1,0:T(8,128)} %bitcast.196, bf16[2048,512]{1,0:T(8,128)(2,1)} %slice_bitcast_fusion.z_ref, f32[2048,1]{1,0:T(8,128)} %copy.102.w_ref, f32[1,512]{1,0:T(1,128)} %compare_convert_fusion.mask_ref), custom_call_target="tpu_custom_call" | custom-call | flops 12582912 | bytes 8388608 | tf_op jit(solution)/shard_map/pallas_call | solution.py:70
  203.0 1.3 convolution_bitcast_fusion
  (121 shorter events, 29.5 us)
Async XLA Ops:
  7.2 94.6 %copy-start = (bf16[1,1,512,2048]{3,2,1,0:T(8,128)(2,1)S(1)}, bf16[1,1,512,2048]{3,2,1,0:T(8,128)(2,1)}, u32[]{:S(2)}) copy-start(bf16[1,1,512,2048]{3,2,1,0:T(8,128)(2,1)} %param.10) | copy-start | bytes 6291460
  7.2 94.6 %all-gather.4.cloned.1.call-start = ((), (), s32[]{:S(2)}) async-start(), calls=%async_computation.1 | async-start | bytes 18923520 | tf_op jit(solution)/shard_map/all_gather | solution.py:143
  7.2 6.7 %collective-permute-start = (bf16[64,1096]{1,0:T(8,128)(2,1)}, bf16[64,1096]{1,0:T(8,128)(2,1)S(1)}, u32[]{:S(2)}, u32[]{:S(2)}) collective-permute-start(bf16[64,1096]{1,0:T(8,128)(2,1)} %param.11), channel_id=1, source_target_pairs={{0,1},{1,2},{2,3},{3,0},{4,5},{5,6},{6,7},{7,4},{8,9},{9,10},{10,1... | collective-permute-start | bytes 420872 | tf_op jit(solution)/shard_map/ppermute | solution.py:136
  9.3 9.1 %collective-permute-start.1 = (bf16[64,1096]{1,0:T(8,128)(2,1)}, bf16[64,1096]{1,0:T(8,128)(2,1)S(1)}, u32[]{:S(2)}, u32[]{:S(2)}) collective-permute-start(bf16[64,1096]{1,0:T(8,128)(2,1)} %param.11), channel_id=1, source_target_pairs={{0,2},{1,3},{2,0},{3,1},{4,6},{5,7},{6,4},{7,5},{8,10},{9,11},{10,... | collective-permute-start | bytes 420872 | tf_op jit(solution)/shard_map/ppermute | solution.py:136
  11.8 6.6 %collective-permute-start.2 = (bf16[64,1096]{1,0:T(8,128)(2,1)}, bf16[64,1096]{1,0:T(8,128)(2,1)S(1)}, u32[]{:S(2)}, u32[]{:S(2)}) collective-permute-start(bf16[64,1096]{1,0:T(8,128)(2,1)} %param.11), channel_id=1, source_target_pairs={{0,3},{1,0},{2,1},{3,2},{4,7},{5,4},{6,5},{7,6},{8,11},{9,8},{10,9... | collective-permute-start | bytes 420872 | tf_op jit(solution)/shard_map/ppermute | solution.py:136
  19.4 2.6 %copy-start.18 = (s32[32]{0:T(128)S(1)}, s32[32]{0:T(128)}, u32[]{:S(2)}) copy-start(s32[32]{0:T(128)} %param.19) | copy-start | bytes 388
  19.4 2.6 %copy-start.21 = (s32[32]{0:T(128)S(1)}, s32[32]{0:T(128)}, u32[]{:S(2)}) copy-start(s32[32]{0:T(128)} %param.18) | copy-start | bytes 388
  19.4 4.6 %copy-start.9 = (f32[4,2304]{1,0:T(4,128)S(1)}, f32[4,2304]{1,0:T(4,128)}, u32[]{:S(2)}) copy-start(f32[4,2304]{1,0:T(4,128)} %param.12) | copy-start | bytes 110596
  20.2 5.2 %copy-start.16 = (f32[2304]{0:T(1024)S(1)}, f32[2304]{0:T(1024)}, u32[]{:S(2)}) copy-start(f32[2304]{0:T(1024)} %param.13) | copy-start | bytes 27652
  20.7 6.1 %copy-start.17 = (f32[2048]{0:T(1024)S(1)}, f32[2048]{0:T(1024)}, u32[]{:S(2)}) copy-start(f32[2048]{0:T(1024)} %param.17) | copy-start | bytes 24580
  22.0 8.8 %copy-start.22 = (f32[32]{0:T(128)S(1)}, f32[32]{0:T(128)}, u32[]{:S(2)}) copy-start(f32[32]{0:T(128)} %param.15) | copy-start | bytes 388
  22.0 151.4 %all-gather.6.cloned.1.call-start = ((), (), s32[]{:S(2)}) async-start(), calls=%async_computation.2 | async-start | bytes 2662400 | tf_op jit(solution)/shard_map/all_gather | solution.py:187
  115.8 2.8 %copy-start.4 = (bf16[512,4384]{0,1:T(8,128)(2,1)}, bf16[512,4384]{0,1:T(8,128)(2,1)S(1)}, u32[]{:S(2)}) copy-start(bf16[512,4384]{0,1:T(8,128)(2,1)S(1)} %fusion) | copy-start | bytes 13467652
  115.8 2.8 %copy-start.19 = (f32[32]{0:T(128)S(1)}, f32[32]{0:T(128)}, u32[]{:S(2)}) copy-start(f32[32]{0:T(128)} %param.14) | copy-start | bytes 388
  122.5 5.8 %collective-permute-start.3 = (bf16[3,2304]{1,0:T(4,128)(2,1)S(1)}, bf16[3,2304]{1,0:T(4,128)(2,1)S(1)}, u32[]{:S(2)}, u32[]{:S(2)}) collective-permute-start(bf16[3,2304]{1,0:T(4,128)(2,1)S(1)} %copy.86), channel_id=1, source_target_pairs={{0,1},{1,2},{2,3},{4,5},{5,6},{6,7},{8,9},{9,10},{10,11},{12,13},{... | collective-permute-start | bytes 41480 | tf_op jit(solution)/shard_map/ppermute | solution.py:14
  138.7 2.3 %copy-start.2 = (bf16[2304,512]{1,0:T(8,128)(2,1)S(1)}, bf16[2304,512]{1,0:T(8,128)(2,1)}, u32[]{:S(2)}) copy-start(bf16[2304,512]{1,0:T(8,128)(2,1)} %shard_map.113) | copy-start | bytes 7077892
  151.1 4.4 %copy-start.11 = (f32[32,256]{1,0:T(8,128)S(1)}, f32[32,256]{1,0:T(8,128)}, u32[]{:S(2)}) copy-start(f32[32,256]{1,0:T(8,128)} %get-tuple-element.38) | copy-start | bytes 98308
  151.1 4.4 %copy-start.12 = (f32[32,256]{1,0:T(8,128)S(1)}, f32[32,256]{1,0:T(8,128)}, u32[]{:S(2)}) copy-start(f32[32,256]{1,0:T(8,128)} %get-tuple-element.30) | copy-start | bytes 98308
  151.1 4.4 %copy-start.13 = (f32[256,32]{0,1:T(8,128)S(1)}, f32[256,32]{0,1:T(8,128)}, u32[]{:S(2)}) copy-start(f32[256,32]{0,1:T(8,128)} %get-tuple-element.36) | copy-start | bytes 98308
  179.6 23.4 %all-to-all-start = ((f32[1,32,16,128]{3,2,0,1:T(8,128)}), f32[1,32,16,128]{3,2,0,1:T(8,128)}, u32[]{:S(2)}, u32[]{:S(2)}) async-start(f32[1,32,16,128]{3,2,0,1:T(8,128)} %bitcast.208), calls=%async_computation | async-start | bytes 524288 | tf_op jit(solution)/shard_map/all_to_all | solution.py:214
  189.3 2.1 copy-start.3
  189.3 2.7 %copy-start.6 = (f32[256,32,64]{0,2,1:T(8,128)S(1)}, f32[256,32,64]{0,2,1:T(8,128)}, u32[]{:S(2)}) copy-start(f32[256,32,64]{0,2,1:T(8,128)} %bitcast_add_fusion.1) | copy-start | bytes 6291460
  189.3 2.7 %copy-start.20 = (f32[32]{0:T(128)S(1)}, f32[32]{0:T(128)}, u32[]{:S(2)}) copy-start(f32[32]{0:T(128)} %param.16) | copy-start | bytes 388
  196.4 8.7 %copy-start.1 = (bf16[1,1,512,2048]{3,2,1,0:T(8,128)(2,1)S(1)}, bf16[1,1,512,2048]{3,2,1,0:T(8,128)(2,1)}, u32[]{:S(2)}) copy-start(bf16[1,1,512,2048]{3,2,1,0:T(8,128)(2,1)} %param.10) | copy-start | bytes 6291460
  (6 other events, 6.5 us)
Sparse Core Ops, SparseCore 0:
  22.1 79.5 all-gather.3
  143.3 30.0 all-gather.5
